TPU v7x, 32 devices: a whole 2x2x4 slice. The times are simulated.
32 devices in a mesh: req: 4 (over y, x), exp: 4 (over z), ffn: 2 (over core).
Axes of the slice: x: 2, y: 2, z: 4, core: 2. Of those that a mesh axis runs over, the one named last changes fastest.
Arguments:
- residual: bfloat16 [2048, 2048], P(('req', 'exp')), may hold values from -5 to 5
- queries: bfloat16 [2048, 4608], P(('req', 'exp'), 'ffn'), may hold values from -30 to 30
- new_latent: bfloat16 [2048, 576], P(('req', 'exp')), may hold values from -6 to 6
- cache_pool: bfloat16 [512, 9216], P(('req', 'exp')), may hold values from -5 to 5
- page_table: int32 [8, 64], replicated, may hold values from 0 to 511, as said below
- cached_len: int32 [8], replicated, may hold values from 0 to 1024
- tenant_start: int32 [8], replicated, may hold values from 0 to 512, as said below
- routes: int32 [2048, 6], P(('req', 'exp')), may hold values from 0 to 31, all different within a row; in each aligned block of 64 rows (0 to 63, 64 to 127, ...) at most 16 rows name the same one
- value_up: bfloat16 [512, 1024], P(None, 'ffn'), may hold values from -0.25 to 0.25
- out_proj: bfloat16 [1024, 2048], P('ffn'), may hold values from -0.1875 to 0.1875
- norm_gain: bfloat16 [2048], replicated, may hold values from 0.099609375 to 1.8984375
- router: bfloat16 [2048, 32], replicated, may hold values from -0.125 to 0.125
- gate_weight: bfloat16 [32, 2048, 1408], P('exp', None, 'ffn'), may hold values from -0.125 to 0.125
- up_weight: bfloat16 [32, 2048, 1408], P('exp', None, 'ffn'), may hold values from -0.125 to 0.125
- down_weight: bfloat16 [32, 1408, 2048], P('exp', 'ffn'), may hold values from -0.15625 to 0.15625
Outputs:
- hidden_out: bfloat16 [2048, 2048], P(('req', 'exp'), 'ffn')
- moe_out: bfloat16 [2048, 2048], P(('req', 'exp'), 'ffn')
Inputs may be any that keep to these rules, and one draw needn't show every extreme that they name: `page_table`: row i lists, in order, the pool pages of request i's cache; the 2 requests of group g = i // 2 use pool pages g * 2 * 64 to (g + 1) * 2 * 64 - 1, each exactly once. tenant_start[i] is at most half of cached_len[i]. `routes`: A row names 6 different experts; in each aligned block of 64 rows at most 16 rows name the same expert.
All inputs are finite; a program needn't handle non-finite values.
Results may differ from a plain program's by a relative error of at most 0.025.
Values may be sent and summed in bfloat16 or wider, within the bound.
No kernel may reach another device: no remote copies, remote signals or barrier semaphores. Data moves between devices by JAX's collectives and lax.ppermute only.
A program may use at most 128 MiB of HBM per device.

v0:
```python
import jax
import jax.numpy as jnp
from jax import lax
from jax.sharding import PartitionSpec as P

LATENT = 512
ROPE_DIM = 64
HEAD_DIM = 128
QKD = 576
EXPERTS = 32
TOP = 6
CAPACITY = 16
REQ_GRP = 2
CMAX = 1024


EPSILON = 1e-06
NEG_FILL = -1e30


def slot_numbers(route_block):
    expert_ids = lax.broadcasted_iota(jnp.int32, (1, EXPERTS), 1)
    onehot = (route_block[:, None] == expert_ids).astype(jnp.int32)
    before = jnp.cumsum(onehot, axis=0) - onehot
    return jnp.sum(before * onehot, axis=1)


def local(
    residual,
    queries,
    new_latent,
    cache_pool,
    page_table,
    cached_len,
    tenant_start,
    routes,
    value_up,
    out_proj,
    norm_gain,
    router,
    gate_weight,
    up_weight,
    down_weight,
):
    exp_size = lax.axis_size("exp")
    ffn_size = lax.axis_size("ffn")
    req_index = lax.axis_index("req")
    exp_index = lax.axis_index("exp")
    ffn_index = lax.axis_index("ffn")
    token_rows = residual.shape[0]
    feature_count = residual.shape[1]
    fresh_len = token_rows * exp_size // REQ_GRP
    first_token = (req_index * exp_size + exp_index) * token_rows
    request = first_token // fresh_len
    offset = first_token - request * fresh_len
    pool_all, latent_all = (
        lax.all_gather(cache_pool, "exp", axis=0, tiled=True),
        lax.all_gather(new_latent, "exp", axis=0, tiled=True),
    )
    pool_base = req_index * pool_all.shape[0]
    page_rows = page_table[request] - pool_base
    cached_keys = jnp.take(pool_all, page_rows, axis=0).reshape(CMAX, QKD)
    local_request = request - req_index * REQ_GRP
    fresh_keys = lax.dynamic_slice_in_dim(latent_all, local_request * fresh_len, fresh_len, 0)
    all_keys = jnp.concatenate([cached_keys, fresh_keys], axis=0)
    heads_here = queries.shape[1] // QKD
    query_heads = queries.reshape(token_rows, heads_here, QKD)
    scale_factor = (HEAD_DIM + ROPE_DIM) ** (-0.5)
    scores = (
        jnp.einsum("thd,kd->thk", query_heads, all_keys, preferred_element_type=jnp.float32)
        * scale_factor
    )
    key_pos = lax.broadcasted_iota(jnp.int32, (1, CMAX + fresh_len), 1)
    tok_pos = offset + lax.broadcasted_iota(jnp.int32, (token_rows, 1), 0)
    cached_ok = (key_pos >= tenant_start[request]) & (key_pos < cached_len[request])
    fresh_ok = (key_pos >= CMAX) & (key_pos - CMAX <= tok_pos)
    visible = cached_ok | fresh_ok
    scores = jnp.where(visible[:, None, :], scores, NEG_FILL)
    top_score = jnp.max(scores, axis=2, keepdims=True)
    weights = jnp.exp(scores - top_score)
    attn_probs = (weights / jnp.sum(weights, axis=2, keepdims=True)).astype(jnp.bfloat16)
    latent_out = jnp.einsum(
        "thk,kl->thl", attn_probs, all_keys[:, :LATENT], preferred_element_type=jnp.float32
    ).astype(jnp.bfloat16)
    value_heads = value_up.reshape(LATENT, heads_here, HEAD_DIM)
    head_out = jnp.einsum(
        "thl,lhd->thd", latent_out, value_heads, preferred_element_type=jnp.float32
    )
    head_out = head_out.astype(jnp.bfloat16).reshape(token_rows, heads_here * HEAD_DIM)
    partial_value = jnp.dot(head_out, out_proj, preferred_element_type=jnp.float32)
    block_rows = token_rows // ffn_size
    attn_all = lax.psum(partial_value.astype(jnp.bfloat16), "ffn").astype(jnp.float32)
    hidden = (residual.astype(jnp.float32) + attn_all).astype(jnp.bfloat16)
    blocks = token_rows // block_rows
    hidden_wide = hidden.astype(jnp.float32)
    mean_square = jnp.mean(hidden_wide * hidden_wide, axis=1, keepdims=True)
    normed = (
        hidden_wide * lax.rsqrt(mean_square + EPSILON) * norm_gain.astype(jnp.float32)
    ).astype(jnp.bfloat16)
    logits = jnp.dot(normed, router, preferred_element_type=jnp.float32)
    chosen = jnp.take_along_axis(logits, routes, axis=1)
    raised = jnp.exp(chosen)
    gate_weights = raised / jnp.sum(raised, axis=1, keepdims=True)
    slot_within = jax.vmap(slot_numbers)(routes.reshape(blocks, block_rows * TOP))
    block_base = lax.broadcasted_iota(jnp.int32, (blocks, 1), 0) * CAPACITY
    slot_index = (slot_within + block_base).reshape(token_rows * TOP)
    slot_count = blocks * CAPACITY
    targets = routes.reshape(token_rows * TOP) * slot_count + slot_index
    sender = jnp.zeros((EXPERTS * slot_count, feature_count), jnp.bfloat16)
    sender = (
        sender.at[targets]
        .set(jnp.repeat(normed, TOP, axis=0))
        .reshape(EXPERTS, slot_count, feature_count)
    )
    arrived = lax.all_to_all(sender, "exp", split_axis=0, concat_axis=0, tiled=True)
    local_count = gate_weight.shape[0]
    source_count = arrived.shape[0] // local_count
    item_count = arrived.shape[1]
    grouped = arrived.reshape(source_count, local_count, item_count, feature_count)
    gate_part = jnp.einsum(
        "sjmd,jdf->sjmf", grouped, gate_weight, preferred_element_type=jnp.float32
    )
    up_part = jnp.einsum("sjmd,jdf->sjmf", grouped, up_weight, preferred_element_type=jnp.float32)
    active = (jax.nn.silu(gate_part) * up_part).astype(jnp.bfloat16)
    outputs = jnp.einsum("sjmf,jfd->sjmd", active, down_weight, preferred_element_type=jnp.float32)
    outputs = outputs.reshape(source_count * local_count, item_count, feature_count)
    returned = lax.all_to_all(
        outputs.astype(jnp.bfloat16), "exp", split_axis=0, concat_axis=0, tiled=True
    ).astype(outputs.dtype)
    picked = jnp.take(returned.reshape(EXPERTS * slot_count, feature_count), targets, axis=0)
    picked = picked.reshape(token_rows, TOP, feature_count)
    mixture = jnp.einsum("tk,tkd->td", gate_weights, picked)
    column_count = feature_count // ffn_size
    moe_out = lax.psum_scatter(mixture.astype(jnp.bfloat16), "ffn", scatter_dimension=1, tiled=True)
    hidden_out = lax.dynamic_slice_in_dim(hidden, ffn_index * column_count, column_count, 1)
    return (hidden_out, moe_out)


def solution(mesh):
    in_specs = (
        P(("req", "exp"), None),
        P(("req", "exp"), "ffn"),
        P(("req", "exp"), None),
        P(("req", "exp"), None),
        P(),
        P(),
        P(),
        P(("req", "exp"), None),
        P(None, "ffn"),
        P("ffn", None),
        P(),
        P(),
        P("exp", None, "ffn"),
        P("exp", None, "ffn"),
        P("exp", "ffn", None),
    )
    out_specs = (P(("req", "exp"), "ffn"), P(("req", "exp"), "ffn"))
    return jax.shard_map(local, mesh=mesh, in_specs=in_specs, out_specs=out_specs, check_vma=False)
```

profile of v0, /device:TPU:0, one launch (start us, length us, event | category | flops | bytes accessed | tf_op | source)
XLA Modules:
  0.0 405.0 jit_solution(4807025385626235547)
XLA Ops:
  7.2 0.7 all-gather.2.cloned.1.call-update
  7.9 0.0 all-reduce.2.cloned.1.call-start
  8.0 0.8 copy.27
  8.8 0.1 eq.25
  9.0 0.1 eq.29
  9.1 1.2 dynamic_slice.15
  10.4 1.2 dynamic_slice.16
  11.6 0.7 compare_and_fusion.1
  12.3 0.1 broadcast_in_dim.54
  12.4 0.1 broadcast_in_dim.55
  12.5 0.7 convert_element_type.65
  13.2 0.1 mul.104
  13.3 1.8 reduce-window.6
  15.1 0.1 slice.20
  15.2 0.1 copy.31
  15.3 2.0 copy.41
  17.4 1.1 copy.21
  18.4 0.7 fusion.63
  19.1 1.2 iota_compare_fusion.2
  20.4 32.3 %all_gather.7 = bf16[512,576]{0,1:T(8,128)(2,1)S(1)} all-gather(bf16[128,576]{0,1:T(8,128)(2,1)S(1)} %copy-done.6), channel_id=1, replica_groups=mesh['req'=4,'exp'=4,'ffn'=2] {'exp'}, dimensions={0}, use_global_device_ids=true | all-gather | bytes 737280 | tf_op jit(solution)/shard_map/all_gather | solution.py:58
  52.7 0.7 constant_dynamic-slice_fusion.1
  53.4 1.6 and_or_fusion
  55.0 17.1 %all-gather.2.cloned.1.call-done = bf16[128,9216]{1,0:T(8,128)(2,1)} async-done(((bf16[32,9216]{1,0:T(8,128)(2,1)}), bf16[128,9216]{1,0:T(8,128)(2,1)}) %all-gather.2.cloned.1.call-update) | async-done | bytes 2359312 | tf_op jit(solution)/shard_map/all_gather | solution.py:57
  72.1 5.3 %gather_fusion = bf16[64,9216]{1,0:T(8,128)(2,1)} fusion(bf16[128,9216]{1,0:T(8,128)(2,1)} %all-gather.2.cloned.1.call-done, s32[1024]{0:T(1024)S(1)} %pad_clamp_fusion.1), kind=kCustom, calls=%fused_computation | custom fusion | bytes 2359552 | tf_op jit(solution)/shard_map/jit(_take)/gather | solution.py:62
  77.5 2.2 gather.17
  79.7 1.5 copy.20
  81.2 1.4 broadcast_select_fusion
  82.6 2.9 fusion.76
  85.5 3.9 fusion.17
  89.4 3.9 fusion.42
  93.4 1.3 convolution_convert_fusion
  94.7 0.1 fusion.54
  94.8 0.1 add_bitcast_fusion.1
  94.9 17.4 %all-reduce.2.cloned.1.call-done = bf16[128,2048]{1,0:T(8,128)(2,1)} async-done(((bf16[128,2048]{1,0:T(8,128)(2,1)}), bf16[128,2048]{1,0:T(8,128)(2,1)}) %all-reduce.2.cloned.1.call-update) | async-done | bytes 524304 | tf_op jit(solution)/shard_map/psum | solution.py:92
  112.3 1.3 fusion.45
  113.6 0.2 fusion.47
  113.8 2.6 broadcast_in_dim.62
  116.4 6.3 %reshape.276 = bf16[768,2048]{1,0:T(8,128)(2,1)} reshape(bf16[128,6,2048]{2,1,0:T(8,128)(2,1)} %broadcast_in_dim.62) | data formatting | bytes 6291456 | tf_op jit(solution)/shard_map/reshape | solution.py:112
  122.8 10.6 %scatter_custom_fusion = bf16[1024,2048]{1,0:T(8,128)(2,1)} fusion(s32[768]{0:T(1024)S(1)} %fusion.59, bf16[768,2048]{1,0:T(8,128)(2,1)} %reshape.276, bf16[]{:T(256)} %constant.112.clone.1), kind=kCustom, calls=%fused_computation.33 | custom fusion | bytes 4194816 | tf_op jit(solution)/shard_map/scatter | solution.py:112
  133.4 99.6 %all_to_all.10 = bf16[32,32,2048]{2,1,0:T(8,128)(2,1)} all-to-all(bf16[32,32,2048]{2,1,0:T(8,128)(2,1)} %bitcast.136), channel_id=1, replica_groups=mesh['req'=4,'exp'=4,'ffn'=2] {'exp'}, dimensions={0} | all-to-all | bytes 8388608 | tf_op jit(solution)/shard_map/all_to_all | solution.py:115
  233.0 13.6 %fusion.3 = f32[8,4,32,704]{3,2,1,0:T(8,128)} fusion(bf16[8,2048,704]{1,2,0:T(8,128)(2,1)} %param.28, bf16[4,8,32,2048]{3,2,1,0:T(8,128)(2,1)} %bitcast.137), kind=kOutput, calls=%fused_computation.7 | convolution fusion | flops 2952790016 | bytes 30146560 | tf_op jit(solution)/shard_map/sjmd,jdf->sjmf/dot_general | solution.py:123
  246.6 20.9 %convert_bitcast_fusion = bf16[4,8,32,2048]{3,2,0,1:T(8,128)(2,1)} fusion(bf16[8,704,2048]{2,1,0:T(8,128)(2,1)} %param.29, f32[8,4,32,704]{3,2,1,0:T(8,128)} %fusion.3, bf16[8,2048,704]{1,2,0:T(8,128)(2,1)} %param.27, bf16[4,8,32,2048]{3,2,1,0:T(8,128)(2,1)} %bitcast.138), kind=kOutput, calls=%fused_computation.15 | convolution fusion | flops 5912002560 | bytes 57409536 | tf_op jit(solution)/shard_map/sjmf,jfd->sjmd/dot_general | solution.py:125
  267.5 4.7 %copy.35 = bf16[4,8,32,2048]{3,2,1,0:T(8,128)(2,1)} copy(bf16[4,8,32,2048]{3,2,0,1:T(8,128)(2,1)} %convert_bitcast_fusion) | data formatting | bytes 8388608 | tf_op jit(solution)/shard_map/convert_element_type | solution.py:128
  272.3 5.0 %all-to-all-start.1 = ((bf16[32,32,2048]{2,1,0:T(8,128)(2,1)}), bf16[32,32,2048]{2,1,0:T(8,128)(2,1)}, u32[]{:S(2)}, u32[]{:S(2)}) async-start(bf16[32,32,2048]{2,1,0:T(8,128)(2,1)} %bitcast.135), calls=%async_computation.1 | async-start | bytes 8388608 | tf_op jit(solution)/shard_map/all_to_all | solution.py:127
  277.3 0.0 reduce-scatter.2.cloned.1.call-start
  277.3 0.1 reduce_sum.42
  277.5 0.1 add.167
  277.5 0.1 add.168
  277.6 0.1 copy.25
  277.8 0.1 copy.26
  277.9 0.1 reshape.266
  278.1 0.1 compare_and_fusion
  278.2 0.3 fusion.79
  278.5 5.3 %gather_fusion.2 = f32[768]{0:T(1024)S(1)} fusion(f32[128,32]{0,1:T(8,128)S(1)} %fusion.79, s32[768]{0:T(1024)S(1)} %reshape.266), kind=kCustom, calls=%fused_computation.2 | custom fusion | bytes 12288 | tf_op jit(solution)/shard_map/jit(take_along_axis)/gather | solution.py:101
  283.8 0.1 reshape.269
  283.9 0.1 fusion.75
  284.0 0.1 broadcast_divide_fusion
  284.1 86.1 %all-to-all-done.1 = bf16[32,32,2048]{2,1,0:T(8,128)(2,1)} async-done(((bf16[32,32,2048]{2,1,0:T(8,128)(2,1)}), bf16[32,32,2048]{2,1,0:T(8,128)(2,1)}, u32[]{:S(2)}, u32[]{:S(2)}) %all-to-all-start.1) | async-done | bytes 4194336 | tf_op jit(solution)/shard_map/all_to_all | solution.py:127
  370.2 9.9 %gather_fusion.1 = bf16[768,2048]{1,0:T(8,128)(2,1)} fusion(bf16[1024,2048]{1,0:T(8,128)(2,1)} %bitcast.118, s32[1024]{0:T(1024)S(1)} %pad_clamp_fusion), kind=kCustom, calls=%fused_computation.1 | custom fusion | bytes 6294528 | tf_op jit(solution)/shard_map/jit(_take)/gather | solution.py:130
  380.0 6.3 %gather.20 = bf16[128,6,2048]{2,1,0:T(8,128)(2,1)} reshape(bf16[768,2048]{1,0:T(8,128)(2,1)} %gather_fusion.1) | data formatting | bytes 6291456 | tf_op jit(solution)/shard_map/jit(_take)/gather | solution.py:130
  386.3 3.7 fusion.7
  390.0 1.1 copy.65
  391.1 0.7 constant_dynamic-slice_fusion
  391.8 6.7 %reduce-scatter.2.cloned.1.call-done = bf16[128,1024]{1,0:T(8,128)(2,1)} async-done(((bf16[128,2048]{1,0:T(8,128)(2,1)}), bf16[128,1024]{1,0:T(8,128)(2,1)}) %reduce-scatter.2.cloned.1.call-update) | async-done | bytes 262160 | tf_op jit(solution)/shard_map/reduce_scatter | solution.py:134
  (37 shorter events, 0.2 us)
Async XLA Ops:
  7.2 86.2 %copy-start = (bf16[512,2048]{1,0:T(8,128)(2,1)S(1)}, bf16[512,2048]{1,0:T(8,128)(2,1)}, u32[]{:S(2)}) copy-start(bf16[512,2048]{1,0:T(8,128)(2,1)} %param.24) | copy-start | bytes 6291460
  7.2 10.2 %copy-start.4 = (bf16[128,2304]{1,0:T(8,128)(2,1)S(1)}, bf16[128,2304]{1,0:T(8,128)(2,1)}, u32[]{:S(2)}) copy-start(bf16[128,2304]{1,0:T(8,128)(2,1)} %param.16) | copy-start | bytes 1769476
  7.2 13.2 %copy-start.6 = (bf16[128,576]{0,1:T(8,128)(2,1)S(1)}, bf16[128,576]{0,1:T(8,128)(2,1)}, u32[]{:S(2)}) copy-start(bf16[128,576]{0,1:T(8,128)(2,1)} %param.17) | copy-start | bytes 442372
  7.2 64.9 %all-gather.2.cloned.1.call-start = ((), (), s32[]{:S(2)}) async-start(), calls=%async_computation.3 | async-start | bytes 2949120 | tf_op jit(solution)/shard_map/all_gather | solution.py:57
  7.9 104.4 %all-reduce.2.cloned.1.call-start = ((), (), s32[]{:S(2)}) async-start(), calls=%async_computation.4 | async-start | bytes 1048576 | tf_op jit(solution)/shard_map/psum | solution.py:92
  15.1 57.0 %copy-start.2 = (s32[2,32,3,128]{3,1,2,0:T(8,128)}, s32[2,32,3,128]{3,1,2,0:T(8,128)S(1)}, u32[]{:S(2)}) copy-start(s32[2,32,3,128]{3,1,2,0:T(8,128)S(1)} %reduce-window.6) | copy-start | bytes 294916
  93.4 1.4 copy-start.3
  93.4 18.9 %copy-start.5 = (bf16[128,2048]{1,0:T(8,128)(2,1)S(1)}, bf16[128,2048]{1,0:T(8,128)(2,1)}, u32[]{:S(2)}) copy-start(bf16[128,2048]{1,0:T(8,128)(2,1)} %param.15) | copy-start | bytes 1572868
  272.3 5.3 %copy-start.8 = (s32[128,6]{0,1:T(8,128)S(1)}, s32[128,6]{0,1:T(8,128)}, u32[]{:S(2)}) copy-start(s32[128,6]{0,1:T(8,128)} %param.22) | copy-start | bytes 9220
  272.3 5.9 %copy-start.7 = (bf16[2048,32]{0,1:T(8,128)(2,1)S(1)}, bf16[2048,32]{0,1:T(8,128)(2,1)}, u32[]{:S(2)}) copy-start(bf16[2048,32]{0,1:T(8,128)(2,1)} %param.26) | copy-start | bytes 393220
  272.3 97.9 %all-to-all-start.1 = ((bf16[32,32,2048]{2,1,0:T(8,128)(2,1)}), bf16[32,32,2048]{2,1,0:T(8,128)(2,1)}, u32[]{:S(2)}, u32[]{:S(2)}) async-start(bf16[32,32,2048]{2,1,0:T(8,128)(2,1)} %bitcast.135), calls=%async_computation.1 | async-start | bytes 8388608 | tf_op jit(solution)/shard_map/all_to_all | solution.py:127
  277.3 121.2 %reduce-scatter.2.cloned.1.call-start = ((), (), s32[]{:S(2)}) async-start(), calls=%async_computation.5 | async-start | bytes 786432 | tf_op jit(solution)/shard_map/reduce_scatter | solution.py:134
  386.3 12.2 %copy-start.1 = (bf16[512,2048]{1,0:T(8,128)(2,1)S(1)}, bf16[512,2048]{1,0:T(8,128)(2,1)}, u32[]{:S(2)}) copy-start(bf16[512,2048]{1,0:T(8,128)(2,1)} %param.24) | copy-start | bytes 6291460
Sparse Core Ops, SparseCore 0:
  9.6 62.4 all-gather.1
  94.8 17.4 all-reduce.1
  391.2 7.2 reduce-scatter.1
where the time goes:
time: 406 us; the launch traced here: 405 us
  blocking collectives  132 us (33%)
  waiting for transfers between devices  128 us (32%)
  local copies, waits for them, and re-layouts  65.3 us (16%)
  matrix products  50.6 us (12%)
  between operations  14 us (3%)
  other arithmetic  10.2 us (3%)
  starting transfers between devices  5.11 us (1%)
    all_to_all x1, blocking collectives, local(): lax.all_to_all(sender, 'exp', split_axis=0, concat_axis=0, tiled=True)  99.6 us
    all_to_all x1, waiting for transfers between devices, local(): lax.all_to_all(outputs.astype(jnp.bfloat16), 'exp', split_axis=0, concat_...  86.1 us
    all_gather x1, blocking collectives, local(): lax.all_gather(new_latent, 'exp', axis=0, tiled=True)  32.3 us
    dot_general x1, matrix products, local(): jnp.einsum('sjmf,jfd->sjmd', active, down_weight, preferred_element_type=...  20.9 us
    psum x1, waiting for transfers between devices, local(): lax.psum(partial_value.astype(jnp.bfloat16), 'ffn').astype(jnp.float32)  17.4 us
    all_gather x1, waiting for transfers between devices, local(): lax.all_gather(cache_pool, 'exp', axis=0, tiled=True)  17.1 us
    gather x2, local copies, waits for them, and re-layouts, local(): jnp.take(returned.reshape(EXPERTS * slot_count, feature_count), targets,...  16.1 us
    dot_general x1, matrix products, local(): jnp.einsum('sjmd,jdf->sjmf', grouped, up_weight, preferred_element_type=j...  13.6 us
  transfers between devices with their start and end apart: 4, of which 4 were waited for; matrix products, arithmetic and copies ran while one was open for 6% of the time, Pallas kernels for 0%

commit v1 on v0

--- a/solution.py
+++ b/solution.py
@@ -12,6 +12,7 @@
 CAPACITY = 16
 REQ_GRP = 2
 CMAX = 1024
+BLOCK_ROWS = 64
 
 
 EPSILON = 1e-06
@@ -88,51 +89,68 @@
     )
     head_out = head_out.astype(jnp.bfloat16).reshape(token_rows, heads_here * HEAD_DIM)
     partial_value = jnp.dot(head_out, out_proj, preferred_element_type=jnp.float32)
-    block_rows = token_rows // ffn_size
-    attn_all = lax.psum(partial_value.astype(jnp.bfloat16), "ffn").astype(jnp.float32)
-    hidden = (residual.astype(jnp.float32) + attn_all).astype(jnp.bfloat16)
-    blocks = token_rows // block_rows
-    hidden_wide = hidden.astype(jnp.float32)
-    mean_square = jnp.mean(hidden_wide * hidden_wide, axis=1, keepdims=True)
-    normed = (
-        hidden_wide * lax.rsqrt(mean_square + EPSILON) * norm_gain.astype(jnp.float32)
+    column_count = feature_count // ffn_size
+    attn_cols = lax.psum_scatter(
+        partial_value.astype(jnp.bfloat16), "ffn", scatter_dimension=1, tiled=True
+    ).astype(jnp.float32)
+    residual_cols = lax.dynamic_slice_in_dim(residual, ffn_index * column_count, column_count, 1)
+    hidden_out = (residual_cols.astype(jnp.float32) + attn_cols).astype(jnp.bfloat16)
+    hidden_wide = hidden_out.astype(jnp.float32)
+    square_sum = lax.psum(jnp.sum(hidden_wide * hidden_wide, axis=1, keepdims=True), "ffn")
+    mean_square = square_sum / feature_count
+    gain_cols = lax.dynamic_slice_in_dim(norm_gain, ffn_index * column_count, column_count, 0)
+    normed_cols = (
+        hidden_wide * lax.rsqrt(mean_square + EPSILON) * gain_cols.astype(jnp.float32)
     ).astype(jnp.bfloat16)
-    logits = jnp.dot(normed, router, preferred_element_type=jnp.float32)
-    chosen = jnp.take_along_axis(logits, routes, axis=1)
+    normed_grid = lax.all_gather(normed_cols, ("exp", "ffn"), axis=0, tiled=False)
+    normed_grid = normed_grid.reshape(exp_size, ffn_size, token_rows, column_count)
+    group_rows = exp_size * token_rows
+    routes_all = lax.all_gather(routes, "exp", axis=0, tiled=True)
+    logits = jnp.einsum(
+        "efrc,fck->erk",
+        normed_grid,
+        router.reshape(ffn_size, column_count, EXPERTS),
+        preferred_element_type=jnp.float32,
+    ).reshape(group_rows, EXPERTS)
+    chosen = jnp.take_along_axis(logits, routes_all, axis=1)
     raised = jnp.exp(chosen)
     gate_weights = raised / jnp.sum(raised, axis=1, keepdims=True)
-    slot_within = jax.vmap(slot_numbers)(routes.reshape(blocks, block_rows * TOP))
+    blocks = group_rows // BLOCK_ROWS
+    slot_within = jax.vmap(slot_numbers)(routes_all.reshape(blocks, BLOCK_ROWS * TOP))
     block_base = lax.broadcasted_iota(jnp.int32, (blocks, 1), 0) * CAPACITY
-    slot_index = (slot_within + block_base).reshape(token_rows * TOP)
+    slot_index = (slot_within + block_base).reshape(group_rows * TOP)
     slot_count = blocks * CAPACITY
-    targets = routes.reshape(token_rows * TOP) * slot_count + slot_index
-    sender = jnp.zeros((EXPERTS * slot_count, feature_count), jnp.bfloat16)
-    sender = (
-        sender.at[targets]
-        .set(jnp.repeat(normed, TOP, axis=0))
-        .reshape(EXPERTS, slot_count, feature_count)
+    local_count = gate_weight.shape[0]
+    total_slots = local_count * slot_count
+    local_expert = routes_all.reshape(group_rows * TOP) - exp_index * local_count
+    is_local = (local_expert >= 0) & (local_expert < local_count)
+    local_target = jnp.where(is_local, local_expert * slot_count + slot_index, total_slots)
+    token_ids = lax.broadcasted_iota(jnp.int32, (group_rows, TOP), 0).reshape(group_rows * TOP)
+    slot_token = jnp.zeros((total_slots,), jnp.int32).at[local_target].set(token_ids, mode="drop")
+    slot_weight = (
+        jnp.zeros((total_slots,), jnp.float32)
+        .at[local_target]
+        .set(gate_weights.reshape(group_rows * TOP), mode="drop")
     )
-    arrived = lax.all_to_all(sender, "exp", split_axis=0, concat_axis=0, tiled=True)
-    local_count = gate_weight.shape[0]
-    source_count = arrived.shape[0] // local_count
-    item_count = arrived.shape[1]
-    grouped = arrived.reshape(source_count, local_count, item_count, feature_count)
-    gate_part = jnp.einsum(
-        "sjmd,jdf->sjmf", grouped, gate_weight, preferred_element_type=jnp.float32
+    grouped = normed_grid[slot_token // token_rows, :, slot_token % token_rows, :]
+    grouped = grouped.reshape(local_count, slot_count, feature_count)
+    gate_part = jnp.einsum("jmd,jdf->jmf", grouped, gate_weight, preferred_element_type=jnp.float32)
+    up_part = jnp.einsum("jmd,jdf->jmf", grouped, up_weight, preferred_element_type=jnp.float32)
+    active = (jax.nn.silu(gate_part) * up_part).astype(jnp.bfloat16)
+    outputs = jnp.einsum("jmf,jfd->jmd", active, down_weight, preferred_element_type=jnp.float32)
+    weighted = (outputs.reshape(total_slots, feature_count) * slot_weight[:, None]).astype(
+        jnp.bfloat16
     )
-    up_part = jnp.einsum("sjmd,jdf->sjmf", grouped, up_weight, preferred_element_type=jnp.float32)
-    active = (jax.nn.silu(gate_part) * up_part).astype(jnp.bfloat16)
-    outputs = jnp.einsum("sjmf,jfd->sjmd", active, down_weight, preferred_element_type=jnp.float32)
-    outputs = outputs.reshape(source_count * local_count, item_count, feature_count)
-    returned = lax.all_to_all(
-        outputs.astype(jnp.bfloat16), "exp", split_axis=0, concat_axis=0, tiled=True
-    ).astype(outputs.dtype)
-    picked = jnp.take(returned.reshape(EXPERTS * slot_count, feature_count), targets, axis=0)
-    picked = picked.reshape(token_rows, TOP, feature_count)
-    mixture = jnp.einsum("tk,tkd->td", gate_weights, picked)
-    column_count = feature_count // ffn_size
-    moe_out = lax.psum_scatter(mixture.astype(jnp.bfloat16), "ffn", scatter_dimension=1, tiled=True)
-    hidden_out = lax.dynamic_slice_in_dim(hidden, ffn_index * column_count, column_count, 1)
+    row_ids = lax.broadcasted_iota(jnp.int32, (group_rows, 1), 0)
+    onehot = (slot_token[None, :] == row_ids).astype(jnp.bfloat16)
+    mixture = jnp.einsum(
+        "ers,sfc->efrc",
+        onehot.reshape(exp_size, token_rows, total_slots),
+        weighted.reshape(total_slots, ffn_size, column_count),
+        preferred_element_type=jnp.float32,
+    ).astype(jnp.bfloat16)
+    mixture = mixture.reshape(exp_size * ffn_size * token_rows, column_count)
+    moe_out = lax.psum_scatter(mixture, ("exp", "ffn"), scatter_dimension=0, tiled=True)
     return (hidden_out, moe_out)
 
 

time: 406 us -> 306 us (0.75)
  blocking collectives: 132 us -> 49 us
  waiting for transfers between devices: 128 us -> 66.3 us
  local copies, waits for them, and re-layouts: 65.3 us -> 109 us
  other arithmetic: 10.2 us -> 15.6 us
  starting transfers between devices: 5.11 us -> 0.16 us
    all_to_all x1 -> x0, blocking collectives: 99.6 us -> none  [local(): lax.all_to_all(sender, 'exp', split_axis=0, concat_axis=0, tiled=True)]
    all_to_all x1 -> x0, waiting for transfers between devices: 86.1 us -> none  [local(): lax.all_to_all(outputs.astype(jnp.bfloat16), 'exp', split_axis=0, concat_...]
    reduce_scatter x1 -> x2, waiting for transfers between devices: 6.69 us -> 44.5 us  [the longest x1 37.5 us: local(): lax.psum_scatter(mixture, ('exp', 'ffn'), scatter_dimension=0, tiled=True)]
    gather x5 -> x4, local copies, waits for them, and re-layouts: 21.7 us -> 43.7 us  [the longest x3 25.3 us: local(): chosen = jnp.take_along_axis(logits, routes_all, axis=1)]
    psum x1 -> x0, waiting for transfers between devices: 17.4 us -> none  [local(): lax.psum(partial_value.astype(jnp.bfloat16), 'ffn').astype(jnp.float32)]
    all_gather x0 -> x1, blocking collectives: none -> 15.2 us  [local(): routes_all = lax.all_gather(routes, 'exp', axis=0, tiled=True)]
    scatter x1 -> x2, local copies, waits for them, and re-layouts: 10.6 us -> 23.8 us  [the longest x1 12 us: local(): slot_weight = jnp.zeros((total_slots,), jnp.float32).at[local_target].set...]
    reshape x1 -> x3, local copies, waits for them, and re-layouts: 6.31 us -> 13.1 us  [the longest x1 7.79 us: local(): grouped = grouped.reshape(local_count, slot_count, feature_count)]
  transfers between devices with their start and end apart: 4 -> 4, of which waited for: 4 -> 3; matrix products, arithmetic and copies ran while one was open for 6% -> 10% of each run, Pallas kernels for 0% -> 0%
where the time goes in v1:
time: 306 us; the launch traced here: 305 us
  local copies, waits for them, and re-layouts  109 us (36%)
  waiting for transfers between devices  66.3 us (22%)
  matrix products  51.3 us (17%)
  blocking collectives  49 us (16%)
  other arithmetic  15.6 us (5%)
  between operations  14.1 us (5%)
    reduce_scatter x1, waiting for transfers between devices, local(): lax.psum_scatter(mixture, ('exp', 'ffn'), scatter_dimension=0, tiled=True)  37.5 us
    all_gather x1, blocking collectives, local(): lax.all_gather(new_latent, 'exp', axis=0, tiled=True)  31.2 us
    gather x3, local copies, waits for them, and re-layouts, local(): chosen = jnp.take_along_axis(logits, routes_all, axis=1)  25.3 us
    all_gather x1, waiting for transfers between devices, local(): lax.all_gather(cache_pool, 'exp', axis=0, tiled=True)  21.1 us
    dot_general x1, matrix products, local(): jnp.einsum('jmf,jfd->jmd', active, down_weight, preferred_element_type=jn...  20.7 us
    gather x1, local copies, waits for them, and re-layouts, local(): normed_grid[slot_token // token_rows, :, slot_token % token_rows, :]  18.4 us
    all_gather x1, blocking collectives, local(): routes_all = lax.all_gather(routes, 'exp', axis=0, tiled=True)  15.2 us
    dot_general x1, matrix products, local(): jnp.einsum('jmd,jdf->jmf', grouped, gate_weight, preferred_element_type=j...  13.1 us
  transfers between devices with their start and end apart: 4, of which 3 were waited for; matrix products, arithmetic and copies ran while one was open for 10% of the time, Pallas kernels for 0%

profile of v1, /device:TPU:0, one launch (start us, length us, event | category | flops | bytes accessed | tf_op | source)
XLA Modules:
  0.0 305.0 jit_solution(3223588927788097875)
XLA Ops:
  7.2 0.0 all-gather.4.cloned.1.call-start
  7.3 0.7 all-gather.4.cloned.1.call-update
  7.9 0.0 reduce-scatter.3.cloned.1.call-start
  8.0 2.0 copy.36
  10.1 0.7 compare_and_fusion.1
  10.8 0.1 broadcast_in_dim.56
  10.8 0.1 broadcast_in_dim.57
  10.9 2.1 copy.24
  13.1 0.6 dynamic_slice.20
  13.6 0.6 dynamic_slice.19
  14.2 0.7 fusion.61
  14.9 1.3 iota_compare_fusion.2
  16.3 31.2 %all_gather.16 = bf16[512,576]{0,1:T(8,128)(2,1)S(1)} all-gather(bf16[128,576]{0,1:T(8,128)(2,1)S(1)} %copy-done.4), channel_id=1, replica_groups=mesh['req'=4,'exp'=4,'ffn'=2] {'exp'}, dimensions={0}, use_global_device_ids=true | all-gather | bytes 737280 | tf_op jit(solution)/shard_map/all_gather | solution.py:59
  47.5 0.7 constant_dynamic-slice_fusion
  48.2 1.6 and_or_fusion
  49.9 21.1 %all-gather.4.cloned.1.call-done = bf16[128,9216]{1,0:T(8,128)(2,1)} async-done(((bf16[32,9216]{1,0:T(8,128)(2,1)}), bf16[128,9216]{1,0:T(8,128)(2,1)}) %all-gather.4.cloned.1.call-update) | async-done | bytes 2359312 | tf_op jit(solution)/shard_map/all_gather | solution.py:58
  70.9 5.3 %gather_fusion = bf16[64,9216]{1,0:T(8,128)(2,1)} fusion(bf16[128,9216]{1,0:T(8,128)(2,1)} %all-gather.4.cloned.1.call-done, s32[1024]{0:T(1024)S(1)} %pad_clamp_fusion), kind=kCustom, calls=%fused_computation | custom fusion | bytes 2359552 | tf_op jit(solution)/shard_map/jit(_take)/gather | solution.py:63
  76.3 2.2 gather.14
  78.5 1.5 copy.23
  80.0 1.4 broadcast_select_fusion
  81.4 3.0 fusion.72
  84.4 3.9 %fusion.5 = f32[128,4,1280]{0,2,1:T(8,128)} fusion(bf16[128,4,576]{0,2,1:T(8,128)(2,1)} %bitcast.110, bf16[256,576]{0,1:T(8,128)(2,1)} %constant_dynamic-slice_fusion, bf16[1024,576]{0,1:T(8,128)(2,1)S(1)} %broadcast_select_fusion, pred[128,1280]{0,1:T(8,128)(4,1)S(1)} %copy-done.3), kind=kOutput, calls=%fused_computation.12 | convolution fusion | flops 759234560 | bytes 4849664 | tf_op jit(solution)/shard_map/thd,kd->thk/dot_general | solution.py:71
  88.3 3.9 %fusion.27 = bf16[4,128,128]{1,2,0:T(8,128)(2,1)S(1)} fusion(bf16[512,4,128]{0,2,1:T(8,128)(2,1)} %bitcast.111, bf16[1024,576]{0,1:T(8,128)(2,1)S(1)} %broadcast_select_fusion, bf16[256,576]{0,1:T(8,128)(2,1)} %constant_dynamic-slice_fusion, f32[128,4]{0,1:T(4,128)S(1)} %fusion.72, f32[128,4,1280]{0,2,1:T(8,128)} %fusion.5), kind=kOutput, calls=%fused_computation.32 | convolution fusion | flops 743114496 | bytes 7374848 | tf_op jit(solution)/shard_map/thl,lhd->thd/dot_general | solution.py:87
  92.2 1.3 convolution_convert_fusion
  93.5 0.0 all-gather.6.cloned.1.call-start
  93.6 7.0 %reduce-scatter.3.cloned.1.call-done = bf16[128,1024]{1,0:T(8,128)(2,1)} async-done(((bf16[128,2048]{1,0:T(8,128)(2,1)}), bf16[128,1024]{1,0:T(8,128)(2,1)}) %reduce-scatter.3.cloned.1.call-update) | async-done | bytes 262160 | tf_op jit(solution)/shard_map/reduce_scatter | solution.py:93
  100.6 1.1 fusion.32
  101.8 2.5 psum.7
  104.2 0.8 fusion.34
  105.1 0.0 reduce-scatter.5.cloned.1.call-start
  105.2 0.1 copy.26
  105.3 15.2 %all_gather.19 = s32[512,6]{1,0:T(8,128)S(1)} all-gather(s32[128,6]{1,0:T(8,128)S(1)} %copy.26), channel_id=1, replica_groups=mesh['req'=4,'exp'=4,'ffn'=2] {'exp'}, dimensions={0}, use_global_device_ids=true | all-gather | bytes 15360 | tf_op jit(solution)/shard_map/all_gather | solution.py:108
  120.5 0.2 eq.51
  120.7 0.2 eq.55
  120.9 0.1 compare_and_fusion
  120.9 0.2 and.69
  121.2 0.2 mul.120
  121.4 6.9 %reduce-window.6 = s32[8,32,3,128]{3,1,2,0:T(8,128)S(1)} reduce-window(s32[8,32,3,128]{3,1,2,0:T(8,128)S(1)} %fusion.38, s32[]{:T(128)} %constant.65.clone.1), window={size=1x1x1x128 pad=0_0x0_0x0_0x127_0}, to_apply=%region_5.6 | reduce-window | flops 12484608 | bytes 786436 | tf_op jit(solution)/shard_map/reduce-window
  128.4 0.2 slice.20
  128.5 0.2 copy.27
  128.7 0.1 fusion.43
  128.9 0.2 fusion.37
  129.1 0.1 add_bitcast_fusion.1
  129.2 0.1 bitcast_or_fusion
  129.3 0.2 reshape.297
  129.5 0.2 reshape.307
  129.7 11.8 %scatter_custom_fusion = s32[1024]{0:T(1024)S(1)} fusion(s32[3072]{0:T(1024)S(1)} %bitcast.115, s32[3072]{0:T(1024)S(1)} %reshape.307, s32[]{:T(128)} %constant.65.clone.1), kind=kCustom, calls=%fused_computation.89 | custom fusion | bytes 4100 | tf_op jit(solution)/shard_map/scatter | solution.py:129
  141.5 1.8 copy.31
  143.3 0.7 convolution_bitcast_fusion
  144.0 24.9 %gather_fusion.2 = f32[3072]{0:T(1024)S(1)} fusion(f32[512,32]{0,1:T(8,128)S(1)} %convolution_bitcast_fusion, s32[3072]{0:T(1024)S(1)} %reshape.297), kind=kCustom, calls=%fused_computation.2 | custom fusion | bytes 49152 | tf_op jit(solution)/shard_map/jit(take_along_axis)/gather | solution.py:115
  168.9 0.2 reshape.300
  169.1 0.2 fusion.46
  169.3 0.1 broadcast_divide_fusion
  169.5 0.2 reshape.315
  169.6 5.1 %copy.30 = bf16[4,2,128,1024]{3,1,2,0:T(2,128)(2,1)} copy(bf16[4,2,128,1024]{3,2,1,0:T(8,128)(2,1)} %bitcast.105) | data formatting | bytes 4194304 | tf_op jit(solution)/shard_map/reshape | solution.py:106
  174.7 18.4 %gather_fusion.1 = bf16[1024,2,1024]{2,1,0:T(2,128)(2,1)} fusion(bf16[4,2,128,1024]{3,1,2,0:T(2,128)(2,1)} %copy.30, s32[1024]{0:T(1024)S(1)} %fusion.49), kind=kCustom, calls=%fused_computation.1 | custom fusion | bytes 8396800 | tf_op jit(solution)/shard_map/gather | solution.py:135
  193.2 7.8 %reshape.279 = bf16[8,128,2048]{2,1,0:T(8,128)(2,1)} reshape(bf16[1024,2,1024]{2,1,0:T(2,128)(2,1)} %gather_fusion.1) | data formatting | bytes 8388608 | tf_op jit(solution)/shard_map/reshape | solution.py:136
  201.0 12.0 %scatter_custom_fusion.1 = f32[1024]{0:T(1024)S(1)} fusion(s32[3072]{0:T(1024)S(1)} %bitcast.116, f32[3072]{0:T(1024)S(1)} %reshape.315, f32[]{:T(128)} %constant.118.clone.1), kind=kCustom, calls=%fused_computation.92 | custom fusion | bytes 4100 | tf_op jit(solution)/shard_map/scatter | solution.py:133
  213.0 13.1 %fusion.75 = f32[8,128,704]{1,2,0:T(8,128)} fusion(bf16[8,128,2048]{2,1,0:T(8,128)(2,1)} %reshape.279, bf16[8,2048,704]{1,2,0:T(8,128)(2,1)} %param.27), kind=kOutput, calls=%fused_computation.111 | convolution fusion | flops 2952790016 | bytes 30146560 | tf_op jit(solution)/shard_map/jmd,jdf->jmf/dot_general | solution.py:137
  226.1 20.7 %multiply_convert_fusion = bf16[8,128,2048]{2,1,0:T(8,128)(2,1)} fusion(f32[8,128]{1,0:T(8,128)S(1)} %bitcast.117, bf16[8,704,2048]{2,1,0:T(8,128)(2,1)} %param.29, f32[8,128,704]{1,2,0:T(8,128)} %fusion.75, bf16[8,128,2048]{2,1,0:T(8,128)(2,1)} %reshape.279, bf16[8,2048,704]{1,2,0:T(8,128)(2,1)} %param.28), kind=kOutput, calls=%fused_computation.6 | convolution fusion | flops 5914099712 | bytes 57413632 | tf_op jit(solution)/shard_map/jmf,jfd->jmd/dot_general | solution.py:140
  246.8 7.8 %convert_element_type.72 = bf16[1024,2,1024]{2,1,0:T(2,128)(2,1)} reshape(bf16[8,128,2048]{2,1,0:T(8,128)(2,1)} %multiply_convert_fusion) | data formatting | bytes 8388608 | tf_op jit(solution)/shard_map/convert_element_type | solution.py:141
  254.6 4.8 %convert_bitcast_fusion = bf16[4,2,128,1024]{3,2,0,1:T(8,128)(2,1)S(1)} fusion(bf16[1024,2,1024,1]{2,1,0,3:T(2,128)(2,1)} %bitcast.108, s32[4,128]{1,0:T(4,128)S(1)} %multiply_add_fusion, s32[1024]{0:T(1024)S(1)} %scatter_custom_fusion), kind=kOutput, calls=%fused_computation.17 | convolution fusion | flops 2149056512 | bytes 6297600 | tf_op jit(solution)/shard_map/ers,sfc->efrc/dot_general | solution.py:146
  259.3 1.6 copy.34
  261.0 37.5 %reduce-scatter.5.cloned.1.call-done = bf16[128,1024]{1,0:T(8,128)(2,1)} async-done(((bf16[1024,1024]{1,0:T(8,128)(2,1)}), bf16[128,1024]{1,0:T(8,128)(2,1)}) %reduce-scatter.5.cloned.1.call-update) | async-done | bytes 262160 | tf_op jit(solution)/shard_map/reduce_scatter | solution.py:153
  (41 shorter events, 0.3 us)
Async XLA Ops:
  7.2 85.1 %copy-start = (bf16[512,2048]{1,0:T(8,128)(2,1)S(1)}, bf16[512,2048]{1,0:T(8,128)(2,1)}, u32[]{:S(2)}) copy-start(bf16[512,2048]{1,0:T(8,128)(2,1)} %param.24) | copy-start | bytes 6291460
  7.2 5.9 %copy-start.9 = (s32[8]{0:T(128)S(1)}, s32[8]{0:T(128)}, u32[]{:S(2)}) copy-start(s32[8]{0:T(128)} %param.20) | copy-start | bytes 100
  7.2 6.5 %copy-start.10 = (s32[8]{0:T(128)S(1)}, s32[8]{0:T(128)}, u32[]{:S(2)}) copy-start(s32[8]{0:T(128)} %param.21) | copy-start | bytes 100
  7.2 9.1 %copy-start.4 = (bf16[128,576]{0,1:T(8,128)(2,1)S(1)}, bf16[128,576]{0,1:T(8,128)(2,1)}, u32[]{:S(2)}) copy-start(bf16[128,576]{0,1:T(8,128)(2,1)} %param.17) | copy-start | bytes 442372
  7.2 63.7 %all-gather.4.cloned.1.call-start = ((), (), s32[]{:S(2)}) async-start(), calls=%async_computation.2 | async-start | bytes 2949120 | tf_op jit(solution)/shard_map/all_gather | solution.py:58
  7.9 92.7 %reduce-scatter.3.cloned.1.call-start = ((), (), s32[]{:S(2)}) async-start(), calls=%async_computation.3 | async-start | bytes 786432 | tf_op jit(solution)/shard_map/reduce_scatter | solution.py:93
  81.4 3.0 copy-start.3
  92.2 1.4 copy-start.8
  92.2 8.4 %copy-start.6 = (bf16[128,2048]{1,0:T(8,128)(2,1)S(1)}, bf16[128,2048]{1,0:T(8,128)(2,1)}, u32[]{:S(2)}) copy-start(bf16[128,2048]{1,0:T(8,128)(2,1)} %param.15) | copy-start | bytes 1572868
  92.2 12.9 %copy-start.7 = (s32[128,6]{0,1:T(8,128)S(1)}, s32[128,6]{0,1:T(8,128)}, u32[]{:S(2)}) copy-start(s32[128,6]{0,1:T(8,128)} %param.22) | copy-start | bytes 9220
  93.5 48.0 %all-gather.6.cloned.1.call-start = ((), (), s32[]{:S(2)}) async-start(), calls=%async_computation.5 | async-start | bytes 2359296 | tf_op jit(solution)/shard_map/all_gather | solution.py:105
  101.8 27.0 %copy-start.2 = (bf16[128,1024]{1,0:T(8,128)(2,1)}, bf16[128,1024]{1,0:T(8,128)(2,1)S(1)}, u32[]{:S(2)}) copy-start(bf16[128,1024]{1,0:T(8,128)(2,1)S(1)} %get-tuple-element.3) | copy-start | bytes 786436
  105.1 193.3 %reduce-scatter.5.cloned.1.call-start = ((), (), s32[]{:S(2)}) async-start(), calls=%async_computation.4 | async-start | bytes 2359296 | tf_op jit(solution)/shard_map/reduce_scatter | solution.py:153
  129.2 14.0 %copy-start.5 = (bf16[2048,32]{0,1:T(8,128)(2,1)S(1)}, bf16[2048,32]{0,1:T(8,128)(2,1)}, u32[]{:S(2)}) copy-start(bf16[2048,32]{0,1:T(8,128)(2,1)} %param.26) | copy-start | bytes 393220
  254.6 43.9 %copy-start.1 = (bf16[512,2048]{1,0:T(8,128)(2,1)S(1)}, bf16[512,2048]{1,0:T(8,128)(2,1)}, u32[]{:S(2)}) copy-start(bf16[512,2048]{1,0:T(8,128)(2,1)} %param.24) | copy-start | bytes 6291460
Sparse Core Ops, SparseCore 0:
  9.6 61.2 all-gather.3
  93.6 6.9 reduce-scatter.2
  105.2 31.7 all-gather.5
  261.1 37.2 reduce-scatter.4

commit v2 on v1

--- a/solution.py
+++ b/solution.py
@@ -17,13 +17,6 @@
 
 EPSILON = 1e-06
 NEG_FILL = -1e30
-
-
-def slot_numbers(route_block):
-    expert_ids = lax.broadcasted_iota(jnp.int32, (1, EXPERTS), 1)
-    onehot = (route_block[:, None] == expert_ids).astype(jnp.int32)
-    before = jnp.cumsum(onehot, axis=0) - onehot
-    return jnp.sum(before * onehot, axis=1)
 
 
 def local(
@@ -54,9 +47,29 @@
     first_token = (req_index * exp_size + exp_index) * token_rows
     request = first_token // fresh_len
     offset = first_token - request * fresh_len
-    pool_all, latent_all = (
-        lax.all_gather(cache_pool, "exp", axis=0, tiled=True),
-        lax.all_gather(new_latent, "exp", axis=0, tiled=True),
+    pool_pages = cache_pool.shape[0]
+    page_width = cache_pool.shape[1]
+    latent_pages = token_rows * QKD // page_width
+    route_count = token_rows * TOP
+    route_pages = -(-route_count // page_width)
+    route_rows = jnp.pad(
+        routes.reshape(route_count).astype(jnp.bfloat16),
+        (0, route_pages * page_width - route_count),
+    ).reshape(route_pages, page_width)
+    packed = jnp.concatenate(
+        [cache_pool, new_latent.reshape(latent_pages, page_width), route_rows], axis=0
+    )
+    gathered = lax.all_gather(packed, "exp", axis=0, tiled=False)
+    pool_all = gathered[:, :pool_pages].reshape(exp_size * pool_pages, page_width)
+    latent_all = gathered[:, pool_pages : pool_pages + latent_pages].reshape(
+        exp_size * token_rows, QKD
+    )
+    group_rows = exp_size * token_rows
+    routes_all = (
+        gathered[:, pool_pages + latent_pages :]
+        .reshape(exp_size, route_pages * page_width)[:, :route_count]
+        .reshape(group_rows, TOP)
+        .astype(jnp.int32)
     )
     pool_base = req_index * pool_all.shape[0]
     page_rows = page_table[request] - pool_base
@@ -102,37 +115,43 @@
     normed_cols = (
         hidden_wide * lax.rsqrt(mean_square + EPSILON) * gain_cols.astype(jnp.float32)
     ).astype(jnp.bfloat16)
-    normed_grid = lax.all_gather(normed_cols, ("exp", "ffn"), axis=0, tiled=False)
-    normed_grid = normed_grid.reshape(exp_size, ffn_size, token_rows, column_count)
-    group_rows = exp_size * token_rows
-    routes_all = lax.all_gather(routes, "exp", axis=0, tiled=True)
-    logits = jnp.einsum(
-        "efrc,fck->erk",
-        normed_grid,
-        router.reshape(ffn_size, column_count, EXPERTS),
-        preferred_element_type=jnp.float32,
-    ).reshape(group_rows, EXPERTS)
-    chosen = jnp.take_along_axis(logits, routes_all, axis=1)
-    raised = jnp.exp(chosen)
-    gate_weights = raised / jnp.sum(raised, axis=1, keepdims=True)
+    normed_half = lax.all_gather(normed_cols, "exp", axis=0, tiled=True)
+    normed_all = lax.all_gather(normed_half, "ffn", axis=1, tiled=True)
+
+    expert_ids = lax.broadcasted_iota(jnp.int32, (1, 1, EXPERTS), 2)
+    route_hot = routes_all[:, :, None] == expert_ids
     blocks = group_rows // BLOCK_ROWS
-    slot_within = jax.vmap(slot_numbers)(routes_all.reshape(blocks, BLOCK_ROWS * TOP))
+    pair_count = BLOCK_ROWS * TOP
+    pair_hot = route_hot.reshape(blocks, pair_count, EXPERTS).astype(jnp.bfloat16)
+    earlier = (
+        lax.broadcasted_iota(jnp.int32, (pair_count, pair_count), 1)
+        < lax.broadcasted_iota(jnp.int32, (pair_count, pair_count), 0)
+    ).astype(jnp.bfloat16)
+    before = jnp.einsum("pq,bqx->bpx", earlier, pair_hot, preferred_element_type=jnp.float32)
+    rank = jnp.sum(before * pair_hot.astype(jnp.float32), axis=2).astype(jnp.int32)
     block_base = lax.broadcasted_iota(jnp.int32, (blocks, 1), 0) * CAPACITY
-    slot_index = (slot_within + block_base).reshape(group_rows * TOP)
+    slot_index = (rank + block_base).reshape(group_rows, TOP)
     slot_count = blocks * CAPACITY
     local_count = gate_weight.shape[0]
     total_slots = local_count * slot_count
-    local_expert = routes_all.reshape(group_rows * TOP) - exp_index * local_count
+    local_expert = routes_all - exp_index * local_count
     is_local = (local_expert >= 0) & (local_expert < local_count)
-    local_target = jnp.where(is_local, local_expert * slot_count + slot_index, total_slots)
-    token_ids = lax.broadcasted_iota(jnp.int32, (group_rows, TOP), 0).reshape(group_rows * TOP)
-    slot_token = jnp.zeros((total_slots,), jnp.int32).at[local_target].set(token_ids, mode="drop")
-    slot_weight = (
-        jnp.zeros((total_slots,), jnp.float32)
-        .at[local_target]
-        .set(gate_weights.reshape(group_rows * TOP), mode="drop")
+    target = jnp.where(is_local, local_expert * slot_count + slot_index, -1)
+
+    logits = jnp.dot(normed_all, router, preferred_element_type=jnp.float32)
+    chosen = jnp.sum(jnp.where(route_hot, logits[:, None, :], 0.0), axis=2)
+    raised = jnp.exp(chosen)
+    gate_weights = raised / jnp.sum(raised, axis=1, keepdims=True)
+
+    slot_ids = lax.broadcasted_iota(jnp.int32, (1, 1, total_slots), 2)
+    slot_hit = target[:, :, None] == slot_ids
+    combine = jnp.any(slot_hit, axis=1).astype(jnp.bfloat16)
+    slot_weight = jnp.sum(jnp.where(slot_hit, gate_weights[:, :, None], 0.0), axis=(0, 1))
+    dispatch_ids = lax.broadcasted_iota(jnp.int32, (total_slots, 1, 1), 0)
+    dispatch = jnp.any(target[None, :, :] == dispatch_ids, axis=2).astype(jnp.bfloat16)
+    grouped = jnp.dot(dispatch, normed_all, preferred_element_type=jnp.float32).astype(
+        jnp.bfloat16
     )
-    grouped = normed_grid[slot_token // token_rows, :, slot_token % token_rows, :]
     grouped = grouped.reshape(local_count, slot_count, feature_count)
     gate_part = jnp.einsum("jmd,jdf->jmf", grouped, gate_weight, preferred_element_type=jnp.float32)
     up_part = jnp.einsum("jmd,jdf->jmf", grouped, up_weight, preferred_element_type=jnp.float32)
@@ -141,16 +160,9 @@
     weighted = (outputs.reshape(total_slots, feature_count) * slot_weight[:, None]).astype(
         jnp.bfloat16
     )
-    row_ids = lax.broadcasted_iota(jnp.int32, (group_rows, 1), 0)
-    onehot = (slot_token[None, :] == row_ids).astype(jnp.bfloat16)
-    mixture = jnp.einsum(
-        "ers,sfc->efrc",
-        onehot.reshape(exp_size, token_rows, total_slots),
-        weighted.reshape(total_slots, ffn_size, column_count),
-        preferred_element_type=jnp.float32,
-    ).astype(jnp.bfloat16)
-    mixture = mixture.reshape(exp_size * ffn_size * token_rows, column_count)
-    moe_out = lax.psum_scatter(mixture, ("exp", "ffn"), scatter_dimension=0, tiled=True)
+    mixture = jnp.dot(combine, weighted, preferred_element_type=jnp.float32).astype(jnp.bfloat16)
+    moe_cols = lax.psum_scatter(mixture, "ffn", scatter_dimension=1, tiled=True)
+    moe_out = lax.psum_scatter(moe_cols, "exp", scatter_dimension=0, tiled=True)
     return (hidden_out, moe_out)
 
 

time: 306 us -> 274 us (0.90)
  waiting for transfers between devices: 66.3 us -> 148 us
  local copies, waits for them, and re-layouts: 109 us -> 30.6 us
  blocking collectives: 49 us -> 2.47 us
  matrix products: 51.3 us -> 58.7 us
  other arithmetic: 15.6 us -> 18.8 us
    all_gather x2 -> x3, waiting for transfers between devices: 21.1 us -> 99.3 us  [the longest x1 64.9 us: local(): gathered = lax.all_gather(packed, 'exp', axis=0, tiled=False)]
    all_gather x2 -> x0, blocking collectives: 46.5 us -> none  [the longest x1 31.2 us: local(): lax.all_gather(new_latent, 'exp', axis=0, tiled=True)]
    gather x4 -> x0, local copies, waits for them, and re-layouts: 43.7 us -> none  [the longest x3 25.3 us: local(): chosen = jnp.take_along_axis(logits, routes_all, axis=1)]
    scatter x2 -> x0, local copies, waits for them, and re-layouts: 23.8 us -> none  [the longest x1 12 us: local(): slot_weight = jnp.zeros((total_slots,), jnp.float32).at[local_target].set...]
    reshape x3, local copies, waits for them, and re-layouts: 13.1 us -> 2.7 us  [the longest x1 2.51 us: local(): gathered[:, pool_pages:pool_pages + latent_pages]]
    convert_element_type x2 -> x6, local copies, waits for them, and re-layouts: 9.44 us -> 0.83 us  [the longest x3 0.34 us: local(): routes_all = gathered[:, pool_pages + latent_pages:].reshape(exp_size, ro...]
    another operation x2 -> x0, other arithmetic: 7.03 us -> none
    slice x2 -> x3, local copies, waits for them, and re-layouts: 0.37 us -> 6.44 us  [the longest x1 3.25 us: local(): gathered[:, :pool_pages].reshape(exp_size * pool_pages, page_width)]
  transfers between devices with their start and end apart: 4 -> 6, of which waited for: 3 -> 6; matrix products, arithmetic and copies ran while one was open for 10% -> 5% of each run, Pallas kernels for 0% -> 0%
where the time goes in v2:
time: 274 us; the launch traced here: 273 us
  waiting for transfers between devices  148 us (54%)
  matrix products  58.7 us (21%)
  local copies, waits for them, and re-layouts  30.6 us (11%)
  other arithmetic  18.8 us (7%)
  between operations  14.5 us (5%)
    all_gather x1, waiting for transfers between devices, local(): gathered = lax.all_gather(packed, 'exp', axis=0, tiled=False)  64.9 us
    reduce_scatter x1, waiting for transfers between devices, local(): moe_out = lax.psum_scatter(moe_cols, 'exp', scatter_dimension=0, tiled=True)  31.1 us
    all_gather x1, waiting for transfers between devices, local(): normed_half = lax.all_gather(normed_cols, 'exp', axis=0, tiled=True)  29.2 us
    dot_general x1, matrix products, local(): jnp.einsum('jmf,jfd->jmd', active, down_weight, preferred_element_type=jn...  23.6 us
    dot_general x1, matrix products, local(): jnp.einsum('jmd,jdf->jmf', grouped, gate_weight, preferred_element_type=j...  12.3 us
    reduce_scatter x1, waiting for transfers between devices, local(): moe_cols = lax.psum_scatter(mixture, 'ffn', scatter_dimension=1, tiled=True)  10.9 us
    gather x3, local copies, waits for them, and re-layouts, local(): cached_keys = jnp.take(pool_all, page_rows, axis=0).reshape(CMAX, QKD)  9.01 us
    unnamed x34, local copies, waits for them, and re-layouts  7.24 us
  transfers between devices with their start and end apart: 6, of which 6 were waited for; matrix products, arithmetic and copies ran while one was open for 5% of the time, Pallas kernels for 0%

profile of v2, /device:TPU:0, one launch (start us, length us, event | category | flops | bytes accessed | tf_op | source)
XLA Modules:
  0.0 273.3 jit_solution(11464802684706153891)
XLA Ops:
  7.3 1.2 copy.37
  8.5 0.2 reshape.252
  8.7 0.7 convert_element_type.101
  9.3 0.1 copy.38
  9.5 0.2 convert_element_type.102
  9.7 2.1 maximum_bitcast_fusion
  11.8 0.0 reduce-scatter.4.cloned.1.call-start
  11.8 0.7 compare_and_fusion
  12.5 0.1 broadcast_in_dim.69
  12.6 0.1 broadcast_in_dim.70
  12.7 0.6 dynamic_slice.19
  13.3 0.6 dynamic_slice.20
  13.9 1.0 copy.41
  14.9 1.0 copy.51
  16.0 0.7 fusion.39
  16.7 1.3 iota_compare_fusion.6
  18.0 1.7 and_or_fusion
  19.7 64.9 %all-gather.10.cloned.1.call-done = bf16[4,41,9216]{2,1,0:T(8,128)(2,1)} async-done(((bf16[1,41,9216]{2,1,0:T(8,128)(2,1)}), bf16[4,41,9216]{2,1,0:T(8,128)(2,1)}) %all-gather.10.cloned.1.call-update) | async-done | bytes 3022864 | tf_op jit(solution)/shard_map/all_gather | solution.py:62
  84.6 3.2 %slice.22 = bf16[4,32,9216]{2,1,0:T(8,128)(2,1)} slice(bf16[4,41,9216]{2,1,0:T(8,128)(2,1)} %all-gather.10.cloned.1.call-done), slice={[0:4], [0:32], [0:9216]} | slice | bytes 4718592 | tf_op jit(solution)/shard_map/slice | solution.py:63
  87.9 5.3 %gather_fusion = bf16[64,9216]{1,0:T(8,128)(2,1)} fusion(bf16[128,9216]{1,0:T(8,128)(2,1)} %bitcast.77, s32[1024]{0:T(1024)S(1)} %pad_clamp_fusion), kind=kCustom, calls=%fused_computation | custom fusion | bytes 2359552 | tf_op jit(solution)/shard_map/jit(_take)/gather | solution.py:76
  93.2 2.2 gather.7
  95.4 1.4 copy.39
  96.9 2.0 slice.23
  98.9 2.5 reshape.255
  101.4 1.7 constant_dynamic-slice_fusion
  103.2 1.9 copy.53
  105.0 0.1 broadcast_select_fusion
  105.2 1.0 copy-done.4
  106.2 3.9 %fusion.6 = f32[128,4,1280]{0,2,1:T(8,128)} fusion(bf16[128,4,576]{0,2,1:T(8,128)(2,1)} %bitcast.80, bf16[256,576]{0,1:T(8,128)(2,1)} %copy.53, bf16[1024,576]{0,1:T(8,128)(2,1)S(1)} %broadcast_select_fusion, pred[128,1280]{0,1:T(8,128)(4,1)S(1)} %copy-done.9), kind=kOutput, calls=%fused_computation.13 | convolution fusion | flops 759234560 | bytes 4849664 | tf_op jit(solution)/shard_map/thd,kd->thk/dot_general | solution.py:84
  110.1 3.3 %fusion.50 = f32[128,4]{0,1:T(4,128)S(1)} fusion(bf16[128,4,576]{0,2,1:T(8,128)(2,1)} %bitcast.81, bf16[256,576]{0,1:T(8,128)(2,1)} %copy.53, bf16[1024,576]{0,1:T(8,128)(2,1)} %copy-done.4, pred[128,1280]{0,1:T(8,128)(4,1)S(1)} %copy-done.9), kind=kOutput, calls=%fused_computation.80 | convolution fusion | flops 760546560 | bytes 2230272 | tf_op jit(solution)/shard_map/sub | solution.py:94
  113.5 4.0 %fusion.25 = bf16[4,128,128]{1,2,0:T(8,128)(2,1)S(1)} fusion(bf16[512,4,128]{0,2,1:T(8,128)(2,1)} %bitcast.82, bf16[1024,576]{0,1:T(8,128)(2,1)S(1)} %copy-done.5, bf16[256,576]{0,1:T(8,128)(2,1)} %copy.53, f32[128,4]{0,1:T(4,128)S(1)} %fusion.50, f32[128,4,1280]{0,2,1:T(8,128)} %fusion.6), kind=kOutput, calls=%fused_computation.35 | convolution fusion | flops 743114496 | bytes 7374848 | tf_op jit(solution)/shard_map/thl,lhd->thd/dot_general | solution.py:100
  117.5 1.3 convolution_convert_fusion.2
  118.8 0.0 all-gather.6.cloned.1.call-start
  118.9 6.6 %reduce-scatter.4.cloned.1.call-done = bf16[128,1024]{1,0:T(8,128)(2,1)} async-done(((bf16[128,2048]{1,0:T(8,128)(2,1)}), bf16[128,1024]{1,0:T(8,128)(2,1)}) %reduce-scatter.4.cloned.1.call-update) | async-done | bytes 262160 | tf_op jit(solution)/shard_map/reduce_scatter | solution.py:106
  125.5 1.1 fusion.30
  126.7 2.5 psum.7
  129.1 0.8 fusion.32
  130.0 0.0 all-gather.8.cloned.1.call-start
  130.0 29.2 %all-gather.6.cloned.1.call-done = bf16[512,1024]{1,0:T(8,128)(2,1)} async-done(((bf16[128,1024]{1,0:T(8,128)(2,1)}), bf16[512,1024]{1,0:T(8,128)(2,1)}) %all-gather.6.cloned.1.call-update) | async-done | bytes 1048592 | tf_op jit(solution)/shard_map/all_gather | solution.py:118
  159.3 0.2 reduce-scatter.6.cloned.1.call-start
  159.5 0.1 add.120
  159.6 0.1 add.121
  159.7 1.1 slice.26
  160.9 0.2 reshape.262
  161.1 0.1 copy.47
  161.2 0.3 fusion.24
  161.5 0.2 convert_element_type.117
  161.7 0.1 add_select_fusion
  161.9 0.1 copy.45
  162.0 2.3 fusion.2
  164.3 1.4 fusion.1
  165.7 5.1 %all-gather.8.cloned.1.call-done = bf16[512,2048]{1,0:T(8,128)(2,1)} async-done(((bf16[512,1024]{1,0:T(8,128)(2,1)}), bf16[512,2048]{1,0:T(8,128)(2,1)}) %all-gather.8.cloned.1.call-update) | async-done | bytes 2097168 | tf_op jit(solution)/shard_map/all_gather | solution.py:119
  170.8 2.3 fusion.54
  173.1 0.1 select_reduce_fusion.1
  173.3 1.7 select_reduce_fusion
  175.0 3.9 %convolution_convert_fusion = bf16[1024,2048]{1,0:T(8,128)(2,1)S(1)} fusion(pred[1024,512]{1,0:T(8,128)(4,1)S(1)} %fusion.2, bf16[512,2048]{1,0:T(8,128)(2,1)} %all-gather.8.cloned.1.call-done), kind=kOutput, calls=%fused_computation.9 | convolution fusion | flops 2149580800 | bytes 6815744 | tf_op jit(solution)/shard_map/dot_general | solution.py:152
  178.9 2.0 copy-done.3
  180.9 12.3 %fusion.53 = f32[8,128,704]{1,2,0:T(8,128)} fusion(bf16[8,128,2048]{2,1,0:T(8,128)(2,1)S(1)} %bitcast.78, bf16[8,2048,704]{1,2,0:T(8,128)(2,1)} %param.27), kind=kOutput, calls=%fused_computation.81 | convolution fusion | flops 2952790016 | bytes 30146560 | tf_op jit(solution)/shard_map/jmd,jdf->jmf/dot_general | solution.py:156
  193.2 23.6 %fusion.8 = f32[8,128,2048]{2,1,0:T(8,128)} fusion(bf16[8,704,2048]{2,1,0:T(8,128)(2,1)} %param.29, f32[8,128,704]{1,2,0:T(8,128)} %fusion.53, bf16[8,128,2048]{2,1,0:T(8,128)(2,1)} %bitcast.79, bf16[8,2048,704]{1,2,0:T(8,128)(2,1)} %param.28), kind=kOutput, calls=%fused_computation.21 | convolution fusion | flops 5909905408 | bytes 61603840 | tf_op jit(solution)/shard_map/jmf,jfd->jmd/dot_general | solution.py:159
  216.8 3.9 %fusion.3 = bf16[1024,2048]{1,0:T(8,128)(2,1)S(1)} fusion(f32[8,128,2048]{2,1,0:T(8,128)} %fusion.8, f32[1024]{0:T(1024)S(1)} %select_reduce_fusion), kind=kLoop, calls=%fused_computation.8 | loop fusion | flops 4194304 | bytes 12587008 | tf_op jit(solution)/shard_map/convert_element_type | solution.py:160
  220.7 3.8 %convolution_convert_fusion.1 = bf16[512,2048]{1,0:T(8,128)(2,1)} fusion(pred[512,1024]{1,0:T(8,128)(4,1)S(1)} %fusion.1, bf16[1024,2048]{1,0:T(8,128)(2,1)S(1)} %fusion.3), kind=kOutput, calls=%fused_computation.15 | convolution fusion | flops 2148532224 | bytes 6815744 | tf_op jit(solution)/shard_map/dot_general | solution.py:163
  224.4 0.0 reduce-scatter.8.cloned.1.call-start
  224.5 10.9 %reduce-scatter.6.cloned.1.call-done = bf16[512,1024]{1,0:T(8,128)(2,1)} async-done(((bf16[512,2048]{1,0:T(8,128)(2,1)}), bf16[512,1024]{1,0:T(8,128)(2,1)}) %reduce-scatter.6.cloned.1.call-update) | async-done | bytes 1048592 | tf_op jit(solution)/shard_map/reduce_scatter | solution.py:164
  235.4 31.1 %reduce-scatter.8.cloned.1.call-done = bf16[128,1024]{1,0:T(8,128)(2,1)} async-done(((bf16[512,1024]{1,0:T(8,128)(2,1)}), bf16[128,1024]{1,0:T(8,128)(2,1)}) %reduce-scatter.8.cloned.1.call-update) | async-done | bytes 262160 | tf_op jit(solution)/shard_map/reduce_scatter | solution.py:165
  (49 shorter events, 0.4 us)
Async XLA Ops:
  7.2 110.4 %copy-start = (bf16[512,2048]{1,0:T(8,128)(2,1)S(1)}, bf16[512,2048]{1,0:T(8,128)(2,1)}, u32[]{:S(2)}) copy-start(bf16[512,2048]{1,0:T(8,128)(2,1)} %param.24) | copy-start | bytes 6291460
  7.2 5.5 %copy-start.13 = (s32[8]{0:T(128)S(1)}, s32[8]{0:T(128)}, u32[]{:S(2)}) copy-start(s32[8]{0:T(128)} %param.21) | copy-start | bytes 100
  7.2 6.1 %copy-start.14 = (s32[8]{0:T(128)S(1)}, s32[8]{0:T(128)}, u32[]{:S(2)}) copy-start(s32[8]{0:T(128)} %param.20) | copy-start | bytes 100
  7.2 6.7 %copy-start.7 = (bf16[128,2304]{1,0:T(8,128)(2,1)S(1)}, bf16[128,2304]{1,0:T(8,128)(2,1)}, u32[]{:S(2)}) copy-start(bf16[128,2304]{1,0:T(8,128)(2,1)} %param.16) | copy-start | bytes 1769476
  7.2 7.7 %copy-start.8 = (bf16[512,512]{1,0:T(8,128)(2,1)S(1)}, bf16[512,512]{1,0:T(8,128)(2,1)}, u32[]{:S(2)}) copy-start(bf16[512,512]{1,0:T(8,128)(2,1)} %param.23) | copy-start | bytes 1572868
  7.2 77.4 %all-gather.10.cloned.1.call-start = ((), (), s32[]{:S(2)}) async-start(), calls=%async_computation.8 | async-start | bytes 4423680 | tf_op jit(solution)/shard_map/all_gather | solution.py:62
  11.8 113.8 %reduce-scatter.4.cloned.1.call-start = ((), (), s32[]{:S(2)}) async-start(), calls=%async_computation.3 | async-start | bytes 786432 | tf_op jit(solution)/shard_map/reduce_scatter | solution.py:106
  96.9 8.2 %copy-start.2 = (bf16[1024,576]{0,1:T(8,128)(2,1)S(1)}, bf16[1024,576]{0,1:T(8,128)(2,1)}, u32[]{:S(2)}) copy-start(bf16[1024,576]{0,1:T(8,128)(2,1)} %copy.39) | copy-start | bytes 3538948
  98.9 7.3 %copy-start.9 = (pred[128,1280]{0,1:T(8,128)(4,1)S(1)}, pred[128,1280]{0,1:T(8,128)(4,1)}, u32[]{:S(2)}) copy-start(pred[128,1280]{0,1:T(8,128)(4,1)} %and_or_fusion) | copy-start | bytes 491524
  105.2 1.1 copy-start.4
  110.1 3.3 %copy-start.5 = (bf16[1024,576]{0,1:T(8,128)(2,1)S(1)}, bf16[1024,576]{0,1:T(8,128)(2,1)}, u32[]{:S(2)}) copy-start(bf16[1024,576]{0,1:T(8,128)(2,1)} %copy-done.4) | copy-start | bytes 3538948
  117.5 1.4 copy-start.12
  117.5 8.0 %copy-start.11 = (bf16[128,2048]{1,0:T(8,128)(2,1)S(1)}, bf16[128,2048]{1,0:T(8,128)(2,1)}, u32[]{:S(2)}) copy-start(bf16[128,2048]{1,0:T(8,128)(2,1)} %param.15) | copy-start | bytes 1572868
  118.8 40.4 %all-gather.6.cloned.1.call-start = ((), (), s32[]{:S(2)}) async-start(), calls=%async_computation.4 | async-start | bytes 1310720 | tf_op jit(solution)/shard_map/all_gather | solution.py:118
  126.6 37.7 %copy-start.6 = (bf16[128,1024]{1,0:T(8,128)(2,1)}, bf16[128,1024]{1,0:T(8,128)(2,1)S(1)}, u32[]{:S(2)}) copy-start(bf16[128,1024]{1,0:T(8,128)(2,1)S(1)} %get-tuple-element.3) | copy-start | bytes 786436
  130.0 40.8 %all-gather.8.cloned.1.call-start = ((), (), s32[]{:S(2)}) async-start(), calls=%async_computation.5 | async-start | bytes 3145728 | tf_op jit(solution)/shard_map/all_gather | solution.py:119
  159.2 11.6 %copy-start.10 = (bf16[2048,32]{0,1:T(8,128)(2,1)S(1)}, bf16[2048,32]{0,1:T(8,128)(2,1)}, u32[]{:S(2)}) copy-start(bf16[2048,32]{0,1:T(8,128)(2,1)} %param.26) | copy-start | bytes 393220
  159.3 76.1 %reduce-scatter.6.cloned.1.call-start = ((), (), s32[]{:S(2)}) async-start(), calls=%async_computation.6 | async-start | bytes 3145728 | tf_op jit(solution)/shard_map/reduce_scatter | solution.py:164
  178.9 2.0 copy-start.3
  220.7 45.8 %copy-start.1 = (bf16[512,2048]{1,0:T(8,128)(2,1)S(1)}, bf16[512,2048]{1,0:T(8,128)(2,1)}, u32[]{:S(2)}) copy-start(bf16[512,2048]{1,0:T(8,128)(2,1)} %param.24) | copy-start | bytes 6291460
  224.4 42.0 %reduce-scatter.8.cloned.1.call-start = ((), (), s32[]{:S(2)}) async-start(), calls=%async_computation.7 | async-start | bytes 1310720 | tf_op jit(solution)/shard_map/reduce_scatter | solution.py:165
Sparse Core Ops, SparseCore 0:
  11.9 72.6 all-gather.9
  118.9 6.5 reduce-scatter.3
  130.1 29.0 all-gather.5
  160.7 10.0 all-gather.7
  224.6 10.7 reduce-scatter.5
  238.1 28.3 reduce-scatter.7

commit v3 on v2

--- a/solution.py
+++ b/solution.py
@@ -56,17 +56,27 @@
         routes.reshape(route_count).astype(jnp.bfloat16),
         (0, route_pages * page_width - route_count),
     ).reshape(route_pages, page_width)
+    packed_rows = pool_pages + latent_pages + route_pages
+    share_rows = -(-packed_rows // ffn_size)
     packed = jnp.concatenate(
-        [cache_pool, new_latent.reshape(latent_pages, page_width), route_rows], axis=0
+        [
+            cache_pool,
+            new_latent.reshape(latent_pages, page_width),
+            route_rows,
+            jnp.zeros((share_rows * ffn_size - packed_rows, page_width), jnp.bfloat16),
+        ],
+        axis=0,
     )
-    gathered = lax.all_gather(packed, "exp", axis=0, tiled=False)
+    share = lax.dynamic_slice_in_dim(packed, ffn_index * share_rows, share_rows, 0)
+    gathered = lax.all_gather(share, ("exp", "ffn"), axis=0, tiled=False)
+    gathered = gathered.reshape(exp_size, ffn_size * share_rows, page_width)
     pool_all = gathered[:, :pool_pages].reshape(exp_size * pool_pages, page_width)
     latent_all = gathered[:, pool_pages : pool_pages + latent_pages].reshape(
         exp_size * token_rows, QKD
     )
     group_rows = exp_size * token_rows
     routes_all = (
-        gathered[:, pool_pages + latent_pages :]
+        gathered[:, pool_pages + latent_pages : packed_rows]
         .reshape(exp_size, route_pages * page_width)[:, :route_count]
         .reshape(group_rows, TOP)
         .astype(jnp.int32)

time: 274 us -> 246 us (0.90)
  waiting for transfers between devices: 148 us -> 119 us
    all_gather x1, waiting for transfers between devices: 64.9 us -> 35.8 us  [local(): gathered = lax.all_gather(share, ('exp', 'ffn'), axis=0, tiled=False)]
    reshape x0 -> x1, local copies, waits for them, and re-layouts: none -> 4.67 us  [local(): gathered = gathered.reshape(exp_size, ffn_size * share_rows, page_width)]
    unnamed x34 -> x22, local copies, waits for them, and re-layouts: 7.24 us -> 5.19 us
  transfers between devices with their start and end apart: 6 -> 6, of which waited for: 6 -> 6; matrix products, arithmetic and copies ran while one was open for 5% -> 6% of each run, Pallas kernels for 0% -> 0%
where the time goes in v3:
time: 246 us; the launch traced here: 245 us
  waiting for transfers between devices  119 us (48%)
  matrix products  58.2 us (24%)
  local copies, waits for them, and re-layouts  30.9 us (13%)
  other arithmetic  19.7 us (8%)
  between operations  14.5 us (6%)
  blocking collectives  2.47 us (1%)
    all_gather x1, waiting for transfers between devices, local(): gathered = lax.all_gather(share, ('exp', 'ffn'), axis=0, tiled=False)  35.8 us
    reduce_scatter x1, waiting for transfers between devices, local(): moe_out = lax.psum_scatter(moe_cols, 'exp', scatter_dimension=0, tiled=True)  31.1 us
    all_gather x1, waiting for transfers between devices, local(): normed_half = lax.all_gather(normed_cols, 'exp', axis=0, tiled=True)  29.2 us
    dot_general x1, matrix products, local(): jnp.einsum('jmf,jfd->jmd', active, down_weight, preferred_element_type=jn...  23.6 us
    dot_general x1, matrix products, local(): jnp.einsum('jmd,jdf->jmf', grouped, gate_weight, preferred_element_type=j...  12.3 us
    gather x3, local copies, waits for them, and re-layouts, local(): cached_keys = jnp.take(pool_all, page_rows, axis=0).reshape(CMAX, QKD)  10.9 us
    reduce_scatter x1, waiting for transfers between devices, local(): moe_cols = lax.psum_scatter(mixture, 'ffn', scatter_dimension=1, tiled=True)  10.9 us
    reduce_scatter x1, waiting for transfers between devices, local(): lax.psum_scatter(partial_value.astype(jnp.bfloat16), 'ffn', scatter_dimen...  6.9 us
  transfers between devices with their start and end apart: 6, of which 6 were waited for; matrix products, arithmetic and copies ran while one was open for 6% of the time, Pallas kernels for 0%

profile of v3, /device:TPU:0, one launch (start us, length us, event | category | flops | bytes accessed | tf_op | source)
XLA Modules:
  0.0 245.1 jit_solution(17486764238863235571)
XLA Ops:
  7.3 1.2 copy.37
  8.5 0.2 reshape.255
  8.6 0.7 convert_element_type.101
  9.3 0.1 copy.38
  9.5 0.2 convert_element_type.102
  9.7 0.1 pad.10.clone
  9.7 0.1 dynamic-slice
  9.8 2.3 fusion.36
  12.2 0.0 reduce-scatter.4.cloned.1.call-start
  12.2 0.7 compare_and_fusion
  12.9 0.1 broadcast_in_dim.72
  13.0 0.1 broadcast_in_dim.73
  13.1 1.2 dynamic_slice.22
  14.4 1.2 dynamic_slice.23
  15.6 1.1 copy.41
  16.7 1.0 copy.51
  17.7 0.7 fusion.43
  18.4 1.3 iota_compare_fusion.6
  19.7 1.0 and_or_fusion
  20.7 35.8 %all-gather.10.cloned.1.call-done = bf16[8,21,9216]{2,1,0:T(8,128)(2,1)} async-done(((bf16[1,21,9216]{2,1,0:T(8,128)(2,1)}), bf16[8,21,9216]{2,1,0:T(8,128)(2,1)}) %all-gather.10.cloned.1.call-update) | async-done | bytes 3096592 | tf_op jit(solution)/shard_map/all_gather | solution.py:71
  56.5 4.7 %reshape.257 = bf16[4,42,9216]{2,1,0:T(8,128)(2,1)} reshape(bf16[8,21,9216]{2,1,0:T(8,128)(2,1)} %all-gather.10.cloned.1.call-done) | data formatting | bytes 6193152 | tf_op jit(solution)/shard_map/reshape | solution.py:72
  61.2 3.2 %slice.22 = bf16[4,32,9216]{2,1,0:T(8,128)(2,1)} slice(bf16[4,42,9216]{2,1,0:T(8,128)(2,1)} %reshape.257), slice={[0:4], [0:32], [0:9216]} | slice | bytes 4718592 | tf_op jit(solution)/shard_map/slice | solution.py:73
  64.5 5.3 %gather_fusion = bf16[64,9216]{1,0:T(8,128)(2,1)} fusion(bf16[128,9216]{1,0:T(8,128)(2,1)} %bitcast.78, s32[1024]{0:T(1024)S(1)} %pad_clamp_fusion), kind=kCustom, calls=%fused_computation | custom fusion | bytes 2359552 | tf_op jit(solution)/shard_map/jit(_take)/gather | solution.py:86
  69.8 3.1 %gather.7 = bf16[1024,576]{1,0:T(8,128)(2,1)} reshape(bf16[64,9216]{1,0:T(8,128)(2,1)} %gather_fusion) | data formatting | bytes 2359296 | tf_op jit(solution)/shard_map/jit(_take)/gather | solution.py:86
  72.9 2.5 %copy.39 = bf16[1024,576]{0,1:T(8,128)(2,1)} copy(bf16[1024,576]{1,0:T(8,128)(2,1)} %gather.7) | data formatting | bytes 2359296 | tf_op jit(solution)/shard_map/jit(_take)/gather | solution.py:86
  75.4 0.5 reshape.259
  76.0 0.9 copy.53
  76.8 1.4 broadcast_select_fusion
  78.2 3.9 %fusion.6 = f32[128,4,1280]{0,2,1:T(8,128)} fusion(bf16[128,4,576]{0,2,1:T(8,128)(2,1)} %bitcast.81, bf16[256,576]{0,1:T(8,128)(2,1)} %copy.53, bf16[1024,576]{0,1:T(8,128)(2,1)S(1)} %broadcast_select_fusion, pred[128,1280]{0,1:T(8,128)(4,1)S(1)} %and_or_fusion), kind=kOutput, calls=%fused_computation.13 | convolution fusion | flops 759234560 | bytes 4849664 | tf_op jit(solution)/shard_map/thd,kd->thk/dot_general | solution.py:94
  82.2 2.9 %fusion.54 = f32[128,4]{0,1:T(4,128)S(1)} fusion(bf16[128,4,576]{0,2,1:T(8,128)(2,1)} %bitcast.82, bf16[256,576]{0,1:T(8,128)(2,1)} %copy.53, bf16[1024,576]{0,1:T(8,128)(2,1)S(1)} %broadcast_select_fusion, pred[128,1280]{0,1:T(8,128)(4,1)S(1)} %and_or_fusion), kind=kOutput, calls=%fused_computation.86 | convolution fusion | flops 760546560 | bytes 2230272 | tf_op jit(solution)/shard_map/sub | solution.py:104
  85.0 4.0 %fusion.25 = bf16[4,128,128]{1,2,0:T(8,128)(2,1)S(1)} fusion(bf16[512,4,128]{0,2,1:T(8,128)(2,1)} %bitcast.83, bf16[1024,576]{0,1:T(8,128)(2,1)S(1)} %broadcast_select_fusion, bf16[256,576]{0,1:T(8,128)(2,1)} %copy.53, f32[128,4]{0,1:T(4,128)S(1)} %fusion.54, f32[128,4,1280]{0,2,1:T(8,128)} %fusion.6), kind=kOutput, calls=%fused_computation.35 | convolution fusion | flops 743114496 | bytes 7374848 | tf_op jit(solution)/shard_map/thl,lhd->thd/dot_general | solution.py:110
  89.1 1.3 convolution_convert_fusion.2
  90.4 0.0 all-gather.6.cloned.1.call-start
  90.4 6.9 %reduce-scatter.4.cloned.1.call-done = bf16[128,1024]{1,0:T(8,128)(2,1)} async-done(((bf16[128,2048]{1,0:T(8,128)(2,1)}), bf16[128,1024]{1,0:T(8,128)(2,1)}) %reduce-scatter.4.cloned.1.call-update) | async-done | bytes 262160 | tf_op jit(solution)/shard_map/reduce_scatter | solution.py:116
  97.3 1.1 fusion.30
  98.5 2.5 %psum.7 = f32[128,1]{0,1:T(1,128)S(1)} all-reduce(f32[128,1]{0,1:T(1,128)S(1)} %bitcast.86), channel_id=1, replica_groups=mesh['req'=4,'exp'=4,'ffn'=2] {'ffn'}, use_global_device_ids=true, to_apply=%region_7.8 | all-reduce | flops 128 | bytes 1024 | tf_op jit(solution)/shard_map/psum | solution.py:122
  101.0 0.8 fusion.32
  101.8 0.0 all-gather.8.cloned.1.call-start
  101.9 29.2 %all-gather.6.cloned.1.call-done = bf16[512,1024]{1,0:T(8,128)(2,1)} async-done(((bf16[128,1024]{1,0:T(8,128)(2,1)}), bf16[512,1024]{1,0:T(8,128)(2,1)}) %all-gather.6.cloned.1.call-update) | async-done | bytes 1048592 | tf_op jit(solution)/shard_map/all_gather | solution.py:128
  131.1 0.2 reduce-scatter.6.cloned.1.call-start
  131.3 0.1 add.124
  131.4 0.1 add.125
  131.5 1.1 slice.26
  132.7 0.2 reshape.266
  132.9 0.1 copy.47
  133.0 0.3 fusion.24
  133.3 0.2 convert_element_type.117
  133.5 0.1 add_select_fusion
  133.7 0.1 copy.45
  133.8 2.3 fusion.2
  136.1 1.4 fusion.1
  137.5 5.1 %all-gather.8.cloned.1.call-done = bf16[512,2048]{1,0:T(8,128)(2,1)} async-done(((bf16[512,1024]{1,0:T(8,128)(2,1)}), bf16[512,2048]{1,0:T(8,128)(2,1)}) %all-gather.8.cloned.1.call-update) | async-done | bytes 2097168 | tf_op jit(solution)/shard_map/all_gather | solution.py:129
  142.6 2.3 fusion.58
  144.9 0.1 select_reduce_fusion.1
  145.1 1.7 select_reduce_fusion
  146.8 3.9 %convolution_convert_fusion = bf16[1024,2048]{1,0:T(8,128)(2,1)S(1)} fusion(pred[1024,512]{1,0:T(8,128)(4,1)S(1)} %fusion.2, bf16[512,2048]{1,0:T(8,128)(2,1)} %all-gather.8.cloned.1.call-done), kind=kOutput, calls=%fused_computation.9 | convolution fusion | flops 2149580800 | bytes 6815744 | tf_op jit(solution)/shard_map/dot_general | solution.py:162
  150.8 2.0 copy-done.2
  152.7 12.3 %fusion.57 = f32[8,128,704]{1,2,0:T(8,128)} fusion(bf16[8,128,2048]{2,1,0:T(8,128)(2,1)S(1)} %bitcast.79, bf16[8,2048,704]{1,2,0:T(8,128)(2,1)} %param.27), kind=kOutput, calls=%fused_computation.87 | convolution fusion | flops 2952790016 | bytes 30146560 | tf_op jit(solution)/shard_map/jmd,jdf->jmf/dot_general | solution.py:166
  165.0 23.6 %fusion.8 = f32[8,128,2048]{2,1,0:T(8,128)} fusion(bf16[8,704,2048]{2,1,0:T(8,128)(2,1)} %param.29, f32[8,128,704]{1,2,0:T(8,128)} %fusion.57, bf16[8,128,2048]{2,1,0:T(8,128)(2,1)} %bitcast.80, bf16[8,2048,704]{1,2,0:T(8,128)(2,1)} %param.28), kind=kOutput, calls=%fused_computation.21 | convolution fusion | flops 5909905408 | bytes 61603840 | tf_op jit(solution)/shard_map/jmf,jfd->jmd/dot_general | solution.py:169
  188.6 3.9 %fusion.3 = bf16[1024,2048]{1,0:T(8,128)(2,1)S(1)} fusion(f32[8,128,2048]{2,1,0:T(8,128)} %fusion.8, f32[1024]{0:T(1024)S(1)} %select_reduce_fusion), kind=kLoop, calls=%fused_computation.8 | loop fusion | flops 4194304 | bytes 12587008 | tf_op jit(solution)/shard_map/convert_element_type | solution.py:170
  192.5 3.8 %convolution_convert_fusion.1 = bf16[512,2048]{1,0:T(8,128)(2,1)} fusion(pred[512,1024]{1,0:T(8,128)(4,1)S(1)} %fusion.1, bf16[1024,2048]{1,0:T(8,128)(2,1)S(1)} %fusion.3), kind=kOutput, calls=%fused_computation.15 | convolution fusion | flops 2148532224 | bytes 6815744 | tf_op jit(solution)/shard_map/dot_general | solution.py:173
  196.3 0.0 reduce-scatter.8.cloned.1.call-start
  196.3 10.9 %reduce-scatter.6.cloned.1.call-done = bf16[512,1024]{1,0:T(8,128)(2,1)} async-done(((bf16[512,2048]{1,0:T(8,128)(2,1)}), bf16[512,1024]{1,0:T(8,128)(2,1)}) %reduce-scatter.6.cloned.1.call-update) | async-done | bytes 1048592 | tf_op jit(solution)/shard_map/reduce_scatter | solution.py:174
  207.2 31.1 %reduce-scatter.8.cloned.1.call-done = bf16[128,1024]{1,0:T(8,128)(2,1)} async-done(((bf16[512,1024]{1,0:T(8,128)(2,1)}), bf16[128,1024]{1,0:T(8,128)(2,1)}) %reduce-scatter.8.cloned.1.call-update) | async-done | bytes 262160 | tf_op jit(solution)/shard_map/reduce_scatter | solution.py:175
  (41 shorter events, 0.4 us)
Async XLA Ops:
  7.2 81.9 %copy-start = (bf16[512,2048]{1,0:T(8,128)(2,1)S(1)}, bf16[512,2048]{1,0:T(8,128)(2,1)}, u32[]{:S(2)}) copy-start(bf16[512,2048]{1,0:T(8,128)(2,1)} %param.24) | copy-start | bytes 6291460
  7.2 8.4 %copy-start.4 = (bf16[128,2304]{1,0:T(8,128)(2,1)S(1)}, bf16[128,2304]{1,0:T(8,128)(2,1)}, u32[]{:S(2)}) copy-start(bf16[128,2304]{1,0:T(8,128)(2,1)} %param.16) | copy-start | bytes 1769476
  7.2 9.5 %copy-start.5 = (bf16[512,512]{1,0:T(8,128)(2,1)S(1)}, bf16[512,512]{1,0:T(8,128)(2,1)}, u32[]{:S(2)}) copy-start(bf16[512,512]{1,0:T(8,128)(2,1)} %param.23) | copy-start | bytes 1572868
  7.2 49.3 %all-gather.10.cloned.1.call-start = ((), (), s32[]{:S(2)}) async-start(), calls=%async_computation.8 | async-start | bytes 3981312 | tf_op jit(solution)/shard_map/all_gather | solution.py:71
  12.2 85.2 %reduce-scatter.4.cloned.1.call-start = ((), (), s32[]{:S(2)}) async-start(), calls=%async_computation.3 | async-start | bytes 786432 | tf_op jit(solution)/shard_map/reduce_scatter | solution.py:116
  69.8 5.6 %slice-start = ((bf16[4,42,9216]{2,1,0:T(8,128)(2,1)}), bf16[4,8,9216]{2,1,0:T(8,128)(2,1)S(1)}, s32[]{:S(2)}) async-start(bf16[4,42,9216]{2,1,0:T(8,128)(2,1)} %reshape.257), calls=%async_computation.9 | async-start | bytes 1179648 | tf_op jit(solution)/shard_map/slice | solution.py:74
  89.0 1.4 copy-start.8
  89.1 8.3 %copy-start.7 = (bf16[128,2048]{1,0:T(8,128)(2,1)S(1)}, bf16[128,2048]{1,0:T(8,128)(2,1)}, u32[]{:S(2)}) copy-start(bf16[128,2048]{1,0:T(8,128)(2,1)} %param.15) | copy-start | bytes 1572868
  90.4 40.7 %all-gather.6.cloned.1.call-start = ((), (), s32[]{:S(2)}) async-start(), calls=%async_computation.4 | async-start | bytes 1310720 | tf_op jit(solution)/shard_map/all_gather | solution.py:128
  98.5 37.7 %copy-start.3 = (bf16[128,1024]{1,0:T(8,128)(2,1)}, bf16[128,1024]{1,0:T(8,128)(2,1)S(1)}, u32[]{:S(2)}) copy-start(bf16[128,1024]{1,0:T(8,128)(2,1)S(1)} %get-tuple-element.3) | copy-start | bytes 786436
  101.8 40.8 %all-gather.8.cloned.1.call-start = ((), (), s32[]{:S(2)}) async-start(), calls=%async_computation.5 | async-start | bytes 3145728 | tf_op jit(solution)/shard_map/all_gather | solution.py:129
  131.1 11.6 %copy-start.6 = (bf16[2048,32]{0,1:T(8,128)(2,1)S(1)}, bf16[2048,32]{0,1:T(8,128)(2,1)}, u32[]{:S(2)}) copy-start(bf16[2048,32]{0,1:T(8,128)(2,1)} %param.26) | copy-start | bytes 393220
  131.1 76.1 %reduce-scatter.6.cloned.1.call-start = ((), (), s32[]{:S(2)}) async-start(), calls=%async_computation.6 | async-start | bytes 3145728 | tf_op jit(solution)/shard_map/reduce_scatter | solution.py:174
  150.7 2.0 copy-start.2
  192.5 45.8 %copy-start.1 = (bf16[512,2048]{1,0:T(8,128)(2,1)S(1)}, bf16[512,2048]{1,0:T(8,128)(2,1)}, u32[]{:S(2)}) copy-start(bf16[512,2048]{1,0:T(8,128)(2,1)} %param.24) | copy-start | bytes 6291460
  196.3 42.0 %reduce-scatter.8.cloned.1.call-start = ((), (), s32[]{:S(2)}) async-start(), calls=%async_computation.7 | async-start | bytes 1310720 | tf_op jit(solution)/shard_map/reduce_scatter | solution.py:175
Sparse Core Ops, SparseCore 0:
  12.3 44.2 all-gather.9
  90.5 6.8 reduce-scatter.3
  101.9 29.0 all-gather.5
  132.5 10.0 all-gather.7
  196.4 10.7 reduce-scatter.5
  209.9 28.3 reduce-scatter.7

commit v4 on v3

--- a/solution.py
+++ b/solution.py
@@ -70,10 +70,7 @@
     share = lax.dynamic_slice_in_dim(packed, ffn_index * share_rows, share_rows, 0)
     gathered = lax.all_gather(share, ("exp", "ffn"), axis=0, tiled=False)
     gathered = gathered.reshape(exp_size, ffn_size * share_rows, page_width)
-    pool_all = gathered[:, :pool_pages].reshape(exp_size * pool_pages, page_width)
-    latent_all = gathered[:, pool_pages : pool_pages + latent_pages].reshape(
-        exp_size * token_rows, QKD
-    )
+    stride = ffn_size * share_rows
     group_rows = exp_size * token_rows
     routes_all = (
         gathered[:, pool_pages + latent_pages : packed_rows]
@@ -81,12 +78,20 @@
         .reshape(group_rows, TOP)
         .astype(jnp.int32)
     )
-    pool_base = req_index * pool_all.shape[0]
+    flat_pages = gathered.reshape(exp_size * stride, page_width)
+    pool_base = req_index * exp_size * pool_pages
     page_rows = page_table[request] - pool_base
-    cached_keys = jnp.take(pool_all, page_rows, axis=0).reshape(CMAX, QKD)
+    cached_rows = (page_rows // pool_pages) * stride + page_rows % pool_pages
     local_request = request - req_index * REQ_GRP
-    fresh_keys = lax.dynamic_slice_in_dim(latent_all, local_request * fresh_len, fresh_len, 0)
-    all_keys = jnp.concatenate([cached_keys, fresh_keys], axis=0)
+    fresh_devices = fresh_len // token_rows
+    fresh_index = lax.broadcasted_iota(jnp.int32, (fresh_devices, latent_pages), 0)
+    fresh_rows = (
+        (local_request * fresh_devices + fresh_index) * stride
+        + pool_pages
+        + lax.broadcasted_iota(jnp.int32, (fresh_devices, latent_pages), 1)
+    ).reshape(fresh_devices * latent_pages)
+    key_rows = jnp.concatenate([cached_rows, fresh_rows], axis=0)
+    all_keys = jnp.take(flat_pages, key_rows, axis=0).reshape(CMAX + fresh_len, QKD)
     heads_here = queries.shape[1] // QKD
     query_heads = queries.reshape(token_rows, heads_here, QKD)
     scale_factor = (HEAD_DIM + ROPE_DIM) ** (-0.5)

time: 246 us -> 244 us (level)
  waiting for transfers between devices: 119 us -> 114 us
  local copies, waits for them, and re-layouts: 30.9 us -> 35.3 us
  matrix products: 58.2 us -> 54.4 us
    unnamed x22, local copies, waits for them, and re-layouts: 5.19 us -> 9.92 us
    all_gather x1, waiting for transfers between devices: 5.14 us -> 0.62 us  [local(): normed_all = lax.all_gather(normed_half, 'ffn', axis=1, tiled=True)]
    select_n x0 -> x1, local copies, waits for them, and re-layouts: none -> 3.9 us  [local(): jnp.take(flat_pages, key_rows, axis=0).reshape(CMAX + fresh_len, QKD)]
    slice x3 -> x0, local copies, waits for them, and re-layouts: 3.25 us -> none  [the longest x1 3.25 us: local(): gathered[:, :pool_pages].reshape(exp_size * pool_pages, page_width)]
    sub x1 -> x0, matrix products: 2.89 us -> none  [local(): weights = jnp.exp(scores - top_score)]
    gather x3 -> x2, local copies, waits for them, and re-layouts: 10.9 us -> 10.1 us  [local(): jnp.take(flat_pages, key_rows, axis=0).reshape(CMAX + fresh_len, QKD)]
  transfers between devices with their start and end apart: 6 -> 6, of which waited for: 6 -> 6; matrix products, arithmetic and copies ran while one was open for 6% -> 8% of each run, Pallas kernels for 0% -> 0%
where the time goes in v4:
time: 244 us; the launch traced here: 243 us
  waiting for transfers between devices  114 us (47%)
  matrix products  54.4 us (22%)
  local copies, waits for them, and re-layouts  35.3 us (14%)
  other arithmetic  21.8 us (9%)
  between operations  14.5 us (6%)
  blocking collectives  2.47 us (1%)
    all_gather x1, waiting for transfers between devices, local(): gathered = lax.all_gather(share, ('exp', 'ffn'), axis=0, tiled=False)  35.9 us
    reduce_scatter x1, waiting for transfers between devices, local(): moe_out = lax.psum_scatter(moe_cols, 'exp', scatter_dimension=0, tiled=True)  31.1 us
    all_gather x1, waiting for transfers between devices, local(): normed_half = lax.all_gather(normed_cols, 'exp', axis=0, tiled=True)  29.2 us
    dot_general x1, matrix products, local(): jnp.einsum('jmf,jfd->jmd', active, down_weight, preferred_element_type=jn...  23.6 us
    dot_general x1, matrix products, local(): jnp.einsum('jmd,jdf->jmf', grouped, gate_weight, preferred_element_type=j...  12.3 us
    reduce_scatter x1, waiting for transfers between devices, local(): moe_cols = lax.psum_scatter(mixture, 'ffn', scatter_dimension=1, tiled=True)  10.9 us
    gather x2, local copies, waits for them, and re-layouts, local(): jnp.take(flat_pages, key_rows, axis=0).reshape(CMAX + fresh_len, QKD)  10.1 us
    unnamed x22, local copies, waits for them, and re-layouts  9.92 us
  transfers between devices with their start and end apart: 6, of which 6 were waited for; matrix products, arithmetic and copies ran while one was open for 8% of the time, Pallas kernels for 0%

profile of v4, /device:TPU:0, one launch (start us, length us, event | category | flops | bytes accessed | tf_op | source)
XLA Modules:
  0.0 243.3 jit_solution(17411121236919590765)
XLA Ops:
  7.2 1.2 copy.43
  8.5 0.2 reshape.346
  8.7 0.7 convert_element_type.101
  9.4 0.1 copy.44
  9.5 0.2 convert_element_type.102
  9.7 0.1 pad.10.clone
  9.8 0.1 dynamic-slice
  9.8 2.3 fusion.36
  12.3 0.1 iota_add_fusion.1
  12.3 0.1 concatenate.36
  12.4 0.1 add.210
  12.5 1.2 dynamic_slice.19
  13.7 1.2 dynamic_slice.20
  15.0 0.3 copy.45
  15.3 0.7 fusion.40
  16.0 0.1 compare_and_fusion
  16.1 0.1 broadcast_in_dim.80
  16.2 0.1 broadcast_in_dim.81
  16.3 1.3 copy.55
  17.5 0.7 fusion.69
  18.2 0.1 fusion.43
  18.3 1.3 iota_compare_fusion.6
  19.6 1.0 and_or_fusion
  20.7 35.9 %all-gather.10.cloned.1.call-done = bf16[8,21,9216]{2,1,0:T(8,128)(2,1)} async-done(((bf16[1,21,9216]{2,1,0:T(8,128)(2,1)}), bf16[8,21,9216]{2,1,0:T(8,128)(2,1)}) %all-gather.10.cloned.1.call-update) | async-done | bytes 3096592 | tf_op jit(solution)/shard_map/all_gather | solution.py:71
  56.6 4.8 %reshape.369 = bf16[168,9216]{1,0:T(8,128)(2,1)} reshape(bf16[8,21,9216]{2,1,0:T(8,128)(2,1)} %all-gather.10.cloned.1.call-done) | data formatting | bytes 6193152
  61.4 6.3 %gather_fusion = bf16[80,9216]{1,0:T(8,128)(2,1)} fusion(bf16[168,9216]{1,0:T(8,128)(2,1)} %reshape.369, s32[1024]{0:T(1024)S(1)} %pad_clamp_fusion), kind=kCustom, calls=%fused_computation | custom fusion | bytes 2949440 | tf_op jit(solution)/shard_map/jit(_take)/gather | solution.py:94
  67.7 2.7 %broadcast_select_fusion = bf16[80,9216]{1,0:T(8,128)(2,1)} fusion(bf16[80,9216]{1,0:T(8,128)(2,1)} %gather_fusion, pred[80]{0:T(512)(128)(4,1)S(1)} %compare_and_fusion), kind=kLoop, calls=%fused_computation.21 | loop fusion | flops 737280 | bytes 2949200 | tf_op jit(solution)/shard_map/jit(_take)/select_n | solution.py:94
  70.3 3.9 %gather.7 = bf16[1280,576]{1,0:T(8,128)(2,1)} reshape(bf16[80,9216]{1,0:T(8,128)(2,1)} %gather_fusion) | data formatting | bytes 2949120 | tf_op jit(solution)/shard_map/jit(_take)/gather | solution.py:94
  74.2 3.9 %select_n.117 = bf16[1280,576]{1,0:T(8,128)(2,1)} reshape(bf16[80,9216]{1,0:T(8,128)(2,1)} %broadcast_select_fusion) | data formatting | bytes 2949120 | tf_op jit(solution)/shard_map/jit(_take)/select_n | solution.py:94
  78.1 2.6 %fusion.6 = f32[128,4,1280]{0,2,1:T(8,128)S(1)} fusion(bf16[128,4,576]{0,2,1:T(8,128)(2,1)S(1)} %bitcast.75, bf16[1280,576]{1,0:T(8,128)(2,1)} %select_n.117, pred[128,1280]{0,1:T(8,128)(4,1)S(1)} %and_or_fusion), kind=kOutput, calls=%fused_computation.13 | convolution fusion | flops 756285440 | bytes 4849664 | tf_op jit(solution)/shard_map/thd,kd->thk/dot_general | solution.py:99
  80.8 1.5 copy-done.3
  82.3 0.6 fusion.49
  82.9 4.4 %fusion.23 = bf16[4,128,128]{1,2,0:T(8,128)(2,1)S(1)} fusion(bf16[512,4,128]{0,2,1:T(8,128)(2,1)S(1)} %bitcast.76, bf16[1280,576]{1,0:T(8,128)(2,1)} %gather.7, pred[1280]{0:T(1024)(128)(4,1)S(1)} %broadcast_in_dim.81, f32[128,4]{0,1:T(4,128)S(1)} %fusion.49, f32[128,4,1280]{0,2,1:T(8,128)} %copy-done.3), kind=kOutput, calls=%fused_computation.32 | convolution fusion | flops 741148416 | bytes 7212288 | tf_op jit(solution)/shard_map/thl,lhd->thd/dot_general | solution.py:115
  87.3 1.3 convolution_convert_fusion.2
  88.5 0.2 all-gather.6.cloned.1.call-start
  88.8 6.7 %reduce-scatter.4.cloned.1.call-done = bf16[128,1024]{1,0:T(8,128)(2,1)} async-done(((bf16[128,2048]{1,0:T(8,128)(2,1)}), bf16[128,1024]{1,0:T(8,128)(2,1)}) %reduce-scatter.4.cloned.1.call-update) | async-done | bytes 262160 | tf_op jit(solution)/shard_map/reduce_scatter | solution.py:121
  95.5 1.1 fusion.30
  96.6 2.5 %psum.7 = f32[128,1]{0,1:T(1,128)S(1)} all-reduce(f32[128,1]{0,1:T(1,128)S(1)} %bitcast.79), channel_id=1, replica_groups=mesh['req'=4,'exp'=4,'ffn'=2] {'ffn'}, use_global_device_ids=true, to_apply=%region_7.8 | all-reduce | flops 128 | bytes 1024 | tf_op jit(solution)/shard_map/psum | solution.py:127
  99.1 0.8 fusion.32
  100.0 29.2 %all-gather.6.cloned.1.call-done = bf16[512,1024]{1,0:T(8,128)(2,1)} async-done(((bf16[128,1024]{1,0:T(8,128)(2,1)}), bf16[512,1024]{1,0:T(8,128)(2,1)}) %all-gather.6.cloned.1.call-update) | async-done | bytes 1048592 | tf_op jit(solution)/shard_map/all_gather | solution.py:133
  129.3 0.1 add.217
  129.4 0.1 add.218
  129.4 4.7 %reshape.351 = bf16[4,42,9216]{2,1,0:T(8,128)(2,1)} reshape(bf16[8,21,9216]{2,1,0:T(8,128)(2,1)} %all-gather.10.cloned.1.call-done) | data formatting | bytes 6193152 | tf_op jit(solution)/shard_map/reshape | solution.py:72
  134.1 1.2 slice.15
  135.4 0.2 reshape.355
  135.6 0.1 copy.51
  135.7 0.3 fusion.22
  136.0 0.2 convert_element_type.117
  136.2 0.1 add_select_fusion
  136.4 0.1 copy.49
  136.5 2.3 fusion.2
  138.8 1.4 fusion.1
  140.2 0.6 all-gather.8.cloned.1.call-done
  140.8 2.3 fusion.51
  143.1 0.1 select_reduce_fusion.1
  143.2 1.7 select_reduce_fusion
  145.0 3.9 %convolution_convert_fusion = bf16[1024,2048]{1,0:T(8,128)(2,1)S(1)} fusion(pred[1024,512]{1,0:T(8,128)(4,1)S(1)} %fusion.2, bf16[512,2048]{1,0:T(8,128)(2,1)} %all-gather.8.cloned.1.call-done), kind=kOutput, calls=%fused_computation.9 | convolution fusion | flops 2149580800 | bytes 6815744 | tf_op jit(solution)/shard_map/dot_general | solution.py:167
  148.9 2.0 copy-done.2
  150.9 12.3 %fusion.50 = f32[8,128,704]{1,2,0:T(8,128)} fusion(bf16[8,128,2048]{2,1,0:T(8,128)(2,1)S(1)} %bitcast.73, bf16[8,2048,704]{1,2,0:T(8,128)(2,1)} %param.27), kind=kOutput, calls=%fused_computation.89 | convolution fusion | flops 2952790016 | bytes 30146560 | tf_op jit(solution)/shard_map/jmd,jdf->jmf/dot_general | solution.py:171
  163.2 23.6 %fusion.8 = f32[8,128,2048]{2,1,0:T(8,128)} fusion(bf16[8,704,2048]{2,1,0:T(8,128)(2,1)} %param.29, f32[8,128,704]{1,2,0:T(8,128)} %fusion.50, bf16[8,128,2048]{2,1,0:T(8,128)(2,1)} %bitcast.74, bf16[8,2048,704]{1,2,0:T(8,128)(2,1)} %param.28), kind=kOutput, calls=%fused_computation.19 | convolution fusion | flops 5909905408 | bytes 61603840 | tf_op jit(solution)/shard_map/jmf,jfd->jmd/dot_general | solution.py:174
  186.7 3.9 %fusion.3 = bf16[1024,2048]{1,0:T(8,128)(2,1)S(1)} fusion(f32[8,128,2048]{2,1,0:T(8,128)} %fusion.8, f32[1024]{0:T(1024)S(1)} %select_reduce_fusion), kind=kLoop, calls=%fused_computation.8 | loop fusion | flops 4194304 | bytes 12587008 | tf_op jit(solution)/shard_map/convert_element_type | solution.py:175
  190.6 3.7 %convolution_convert_fusion.1 = bf16[512,2048]{1,0:T(8,128)(2,1)} fusion(pred[512,1024]{1,0:T(8,128)(4,1)S(1)} %fusion.1, bf16[1024,2048]{1,0:T(8,128)(2,1)S(1)} %fusion.3), kind=kOutput, calls=%fused_computation.15 | convolution fusion | flops 2148532224 | bytes 6815744 | tf_op jit(solution)/shard_map/dot_general | solution.py:178
  194.5 10.9 %reduce-scatter.6.cloned.1.call-done = bf16[512,1024]{1,0:T(8,128)(2,1)} async-done(((bf16[512,2048]{1,0:T(8,128)(2,1)}), bf16[512,1024]{1,0:T(8,128)(2,1)}) %reduce-scatter.6.cloned.1.call-update) | async-done | bytes 1048592 | tf_op jit(solution)/shard_map/reduce_scatter | solution.py:179
  205.4 31.1 %reduce-scatter.8.cloned.1.call-done = bf16[128,1024]{1,0:T(8,128)(2,1)} async-done(((bf16[512,1024]{1,0:T(8,128)(2,1)}), bf16[128,1024]{1,0:T(8,128)(2,1)}) %reduce-scatter.8.cloned.1.call-update) | async-done | bytes 262160 | tf_op jit(solution)/shard_map/reduce_scatter | solution.py:180
  (42 shorter events, 0.5 us)
Async XLA Ops:
  7.2 80.1 %copy-start = (bf16[512,2048]{1,0:T(8,128)(2,1)S(1)}, bf16[512,2048]{1,0:T(8,128)(2,1)}, u32[]{:S(2)}) copy-start(bf16[512,2048]{1,0:T(8,128)(2,1)} %param.24) | copy-start | bytes 6291460
  7.2 7.8 %copy-start.5 = (bf16[128,2304]{1,0:T(8,128)(2,1)S(1)}, bf16[128,2304]{1,0:T(8,128)(2,1)}, u32[]{:S(2)}) copy-start(bf16[128,2304]{1,0:T(8,128)(2,1)} %param.16) | copy-start | bytes 1769476
  7.2 49.4 %all-gather.10.cloned.1.call-start = ((), (), s32[]{:S(2)}) async-start(), calls=%async_computation.8 | async-start | bytes 3981312 | tf_op jit(solution)/shard_map/all_gather | solution.py:71
  12.2 83.3 %reduce-scatter.4.cloned.1.call-start = ((), (), s32[]{:S(2)}) async-start(), calls=%async_computation.3 | async-start | bytes 786432 | tf_op jit(solution)/shard_map/reduce_scatter | solution.py:121
  80.8 1.5 copy-start.3
  87.2 1.6 copy-start.8
  87.2 8.3 %copy-start.7 = (bf16[128,2048]{1,0:T(8,128)(2,1)S(1)}, bf16[128,2048]{1,0:T(8,128)(2,1)}, u32[]{:S(2)}) copy-start(bf16[128,2048]{1,0:T(8,128)(2,1)} %param.15) | copy-start | bytes 1572868
  88.5 40.7 %all-gather.6.cloned.1.call-start = ((), (), s32[]{:S(2)}) async-start(), calls=%async_computation.4 | async-start | bytes 1310720 | tf_op jit(solution)/shard_map/all_gather | solution.py:133
  96.6 37.5 %copy-start.4 = (bf16[128,1024]{1,0:T(8,128)(2,1)}, bf16[128,1024]{1,0:T(8,128)(2,1)S(1)}, u32[]{:S(2)}) copy-start(bf16[128,1024]{1,0:T(8,128)(2,1)S(1)} %get-tuple-element.3) | copy-start | bytes 786436
  100.0 40.8 %all-gather.8.cloned.1.call-start = ((), (), s32[]{:S(2)}) async-start(), calls=%async_computation.5 | async-start | bytes 3145728 | tf_op jit(solution)/shard_map/all_gather | solution.py:134
  129.2 76.1 %reduce-scatter.6.cloned.1.call-start = ((), (), s32[]{:S(2)}) async-start(), calls=%async_computation.6 | async-start | bytes 3145728 | tf_op jit(solution)/shard_map/reduce_scatter | solution.py:179
  134.1 6.7 %copy-start.6 = (bf16[2048,32]{0,1:T(8,128)(2,1)S(1)}, bf16[2048,32]{0,1:T(8,128)(2,1)}, u32[]{:S(2)}) copy-start(bf16[2048,32]{0,1:T(8,128)(2,1)} %param.26) | copy-start | bytes 393220
  148.9 2.0 copy-start.2
  190.6 45.8 %copy-start.1 = (bf16[512,2048]{1,0:T(8,128)(2,1)S(1)}, bf16[512,2048]{1,0:T(8,128)(2,1)}, u32[]{:S(2)}) copy-start(bf16[512,2048]{1,0:T(8,128)(2,1)} %param.24) | copy-start | bytes 6291460
  194.4 42.0 %reduce-scatter.8.cloned.1.call-start = ((), (), s32[]{:S(2)}) async-start(), calls=%async_computation.7 | async-start | bytes 1310720 | tf_op jit(solution)/shard_map/reduce_scatter | solution.py:180
Sparse Core Ops, SparseCore 0:
  12.3 44.2 all-gather.9
  88.7 6.7 reduce-scatter.3
  100.1 29.0 all-gather.5
  130.7 10.0 all-gather.7
  194.5 10.7 reduce-scatter.5
  208.1 28.3 reduce-scatter.7

commit v5 on v4

--- a/solution.py
+++ b/solution.py
@@ -17,6 +17,24 @@
 
 EPSILON = 1e-06
 NEG_FILL = -1e30
+
+
+def line_gather(x, axis_name):
+    size = lax.axis_size(axis_name)
+    position = lax.axis_index(axis_name)
+    to_right = [(i, i + 1) for i in range(size - 1)]
+    to_left = [(i + 1, i) for i in range(size - 1)]
+    from_left = x
+    from_right = x
+    left_pieces = []
+    right_pieces = []
+    for _ in range(size - 1):
+        from_left = lax.ppermute(from_left, axis_name, to_right)
+        from_right = lax.ppermute(from_right, axis_name, to_left)
+        left_pieces.append(from_left)
+        right_pieces.append(from_right)
+    stack = jnp.stack(left_pieces[::-1] + [x] + right_pieces)
+    return lax.dynamic_slice_in_dim(stack, size - 1 - position, size, 0)
 
 
 def local(
@@ -130,7 +148,7 @@
     normed_cols = (
         hidden_wide * lax.rsqrt(mean_square + EPSILON) * gain_cols.astype(jnp.float32)
     ).astype(jnp.bfloat16)
-    normed_half = lax.all_gather(normed_cols, "exp", axis=0, tiled=True)
+    normed_half = line_gather(normed_cols, "exp").reshape(group_rows, column_count)
     normed_all = lax.all_gather(normed_half, "ffn", axis=1, tiled=True)
 
     expert_ids = lax.broadcasted_iota(jnp.int32, (1, 1, EXPERTS), 2)

time: 244 us -> 246 us (level)
  starting transfers between devices: 0.42 us -> 16.7 us
  waiting for transfers between devices: 114 us -> 99.8 us
    all_gather x1 -> x0, waiting for transfers between devices: 29.2 us -> none  [local(): normed_half = lax.all_gather(normed_cols, 'exp', axis=0, tiled=True)]
    ppermute x0 -> x6, starting transfers between devices: none -> 16.3 us  [the longest x3 12.4 us: line_gather(): from_left = lax.ppermute(from_left, axis_name, to_right)]
    ppermute x0 -> x6, waiting for transfers between devices: none -> 15.5 us  [the longest x3 11.7 us: line_gather(): from_left = lax.ppermute(from_left, axis_name, to_right)]
    unnamed x22 -> x27, local copies, waits for them, and re-layouts: 9.92 us -> 10 us
  transfers between devices with their start and end apart: 6 -> 11, of which waited for: 6 -> 8; matrix products, arithmetic and copies ran while one was open for 8% -> 8% of each run, Pallas kernels for 0% -> 0%
where the time goes in v5:
time: 246 us; the launch traced here: 245 us
  waiting for transfers between devices  99.8 us (41%)
  matrix products  54.4 us (22%)
  local copies, waits for them, and re-layouts  36.5 us (15%)
  other arithmetic  21.3 us (9%)
  starting transfers between devices  16.7 us (7%)
  between operations  14.3 us (6%)
  blocking collectives  2.47 us (1%)
    all_gather x1, waiting for transfers between devices, local(): gathered = lax.all_gather(share, ('exp', 'ffn'), axis=0, tiled=False)  35.9 us
    reduce_scatter x1, waiting for transfers between devices, local(): moe_out = lax.psum_scatter(moe_cols, 'exp', scatter_dimension=0, tiled=True)  31 us
    dot_general x1, matrix products, local(): jnp.einsum('jmf,jfd->jmd', active, down_weight, preferred_element_type=jn...  23.6 us
    ppermute x3, starting transfers between devices, line_gather(): from_left = lax.ppermute(from_left, axis_name, to_right)  12.4 us
    dot_general x1, matrix products, local(): jnp.einsum('jmd,jdf->jmf', grouped, gate_weight, preferred_element_type=j...  12.3 us
    ppermute x3, waiting for transfers between devices, line_gather(): from_left = lax.ppermute(from_left, axis_name, to_right)  11.7 us
    reduce_scatter x1, waiting for transfers between devices, local(): moe_cols = lax.psum_scatter(mixture, 'ffn', scatter_dimension=1, tiled=True)  10.5 us
    gather x2, local copies, waits for them, and re-layouts, local(): jnp.take(flat_pages, key_rows, axis=0).reshape(CMAX + fresh_len, QKD)  10.1 us
  transfers between devices with their start and end apart: 11, of which 8 were waited for; matrix products, arithmetic and copies ran while one was open for 8% of the time, Pallas kernels for 0%

profile of v5, /device:TPU:0, one launch (start us, length us, event | category | flops | bytes accessed | tf_op | source)
XLA Modules:
  0.0 245.3 jit_solution(10133127418376307781)
XLA Ops:
  7.2 1.2 copy.43
  8.5 0.2 reshape.349
  8.7 0.7 convert_element_type.101
  9.4 0.1 copy.44
  9.5 0.2 convert_element_type.102
  9.8 2.3 fusion.36
  12.3 0.1 concatenate.36
  12.5 1.2 dynamic_slice.22
  13.7 1.2 dynamic_slice.23
  15.0 0.3 copy.45
  15.3 0.7 fusion.40
  16.2 0.1 broadcast_in_dim.81
  16.3 1.3 copy.55
  17.5 0.7 fusion.69
  18.3 1.3 iota_compare_fusion.6
  19.6 1.0 and_or_fusion
  20.7 35.9 %all-gather.7.cloned.1.call-done = bf16[8,21,9216]{2,1,0:T(8,128)(2,1)} async-done(((bf16[1,21,9216]{2,1,0:T(8,128)(2,1)}), bf16[8,21,9216]{2,1,0:T(8,128)(2,1)}) %all-gather.7.cloned.1.call-update) | async-done | bytes 3096592 | tf_op jit(solution)/shard_map/all_gather | solution.py:89
  56.6 4.8 %reshape.373 = bf16[168,9216]{1,0:T(8,128)(2,1)} reshape(bf16[8,21,9216]{2,1,0:T(8,128)(2,1)} %all-gather.7.cloned.1.call-done) | data formatting | bytes 6193152
  61.4 6.3 %gather_fusion = bf16[80,9216]{1,0:T(8,128)(2,1)} fusion(bf16[168,9216]{1,0:T(8,128)(2,1)} %reshape.373, s32[1024]{0:T(1024)S(1)} %pad_clamp_fusion), kind=kCustom, calls=%fused_computation | custom fusion | bytes 2949440 | tf_op jit(solution)/shard_map/jit(_take)/gather | solution.py:112
  67.7 2.7 %broadcast_select_fusion = bf16[80,9216]{1,0:T(8,128)(2,1)} fusion(bf16[80,9216]{1,0:T(8,128)(2,1)} %gather_fusion, pred[80]{0:T(512)(128)(4,1)S(1)} %compare_and_fusion), kind=kLoop, calls=%fused_computation.21 | loop fusion | flops 737280 | bytes 2949200 | tf_op jit(solution)/shard_map/jit(_take)/select_n | solution.py:112
  70.3 3.9 %gather.7 = bf16[1280,576]{1,0:T(8,128)(2,1)} reshape(bf16[80,9216]{1,0:T(8,128)(2,1)} %gather_fusion) | data formatting | bytes 2949120 | tf_op jit(solution)/shard_map/jit(_take)/gather | solution.py:112
  74.2 3.9 %select_n.120 = bf16[1280,576]{1,0:T(8,128)(2,1)} reshape(bf16[80,9216]{1,0:T(8,128)(2,1)} %broadcast_select_fusion) | data formatting | bytes 2949120 | tf_op jit(solution)/shard_map/jit(_take)/select_n | solution.py:112
  78.1 2.6 %fusion.6 = f32[128,4,1280]{0,2,1:T(8,128)S(1)} fusion(bf16[128,4,576]{0,2,1:T(8,128)(2,1)S(1)} %bitcast.91, bf16[1280,576]{1,0:T(8,128)(2,1)} %select_n.120, pred[128,1280]{0,1:T(8,128)(4,1)S(1)} %and_or_fusion), kind=kOutput, calls=%fused_computation.13 | convolution fusion | flops 756285440 | bytes 4849664 | tf_op jit(solution)/shard_map/thd,kd->thk/dot_general | solution.py:117
  80.8 1.5 copy-done.3
  82.3 0.6 fusion.49
  82.9 4.4 %fusion.23 = bf16[4,128,128]{1,2,0:T(8,128)(2,1)S(1)} fusion(bf16[512,4,128]{0,2,1:T(8,128)(2,1)S(1)} %bitcast.92, bf16[1280,576]{1,0:T(8,128)(2,1)} %gather.7, pred[1280]{0:T(1024)(128)(4,1)S(1)} %broadcast_in_dim.81, f32[128,4]{0,1:T(4,128)S(1)} %fusion.49, f32[128,4,1280]{0,2,1:T(8,128)} %copy-done.3), kind=kOutput, calls=%fused_computation.32 | convolution fusion | flops 741148416 | bytes 7212288 | tf_op jit(solution)/shard_map/thl,lhd->thd/dot_general | solution.py:133
  87.3 1.3 convolution_convert_fusion.2
  88.5 0.2 all-gather.5.cloned.1.call-start
  88.8 6.7 %reduce-scatter.4.cloned.1.call-done = bf16[128,1024]{1,0:T(8,128)(2,1)} async-done(((bf16[128,2048]{1,0:T(8,128)(2,1)}), bf16[128,1024]{1,0:T(8,128)(2,1)}) %reduce-scatter.4.cloned.1.call-update) | async-done | bytes 262160 | tf_op jit(solution)/shard_map/reduce_scatter | solution.py:139
  95.5 1.1 fusion.30
  96.6 2.5 %psum.7 = f32[128,1]{0,1:T(1,128)S(1)} all-reduce(f32[128,1]{0,1:T(1,128)S(1)} %bitcast.95), channel_id=1, replica_groups=mesh['req'=4,'exp'=4,'ffn'=2] {'ffn'}, use_global_device_ids=true, to_apply=%region_7.8 | all-reduce | flops 128 | bytes 1024 | tf_op jit(solution)/shard_map/psum | solution.py:145
  99.1 0.1 fusion.32
  99.2 3.6 %collective-permute-start = (bf16[128,1024]{1,0:T(8,128)(2,1)S(1)}, bf16[128,1024]{1,0:T(8,128)(2,1)S(1)}, u32[]{:S(2)}, u32[]{:S(2)}) collective-permute-start(bf16[128,1024]{1,0:T(8,128)(2,1)S(1)} %fusion.32), channel_id=1, source_target_pairs={{0,2},{2,4},{4,6},{1,3},{3,5},{5,7},{8,10},{10,12},{12,14},{9,11},... | collective-permute-start | bytes 786440 | tf_op jit(solution)/shard_map/ppermute | solution.py:32
  102.9 1.3 collective-permute-start.3
  104.2 4.7 %collective-permute-done = bf16[128,1024]{1,0:T(8,128)(2,1)S(1)} collective-permute-done((bf16[128,1024]{1,0:T(8,128)(2,1)S(1)}, bf16[128,1024]{1,0:T(8,128)(2,1)S(1)}, u32[]{:S(2)}, u32[]{:S(2)}) %collective-permute-start) | collective-permute-done | bytes 262176 | tf_op jit(solution)/shard_map/ppermute | solution.py:32
  108.9 4.4 %collective-permute-start.1 = (bf16[128,1024]{1,0:T(8,128)(2,1)S(1)}, bf16[128,1024]{1,0:T(8,128)(2,1)S(1)}, u32[]{:S(2)}, u32[]{:S(2)}) collective-permute-start(bf16[128,1024]{1,0:T(8,128)(2,1)S(1)} %collective-permute-done), channel_id=1, source_target_pairs={{0,2},{2,4},{4,6},{1,3},{3,5},{5,7},{8,10},{10,12},{12,14},{9,11},... | collective-permute-start | bytes 786440 | tf_op jit(solution)/shard_map/ppermute | solution.py:32
  113.3 1.3 collective-permute-start.4
  114.6 3.9 %collective-permute-done.1 = bf16[128,1024]{1,0:T(8,128)(2,1)S(1)} collective-permute-done((bf16[128,1024]{1,0:T(8,128)(2,1)S(1)}, bf16[128,1024]{1,0:T(8,128)(2,1)S(1)}, u32[]{:S(2)}, u32[]{:S(2)}) %collective-permute-start.1) | collective-permute-done | bytes 262176 | tf_op jit(solution)/shard_map/ppermute | solution.py:32
  118.6 4.4 %collective-permute-start.2 = (bf16[128,1024]{1,0:T(8,128)(2,1)S(1)}, bf16[128,1024]{1,0:T(8,128)(2,1)S(1)}, u32[]{:S(2)}, u32[]{:S(2)}) collective-permute-start(bf16[128,1024]{1,0:T(8,128)(2,1)S(1)} %collective-permute-done.1), channel_id=1, source_target_pairs={{0,2},{2,4},{4,6},{1,3},{3,5},{5,7},{8,10},{10,12},{12,14},{9,11},... | collective-permute-start | bytes 786440 | tf_op jit(solution)/shard_map/ppermute | solution.py:32
  123.0 1.3 collective-permute-start.5
  124.3 3.0 %collective-permute-done.2 = bf16[128,1024]{1,0:T(8,128)(2,1)S(1)} collective-permute-done((bf16[128,1024]{1,0:T(8,128)(2,1)S(1)}, bf16[128,1024]{1,0:T(8,128)(2,1)S(1)}, u32[]{:S(2)}, u32[]{:S(2)}) %collective-permute-start.2) | collective-permute-done | bytes 262176 | tf_op jit(solution)/shard_map/ppermute | solution.py:32
  127.4 0.1 bitcast_dynamic-update-slice_fusion.3
  127.5 3.9 %collective-permute-done.5 = bf16[128,1024]{1,0:T(8,128)(2,1)S(1)} collective-permute-done((bf16[128,1024]{1,0:T(8,128)(2,1)S(1)}, bf16[128,1024]{1,0:T(8,128)(2,1)S(1)}, u32[]{:S(2)}, u32[]{:S(2)}) %collective-permute-start.5) | collective-permute-done | bytes 262176 | tf_op jit(solution)/shard_map/ppermute | solution.py:33
  131.4 1.0 constant_dynamic-slice_fusion
  132.7 4.7 %reshape.354 = bf16[4,42,9216]{2,1,0:T(8,128)(2,1)} reshape(bf16[8,21,9216]{2,1,0:T(8,128)(2,1)} %all-gather.7.cloned.1.call-done) | data formatting | bytes 6193152 | tf_op jit(solution)/shard_map/reshape | solution.py:90
  137.4 1.2 slice.15
  138.7 0.2 reshape.359
  138.9 0.1 copy.51
  139.0 0.3 fusion.22
  139.3 0.2 convert_element_type.117
  139.6 0.1 add_select_fusion
  139.7 0.1 copy.49
  139.8 2.3 fusion.2
  142.1 1.4 fusion.1
  143.5 2.3 fusion.51
  146.0 1.7 select_reduce_fusion
  147.7 3.9 %convolution_convert_fusion = bf16[1024,2048]{1,0:T(8,128)(2,1)S(1)} fusion(pred[1024,512]{1,0:T(8,128)(4,1)S(1)} %fusion.2, bf16[512,2048]{1,0:T(8,128)(2,1)} %all-gather.5.cloned.1.call-done), kind=kOutput, calls=%fused_computation.9 | convolution fusion | flops 2149580800 | bytes 6815744 | tf_op jit(solution)/shard_map/dot_general | solution.py:185
  151.7 2.0 copy-done.2
  153.6 12.3 %fusion.50 = f32[8,128,704]{1,2,0:T(8,128)} fusion(bf16[8,128,2048]{2,1,0:T(8,128)(2,1)S(1)} %bitcast.88, bf16[8,2048,704]{1,2,0:T(8,128)(2,1)} %param.27), kind=kOutput, calls=%fused_computation.97 | convolution fusion | flops 2952790016 | bytes 30146560 | tf_op jit(solution)/shard_map/jmd,jdf->jmf/dot_general | solution.py:189
  165.9 23.6 %fusion.8 = f32[8,128,2048]{2,1,0:T(8,128)} fusion(bf16[8,704,2048]{2,1,0:T(8,128)(2,1)} %param.29, f32[8,128,704]{1,2,0:T(8,128)} %fusion.50, bf16[8,128,2048]{2,1,0:T(8,128)(2,1)} %bitcast.89, bf16[8,2048,704]{1,2,0:T(8,128)(2,1)} %param.28), kind=kOutput, calls=%fused_computation.19 | convolution fusion | flops 5909905408 | bytes 61603840 | tf_op jit(solution)/shard_map/jmf,jfd->jmd/dot_general | solution.py:192
  189.5 3.9 %fusion.3 = bf16[1024,2048]{1,0:T(8,128)(2,1)S(1)} fusion(f32[8,128,2048]{2,1,0:T(8,128)} %fusion.8, f32[1024]{0:T(1024)S(1)} %select_reduce_fusion), kind=kLoop, calls=%fused_computation.8 | loop fusion | flops 4194304 | bytes 12587008 | tf_op jit(solution)/shard_map/convert_element_type | solution.py:193
  193.4 3.7 %convolution_convert_fusion.1 = bf16[512,2048]{1,0:T(8,128)(2,1)} fusion(pred[512,1024]{1,0:T(8,128)(4,1)S(1)} %fusion.1, bf16[1024,2048]{1,0:T(8,128)(2,1)S(1)} %fusion.3), kind=kOutput, calls=%fused_computation.15 | convolution fusion | flops 2148532224 | bytes 6815744 | tf_op jit(solution)/shard_map/dot_general | solution.py:196
  197.2 10.5 %reduce-scatter.6.cloned.1.call-done = bf16[512,1024]{1,0:T(8,128)(2,1)} async-done(((bf16[512,2048]{1,0:T(8,128)(2,1)}), bf16[512,1024]{1,0:T(8,128)(2,1)}) %reduce-scatter.6.cloned.1.call-update) | async-done | bytes 1048592 | tf_op jit(solution)/shard_map/reduce_scatter | solution.py:197
  207.8 31.0 %reduce-scatter.8.cloned.1.call-done = bf16[128,1024]{1,0:T(8,128)(2,1)} async-done(((bf16[512,1024]{1,0:T(8,128)(2,1)}), bf16[128,1024]{1,0:T(8,128)(2,1)}) %reduce-scatter.8.cloned.1.call-update) | async-done | bytes 262160 | tf_op jit(solution)/shard_map/reduce_scatter | solution.py:198
  (59 shorter events, 1.4 us)
Async XLA Ops:
  7.2 80.1 %copy-start = (bf16[512,2048]{1,0:T(8,128)(2,1)S(1)}, bf16[512,2048]{1,0:T(8,128)(2,1)}, u32[]{:S(2)}) copy-start(bf16[512,2048]{1,0:T(8,128)(2,1)} %param.24) | copy-start | bytes 6291460
  7.2 7.8 %copy-start.5 = (bf16[128,2304]{1,0:T(8,128)(2,1)S(1)}, bf16[128,2304]{1,0:T(8,128)(2,1)}, u32[]{:S(2)}) copy-start(bf16[128,2304]{1,0:T(8,128)(2,1)} %param.16) | copy-start | bytes 1769476
  7.2 49.4 %all-gather.7.cloned.1.call-start = ((), (), s32[]{:S(2)}) async-start(), calls=%async_computation.7 | async-start | bytes 3981312 | tf_op jit(solution)/shard_map/all_gather | solution.py:89
  12.2 83.3 %reduce-scatter.4.cloned.1.call-start = ((), (), s32[]{:S(2)}) async-start(), calls=%async_computation.3 | async-start | bytes 786432 | tf_op jit(solution)/shard_map/reduce_scatter | solution.py:139
  80.8 1.5 copy-start.3
  87.2 1.6 copy-start.8
  87.2 8.3 %copy-start.7 = (bf16[128,2048]{1,0:T(8,128)(2,1)S(1)}, bf16[128,2048]{1,0:T(8,128)(2,1)}, u32[]{:S(2)}) copy-start(bf16[128,2048]{1,0:T(8,128)(2,1)} %param.15) | copy-start | bytes 1572868
  88.5 55.0 %all-gather.5.cloned.1.call-start = ((), (), s32[]{:S(2)}) async-start(), calls=%async_computation.4 | async-start | bytes 3145728 | tf_op jit(solution)/shard_map/all_gather | solution.py:152
  96.6 35.9 %copy-start.4 = (bf16[128,1024]{1,0:T(8,128)(2,1)}, bf16[128,1024]{1,0:T(8,128)(2,1)S(1)}, u32[]{:S(2)}) copy-start(bf16[128,1024]{1,0:T(8,128)(2,1)S(1)} %get-tuple-element.3) | copy-start | bytes 786436
  99.2 9.7 %collective-permute-start = (bf16[128,1024]{1,0:T(8,128)(2,1)S(1)}, bf16[128,1024]{1,0:T(8,128)(2,1)S(1)}, u32[]{:S(2)}, u32[]{:S(2)}) collective-permute-start(bf16[128,1024]{1,0:T(8,128)(2,1)S(1)} %fusion.32), channel_id=1, source_target_pairs={{0,2},{2,4},{4,6},{1,3},{3,5},{5,7},{8,10},{10,12},{12,14},{9,11},... | collective-permute-start | bytes 786440 | tf_op jit(solution)/shard_map/ppermute | solution.py:32
  102.9 10.4 %collective-permute-start.3 = (bf16[128,1024]{1,0:T(8,128)(2,1)S(1)}, bf16[128,1024]{1,0:T(8,128)(2,1)S(1)}, u32[]{:S(2)}, u32[]{:S(2)}) collective-permute-start(bf16[128,1024]{1,0:T(8,128)(2,1)S(1)} %fusion.32), channel_id=1, source_target_pairs={{2,0},{4,2},{6,4},{3,1},{5,3},{7,5},{10,8},{12,10},{14,12},{11,9},... | collective-permute-start | bytes 786440 | tf_op jit(solution)/shard_map/ppermute | solution.py:33
  108.9 9.6 %collective-permute-start.1 = (bf16[128,1024]{1,0:T(8,128)(2,1)S(1)}, bf16[128,1024]{1,0:T(8,128)(2,1)S(1)}, u32[]{:S(2)}, u32[]{:S(2)}) collective-permute-start(bf16[128,1024]{1,0:T(8,128)(2,1)S(1)} %collective-permute-done), channel_id=1, source_target_pairs={{0,2},{2,4},{4,6},{1,3},{3,5},{5,7},{8,10},{10,12},{12,14},{9,11},... | collective-permute-start | bytes 786440 | tf_op jit(solution)/shard_map/ppermute | solution.py:32
  113.3 9.6 %collective-permute-start.4 = (bf16[128,1024]{1,0:T(8,128)(2,1)S(1)}, bf16[128,1024]{1,0:T(8,128)(2,1)S(1)}, u32[]{:S(2)}, u32[]{:S(2)}) collective-permute-start(bf16[128,1024]{1,0:T(8,128)(2,1)S(1)} %collective-permute-done.3), channel_id=1, source_target_pairs={{2,0},{4,2},{6,4},{3,1},{5,3},{7,5},{10,8},{12,10},{14,12},{11,9},... | collective-permute-start | bytes 786440 | tf_op jit(solution)/shard_map/ppermute | solution.py:33
  118.6 8.7 %collective-permute-start.2 = (bf16[128,1024]{1,0:T(8,128)(2,1)S(1)}, bf16[128,1024]{1,0:T(8,128)(2,1)S(1)}, u32[]{:S(2)}, u32[]{:S(2)}) collective-permute-start(bf16[128,1024]{1,0:T(8,128)(2,1)S(1)} %collective-permute-done.1), channel_id=1, source_target_pairs={{0,2},{2,4},{4,6},{1,3},{3,5},{5,7},{8,10},{10,12},{12,14},{9,11},... | collective-permute-start | bytes 786440 | tf_op jit(solution)/shard_map/ppermute | solution.py:32
  123.0 8.4 %collective-permute-start.5 = (bf16[128,1024]{1,0:T(8,128)(2,1)S(1)}, bf16[128,1024]{1,0:T(8,128)(2,1)S(1)}, u32[]{:S(2)}, u32[]{:S(2)}) collective-permute-start(bf16[128,1024]{1,0:T(8,128)(2,1)S(1)} %collective-permute-done.4), channel_id=1, source_target_pairs={{2,0},{4,2},{6,4},{3,1},{5,3},{7,5},{10,8},{12,10},{14,12},{11,9},... | collective-permute-start | bytes 786440 | tf_op jit(solution)/shard_map/ppermute | solution.py:33
  132.5 75.2 %reduce-scatter.6.cloned.1.call-start = ((), (), s32[]{:S(2)}) async-start(), calls=%async_computation.5 | async-start | bytes 3145728 | tf_op jit(solution)/shard_map/reduce_scatter | solution.py:197
  137.4 6.1 %copy-start.6 = (bf16[2048,32]{0,1:T(8,128)(2,1)S(1)}, bf16[2048,32]{0,1:T(8,128)(2,1)}, u32[]{:S(2)}) copy-start(bf16[2048,32]{0,1:T(8,128)(2,1)} %param.26) | copy-start | bytes 393220
  151.6 2.0 copy-start.2
  193.4 45.4 %copy-start.1 = (bf16[512,2048]{1,0:T(8,128)(2,1)S(1)}, bf16[512,2048]{1,0:T(8,128)(2,1)}, u32[]{:S(2)}) copy-start(bf16[512,2048]{1,0:T(8,128)(2,1)} %param.24) | copy-start | bytes 6291460
  197.2 41.6 %reduce-scatter.8.cloned.1.call-start = ((), (), s32[]{:S(2)}) async-start(), calls=%async_computation.6 | async-start | bytes 1310720 | tf_op jit(solution)/shard_map/reduce_scatter | solution.py:198
Sparse Core Ops, SparseCore 0:
  12.3 44.2 all-gather.6
  88.7 6.7 reduce-scatter.3
  132.6 10.5 all-gather.4
  197.3 10.4 reduce-scatter.5
  210.4 28.3 reduce-scatter.7

commit v6 on v4

--- a/solution.py
+++ b/solution.py
@@ -1,6 +1,8 @@
 import jax
 import jax.numpy as jnp
 from jax import lax
+from jax.experimental import pallas as pl
+from jax.experimental.pallas import tpu as pltpu
 from jax.sharding import PartitionSpec as P
 
 LATENT = 512
@@ -17,6 +19,44 @@
 
 EPSILON = 1e-06
 NEG_FILL = -1e30
+
+
+SLOT_TILE = 128
+
+
+def expert_kernel(rows_ref, gate_ref, up_ref, down_ref, scale_ref, out_ref):
+    rows = rows_ref[0]
+    contract = (((1,), (1,)), ((), ()))
+    gate_part = lax.dot_general(rows, gate_ref[0], contract, preferred_element_type=jnp.float32)
+    up_part = lax.dot_general(rows, up_ref[0], contract, preferred_element_type=jnp.float32)
+    active = (gate_part / (1.0 + jnp.exp(-gate_part)) * up_part).astype(jnp.bfloat16)
+    result = jnp.dot(active, down_ref[0], preferred_element_type=jnp.float32)
+    out_ref[0] = (result * scale_ref[0]).astype(out_ref.dtype)
+
+
+def expert_ffn(grouped, gate_weight, up_weight, down_weight, scale):
+    local_count, slot_count, feature_count = grouped.shape
+    hidden = gate_weight.shape[2]
+    gate_rows = jnp.transpose(gate_weight, (0, 2, 1))
+    up_rows = jnp.transpose(up_weight, (0, 2, 1))
+    tile = min(SLOT_TILE, slot_count)
+    return pl.pallas_call(
+        expert_kernel,
+        grid=(local_count, slot_count // tile),
+        in_specs=[
+            pl.BlockSpec((1, tile, feature_count), lambda j, m: (j, m, 0)),
+            pl.BlockSpec((1, hidden, feature_count), lambda j, m: (j, 0, 0)),
+            pl.BlockSpec((1, hidden, feature_count), lambda j, m: (j, 0, 0)),
+            pl.BlockSpec((1, hidden, feature_count), lambda j, m: (j, 0, 0)),
+            pl.BlockSpec((1, tile, 1), lambda j, m: (j, m, 0)),
+        ],
+        out_specs=pl.BlockSpec((1, tile, feature_count), lambda j, m: (j, m, 0)),
+        out_shape=jax.ShapeDtypeStruct((local_count, slot_count, feature_count), jnp.bfloat16),
+        compiler_params=pltpu.CompilerParams(
+            dimension_semantics=("arbitrary", "arbitrary"),
+            vmem_limit_bytes=56 * 1024 * 1024,
+        ),
+    )(grouped, gate_rows, up_rows, down_weight, scale)
 
 
 def local(
@@ -168,13 +208,13 @@
         jnp.bfloat16
     )
     grouped = grouped.reshape(local_count, slot_count, feature_count)
-    gate_part = jnp.einsum("jmd,jdf->jmf", grouped, gate_weight, preferred_element_type=jnp.float32)
-    up_part = jnp.einsum("jmd,jdf->jmf", grouped, up_weight, preferred_element_type=jnp.float32)
-    active = (jax.nn.silu(gate_part) * up_part).astype(jnp.bfloat16)
-    outputs = jnp.einsum("jmf,jfd->jmd", active, down_weight, preferred_element_type=jnp.float32)
-    weighted = (outputs.reshape(total_slots, feature_count) * slot_weight[:, None]).astype(
-        jnp.bfloat16
-    )
+    weighted = expert_ffn(
+        grouped,
+        gate_weight,
+        up_weight,
+        down_weight,
+        slot_weight.reshape(local_count, slot_count, 1),
+    ).reshape(total_slots, feature_count)
     mixture = jnp.dot(combine, weighted, preferred_element_type=jnp.float32).astype(jnp.bfloat16)
     moe_cols = lax.psum_scatter(mixture, "ffn", scatter_dimension=1, tiled=True)
     moe_out = lax.psum_scatter(moe_cols, "exp", scatter_dimension=0, tiled=True)

time: 244 us -> 236 us (0.967)
  matrix products: 54.4 us -> 21.3 us
  Pallas kernels: 0 us -> 29.1 us
  other arithmetic: 21.8 us -> 18.1 us
    dot_general x2 -> x0, matrix products: 35.9 us -> none  [the longest x1 23.6 us: local(): jnp.einsum('jmf,jfd->jmd', active, down_weight, preferred_element_type=jn...]
    pallas_call x0 -> x1, Pallas kernels: none -> 29.1 us  [expert_ffn(): pl.pallas_call(expert_kernel, grid=(local_count, slot_count // tile), in_...]
    convert_element_type x1 -> x0, other arithmetic: 3.88 us -> none  [local(): (outputs.reshape(total_slots, feature_count) * slot_weight[:, None]).asty...]
    unnamed x22 -> x26, local copies, waits for them, and re-layouts: 9.92 us -> 8.24 us
where the time goes in v6:
time: 236 us
  waiting for transfers between devices  115 us (49%)
  local copies, waits for them, and re-layouts  35 us (15%)
  Pallas kernels  29.1 us (12%)
  matrix products  21.3 us (9%)
  other arithmetic  18.1 us (8%)
  between operations  14.4 us (6%)
  blocking collectives  2.47 us (1%)
    all_gather x1, waiting for transfers between devices, local(): gathered = lax.all_gather(share, ('exp', 'ffn'), axis=0, tiled=False)  36.1 us
    reduce_scatter x1, waiting for transfers between devices, local(): moe_out = lax.psum_scatter(moe_cols, 'exp', scatter_dimension=0, tiled=True)  31.1 us
    all_gather x1, waiting for transfers between devices, local(): normed_half = lax.all_gather(normed_cols, 'exp', axis=0, tiled=True)  29.2 us
    pallas_call x1, Pallas kernels, expert_ffn(): pl.pallas_call(expert_kernel, grid=(local_count, slot_count // tile), in_...  29.1 us
    reduce_scatter x1, waiting for transfers between devices, local(): moe_cols = lax.psum_scatter(mixture, 'ffn', scatter_dimension=1, tiled=True)  10.9 us
    gather x2, local copies, waits for them, and re-layouts, local(): jnp.take(flat_pages, key_rows, axis=0).reshape(CMAX + fresh_len, QKD)  10.1 us
    unnamed x26, local copies, waits for them, and re-layouts  8.24 us
    reduce_scatter x1, waiting for transfers between devices, local(): lax.psum_scatter(partial_value.astype(jnp.bfloat16), 'ffn', scatter_dimen...  6.72 us
  transfers between devices with their start and end apart: 6, of which 6 were waited for; matrix products, arithmetic and copies ran while one was open for 8% of the time, Pallas kernels for 0%

profile of v6, /device:TPU:0, one launch (start us, length us, event | category | flops | bytes accessed | tf_op | source)
XLA Modules:
  0.0 235.5 jit_solution(14917882684781342401)
XLA Ops:
  7.3 0.8 convert_element_type.95
  8.1 0.1 copy.47
  8.2 0.2 convert_element_type.96
  8.4 0.6 reshape.349
  9.0 1.1 copy.46
  10.1 0.2 reshape.348
  10.3 0.1 pad.10.clone
  10.4 0.1 dynamic-slice
  10.4 2.3 fusion.33
  12.8 0.1 iota_add_fusion.1
  12.9 0.1 concatenate.36
  13.0 0.1 add.206
  13.1 1.2 dynamic_slice.19
  14.3 1.2 dynamic_slice.20
  15.6 0.7 fusion.37
  16.3 0.1 compare_and_fusion
  16.3 0.1 broadcast_in_dim.79
  16.4 0.1 broadcast_in_dim.80
  16.5 1.0 copy.59
  17.5 0.3 copy.48
  17.8 0.7 fusion.59
  18.6 0.1 fusion.40
  18.6 1.3 iota_compare_fusion.6
  20.0 1.0 and_or_fusion
  21.0 36.1 %all-gather.10.cloned.1.call-done = bf16[8,21,9216]{2,1,0:T(8,128)(2,1)} async-done(((bf16[1,21,9216]{2,1,0:T(8,128)(2,1)}), bf16[8,21,9216]{2,1,0:T(8,128)(2,1)}) %all-gather.10.cloned.1.call-update) | async-done | bytes 3096592 | tf_op jit(solution)/shard_map/all_gather | solution.py:111
  57.1 4.9 %reshape.372 = bf16[168,9216]{1,0:T(8,128)(2,1)} reshape(bf16[8,21,9216]{2,1,0:T(8,128)(2,1)} %all-gather.10.cloned.1.call-done) | data formatting | bytes 6193152
  62.0 6.2 %gather_fusion = bf16[80,9216]{1,0:T(8,128)(2,1)} fusion(bf16[168,9216]{1,0:T(8,128)(2,1)} %reshape.372, s32[1024]{0:T(1024)S(1)} %pad_clamp_fusion), kind=kCustom, calls=%fused_computation | custom fusion | bytes 2949440 | tf_op jit(solution)/shard_map/jit(_take)/gather | solution.py:134
  68.2 2.7 %broadcast_select_fusion = bf16[80,9216]{1,0:T(8,128)(2,1)} fusion(bf16[80,9216]{1,0:T(8,128)(2,1)} %gather_fusion, pred[80]{0:T(512)(128)(4,1)S(1)} %compare_and_fusion), kind=kLoop, calls=%fused_computation.17 | loop fusion | flops 737280 | bytes 2949200 | tf_op jit(solution)/shard_map/jit(_take)/select_n | solution.py:134
  70.9 3.9 %gather.7 = bf16[1280,576]{1,0:T(8,128)(2,1)} reshape(bf16[80,9216]{1,0:T(8,128)(2,1)} %gather_fusion) | data formatting | bytes 2949120 | tf_op jit(solution)/shard_map/jit(_take)/gather | solution.py:134
  74.8 3.9 %select_n.117 = bf16[1280,576]{1,0:T(8,128)(2,1)} reshape(bf16[80,9216]{1,0:T(8,128)(2,1)} %broadcast_select_fusion) | data formatting | bytes 2949120 | tf_op jit(solution)/shard_map/jit(_take)/select_n | solution.py:134
  78.7 2.6 %fusion.5 = f32[128,4,1280]{0,2,1:T(8,128)S(1)} fusion(bf16[128,4,576]{0,2,1:T(8,128)(2,1)S(1)} %bitcast.72, bf16[1280,576]{1,0:T(8,128)(2,1)} %select_n.117, pred[128,1280]{0,1:T(8,128)(4,1)S(1)} %and_or_fusion), kind=kOutput, calls=%fused_computation.11 | convolution fusion | flops 756285440 | bytes 4849664 | tf_op jit(solution)/shard_map/thd,kd->thk/dot_general | solution.py:139
  81.3 1.5 copy-done.2
  82.8 0.6 fusion.45
  83.4 0.4 copy-done.7
  83.9 4.3 %fusion.20 = bf16[4,128,128]{1,2,0:T(8,128)(2,1)S(1)} fusion(bf16[512,4,128]{0,2,1:T(8,128)(2,1)S(1)} %bitcast.73, bf16[1280,576]{1,0:T(8,128)(2,1)} %gather.7, pred[1280]{0:T(1024)(128)(4,1)S(1)} %broadcast_in_dim.80, f32[128,4]{0,1:T(4,128)S(1)} %fusion.45, f32[128,4,1280]{0,2,1:T(8,128)} %copy-done.2), kind=kOutput, calls=%fused_computation.27 | convolution fusion | flops 741148416 | bytes 7212288 | tf_op jit(solution)/shard_map/thl,lhd->thd/dot_general | solution.py:155
  88.2 1.3 convolution_convert_fusion.2
  89.5 0.2 all-gather.6.cloned.1.call-start
  89.8 6.7 %reduce-scatter.4.cloned.1.call-done = bf16[128,1024]{1,0:T(8,128)(2,1)} async-done(((bf16[128,2048]{1,0:T(8,128)(2,1)}), bf16[128,1024]{1,0:T(8,128)(2,1)}) %reduce-scatter.4.cloned.1.call-update) | async-done | bytes 262160 | tf_op jit(solution)/shard_map/reduce_scatter | solution.py:161
  96.5 1.1 fusion.27
  97.6 2.5 %psum.7 = f32[128,1]{0,1:T(1,128)S(1)} all-reduce(f32[128,1]{0,1:T(1,128)S(1)} %bitcast.77), channel_id=1, replica_groups=mesh['req'=4,'exp'=4,'ffn'=2] {'ffn'}, use_global_device_ids=true, to_apply=%region_7.8 | all-reduce | flops 128 | bytes 1024 | tf_op jit(solution)/shard_map/psum | solution.py:167
  100.1 0.8 fusion.29
  101.0 29.2 %all-gather.6.cloned.1.call-done = bf16[512,1024]{1,0:T(8,128)(2,1)} async-done(((bf16[128,1024]{1,0:T(8,128)(2,1)}), bf16[512,1024]{1,0:T(8,128)(2,1)}) %all-gather.6.cloned.1.call-update) | async-done | bytes 1048592 | tf_op jit(solution)/shard_map/all_gather | solution.py:173
  130.3 0.1 add.213
  130.4 0.1 add.214
  130.5 4.7 %reshape.353 = bf16[4,42,9216]{2,1,0:T(8,128)(2,1)} reshape(bf16[8,21,9216]{2,1,0:T(8,128)(2,1)} %all-gather.10.cloned.1.call-done) | data formatting | bytes 6193152 | tf_op jit(solution)/shard_map/reshape | solution.py:112
  135.2 1.2 slice.15
  136.4 0.2 reshape.358
  136.6 0.3 fusion.19
  136.9 0.1 copy.54
  137.0 0.2 convert_element_type.111
  137.3 0.1 add_select_fusion
  137.4 0.1 copy.52
  137.5 2.3 fusion.2
  139.8 1.4 fusion.1
  141.2 0.6 all-gather.8.cloned.1.call-done
  141.8 2.5 %fusion.46 = f32[512,32]{0,1:T(8,128)S(1)} fusion(bf16[512,2048]{1,0:T(8,128)(2,1)} %all-gather.8.cloned.1.call-done, bf16[2048,32]{0,1:T(8,128)(2,1)S(1)} %copy-done.8), kind=kOutput, calls=%fused_computation.83 | convolution fusion | flops 67108864 | bytes 2293760 | tf_op jit(solution)/shard_map/dot_general | solution.py:196
  144.3 0.1 select_reduce_fusion.1
  144.4 1.7 select_reduce_fusion
  146.2 1.0 copy.55.scale_ref
  147.2 4.4 %convolution_convert_fusion = bf16[1024,2048]{1,0:T(8,128)(2,1)} fusion(pred[1024,512]{1,0:T(8,128)(4,1)S(1)} %fusion.2, bf16[512,2048]{1,0:T(8,128)(2,1)S(1)} %copy-done.3), kind=kOutput, calls=%fused_computation.7 | convolution fusion | flops 2149580800 | bytes 6815744 | tf_op jit(solution)/shard_map/dot_general | solution.py:207
  151.5 29.1 %shard_map.158 = bf16[8,128,2048]{2,1,0:T(8,128)(2,1)} custom-call(bf16[8,128,2048]{2,1,0:T(8,128)(2,1)} %bitcast.70, bf16[8,704,2048]{2,1,0:T(8,128)(2,1)} %bitcast.68, bf16[8,704,2048]{2,1,0:T(8,128)(2,1)} %bitcast.69, bf16[8,704,2048]{2,1,0:T(8,128)(2,1)} %down_ref.1, f32[8,128,1]{2,1,0:T(8,128)} %copy.55.scale_ref), custom_call_target="tpu_custom_call" | custom-call | tf_op jit(solution)/shard_map/pallas_call | solution.py:43
  180.6 6.0 %convolution_convert_fusion.1 = bf16[512,2048]{1,0:T(8,128)(2,1)} fusion(pred[512,1024]{1,0:T(8,128)(4,1)S(1)} %fusion.1, bf16[1024,2048]{1,0:T(8,128)(2,1)} %bitcast.71), kind=kOutput, calls=%fused_computation.13 | convolution fusion | flops 2148532224 | bytes 6815744 | tf_op jit(solution)/shard_map/dot_general | solution.py:218
  186.7 10.9 %reduce-scatter.6.cloned.1.call-done = bf16[512,1024]{1,0:T(8,128)(2,1)} async-done(((bf16[512,2048]{1,0:T(8,128)(2,1)}), bf16[512,1024]{1,0:T(8,128)(2,1)}) %reduce-scatter.6.cloned.1.call-update) | async-done | bytes 1048592 | tf_op jit(solution)/shard_map/reduce_scatter | solution.py:219
  197.6 31.1 %reduce-scatter.8.cloned.1.call-done = bf16[128,1024]{1,0:T(8,128)(2,1)} async-done(((bf16[512,1024]{1,0:T(8,128)(2,1)}), bf16[128,1024]{1,0:T(8,128)(2,1)}) %reduce-scatter.8.cloned.1.call-update) | async-done | bytes 262160 | tf_op jit(solution)/shard_map/reduce_scatter | solution.py:220
  (45 shorter events, 0.5 us)
Async XLA Ops:
  7.2 81.1 %copy-start = (bf16[512,2048]{1,0:T(8,128)(2,1)S(1)}, bf16[512,2048]{1,0:T(8,128)(2,1)}, u32[]{:S(2)}) copy-start(bf16[512,2048]{1,0:T(8,128)(2,1)} %param.24) | copy-start | bytes 6291460
  7.2 9.4 %copy-start.6 = (bf16[512,512]{1,0:T(8,128)(2,1)S(1)}, bf16[512,512]{1,0:T(8,128)(2,1)}, u32[]{:S(2)}) copy-start(bf16[512,512]{1,0:T(8,128)(2,1)} %param.23) | copy-start | bytes 1572868
  7.2 10.3 %copy-start.5 = (bf16[128,2304]{1,0:T(8,128)(2,1)S(1)}, bf16[128,2304]{1,0:T(8,128)(2,1)}, u32[]{:S(2)}) copy-start(bf16[128,2304]{1,0:T(8,128)(2,1)} %param.16) | copy-start | bytes 1769476
  7.2 49.9 %all-gather.10.cloned.1.call-start = ((), (), s32[]{:S(2)}) async-start(), calls=%async_computation.8 | async-start | bytes 3981312 | tf_op jit(solution)/shard_map/all_gather | solution.py:111
  12.8 83.7 %reduce-scatter.4.cloned.1.call-start = ((), (), s32[]{:S(2)}) async-start(), calls=%async_computation.3 | async-start | bytes 786432 | tf_op jit(solution)/shard_map/reduce_scatter | solution.py:161
  81.3 1.5 copy-start.2
  82.8 1.0 copy-start.7
  88.2 1.6 copy-start.10
  88.2 8.3 %copy-start.9 = (bf16[128,2048]{1,0:T(8,128)(2,1)S(1)}, bf16[128,2048]{1,0:T(8,128)(2,1)}, u32[]{:S(2)}) copy-start(bf16[128,2048]{1,0:T(8,128)(2,1)} %param.15) | copy-start | bytes 1572868
  89.5 40.7 %all-gather.6.cloned.1.call-start = ((), (), s32[]{:S(2)}) async-start(), calls=%async_computation.4 | async-start | bytes 1310720 | tf_op jit(solution)/shard_map/all_gather | solution.py:173
  97.6 37.5 %copy-start.4 = (bf16[128,1024]{1,0:T(8,128)(2,1)}, bf16[128,1024]{1,0:T(8,128)(2,1)S(1)}, u32[]{:S(2)}) copy-start(bf16[128,1024]{1,0:T(8,128)(2,1)S(1)} %get-tuple-element.3) | copy-start | bytes 786436
  101.0 40.9 %all-gather.8.cloned.1.call-start = ((), (), s32[]{:S(2)}) async-start(), calls=%async_computation.5 | async-start | bytes 3145728 | tf_op jit(solution)/shard_map/all_gather | solution.py:174
  130.3 67.3 %reduce-scatter.6.cloned.1.call-start = ((), (), s32[]{:S(2)}) async-start(), calls=%async_computation.6 | async-start | bytes 3145728 | tf_op jit(solution)/shard_map/reduce_scatter | solution.py:219
  135.2 6.7 %copy-start.8 = (bf16[2048,32]{0,1:T(8,128)(2,1)S(1)}, bf16[2048,32]{0,1:T(8,128)(2,1)}, u32[]{:S(2)}) copy-start(bf16[2048,32]{0,1:T(8,128)(2,1)} %param.26) | copy-start | bytes 393220
  141.8 5.4 %copy-start.3 = (bf16[512,2048]{1,0:T(8,128)(2,1)S(1)}, bf16[512,2048]{1,0:T(8,128)(2,1)}, u32[]{:S(2)}) copy-start(bf16[512,2048]{1,0:T(8,128)(2,1)} %all-gather.8.cloned.1.call-done) | copy-start | bytes 6291460
  180.6 48.0 %copy-start.1 = (bf16[512,2048]{1,0:T(8,128)(2,1)S(1)}, bf16[512,2048]{1,0:T(8,128)(2,1)}, u32[]{:S(2)}) copy-start(bf16[512,2048]{1,0:T(8,128)(2,1)} %param.24) | copy-start | bytes 6291460
  186.7 42.0 %reduce-scatter.8.cloned.1.call-start = ((), (), s32[]{:S(2)}) async-start(), calls=%async_computation.7 | async-start | bytes 1310720 | tf_op jit(solution)/shard_map/reduce_scatter | solution.py:220
Sparse Core Ops, SparseCore 0:
  12.9 44.2 all-gather.9
  89.6 6.8 reduce-scatter.3
  101.1 29.1 all-gather.5
  131.7 10.0 all-gather.7
  186.8 10.7 reduce-scatter.5
  200.3 28.3 reduce-scatter.7

commit v7 on v6

--- a/solution.py
+++ b/solution.py
@@ -97,7 +97,7 @@
         (0, route_pages * page_width - route_count),
     ).reshape(route_pages, page_width)
     packed_rows = pool_pages + latent_pages + route_pages
-    share_rows = -(-packed_rows // ffn_size)
+    share_rows = -(-packed_rows // (ffn_size * 8)) * 8
     packed = jnp.concatenate(
         [
             cache_pool,
@@ -131,7 +131,7 @@
         + lax.broadcasted_iota(jnp.int32, (fresh_devices, latent_pages), 1)
     ).reshape(fresh_devices * latent_pages)
     key_rows = jnp.concatenate([cached_rows, fresh_rows], axis=0)
-    all_keys = jnp.take(flat_pages, key_rows, axis=0).reshape(CMAX + fresh_len, QKD)
+    all_keys = jnp.take(flat_pages, key_rows, axis=0, mode="clip").reshape(CMAX + fresh_len, QKD)
     heads_here = queries.shape[1] // QKD
     query_heads = queries.reshape(token_rows, heads_here, QKD)
     scale_factor = (HEAD_DIM + ROPE_DIM) ** (-0.5)

time: 236 us -> 224 us (0.949)
  local copies, waits for them, and re-layouts: 35 us -> 21.4 us
  waiting for transfers between devices: 115 us -> 120 us
  other arithmetic: 18.1 us -> 14.9 us
    unnamed x26 -> x21, local copies, waits for them, and re-layouts: 8.24 us -> 3.12 us
    all_gather x1, waiting for transfers between devices: 0.61 us -> 4.54 us  [local(): normed_all = lax.all_gather(normed_half, 'ffn', axis=1, tiled=True)]
    select_n x1 -> x0, local copies, waits for them, and re-layouts: 3.89 us -> none  [local(): jnp.take(flat_pages, key_rows, axis=0).reshape(CMAX + fresh_len, QKD)]
    gather x2 -> x1, local copies, waits for them, and re-layouts: 10.1 us -> 6.36 us  [local(): jnp.take(flat_pages, key_rows, axis=0, mode='clip')]
    select_n x2 -> x0, other arithmetic: 2.81 us -> none  [local(): jnp.take(flat_pages, key_rows, axis=0).reshape(CMAX + fresh_len, QKD)]
  transfers between devices with their start and end apart: 6 -> 6, of which waited for: 6 -> 6; matrix products, arithmetic and copies ran while one was open for 8% -> 6% of each run, Pallas kernels for 0% -> 0%
where the time goes in v7:
time: 224 us; the launch traced here: 223 us
  waiting for transfers between devices  120 us (54%)
  Pallas kernels  29.1 us (13%)
  local copies, waits for them, and re-layouts  21.4 us (10%)
  matrix products  21.1 us (9%)
  other arithmetic  14.9 us (7%)
  between operations  14.4 us (6%)
  blocking collectives  2.47 us (1%)
    all_gather x1, waiting for transfers between devices, local(): gathered = lax.all_gather(share, ('exp', 'ffn'), axis=0, tiled=False)  36.9 us
    reduce_scatter x1, waiting for transfers between devices, local(): moe_out = lax.psum_scatter(moe_cols, 'exp', scatter_dimension=0, tiled=True)  31.1 us
    all_gather x1, waiting for transfers between devices, local(): normed_half = lax.all_gather(normed_cols, 'exp', axis=0, tiled=True)  29.2 us
    pallas_call x1, Pallas kernels, expert_ffn(): pl.pallas_call(expert_kernel, grid=(local_count, slot_count // tile), in_...  29.1 us
    reduce_scatter x1, waiting for transfers between devices, local(): moe_cols = lax.psum_scatter(mixture, 'ffn', scatter_dimension=1, tiled=True)  10.9 us
    reduce_scatter x1, waiting for transfers between devices, local(): lax.psum_scatter(partial_value.astype(jnp.bfloat16), 'ffn', scatter_dimen...  6.9 us
    gather x1, local copies, waits for them, and re-layouts, local(): jnp.take(flat_pages, key_rows, axis=0, mode='clip')  6.36 us
    dot_general x1, matrix products, local(): jnp.dot(combine, weighted, preferred_element_type=jnp.float32)  6 us
  transfers between devices with their start and end apart: 6, of which 6 were waited for; matrix products, arithmetic and copies ran while one was open for 6% of the time, Pallas kernels for 0%

profile of v7, /device:TPU:0, one launch (start us, length us, event | category | flops | bytes accessed | tf_op | source)
XLA Modules:
  0.0 223.4 jit_solution(11270351787180866489)
XLA Ops:
  7.2 0.0 copy-start
  7.2 0.0 all-gather.9.cloned.1.call-start
  7.2 1.2 copy.30
  8.5 0.2 reshape.232
  8.7 0.7 convert_element_type.95
  9.4 0.1 copy.31
  9.5 0.2 convert_element_type.96
  9.7 0.1 pad_dynamic-slice_fusion.3
  9.8 2.0 fusion.21
  11.8 0.0 all-gather.9.cloned.1.call-update
  11.9 0.0 reduce-scatter.4.cloned.1.call-start
  11.9 0.1 iota_add_fusion.1
  12.0 0.1 add.126
  12.1 1.2 dynamic_slice.19
  13.3 1.2 dynamic_slice.20
  14.6 0.3 copy.32
  14.9 1.3 copy.44
  16.2 0.7 fusion.25
  16.9 0.1 pad_add_fusion
  16.9 1.3 iota_compare_fusion.6
  18.3 1.0 and_or_fusion
  19.3 36.9 %all-gather.9.cloned.1.call-done = bf16[192,9216]{1,0:T(8,128)(2,1)} async-done(((bf16[24,9216]{1,0:T(8,128)(2,1)}), bf16[192,9216]{1,0:T(8,128)(2,1)}) %all-gather.9.cloned.1.call-update) | async-done | bytes 3538960 | tf_op jit(solution)/shard_map/all_gather | solution.py:111
  56.2 6.4 %gather_fusion = bf16[80,9216]{1,0:T(8,128)(2,1)} fusion(bf16[192,9216]{1,0:T(8,128)(2,1)} %all-gather.9.cloned.1.call-done, s32[1024]{0:T(1024)S(1)} %pad_clamp_fusion), kind=kCustom, calls=%fused_computation | custom fusion | bytes 2949440 | tf_op jit(solution)/shard_map/jit(_take)/gather | solution.py:134
  62.6 3.9 %reshape.234 = bf16[1280,576]{1,0:T(8,128)(2,1)} reshape(bf16[80,9216]{1,0:T(8,128)(2,1)} %gather_fusion) | data formatting | bytes 2949120 | tf_op jit(solution)/shard_map/reshape | solution.py:134
  66.5 2.6 %fusion.5 = f32[128,4,1280]{0,2,1:T(8,128)S(1)} fusion(bf16[128,4,576]{0,2,1:T(8,128)(2,1)S(1)} %bitcast.65, bf16[1280,576]{1,0:T(8,128)(2,1)} %reshape.234, pred[128,1280]{0,1:T(8,128)(4,1)S(1)} %and_or_fusion), kind=kOutput, calls=%fused_computation.11 | convolution fusion | flops 756285440 | bytes 4849664 | tf_op jit(solution)/shard_map/thd,kd->thk/dot_general | solution.py:139
  69.1 1.5 copy-done.2
  70.6 0.6 fusion.30
  71.2 4.2 %fusion.13 = bf16[4,128,128]{1,2,0:T(8,128)(2,1)S(1)} fusion(bf16[512,4,128]{0,2,1:T(8,128)(2,1)S(1)} %bitcast.66, bf16[1280,576]{1,0:T(8,128)(2,1)} %reshape.234, f32[128,4]{0,1:T(4,128)S(1)} %fusion.30, f32[128,4,1280]{0,2,1:T(8,128)} %copy-done.2), kind=kOutput, calls=%fused_computation.24 | convolution fusion | flops 740493056 | bytes 7211008 | tf_op jit(solution)/shard_map/thl,lhd->thd/dot_general | solution.py:155
  75.5 1.3 convolution_convert_fusion.2
  76.7 0.0 reduce-scatter.4.cloned.1.call-update
  76.7 0.0 all-gather.5.cloned.1.call-start
  76.8 6.9 %reduce-scatter.4.cloned.1.call-done = bf16[128,1024]{1,0:T(8,128)(2,1)} async-done(((bf16[128,2048]{1,0:T(8,128)(2,1)}), bf16[128,1024]{1,0:T(8,128)(2,1)}) %reduce-scatter.4.cloned.1.call-update) | async-done | bytes 262160 | tf_op jit(solution)/shard_map/reduce_scatter | solution.py:161
  83.7 1.1 fusion.16
  84.9 2.5 %psum.7 = f32[128,1]{0,1:T(1,128)S(1)} all-reduce(f32[128,1]{0,1:T(1,128)S(1)} %bitcast.70), channel_id=1, replica_groups=mesh['req'=4,'exp'=4,'ffn'=2] {'ffn'}, use_global_device_ids=true, to_apply=%region_7.8 | all-reduce | flops 128 | bytes 1024 | tf_op jit(solution)/shard_map/psum | solution.py:167
  87.3 0.8 fusion.18
  88.2 0.0 all-gather.5.cloned.1.call-update
  88.2 0.0 all-gather.7.cloned.1.call-start
  88.2 29.2 %all-gather.5.cloned.1.call-done = bf16[512,1024]{1,0:T(8,128)(2,1)} async-done(((bf16[128,1024]{1,0:T(8,128)(2,1)}), bf16[512,1024]{1,0:T(8,128)(2,1)}) %all-gather.5.cloned.1.call-update) | async-done | bytes 1048592 | tf_op jit(solution)/shard_map/all_gather | solution.py:173
  117.4 0.0 all-gather.7.cloned.1.call-update
  117.5 0.2 reduce-scatter.6.cloned.1.call-start
  117.7 0.1 add.128
  117.8 0.1 add.129
  117.9 1.1 slice.15
  119.1 0.2 reshape.243
  119.3 0.7 copy.39
  120.0 0.3 fusion.12
  120.3 0.2 convert_element_type.111
  120.5 0.1 add_select_fusion
  120.7 0.1 copy.37
  120.8 2.3 %fusion.2 = pred[1024,512]{1,0:T(8,128)(4,1)S(1)} fusion(s32[512,6]{0,1:T(8,128)S(1)} %copy.37), kind=kLoop, calls=%fused_computation.6 | loop fusion | flops 5767168 | bytes 536576 | tf_op jit(solution)/shard_map/reduce_or | solution.py:206
  123.1 1.4 fusion.1
  124.5 4.5 %all-gather.7.cloned.1.call-done = bf16[512,2048]{1,0:T(8,128)(2,1)} async-done(((bf16[512,1024]{1,0:T(8,128)(2,1)}), bf16[512,2048]{1,0:T(8,128)(2,1)}) %all-gather.7.cloned.1.call-update) | async-done | bytes 2097168 | tf_op jit(solution)/shard_map/all_gather | solution.py:174
  129.0 2.5 %fusion.31 = f32[512,32]{0,1:T(8,128)S(1)} fusion(bf16[512,2048]{1,0:T(8,128)(2,1)} %all-gather.7.cloned.1.call-done, bf16[2048,32]{0,1:T(8,128)(2,1)S(1)} %copy-done.6), kind=kOutput, calls=%fused_computation.75 | convolution fusion | flops 67108864 | bytes 2293760 | tf_op jit(solution)/shard_map/dot_general | solution.py:196
  131.5 0.8 select_reduce_fusion.1
  132.3 1.7 select_reduce_fusion
  134.1 1.1 copy.40.scale_ref
  135.2 4.3 %convolution_convert_fusion = bf16[1024,2048]{1,0:T(8,128)(2,1)} fusion(pred[1024,512]{1,0:T(8,128)(4,1)S(1)} %fusion.2, bf16[512,2048]{1,0:T(8,128)(2,1)S(1)} %copy-done.3), kind=kOutput, calls=%fused_computation.7 | convolution fusion | flops 2149580800 | bytes 6815744 | tf_op jit(solution)/shard_map/dot_general | solution.py:207
  139.5 29.1 %shard_map.158 = bf16[8,128,2048]{2,1,0:T(8,128)(2,1)} custom-call(bf16[8,128,2048]{2,1,0:T(8,128)(2,1)} %bitcast.63, bf16[8,704,2048]{2,1,0:T(8,128)(2,1)} %bitcast.61, bf16[8,704,2048]{2,1,0:T(8,128)(2,1)} %bitcast.62, bf16[8,704,2048]{2,1,0:T(8,128)(2,1)} %down_ref.1, f32[8,128,1]{2,1,0:T(8,128)} %copy.40.scale_ref), custom_call_target="tpu_custom_call" | custom-call | tf_op jit(solution)/shard_map/pallas_call | solution.py:43
  168.5 6.0 %convolution_convert_fusion.1 = bf16[512,2048]{1,0:T(8,128)(2,1)} fusion(pred[512,1024]{1,0:T(8,128)(4,1)S(1)} %fusion.1, bf16[1024,2048]{1,0:T(8,128)(2,1)} %bitcast.64), kind=kOutput, calls=%fused_computation.13 | convolution fusion | flops 2148532224 | bytes 6815744 | tf_op jit(solution)/shard_map/dot_general | solution.py:218
  174.5 0.0 reduce-scatter.6.cloned.1.call-update
  174.6 0.0 reduce-scatter.8.cloned.1.call-start
  174.6 10.9 %reduce-scatter.6.cloned.1.call-done = bf16[512,1024]{1,0:T(8,128)(2,1)} async-done(((bf16[512,2048]{1,0:T(8,128)(2,1)}), bf16[512,1024]{1,0:T(8,128)(2,1)}) %reduce-scatter.6.cloned.1.call-update) | async-done | bytes 1048592 | tf_op jit(solution)/shard_map/reduce_scatter | solution.py:219
  185.5 0.0 reduce-scatter.8.cloned.1.call-update
  185.5 31.1 %reduce-scatter.8.cloned.1.call-done = bf16[128,1024]{1,0:T(8,128)(2,1)} async-done(((bf16[512,1024]{1,0:T(8,128)(2,1)}), bf16[128,1024]{1,0:T(8,128)(2,1)}) %reduce-scatter.8.cloned.1.call-update) | async-done | bytes 262160 | tf_op jit(solution)/shard_map/reduce_scatter | solution.py:220
  (32 shorter events, 0.2 us)
Async XLA Ops:
  7.2 68.3 %copy-start = (bf16[512,2048]{1,0:T(8,128)(2,1)S(1)}, bf16[512,2048]{1,0:T(8,128)(2,1)}, u32[]{:S(2)}) copy-start(bf16[512,2048]{1,0:T(8,128)(2,1)} %param.24) | copy-start | bytes 6291460
  7.2 7.4 %copy-start.5 = (bf16[128,2304]{1,0:T(8,128)(2,1)S(1)}, bf16[128,2304]{1,0:T(8,128)(2,1)}, u32[]{:S(2)}) copy-start(bf16[128,2304]{1,0:T(8,128)(2,1)} %param.16) | copy-start | bytes 1769476
  7.2 49.0 %all-gather.9.cloned.1.call-start = ((), (), s32[]{:S(2)}) async-start(), calls=%async_computation.8 | async-start | bytes 3981312 | tf_op jit(solution)/shard_map/all_gather | solution.py:111
  11.9 71.9 %reduce-scatter.4.cloned.1.call-start = ((), (), s32[]{:S(2)}) async-start(), calls=%async_computation.3 | async-start | bytes 786432 | tf_op jit(solution)/shard_map/reduce_scatter | solution.py:161
  69.1 1.5 copy-start.2
  75.4 1.4 copy-start.8
  75.4 8.3 %copy-start.7 = (bf16[128,2048]{1,0:T(8,128)(2,1)S(1)}, bf16[128,2048]{1,0:T(8,128)(2,1)}, u32[]{:S(2)}) copy-start(bf16[128,2048]{1,0:T(8,128)(2,1)} %param.15) | copy-start | bytes 1572868
  76.7 40.7 %all-gather.5.cloned.1.call-start = ((), (), s32[]{:S(2)}) async-start(), calls=%async_computation.4 | async-start | bytes 1310720 | tf_op jit(solution)/shard_map/all_gather | solution.py:173
  84.8 38.3 %copy-start.4 = (bf16[128,1024]{1,0:T(8,128)(2,1)}, bf16[128,1024]{1,0:T(8,128)(2,1)S(1)}, u32[]{:S(2)}) copy-start(bf16[128,1024]{1,0:T(8,128)(2,1)S(1)} %get-tuple-element.3) | copy-start | bytes 786436
  88.2 40.8 %all-gather.7.cloned.1.call-start = ((), (), s32[]{:S(2)}) async-start(), calls=%async_computation.5 | async-start | bytes 3145728 | tf_op jit(solution)/shard_map/all_gather | solution.py:174
  117.4 11.6 %copy-start.6 = (bf16[2048,32]{0,1:T(8,128)(2,1)S(1)}, bf16[2048,32]{0,1:T(8,128)(2,1)}, u32[]{:S(2)}) copy-start(bf16[2048,32]{0,1:T(8,128)(2,1)} %param.26) | copy-start | bytes 393220
  117.5 68.0 %reduce-scatter.6.cloned.1.call-start = ((), (), s32[]{:S(2)}) async-start(), calls=%async_computation.6 | async-start | bytes 3145728 | tf_op jit(solution)/shard_map/reduce_scatter | solution.py:219
  129.0 6.1 %copy-start.3 = (bf16[512,2048]{1,0:T(8,128)(2,1)S(1)}, bf16[512,2048]{1,0:T(8,128)(2,1)}, u32[]{:S(2)}) copy-start(bf16[512,2048]{1,0:T(8,128)(2,1)} %all-gather.7.cloned.1.call-done) | copy-start | bytes 6291460
  168.5 48.0 %copy-start.1 = (bf16[512,2048]{1,0:T(8,128)(2,1)S(1)}, bf16[512,2048]{1,0:T(8,128)(2,1)}, u32[]{:S(2)}) copy-start(bf16[512,2048]{1,0:T(8,128)(2,1)} %param.24) | copy-start | bytes 6291460
  174.6 42.0 %reduce-scatter.8.cloned.1.call-start = ((), (), s32[]{:S(2)}) async-start(), calls=%async_computation.7 | async-start | bytes 1310720 | tf_op jit(solution)/shard_map/reduce_scatter | solution.py:220
Sparse Core Ops, SparseCore 0:
  12.0 44.2 all-gather.8
  76.9 6.8 reduce-scatter.3
  88.3 29.0 all-gather.4
  118.9 10.0 all-gather.6
  174.7 10.7 reduce-scatter.5
  188.2 28.3 reduce-scatter.7

commit v8 on v7

--- a/solution.py
+++ b/solution.py
@@ -215,9 +215,18 @@
         down_weight,
         slot_weight.reshape(local_count, slot_count, 1),
     ).reshape(total_slots, feature_count)
-    mixture = jnp.dot(combine, weighted, preferred_element_type=jnp.float32).astype(jnp.bfloat16)
-    moe_cols = lax.psum_scatter(mixture, "ffn", scatter_dimension=1, tiled=True)
-    moe_out = lax.psum_scatter(moe_cols, "exp", scatter_dimension=0, tiled=True)
+    mixture = jnp.stack(
+        [
+            jnp.dot(
+                combine,
+                weighted[:, part * column_count : (part + 1) * column_count],
+                preferred_element_type=jnp.float32,
+            ).astype(jnp.bfloat16)
+            for part in range(ffn_size)
+        ],
+        axis=0,
+    ).reshape(ffn_size * group_rows, column_count)
+    moe_out = lax.psum_scatter(mixture, ("ffn", "exp"), scatter_dimension=0, tiled=True)
     return (hidden_out, moe_out)
 
 

time: 224 us -> 232 us (1.036)
  waiting for transfers between devices: 120 us -> 128 us
    reduce_scatter x2 -> x1, waiting for transfers between devices: 41.9 us -> 50.5 us  [local(): lax.psum_scatter(mixture, ('ffn', 'exp'), scatter_dimension=0, tiled=True)]
    dot_general x1 -> x2, matrix products: 6 us -> 4.25 us  [local(): jnp.dot(combine, weighted[:, part * column_count:(part + 1) * column_coun...]
  transfers between devices with their start and end apart: 6 -> 5, of which waited for: 6 -> 5; matrix products, arithmetic and copies ran while one was open for 6% -> 6% of each run, Pallas kernels for 0% -> 0%
where the time goes in v8:
time: 232 us; the launch traced here: 231 us
  waiting for transfers between devices  128 us (55%)
  Pallas kernels  29.1 us (13%)
  local copies, waits for them, and re-layouts  21.4 us (9%)
  matrix products  19.3 us (8%)
  other arithmetic  16.4 us (7%)
  between operations  14.1 us (6%)
  blocking collectives  2.47 us (1%)
    reduce_scatter x1, waiting for transfers between devices, local(): lax.psum_scatter(mixture, ('ffn', 'exp'), scatter_dimension=0, tiled=True)  50.5 us
    all_gather x1, waiting for transfers between devices, local(): gathered = lax.all_gather(share, ('exp', 'ffn'), axis=0, tiled=False)  36.9 us
    all_gather x1, waiting for transfers between devices, local(): normed_half = lax.all_gather(normed_cols, 'exp', axis=0, tiled=True)  29.2 us
    pallas_call x1, Pallas kernels, expert_ffn(): pl.pallas_call(expert_kernel, grid=(local_count, slot_count // tile), in_...  29.1 us
    reduce_scatter x1, waiting for transfers between devices, local(): lax.psum_scatter(partial_value.astype(jnp.bfloat16), 'ffn', scatter_dimen...  6.9 us
    gather x1, local copies, waits for them, and re-layouts, local(): jnp.take(flat_pages, key_rows, axis=0, mode='clip')  6.36 us
  transfers between devices with their start and end apart: 5, of which 5 were waited for; matrix products, arithmetic and copies ran while one was open for 6% of the time, Pallas kernels for 0%

profile of v8, /device:TPU:0, one launch (start us, length us, event | category | flops | bytes accessed | tf_op | source)
XLA Modules:
  0.0 231.4 jit_solution(9437405500017710788)
XLA Ops:
  7.2 0.0 copy-start
  7.2 0.0 all-gather.9.cloned.1.call-start
  7.2 1.2 copy.30
  8.5 0.2 reshape.235
  8.7 0.7 convert_element_type.98
  9.4 0.1 copy.31
  9.5 0.2 convert_element_type.99
  9.7 0.1 pad_dynamic-slice_fusion.3
  9.8 2.0 fusion.37
  11.8 0.0 all-gather.9.cloned.1.call-update
  11.9 0.0 reduce-scatter.3.cloned.1.call-start
  11.9 0.1 iota_add_fusion.1
  12.0 0.1 add.124
  12.1 1.2 dynamic_slice.19
  13.3 1.2 dynamic_slice.20
  14.6 0.3 copy.32
  14.9 1.3 copy.44
  16.2 0.7 fusion.41
  16.9 0.1 pad_add_fusion
  16.9 1.3 iota_compare_fusion.6
  18.3 1.0 and_or_fusion
  19.3 36.9 %all-gather.9.cloned.1.call-done = bf16[192,9216]{1,0:T(8,128)(2,1)} async-done(((bf16[24,9216]{1,0:T(8,128)(2,1)}), bf16[192,9216]{1,0:T(8,128)(2,1)}) %all-gather.9.cloned.1.call-update) | async-done | bytes 3538960 | tf_op jit(solution)/shard_map/all_gather | solution.py:111
  56.2 6.4 %gather_fusion = bf16[80,9216]{1,0:T(8,128)(2,1)} fusion(bf16[192,9216]{1,0:T(8,128)(2,1)} %all-gather.9.cloned.1.call-done, s32[1024]{0:T(1024)S(1)} %pad_clamp_fusion), kind=kCustom, calls=%fused_computation | custom fusion | bytes 2949440 | tf_op jit(solution)/shard_map/jit(_take)/gather | solution.py:134
  62.6 3.9 %reshape.237 = bf16[1280,576]{1,0:T(8,128)(2,1)} reshape(bf16[80,9216]{1,0:T(8,128)(2,1)} %gather_fusion) | data formatting | bytes 2949120 | tf_op jit(solution)/shard_map/reshape | solution.py:134
  66.5 2.6 %fusion.5 = f32[128,4,1280]{0,2,1:T(8,128)S(1)} fusion(bf16[128,4,576]{0,2,1:T(8,128)(2,1)S(1)} %bitcast.72, bf16[1280,576]{1,0:T(8,128)(2,1)} %reshape.237, pred[128,1280]{0,1:T(8,128)(4,1)S(1)} %and_or_fusion), kind=kOutput, calls=%fused_computation.11 | convolution fusion | flops 756285440 | bytes 4849664 | tf_op jit(solution)/shard_map/thd,kd->thk/dot_general | solution.py:139
  69.1 1.5 copy-done.3
  70.6 0.6 fusion.46
  71.2 4.2 %fusion.29 = bf16[4,128,128]{1,2,0:T(8,128)(2,1)S(1)} fusion(bf16[512,4,128]{0,2,1:T(8,128)(2,1)S(1)} %bitcast.73, bf16[1280,576]{1,0:T(8,128)(2,1)} %reshape.237, f32[128,4]{0,1:T(4,128)S(1)} %fusion.46, f32[128,4,1280]{0,2,1:T(8,128)} %copy-done.3), kind=kOutput, calls=%fused_computation.32 | convolution fusion | flops 740493056 | bytes 7211008 | tf_op jit(solution)/shard_map/thl,lhd->thd/dot_general | solution.py:155
  75.4 0.0 copy-start.8
  75.5 1.3 convolution_convert_fusion.1
  76.7 0.0 reduce-scatter.3.cloned.1.call-update
  76.7 0.0 all-gather.5.cloned.1.call-start
  76.8 6.9 %reduce-scatter.3.cloned.1.call-done = bf16[128,1024]{1,0:T(8,128)(2,1)} async-done(((bf16[128,2048]{1,0:T(8,128)(2,1)}), bf16[128,1024]{1,0:T(8,128)(2,1)}) %reduce-scatter.3.cloned.1.call-update) | async-done | bytes 262160 | tf_op jit(solution)/shard_map/reduce_scatter | solution.py:161
  83.7 1.1 fusion.32
  84.9 2.5 %psum.7 = f32[128,1]{0,1:T(1,128)S(1)} all-reduce(f32[128,1]{0,1:T(1,128)S(1)} %bitcast.77), channel_id=1, replica_groups=mesh['req'=4,'exp'=4,'ffn'=2] {'ffn'}, use_global_device_ids=true, to_apply=%region_7.8 | all-reduce | flops 128 | bytes 1024 | tf_op jit(solution)/shard_map/psum | solution.py:167
  87.3 0.8 fusion.34
  88.2 0.0 all-gather.5.cloned.1.call-update
  88.2 0.0 all-gather.7.cloned.1.call-start
  88.2 29.2 %all-gather.5.cloned.1.call-done = bf16[512,1024]{1,0:T(8,128)(2,1)} async-done(((bf16[128,1024]{1,0:T(8,128)(2,1)}), bf16[512,1024]{1,0:T(8,128)(2,1)}) %all-gather.5.cloned.1.call-update) | async-done | bytes 1048592 | tf_op jit(solution)/shard_map/all_gather | solution.py:173
  117.4 0.0 all-gather.7.cloned.1.call-update
  117.5 0.2 reduce-scatter.5.cloned.1.call-start
  117.7 0.1 add.126
  117.8 0.1 add.127
  117.9 1.1 slice.23
  119.1 0.2 reshape.247
  119.3 0.7 copy.39
  120.0 0.3 fusion.28
  120.3 0.2 convert_element_type.114
  120.5 0.1 add_select_fusion
  120.7 0.1 copy.37
  120.8 2.3 fusion.2
  123.1 1.4 fusion.1
  124.5 4.5 %all-gather.7.cloned.1.call-done = bf16[512,2048]{1,0:T(8,128)(2,1)} async-done(((bf16[512,1024]{1,0:T(8,128)(2,1)}), bf16[512,2048]{1,0:T(8,128)(2,1)}) %all-gather.7.cloned.1.call-update) | async-done | bytes 2097168 | tf_op jit(solution)/shard_map/all_gather | solution.py:174
  129.0 2.5 %fusion.47 = f32[512,32]{0,1:T(8,128)S(1)} fusion(bf16[512,2048]{1,0:T(8,128)(2,1)} %all-gather.7.cloned.1.call-done, bf16[2048,32]{0,1:T(8,128)(2,1)S(1)} %copy-done.7), kind=kOutput, calls=%fused_computation.83 | convolution fusion | flops 67108864 | bytes 2293760 | tf_op jit(solution)/shard_map/dot_general | solution.py:196
  131.5 0.8 select_reduce_fusion.1
  132.3 1.7 select_reduce_fusion
  134.1 1.1 copy.40.scale_ref
  135.2 4.3 %convolution_convert_fusion = bf16[1024,2048]{1,0:T(8,128)(2,1)} fusion(pred[1024,512]{1,0:T(8,128)(4,1)S(1)} %fusion.2, bf16[512,2048]{1,0:T(8,128)(2,1)S(1)} %copy-done.4), kind=kOutput, calls=%fused_computation.7 | convolution fusion | flops 2149580800 | bytes 6815744 | tf_op jit(solution)/shard_map/dot_general | solution.py:207
  139.4 29.1 %shard_map.158 = bf16[8,128,2048]{2,1,0:T(8,128)(2,1)} custom-call(bf16[8,128,2048]{2,1,0:T(8,128)(2,1)} %bitcast.71, bf16[8,704,2048]{2,1,0:T(8,128)(2,1)} %bitcast.66, bf16[8,704,2048]{2,1,0:T(8,128)(2,1)} %bitcast.67, bf16[8,704,2048]{2,1,0:T(8,128)(2,1)} %down_ref.1, f32[8,128,1]{2,1,0:T(8,128)} %copy.40.scale_ref), custom_call_target="tpu_custom_call" | custom-call | tf_op jit(solution)/shard_map/pallas_call | solution.py:43
  168.5 3.0 %fusion.21 = bf16[1,512,1024]{2,1,0:T(8,128)(2,1)S(1)} fusion(pred[512,1024]{1,0:T(8,128)(4,1)S(1)} %fusion.1, bf16[1024,2048]{1,0:T(8,128)(2,1)} %bitcast.69), kind=kOutput, calls=%fused_computation.24 | convolution fusion | flops 1074266112 | bytes 3670016 | tf_op jit(solution)/shard_map/dot_general | solution.py:220
  171.5 1.3 fusion.18
  172.8 1.5 pad_maximum_fusion
  174.3 0.0 reduce-scatter.5.cloned.1.call-update
  174.4 50.5 %reduce-scatter.5.cloned.1.call-done = bf16[128,1024]{1,0:T(8,128)(2,1)} async-done(((bf16[1024,1024]{1,0:T(8,128)(2,1)}), bf16[128,1024]{1,0:T(8,128)(2,1)}) %reduce-scatter.5.cloned.1.call-update) | async-done | bytes 262160 | tf_op jit(solution)/shard_map/reduce_scatter | solution.py:229
  (33 shorter events, 0.2 us)
Async XLA Ops:
  7.2 68.3 %copy-start = (bf16[512,2048]{1,0:T(8,128)(2,1)S(1)}, bf16[512,2048]{1,0:T(8,128)(2,1)}, u32[]{:S(2)}) copy-start(bf16[512,2048]{1,0:T(8,128)(2,1)} %param.24) | copy-start | bytes 6291460
  7.2 7.4 %copy-start.6 = (bf16[128,2304]{1,0:T(8,128)(2,1)S(1)}, bf16[128,2304]{1,0:T(8,128)(2,1)}, u32[]{:S(2)}) copy-start(bf16[128,2304]{1,0:T(8,128)(2,1)} %param.16) | copy-start | bytes 1769476
  7.2 49.0 %all-gather.9.cloned.1.call-start = ((), (), s32[]{:S(2)}) async-start(), calls=%async_computation.6 | async-start | bytes 3981312 | tf_op jit(solution)/shard_map/all_gather | solution.py:111
  11.9 71.9 %reduce-scatter.3.cloned.1.call-start = ((), (), s32[]{:S(2)}) async-start(), calls=%async_computation.2 | async-start | bytes 786432 | tf_op jit(solution)/shard_map/reduce_scatter | solution.py:161
  69.1 1.5 copy-start.3
  75.4 1.4 copy-start.9
  75.4 8.3 %copy-start.8 = (bf16[128,2048]{1,0:T(8,128)(2,1)S(1)}, bf16[128,2048]{1,0:T(8,128)(2,1)}, u32[]{:S(2)}) copy-start(bf16[128,2048]{1,0:T(8,128)(2,1)} %param.15) | copy-start | bytes 1572868
  76.7 40.7 %all-gather.5.cloned.1.call-start = ((), (), s32[]{:S(2)}) async-start(), calls=%async_computation.3 | async-start | bytes 1310720 | tf_op jit(solution)/shard_map/all_gather | solution.py:173
  84.8 38.3 %copy-start.5 = (bf16[128,1024]{1,0:T(8,128)(2,1)}, bf16[128,1024]{1,0:T(8,128)(2,1)S(1)}, u32[]{:S(2)}) copy-start(bf16[128,1024]{1,0:T(8,128)(2,1)S(1)} %get-tuple-element.3) | copy-start | bytes 786436
  88.2 40.8 %all-gather.7.cloned.1.call-start = ((), (), s32[]{:S(2)}) async-start(), calls=%async_computation.4 | async-start | bytes 3145728 | tf_op jit(solution)/shard_map/all_gather | solution.py:174
  117.4 11.6 %copy-start.7 = (bf16[2048,32]{0,1:T(8,128)(2,1)S(1)}, bf16[2048,32]{0,1:T(8,128)(2,1)}, u32[]{:S(2)}) copy-start(bf16[2048,32]{0,1:T(8,128)(2,1)} %param.26) | copy-start | bytes 393220
  117.5 107.4 %reduce-scatter.5.cloned.1.call-start = ((), (), s32[]{:S(2)}) async-start(), calls=%async_computation.5 | async-start | bytes 2359296 | tf_op jit(solution)/shard_map/reduce_scatter | solution.py:229
  129.0 6.1 %copy-start.4 = (bf16[512,2048]{1,0:T(8,128)(2,1)S(1)}, bf16[512,2048]{1,0:T(8,128)(2,1)}, u32[]{:S(2)}) copy-start(bf16[512,2048]{1,0:T(8,128)(2,1)} %all-gather.7.cloned.1.call-done) | copy-start | bytes 6291460
  168.5 3.0 %copy-start.2 = (bf16[8,128,2048]{2,1,0:T(8,128)(2,1)S(1)}, bf16[8,128,2048]{2,1,0:T(8,128)(2,1)}, u32[]{:S(2)}) copy-start(bf16[8,128,2048]{2,1,0:T(8,128)(2,1)} %shard_map.158) | copy-start | bytes 12582916
  171.5 53.4 %copy-start.1 = (bf16[512,2048]{1,0:T(8,128)(2,1)S(1)}, bf16[512,2048]{1,0:T(8,128)(2,1)}, u32[]{:S(2)}) copy-start(bf16[512,2048]{1,0:T(8,128)(2,1)} %param.24) | copy-start | bytes 6291460
Sparse Core Ops, SparseCore 0:
  12.0 44.2 all-gather.8
  76.9 6.8 reduce-scatter.2
  88.3 29.0 all-gather.4
  118.9 10.0 all-gather.6
  174.5 50.3 reduce-scatter.4

commit v9 on v7

--- a/solution.py
+++ b/solution.py
@@ -161,18 +161,6 @@
     attn_cols = lax.psum_scatter(
         partial_value.astype(jnp.bfloat16), "ffn", scatter_dimension=1, tiled=True
     ).astype(jnp.float32)
-    residual_cols = lax.dynamic_slice_in_dim(residual, ffn_index * column_count, column_count, 1)
-    hidden_out = (residual_cols.astype(jnp.float32) + attn_cols).astype(jnp.bfloat16)
-    hidden_wide = hidden_out.astype(jnp.float32)
-    square_sum = lax.psum(jnp.sum(hidden_wide * hidden_wide, axis=1, keepdims=True), "ffn")
-    mean_square = square_sum / feature_count
-    gain_cols = lax.dynamic_slice_in_dim(norm_gain, ffn_index * column_count, column_count, 0)
-    normed_cols = (
-        hidden_wide * lax.rsqrt(mean_square + EPSILON) * gain_cols.astype(jnp.float32)
-    ).astype(jnp.bfloat16)
-    normed_half = lax.all_gather(normed_cols, "exp", axis=0, tiled=True)
-    normed_all = lax.all_gather(normed_half, "ffn", axis=1, tiled=True)
-
     expert_ids = lax.broadcasted_iota(jnp.int32, (1, 1, EXPERTS), 2)
     route_hot = routes_all[:, :, None] == expert_ids
     blocks = group_rows // BLOCK_ROWS
@@ -193,17 +181,32 @@
     is_local = (local_expert >= 0) & (local_expert < local_count)
     target = jnp.where(is_local, local_expert * slot_count + slot_index, -1)
 
+    slot_ids = lax.broadcasted_iota(jnp.int32, (1, 1, total_slots), 2)
+    combine = jnp.any(target[:, :, None] == slot_ids, axis=1).astype(jnp.bfloat16)
+    dispatch_ids = lax.broadcasted_iota(jnp.int32, (total_slots, 1, 1), 0)
+    dispatch = jnp.any(target[None, :, :] == dispatch_ids, axis=2).astype(jnp.bfloat16)
+    attn_cols, target, combine, dispatch = lax.optimization_barrier(
+        (attn_cols, target, combine, dispatch)
+    )
+    residual_cols = lax.dynamic_slice_in_dim(residual, ffn_index * column_count, column_count, 1)
+    hidden_out = (residual_cols.astype(jnp.float32) + attn_cols).astype(jnp.bfloat16)
+    hidden_wide = hidden_out.astype(jnp.float32)
+    square_sum = lax.psum(jnp.sum(hidden_wide * hidden_wide, axis=1, keepdims=True), "ffn")
+    mean_square = square_sum / feature_count
+    gain_cols = lax.dynamic_slice_in_dim(norm_gain, ffn_index * column_count, column_count, 0)
+    normed_cols = (
+        hidden_wide * lax.rsqrt(mean_square + EPSILON) * gain_cols.astype(jnp.float32)
+    ).astype(jnp.bfloat16)
+    normed_half = lax.all_gather(normed_cols, "exp", axis=0, tiled=True)
+    normed_all = lax.all_gather(normed_half, "ffn", axis=1, tiled=True)
+
     logits = jnp.dot(normed_all, router, preferred_element_type=jnp.float32)
     chosen = jnp.sum(jnp.where(route_hot, logits[:, None, :], 0.0), axis=2)
     raised = jnp.exp(chosen)
     gate_weights = raised / jnp.sum(raised, axis=1, keepdims=True)
 
-    slot_ids = lax.broadcasted_iota(jnp.int32, (1, 1, total_slots), 2)
     slot_hit = target[:, :, None] == slot_ids
-    combine = jnp.any(slot_hit, axis=1).astype(jnp.bfloat16)
     slot_weight = jnp.sum(jnp.where(slot_hit, gate_weights[:, :, None], 0.0), axis=(0, 1))
-    dispatch_ids = lax.broadcasted_iota(jnp.int32, (total_slots, 1, 1), 0)
-    dispatch = jnp.any(target[None, :, :] == dispatch_ids, axis=2).astype(jnp.bfloat16)
     grouped = jnp.dot(dispatch, normed_all, preferred_element_type=jnp.float32).astype(
         jnp.bfloat16
     )

time: 224 us -> 228 us (1.018)
    reduce_scatter x1, waiting for transfers between devices: 6.9 us -> 0.66 us  [local(): lax.psum_scatter(partial_value.astype(jnp.bfloat16), 'ffn', scatter_dimen...]
    all_gather x1, waiting for transfers between devices: 4.54 us -> 10.7 us  [local(): normed_all = lax.all_gather(normed_half, 'ffn', axis=1, tiled=True)]
    convert_element_type x0 -> x3, other arithmetic: none -> 2.35 us  [the longest x1 1.19 us: local(): jnp.any(target[None, :, :] == dispatch_ids, axis=2).astype(jnp.bfloat16)]
where the time goes in v9:
time: 228 us; the launch traced here: 227 us
  waiting for transfers between devices  120 us (53%)
  Pallas kernels  29.1 us (13%)
  matrix products  22.3 us (10%)
  local copies, waits for them, and re-layouts  22.2 us (10%)
  other arithmetic  16.5 us (7%)
  between operations  14.4 us (6%)
  blocking collectives  2.47 us (1%)
    all_gather x1, waiting for transfers between devices, local(): gathered = lax.all_gather(share, ('exp', 'ffn'), axis=0, tiled=False)  37 us
    reduce_scatter x1, waiting for transfers between devices, local(): moe_out = lax.psum_scatter(moe_cols, 'exp', scatter_dimension=0, tiled=True)  31.1 us
    all_gather x1, waiting for transfers between devices, local(): normed_half = lax.all_gather(normed_cols, 'exp', axis=0, tiled=True)  29.2 us
    pallas_call x1, Pallas kernels, expert_ffn(): pl.pallas_call(expert_kernel, grid=(local_count, slot_count // tile), in_...  29.1 us
    reduce_scatter x1, waiting for transfers between devices, local(): moe_cols = lax.psum_scatter(mixture, 'ffn', scatter_dimension=1, tiled=True)  10.9 us
    all_gather x1, waiting for transfers between devices, local(): normed_all = lax.all_gather(normed_half, 'ffn', axis=1, tiled=True)  10.7 us
    gather x1, local copies, waits for them, and re-layouts, local(): jnp.take(flat_pages, key_rows, axis=0, mode='clip')  6.39 us
    dot_general x1, matrix products, local(): jnp.dot(combine, weighted, preferred_element_type=jnp.float32)  6.03 us
  transfers between devices with their start and end apart: 6, of which 6 were waited for; matrix products, arithmetic and copies ran while one was open for 6% of the time, Pallas kernels for 0%

profile of v9, /device:TPU:0, one launch (start us, length us, event | category | flops | bytes accessed | tf_op | source)
XLA Modules:
  0.0 226.9 jit_solution(16717943335402491618)
XLA Ops:
  7.2 0.0 all-gather.9.cloned.1.call-start
  7.3 0.8 convert_element_type.99
  8.1 0.1 copy.31
  8.2 0.2 convert_element_type.100
  8.4 0.6 reshape.234
  9.0 1.1 copy.30
  10.1 0.2 reshape.233
  10.3 0.1 pad_dynamic-slice_fusion.3
  10.4 2.0 fusion.21
  12.4 0.0 all-gather.9.cloned.1.call-update
  12.4 0.0 reduce-scatter.4.cloned.1.call-start
  12.5 1.2 dynamic_slice.19
  13.8 1.2 dynamic_slice.20
  15.0 0.1 iota_add_fusion.1
  15.1 0.1 add.126
  15.2 0.1 add.127
  15.2 0.1 add.128
  15.3 1.0 copy.45
  16.3 0.3 copy.32
  16.7 0.7 fusion.25
  17.4 0.1 pad_add_fusion
  17.5 1.3 iota_compare_fusion.7
  18.8 1.0 and_or_fusion
  19.8 37.0 %all-gather.9.cloned.1.call-done = bf16[192,9216]{1,0:T(8,128)(2,1)} async-done(((bf16[24,9216]{1,0:T(8,128)(2,1)}), bf16[192,9216]{1,0:T(8,128)(2,1)}) %all-gather.9.cloned.1.call-update) | async-done | bytes 3538960 | tf_op jit(solution)/shard_map/all_gather | solution.py:111
  56.8 1.1 slice.15
  58.0 6.4 %gather_fusion = bf16[80,9216]{1,0:T(8,128)(2,1)} fusion(bf16[192,9216]{1,0:T(8,128)(2,1)} %all-gather.9.cloned.1.call-done, s32[1024]{0:T(1024)S(1)} %pad_clamp_fusion), kind=kCustom, calls=%fused_computation | custom fusion | bytes 2949440 | tf_op jit(solution)/shard_map/jit(_take)/gather | solution.py:134
  64.4 3.9 %reshape.235 = bf16[1280,576]{1,0:T(8,128)(2,1)} reshape(bf16[80,9216]{1,0:T(8,128)(2,1)} %gather_fusion) | data formatting | bytes 2949120 | tf_op jit(solution)/shard_map/reshape | solution.py:134
  68.3 2.6 %fusion.5 = f32[128,4,1280]{0,2,1:T(8,128)S(1)} fusion(bf16[128,4,576]{0,2,1:T(8,128)(2,1)S(1)} %bitcast.65, bf16[1280,576]{1,0:T(8,128)(2,1)} %reshape.235, pred[128,1280]{0,1:T(8,128)(4,1)S(1)} %and_or_fusion), kind=kOutput, calls=%fused_computation.12 | convolution fusion | flops 756285440 | bytes 4849664 | tf_op jit(solution)/shard_map/thd,kd->thk/dot_general | solution.py:139
  70.9 1.5 copy-done.2
  72.4 0.6 fusion.30
  73.0 0.4 copy-done.7
  73.5 4.2 %fusion.13 = bf16[4,128,128]{1,2,0:T(8,128)(2,1)S(1)} fusion(bf16[512,4,128]{0,2,1:T(8,128)(2,1)S(1)} %bitcast.66, bf16[1280,576]{1,0:T(8,128)(2,1)} %reshape.235, f32[128,4]{0,1:T(4,128)S(1)} %fusion.30, f32[128,4,1280]{0,2,1:T(8,128)} %copy-done.2), kind=kOutput, calls=%fused_computation.25 | convolution fusion | flops 740493056 | bytes 7211008 | tf_op jit(solution)/shard_map/thl,lhd->thd/dot_general | solution.py:155
  77.7 1.3 convolution_convert_fusion.2
  79.0 0.2 all-gather.5.cloned.1.call-start
  79.2 0.2 reshape.244
  79.4 0.3 fusion.12
  79.7 0.2 convert_element_type.114
  80.0 0.1 add_select_fusion
  80.1 0.1 copy.37
  80.2 1.4 fusion.1
  81.6 0.2 convert_element_type.115
  81.8 2.3 %fusion.2 = pred[1024,512]{1,0:T(8,128)(4,1)S(1)} fusion(s32[512,6]{0,1:T(8,128)S(1)} %copy.37), kind=kLoop, calls=%fused_computation.7 | loop fusion | flops 5767168 | bytes 536576 | tf_op jit(solution)/shard_map/reduce_or | solution.py:187
  84.1 1.2 convert_element_type.116
  85.3 0.7 reduce-scatter.4.cloned.1.call-done
  85.9 1.0 convert_element_type.106
  87.0 0.2 fusion.16
  87.1 2.5 %psum.7 = f32[128,1]{0,1:T(1,128)S(1)} all-reduce(f32[128,1]{0,1:T(1,128)S(1)} %bitcast.70), channel_id=1, replica_groups=mesh['req'=4,'exp'=4,'ffn'=2] {'ffn'}, use_global_device_ids=true, to_apply=%region_7.8 | all-reduce | flops 128 | bytes 1024 | tf_op jit(solution)/shard_map/psum | solution.py:194
  89.6 0.8 fusion.18
  90.5 0.0 all-gather.7.cloned.1.call-start
  90.5 29.2 %all-gather.5.cloned.1.call-done = bf16[512,1024]{1,0:T(8,128)(2,1)} async-done(((bf16[128,1024]{1,0:T(8,128)(2,1)}), bf16[512,1024]{1,0:T(8,128)(2,1)}) %all-gather.5.cloned.1.call-update) | async-done | bytes 1048592 | tf_op jit(solution)/shard_map/all_gather | solution.py:200
  119.7 0.0 reduce-scatter.6.cloned.1.call-start
  119.8 0.7 copy.40
  120.5 0.1 copy.39
  120.6 10.7 %all-gather.7.cloned.1.call-done = bf16[512,2048]{1,0:T(8,128)(2,1)} async-done(((bf16[512,1024]{1,0:T(8,128)(2,1)}), bf16[512,2048]{1,0:T(8,128)(2,1)}) %all-gather.7.cloned.1.call-update) | async-done | bytes 2097168 | tf_op jit(solution)/shard_map/all_gather | solution.py:201
  131.3 2.5 %fusion.31 = f32[512,32]{0,1:T(8,128)S(1)} fusion(bf16[512,2048]{1,0:T(8,128)(2,1)} %all-gather.7.cloned.1.call-done, bf16[2048,32]{0,1:T(8,128)(2,1)S(1)} %copy-done.9), kind=kOutput, calls=%fused_computation.76 | convolution fusion | flops 67108864 | bytes 2293760 | tf_op jit(solution)/shard_map/dot_general | solution.py:203
  133.8 0.8 select_reduce_fusion.1
  134.6 1.7 select_reduce_fusion
  136.3 1.1 copy.41.scale_ref
  137.4 5.5 %convolution_convert_fusion = bf16[1024,2048]{1,0:T(8,128)(2,1)} fusion(bf16[1024,512]{1,0:T(8,128)(2,1)} %convert_element_type.116, bf16[512,2048]{1,0:T(8,128)(2,1)S(1)} %copy-done.3), kind=kOutput, calls=%fused_computation.8 | convolution fusion | flops 2149580800 | bytes 7340032 | tf_op jit(solution)/shard_map/dot_general | solution.py:210
  142.9 29.1 %shard_map.158 = bf16[8,128,2048]{2,1,0:T(8,128)(2,1)} custom-call(bf16[8,128,2048]{2,1,0:T(8,128)(2,1)} %bitcast.63, bf16[8,704,2048]{2,1,0:T(8,128)(2,1)} %bitcast.61, bf16[8,704,2048]{2,1,0:T(8,128)(2,1)} %bitcast.62, bf16[8,704,2048]{2,1,0:T(8,128)(2,1)} %down_ref.1, f32[8,128,1]{2,1,0:T(8,128)} %copy.41.scale_ref), custom_call_target="tpu_custom_call" | custom-call | tf_op jit(solution)/shard_map/pallas_call | solution.py:43
  172.0 6.0 %convolution_convert_fusion.1 = bf16[512,2048]{1,0:T(8,128)(2,1)} fusion(bf16[512,1024]{1,0:T(8,128)(2,1)S(1)} %convert_element_type.115, bf16[1024,2048]{1,0:T(8,128)(2,1)} %bitcast.64), kind=kOutput, calls=%fused_computation.14 | convolution fusion | flops 2148532224 | bytes 7340032 | tf_op jit(solution)/shard_map/dot_general | solution.py:221
  178.1 0.0 reduce-scatter.8.cloned.1.call-start
  178.1 10.9 %reduce-scatter.6.cloned.1.call-done = bf16[512,1024]{1,0:T(8,128)(2,1)} async-done(((bf16[512,2048]{1,0:T(8,128)(2,1)}), bf16[512,1024]{1,0:T(8,128)(2,1)}) %reduce-scatter.6.cloned.1.call-update) | async-done | bytes 1048592 | tf_op jit(solution)/shard_map/reduce_scatter | solution.py:222
  189.0 31.1 %reduce-scatter.8.cloned.1.call-done = bf16[128,1024]{1,0:T(8,128)(2,1)} async-done(((bf16[512,1024]{1,0:T(8,128)(2,1)}), bf16[128,1024]{1,0:T(8,128)(2,1)}) %reduce-scatter.8.cloned.1.call-update) | async-done | bytes 262160 | tf_op jit(solution)/shard_map/reduce_scatter | solution.py:223
  (40 shorter events, 0.3 us)
Async XLA Ops:
  7.2 70.5 %copy-start = (bf16[512,2048]{1,0:T(8,128)(2,1)S(1)}, bf16[512,2048]{1,0:T(8,128)(2,1)}, u32[]{:S(2)}) copy-start(bf16[512,2048]{1,0:T(8,128)(2,1)} %param.24) | copy-start | bytes 6291460
  7.2 8.1 %copy-start.6 = (bf16[512,512]{1,0:T(8,128)(2,1)S(1)}, bf16[512,512]{1,0:T(8,128)(2,1)}, u32[]{:S(2)}) copy-start(bf16[512,512]{1,0:T(8,128)(2,1)} %param.23) | copy-start | bytes 1572868
  7.2 9.2 %copy-start.5 = (bf16[128,2304]{1,0:T(8,128)(2,1)S(1)}, bf16[128,2304]{1,0:T(8,128)(2,1)}, u32[]{:S(2)}) copy-start(bf16[128,2304]{1,0:T(8,128)(2,1)} %param.16) | copy-start | bytes 1769476
  7.2 11.6 %copy-start.10 = (bf16[2048]{0:T(1024)(128)(2,1)S(1)}, bf16[2048]{0:T(1024)(128)(2,1)}, u32[]{:S(2)}) copy-start(bf16[2048]{0:T(1024)(128)(2,1)} %param.25) | copy-start | bytes 12292
  7.2 49.6 %all-gather.9.cloned.1.call-start = ((), (), s32[]{:S(2)}) async-start(), calls=%async_computation.8 | async-start | bytes 3981312 | tf_op jit(solution)/shard_map/all_gather | solution.py:111
  12.4 73.5 %reduce-scatter.4.cloned.1.call-start = ((), (), s32[]{:S(2)}) async-start(), calls=%async_computation.3 | async-start | bytes 786432 | tf_op jit(solution)/shard_map/reduce_scatter | solution.py:161
  70.9 1.5 copy-start.2
  72.4 1.0 copy-start.7
  79.0 40.8 %all-gather.5.cloned.1.call-start = ((), (), s32[]{:S(2)}) async-start(), calls=%async_computation.4 | async-start | bytes 1310720 | tf_op jit(solution)/shard_map/all_gather | solution.py:200
  80.1 6.8 %copy-start.8 = (bf16[128,2048]{1,0:T(8,128)(2,1)S(1)}, bf16[128,2048]{1,0:T(8,128)(2,1)}, u32[]{:S(2)}) copy-start(bf16[128,2048]{1,0:T(8,128)(2,1)} %param.15) | copy-start | bytes 1572868
  84.1 47.2 %copy-start.9 = (bf16[2048,32]{0,1:T(8,128)(2,1)S(1)}, bf16[2048,32]{0,1:T(8,128)(2,1)}, u32[]{:S(2)}) copy-start(bf16[2048,32]{0,1:T(8,128)(2,1)} %param.26) | copy-start | bytes 393220
  87.1 50.3 %copy-start.4 = (bf16[128,1024]{1,0:T(8,128)(2,1)}, bf16[128,1024]{1,0:T(8,128)(2,1)S(1)}, u32[]{:S(2)}) copy-start(bf16[128,1024]{1,0:T(8,128)(2,1)S(1)} %get-tuple-element.11) | copy-start | bytes 786436
  90.5 40.8 %all-gather.7.cloned.1.call-start = ((), (), s32[]{:S(2)}) async-start(), calls=%async_computation.5 | async-start | bytes 3145728 | tf_op jit(solution)/shard_map/all_gather | solution.py:201
  119.7 69.3 %reduce-scatter.6.cloned.1.call-start = ((), (), s32[]{:S(2)}) async-start(), calls=%async_computation.6 | async-start | bytes 3145728 | tf_op jit(solution)/shard_map/reduce_scatter | solution.py:222
  131.3 6.1 %copy-start.3 = (bf16[512,2048]{1,0:T(8,128)(2,1)S(1)}, bf16[512,2048]{1,0:T(8,128)(2,1)}, u32[]{:S(2)}) copy-start(bf16[512,2048]{1,0:T(8,128)(2,1)} %all-gather.7.cloned.1.call-done) | copy-start | bytes 6291460
  172.0 48.1 %copy-start.1 = (bf16[512,2048]{1,0:T(8,128)(2,1)S(1)}, bf16[512,2048]{1,0:T(8,128)(2,1)}, u32[]{:S(2)}) copy-start(bf16[512,2048]{1,0:T(8,128)(2,1)} %param.24) | copy-start | bytes 6291460
  178.1 42.0 %reduce-scatter.8.cloned.1.call-start = ((), (), s32[]{:S(2)}) async-start(), calls=%async_computation.7 | async-start | bytes 1310720 | tf_op jit(solution)/shard_map/reduce_scatter | solution.py:223
Sparse Core Ops, SparseCore 0:
  12.6 44.2 all-gather.8
  79.1 6.8 reduce-scatter.3
  90.6 29.0 all-gather.4
  121.2 10.0 all-gather.6
  178.2 10.7 reduce-scatter.5
  191.7 28.3 reduce-scatter.7

commit v10 on v7

--- a/solution.py
+++ b/solution.py
@@ -21,17 +21,27 @@
 NEG_FILL = -1e30
 
 
-SLOT_TILE = 128
-
-
-def expert_kernel(rows_ref, gate_ref, up_ref, down_ref, scale_ref, out_ref):
+SLOT_TILE = 512
+HIDDEN_STEPS = 2
+
+
+def expert_kernel(rows_ref, gate_ref, up_ref, down_ref, scale_ref, out_ref, acc_ref):
+    step = pl.program_id(2)
+
+    @pl.when(step == 0)
+    def _():
+        acc_ref[...] = jnp.zeros_like(acc_ref)
+
     rows = rows_ref[0]
     contract = (((1,), (1,)), ((), ()))
     gate_part = lax.dot_general(rows, gate_ref[0], contract, preferred_element_type=jnp.float32)
     up_part = lax.dot_general(rows, up_ref[0], contract, preferred_element_type=jnp.float32)
     active = (gate_part / (1.0 + jnp.exp(-gate_part)) * up_part).astype(jnp.bfloat16)
-    result = jnp.dot(active, down_ref[0], preferred_element_type=jnp.float32)
-    out_ref[0] = (result * scale_ref[0]).astype(out_ref.dtype)
+    acc_ref[...] += jnp.dot(active, down_ref[0], preferred_element_type=jnp.float32)
+
+    @pl.when(step == pl.num_programs(2) - 1)
+    def _():
+        out_ref[0] = (acc_ref[...] * scale_ref[0]).astype(out_ref.dtype)
 
 
 def expert_ffn(grouped, gate_weight, up_weight, down_weight, scale):
@@ -40,20 +50,23 @@
     gate_rows = jnp.transpose(gate_weight, (0, 2, 1))
     up_rows = jnp.transpose(up_weight, (0, 2, 1))
     tile = min(SLOT_TILE, slot_count)
+    steps = HIDDEN_STEPS if hidden % (HIDDEN_STEPS * 8) == 0 else 1
+    part = hidden // steps
     return pl.pallas_call(
         expert_kernel,
-        grid=(local_count, slot_count // tile),
+        grid=(local_count, slot_count // tile, steps),
         in_specs=[
-            pl.BlockSpec((1, tile, feature_count), lambda j, m: (j, m, 0)),
-            pl.BlockSpec((1, hidden, feature_count), lambda j, m: (j, 0, 0)),
-            pl.BlockSpec((1, hidden, feature_count), lambda j, m: (j, 0, 0)),
-            pl.BlockSpec((1, hidden, feature_count), lambda j, m: (j, 0, 0)),
-            pl.BlockSpec((1, tile, 1), lambda j, m: (j, m, 0)),
+            pl.BlockSpec((1, tile, feature_count), lambda j, m, h: (j, m, 0)),
+            pl.BlockSpec((1, part, feature_count), lambda j, m, h: (j, h, 0)),
+            pl.BlockSpec((1, part, feature_count), lambda j, m, h: (j, h, 0)),
+            pl.BlockSpec((1, part, feature_count), lambda j, m, h: (j, h, 0)),
+            pl.BlockSpec((1, tile, 1), lambda j, m, h: (j, m, 0)),
         ],
-        out_specs=pl.BlockSpec((1, tile, feature_count), lambda j, m: (j, m, 0)),
+        out_specs=pl.BlockSpec((1, tile, feature_count), lambda j, m, h: (j, m, 0)),
         out_shape=jax.ShapeDtypeStruct((local_count, slot_count, feature_count), jnp.bfloat16),
+        scratch_shapes=[pltpu.VMEM((tile, feature_count), jnp.float32)],
         compiler_params=pltpu.CompilerParams(
-            dimension_semantics=("arbitrary", "arbitrary"),
+            dimension_semantics=("arbitrary", "arbitrary", "arbitrary"),
             vmem_limit_bytes=56 * 1024 * 1024,
         ),
     )(grouped, gate_rows, up_rows, down_weight, scale)

time: 224 us -> 230 us (1.027)
  Pallas kernels: 29.1 us -> 34.9 us
    pallas_call x1, Pallas kernels: 29.1 us -> 34.9 us  [expert_ffn(): pl.pallas_call(expert_kernel, grid=(local_count, slot_count // tile, step...]
where the time goes in v10:
time: 230 us; the launch traced here: 229 us
  waiting for transfers between devices  120 us (52%)
  Pallas kernels  34.9 us (15%)
  local copies, waits for them, and re-layouts  21.4 us (9%)
  matrix products  21.1 us (9%)
  other arithmetic  14.9 us (6%)
  between operations  14.4 us (6%)
  blocking collectives  2.47 us (1%)
    all_gather x1, waiting for transfers between devices, local(): gathered = lax.all_gather(share, ('exp', 'ffn'), axis=0, tiled=False)  36.9 us
    pallas_call x1, Pallas kernels, expert_ffn(): pl.pallas_call(expert_kernel, grid=(local_count, slot_count // tile, step...  34.9 us
    reduce_scatter x1, waiting for transfers between devices, local(): moe_out = lax.psum_scatter(moe_cols, 'exp', scatter_dimension=0, tiled=True)  31.1 us
    all_gather x1, waiting for transfers between devices, local(): normed_half = lax.all_gather(normed_cols, 'exp', axis=0, tiled=True)  29.2 us
    reduce_scatter x1, waiting for transfers between devices, local(): moe_cols = lax.psum_scatter(mixture, 'ffn', scatter_dimension=1, tiled=True)  10.9 us
    reduce_scatter x1, waiting for transfers between devices, local(): lax.psum_scatter(partial_value.astype(jnp.bfloat16), 'ffn', scatter_dimen...  6.9 us
    gather x1, local copies, waits for them, and re-layouts, local(): jnp.take(flat_pages, key_rows, axis=0, mode='clip')  6.36 us
    dot_general x1, matrix products, local(): jnp.dot(combine, weighted, preferred_element_type=jnp.float32)  6 us
  transfers between devices with their start and end apart: 6, of which 6 were waited for; matrix products, arithmetic and copies ran while one was open for 6% of the time, Pallas kernels for 0%

profile of v10, /device:TPU:0, one launch (start us, length us, event | category | flops | bytes accessed | tf_op | source)
XLA Modules:
  0.0 229.3 jit_solution(3909557293716153392)
XLA Ops:
  7.2 0.0 copy-start
  7.2 0.0 all-gather.9.cloned.1.call-start
  7.2 1.2 copy.30
  8.5 0.2 reshape.232
  8.7 0.7 convert_element_type.95
  9.4 0.1 copy.31
  9.5 0.2 convert_element_type.96
  9.7 0.1 pad_dynamic-slice_fusion.3
  9.8 2.0 fusion.21
  11.8 0.0 all-gather.9.cloned.1.call-update
  11.9 0.0 reduce-scatter.4.cloned.1.call-start
  11.9 0.1 iota_add_fusion.1
  12.0 0.1 add.126
  12.1 1.2 dynamic_slice.19
  13.3 1.2 dynamic_slice.20
  14.6 0.3 copy.32
  14.9 1.3 copy.44
  16.2 0.7 fusion.25
  16.9 0.1 pad_add_fusion
  16.9 1.3 iota_compare_fusion.6
  18.3 1.0 and_or_fusion
  19.3 36.9 %all-gather.9.cloned.1.call-done = bf16[192,9216]{1,0:T(8,128)(2,1)} async-done(((bf16[24,9216]{1,0:T(8,128)(2,1)}), bf16[192,9216]{1,0:T(8,128)(2,1)}) %all-gather.9.cloned.1.call-update) | async-done | bytes 3538960 | tf_op jit(solution)/shard_map/all_gather | solution.py:124
  56.2 6.4 %gather_fusion = bf16[80,9216]{1,0:T(8,128)(2,1)} fusion(bf16[192,9216]{1,0:T(8,128)(2,1)} %all-gather.9.cloned.1.call-done, s32[1024]{0:T(1024)S(1)} %pad_clamp_fusion), kind=kCustom, calls=%fused_computation | custom fusion | bytes 2949440 | tf_op jit(solution)/shard_map/jit(_take)/gather | solution.py:147
  62.6 3.9 %reshape.234 = bf16[1280,576]{1,0:T(8,128)(2,1)} reshape(bf16[80,9216]{1,0:T(8,128)(2,1)} %gather_fusion) | data formatting | bytes 2949120 | tf_op jit(solution)/shard_map/reshape | solution.py:147
  66.5 2.6 %fusion.5 = f32[128,4,1280]{0,2,1:T(8,128)S(1)} fusion(bf16[128,4,576]{0,2,1:T(8,128)(2,1)S(1)} %bitcast.65, bf16[1280,576]{1,0:T(8,128)(2,1)} %reshape.234, pred[128,1280]{0,1:T(8,128)(4,1)S(1)} %and_or_fusion), kind=kOutput, calls=%fused_computation.11 | convolution fusion | flops 756285440 | bytes 4849664 | tf_op jit(solution)/shard_map/thd,kd->thk/dot_general | solution.py:152
  69.1 1.5 copy-done.2
  70.6 0.6 fusion.30
  71.2 4.2 %fusion.13 = bf16[4,128,128]{1,2,0:T(8,128)(2,1)S(1)} fusion(bf16[512,4,128]{0,2,1:T(8,128)(2,1)S(1)} %bitcast.66, bf16[1280,576]{1,0:T(8,128)(2,1)} %reshape.234, f32[128,4]{0,1:T(4,128)S(1)} %fusion.30, f32[128,4,1280]{0,2,1:T(8,128)} %copy-done.2), kind=kOutput, calls=%fused_computation.24 | convolution fusion | flops 740493056 | bytes 7211008 | tf_op jit(solution)/shard_map/thl,lhd->thd/dot_general | solution.py:168
  75.5 1.3 convolution_convert_fusion.2
  76.7 0.0 reduce-scatter.4.cloned.1.call-update
  76.7 0.0 all-gather.5.cloned.1.call-start
  76.8 6.9 %reduce-scatter.4.cloned.1.call-done = bf16[128,1024]{1,0:T(8,128)(2,1)} async-done(((bf16[128,2048]{1,0:T(8,128)(2,1)}), bf16[128,1024]{1,0:T(8,128)(2,1)}) %reduce-scatter.4.cloned.1.call-update) | async-done | bytes 262160 | tf_op jit(solution)/shard_map/reduce_scatter | solution.py:174
  83.7 1.1 fusion.16
  84.9 2.5 %psum.7 = f32[128,1]{0,1:T(1,128)S(1)} all-reduce(f32[128,1]{0,1:T(1,128)S(1)} %bitcast.70), channel_id=1, replica_groups=mesh['req'=4,'exp'=4,'ffn'=2] {'ffn'}, use_global_device_ids=true, to_apply=%region_7.8 | all-reduce | flops 128 | bytes 1024 | tf_op jit(solution)/shard_map/psum | solution.py:180
  87.3 0.8 fusion.18
  88.2 0.0 all-gather.5.cloned.1.call-update
  88.2 0.0 all-gather.7.cloned.1.call-start
  88.2 29.2 %all-gather.5.cloned.1.call-done = bf16[512,1024]{1,0:T(8,128)(2,1)} async-done(((bf16[128,1024]{1,0:T(8,128)(2,1)}), bf16[512,1024]{1,0:T(8,128)(2,1)}) %all-gather.5.cloned.1.call-update) | async-done | bytes 1048592 | tf_op jit(solution)/shard_map/all_gather | solution.py:186
  117.4 0.0 all-gather.7.cloned.1.call-update
  117.5 0.2 reduce-scatter.6.cloned.1.call-start
  117.7 0.1 add.128
  117.8 0.1 add.129
  117.9 1.1 slice.15
  119.1 0.2 reshape.243
  119.3 0.7 copy.39
  120.0 0.3 fusion.12
  120.3 0.2 convert_element_type.111
  120.5 0.1 add_select_fusion
  120.7 0.1 copy.37
  120.8 2.3 %fusion.2 = pred[1024,512]{1,0:T(8,128)(4,1)S(1)} fusion(s32[512,6]{0,1:T(8,128)S(1)} %copy.37), kind=kLoop, calls=%fused_computation.6 | loop fusion | flops 5767168 | bytes 536576 | tf_op jit(solution)/shard_map/reduce_or | solution.py:219
  123.1 1.4 fusion.1
  124.5 4.5 %all-gather.7.cloned.1.call-done = bf16[512,2048]{1,0:T(8,128)(2,1)} async-done(((bf16[512,1024]{1,0:T(8,128)(2,1)}), bf16[512,2048]{1,0:T(8,128)(2,1)}) %all-gather.7.cloned.1.call-update) | async-done | bytes 2097168 | tf_op jit(solution)/shard_map/all_gather | solution.py:187
  129.0 2.5 %fusion.31 = f32[512,32]{0,1:T(8,128)S(1)} fusion(bf16[512,2048]{1,0:T(8,128)(2,1)} %all-gather.7.cloned.1.call-done, bf16[2048,32]{0,1:T(8,128)(2,1)S(1)} %copy-done.6), kind=kOutput, calls=%fused_computation.75 | convolution fusion | flops 67108864 | bytes 2293760 | tf_op jit(solution)/shard_map/dot_general | solution.py:209
  131.5 0.8 select_reduce_fusion.1
  132.3 1.7 select_reduce_fusion
  134.1 1.1 copy.40.scale_ref
  135.2 4.3 %convolution_convert_fusion = bf16[1024,2048]{1,0:T(8,128)(2,1)} fusion(pred[1024,512]{1,0:T(8,128)(4,1)S(1)} %fusion.2, bf16[512,2048]{1,0:T(8,128)(2,1)S(1)} %copy-done.3), kind=kOutput, calls=%fused_computation.7 | convolution fusion | flops 2149580800 | bytes 6815744 | tf_op jit(solution)/shard_map/dot_general | solution.py:220
  139.5 34.9 %shard_map.158 = bf16[8,128,2048]{2,1,0:T(8,128)(2,1)} custom-call(bf16[8,128,2048]{2,1,0:T(8,128)(2,1)} %bitcast.63, bf16[8,704,2048]{2,1,0:T(8,128)(2,1)} %bitcast.61, bf16[8,704,2048]{2,1,0:T(8,128)(2,1)} %bitcast.62, bf16[8,704,2048]{2,1,0:T(8,128)(2,1)} %down_ref.1, f32[8,128,1]{2,1,0:T(8,128)} %copy.40.scale_ref), custom_call_target="tpu_custom_call" | custom-call | tf_op jit(solution)/shard_map/pallas_call | solution.py:55
  174.4 6.0 %convolution_convert_fusion.1 = bf16[512,2048]{1,0:T(8,128)(2,1)} fusion(pred[512,1024]{1,0:T(8,128)(4,1)S(1)} %fusion.1, bf16[1024,2048]{1,0:T(8,128)(2,1)} %bitcast.64), kind=kOutput, calls=%fused_computation.13 | convolution fusion | flops 2148532224 | bytes 6815744 | tf_op jit(solution)/shard_map/dot_general | solution.py:231
  180.4 0.0 reduce-scatter.6.cloned.1.call-update
  180.4 0.0 reduce-scatter.8.cloned.1.call-start
  180.5 10.9 %reduce-scatter.6.cloned.1.call-done = bf16[512,1024]{1,0:T(8,128)(2,1)} async-done(((bf16[512,2048]{1,0:T(8,128)(2,1)}), bf16[512,1024]{1,0:T(8,128)(2,1)}) %reduce-scatter.6.cloned.1.call-update) | async-done | bytes 1048592 | tf_op jit(solution)/shard_map/reduce_scatter | solution.py:232
  191.4 0.0 reduce-scatter.8.cloned.1.call-update
  191.4 31.1 %reduce-scatter.8.cloned.1.call-done = bf16[128,1024]{1,0:T(8,128)(2,1)} async-done(((bf16[512,1024]{1,0:T(8,128)(2,1)}), bf16[128,1024]{1,0:T(8,128)(2,1)}) %reduce-scatter.8.cloned.1.call-update) | async-done | bytes 262160 | tf_op jit(solution)/shard_map/reduce_scatter | solution.py:233
  (32 shorter events, 0.2 us)
Async XLA Ops:
  7.2 68.3 %copy-start = (bf16[512,2048]{1,0:T(8,128)(2,1)S(1)}, bf16[512,2048]{1,0:T(8,128)(2,1)}, u32[]{:S(2)}) copy-start(bf16[512,2048]{1,0:T(8,128)(2,1)} %param.24) | copy-start | bytes 6291460
  7.2 7.4 %copy-start.5 = (bf16[128,2304]{1,0:T(8,128)(2,1)S(1)}, bf16[128,2304]{1,0:T(8,128)(2,1)}, u32[]{:S(2)}) copy-start(bf16[128,2304]{1,0:T(8,128)(2,1)} %param.16) | copy-start | bytes 1769476
  7.2 49.0 %all-gather.9.cloned.1.call-start = ((), (), s32[]{:S(2)}) async-start(), calls=%async_computation.8 | async-start | bytes 3981312 | tf_op jit(solution)/shard_map/all_gather | solution.py:124
  11.9 71.9 %reduce-scatter.4.cloned.1.call-start = ((), (), s32[]{:S(2)}) async-start(), calls=%async_computation.3 | async-start | bytes 786432 | tf_op jit(solution)/shard_map/reduce_scatter | solution.py:174
  69.1 1.5 copy-start.2
  75.4 1.4 copy-start.8
  75.4 8.3 %copy-start.7 = (bf16[128,2048]{1,0:T(8,128)(2,1)S(1)}, bf16[128,2048]{1,0:T(8,128)(2,1)}, u32[]{:S(2)}) copy-start(bf16[128,2048]{1,0:T(8,128)(2,1)} %param.15) | copy-start | bytes 1572868
  76.7 40.7 %all-gather.5.cloned.1.call-start = ((), (), s32[]{:S(2)}) async-start(), calls=%async_computation.4 | async-start | bytes 1310720 | tf_op jit(solution)/shard_map/all_gather | solution.py:186
  84.8 38.3 %copy-start.4 = (bf16[128,1024]{1,0:T(8,128)(2,1)}, bf16[128,1024]{1,0:T(8,128)(2,1)S(1)}, u32[]{:S(2)}) copy-start(bf16[128,1024]{1,0:T(8,128)(2,1)S(1)} %get-tuple-element.3) | copy-start | bytes 786436
  88.2 40.8 %all-gather.7.cloned.1.call-start = ((), (), s32[]{:S(2)}) async-start(), calls=%async_computation.5 | async-start | bytes 3145728 | tf_op jit(solution)/shard_map/all_gather | solution.py:187
  117.4 11.6 %copy-start.6 = (bf16[2048,32]{0,1:T(8,128)(2,1)S(1)}, bf16[2048,32]{0,1:T(8,128)(2,1)}, u32[]{:S(2)}) copy-start(bf16[2048,32]{0,1:T(8,128)(2,1)} %param.26) | copy-start | bytes 393220
  117.5 73.9 %reduce-scatter.6.cloned.1.call-start = ((), (), s32[]{:S(2)}) async-start(), calls=%async_computation.6 | async-start | bytes 3145728 | tf_op jit(solution)/shard_map/reduce_scatter | solution.py:232
  129.0 6.1 %copy-start.3 = (bf16[512,2048]{1,0:T(8,128)(2,1)S(1)}, bf16[512,2048]{1,0:T(8,128)(2,1)}, u32[]{:S(2)}) copy-start(bf16[512,2048]{1,0:T(8,128)(2,1)} %all-gather.7.cloned.1.call-done) | copy-start | bytes 6291460
  174.4 48.0 %copy-start.1 = (bf16[512,2048]{1,0:T(8,128)(2,1)S(1)}, bf16[512,2048]{1,0:T(8,128)(2,1)}, u32[]{:S(2)}) copy-start(bf16[512,2048]{1,0:T(8,128)(2,1)} %param.24) | copy-start | bytes 6291460
  180.4 42.0 %reduce-scatter.8.cloned.1.call-start = ((), (), s32[]{:S(2)}) async-start(), calls=%async_computation.7 | async-start | bytes 1310720 | tf_op jit(solution)/shard_map/reduce_scatter | solution.py:233
Sparse Core Ops, SparseCore 0:
  12.0 44.2 all-gather.8
  76.9 6.8 reduce-scatter.3
  88.3 29.0 all-gather.4
  118.9 10.0 all-gather.6
  180.6 10.7 reduce-scatter.5
  194.1 28.3 reduce-scatter.7

commit v11 on v7

--- a/solution.py
+++ b/solution.py
@@ -21,30 +21,32 @@
 NEG_FILL = -1e30
 
 
-SLOT_TILE = 128
+SLOT_TILE = 512
 
 
 def expert_kernel(rows_ref, gate_ref, up_ref, down_ref, scale_ref, out_ref):
-    rows = rows_ref[0]
-    contract = (((1,), (1,)), ((), ()))
-    gate_part = lax.dot_general(rows, gate_ref[0], contract, preferred_element_type=jnp.float32)
-    up_part = lax.dot_general(rows, up_ref[0], contract, preferred_element_type=jnp.float32)
+    columns = rows_ref[...]
+    gate_part = jnp.dot(gate_ref[0], columns, preferred_element_type=jnp.float32)
+    up_part = jnp.dot(up_ref[0], columns, preferred_element_type=jnp.float32)
     active = (gate_part / (1.0 + jnp.exp(-gate_part)) * up_part).astype(jnp.bfloat16)
-    result = jnp.dot(active, down_ref[0], preferred_element_type=jnp.float32)
+    contract = (((0,), (0,)), ((), ()))
+    result = lax.dot_general(active, down_ref[0], contract, preferred_element_type=jnp.float32)
     out_ref[0] = (result * scale_ref[0]).astype(out_ref.dtype)
 
 
-def expert_ffn(grouped, gate_weight, up_weight, down_weight, scale):
-    local_count, slot_count, feature_count = grouped.shape
+def expert_ffn(grouped_t, gate_weight, up_weight, down_weight, scale):
+    feature_count = grouped_t.shape[0]
+    local_count, slot_count, _ = scale.shape
     hidden = gate_weight.shape[2]
     gate_rows = jnp.transpose(gate_weight, (0, 2, 1))
     up_rows = jnp.transpose(up_weight, (0, 2, 1))
     tile = min(SLOT_TILE, slot_count)
+    tiles = slot_count // tile
     return pl.pallas_call(
         expert_kernel,
-        grid=(local_count, slot_count // tile),
+        grid=(local_count, tiles),
         in_specs=[
-            pl.BlockSpec((1, tile, feature_count), lambda j, m: (j, m, 0)),
+            pl.BlockSpec((feature_count, tile), lambda j, m: (0, j * tiles + m)),
             pl.BlockSpec((1, hidden, feature_count), lambda j, m: (j, 0, 0)),
             pl.BlockSpec((1, hidden, feature_count), lambda j, m: (j, 0, 0)),
             pl.BlockSpec((1, hidden, feature_count), lambda j, m: (j, 0, 0)),
@@ -56,7 +58,7 @@
             dimension_semantics=("arbitrary", "arbitrary"),
             vmem_limit_bytes=56 * 1024 * 1024,
         ),
-    )(grouped, gate_rows, up_rows, down_weight, scale)
+    )(grouped_t, gate_rows, up_rows, down_weight, scale)
 
 
 def local(
@@ -202,14 +204,11 @@
     slot_hit = target[:, :, None] == slot_ids
     combine = jnp.any(slot_hit, axis=1).astype(jnp.bfloat16)
     slot_weight = jnp.sum(jnp.where(slot_hit, gate_weights[:, :, None], 0.0), axis=(0, 1))
-    dispatch_ids = lax.broadcasted_iota(jnp.int32, (total_slots, 1, 1), 0)
-    dispatch = jnp.any(target[None, :, :] == dispatch_ids, axis=2).astype(jnp.bfloat16)
-    grouped = jnp.dot(dispatch, normed_all, preferred_element_type=jnp.float32).astype(
-        jnp.bfloat16
-    )
-    grouped = grouped.reshape(local_count, slot_count, feature_count)
+    grouped_t = jnp.einsum(
+        "td,ts->ds", normed_all, combine, preferred_element_type=jnp.float32
+    ).astype(jnp.bfloat16)
     weighted = expert_ffn(
-        grouped,
+        grouped_t,
         gate_weight,
         up_weight,
         down_weight,

time: 224 us -> 224 us (level)
  waiting for transfers between devices: 120 us -> 123 us
  other arithmetic: 14.9 us -> 12 us
    all_gather x1, waiting for transfers between devices: 4.54 us -> 7.45 us  [local(): normed_all = lax.all_gather(normed_half, 'ffn', axis=1, tiled=True)]
    reduce_or x1 -> x0, other arithmetic: 2.3 us -> none  [local(): jnp.any(target[None, :, :] == dispatch_ids, axis=2).astype(jnp.bfloat16)]
  transfers between devices with their start and end apart: 6 -> 6, of which waited for: 6 -> 6; matrix products, arithmetic and copies ran while one was open for 6% -> 5% of each run, Pallas kernels for 0% -> 0%
where the time goes in v11:
time: 224 us; the launch traced here: 223 us
  waiting for transfers between devices  123 us (55%)
  Pallas kernels  28.5 us (13%)
  local copies, waits for them, and re-layouts  21.4 us (10%)
  matrix products  21.2 us (9%)
  between operations  14.4 us (6%)
  other arithmetic  12 us (5%)
  blocking collectives  2.47 us (1%)
    all_gather x1, waiting for transfers between devices, local(): gathered = lax.all_gather(share, ('exp', 'ffn'), axis=0, tiled=False)  37.2 us
    reduce_scatter x1, waiting for transfers between devices, local(): moe_out = lax.psum_scatter(moe_cols, 'exp', scatter_dimension=0, tiled=True)  31.1 us
    all_gather x1, waiting for transfers between devices, local(): normed_half = lax.all_gather(normed_cols, 'exp', axis=0, tiled=True)  29.2 us
    pallas_call x1, Pallas kernels, expert_ffn(): pl.pallas_call(expert_kernel, grid=(local_count, tiles), in_specs=[pl.Blo...  28.5 us
    reduce_scatter x1, waiting for transfers between devices, local(): moe_cols = lax.psum_scatter(mixture, 'ffn', scatter_dimension=1, tiled=True)  10.9 us
    all_gather x1, waiting for transfers between devices, local(): normed_all = lax.all_gather(normed_half, 'ffn', axis=1, tiled=True)  7.45 us
    reduce_scatter x1, waiting for transfers between devices, local(): lax.psum_scatter(partial_value.astype(jnp.bfloat16), 'ffn', scatter_dimen...  6.9 us
    gather x1, local copies, waits for them, and re-layouts, local(): jnp.take(flat_pages, key_rows, axis=0, mode='clip')  6.36 us
  transfers between devices with their start and end apart: 6, of which 6 were waited for; matrix products, arithmetic and copies ran while one was open for 5% of the time, Pallas kernels for 0%

profile of v11, /device:TPU:0, one launch (start us, length us, event | category | flops | bytes accessed | tf_op | source)
XLA Modules:
  0.0 223.3 jit_solution(6211897544054987765)
XLA Ops:
  7.2 0.0 all-gather.9.cloned.1.call-start
  7.3 0.8 convert_element_type.86
  8.1 0.1 copy.31
  8.2 0.2 convert_element_type.87
  8.4 0.6 reshape.199
  9.0 1.1 copy.30
  10.1 0.2 reshape.198
  10.3 0.1 pad_dynamic-slice_fusion.3
  10.4 2.0 fusion.20
  12.4 0.0 all-gather.9.cloned.1.call-update
  12.4 0.0 reduce-scatter.4.cloned.1.call-start
  12.5 1.2 dynamic_slice.19
  13.8 1.2 dynamic_slice.20
  15.0 0.1 iota_add_fusion.1
  15.1 0.1 add.118
  15.2 1.0 copy.43
  16.2 0.3 copy.32
  16.5 0.7 fusion.24
  17.2 0.1 pad_add_fusion
  17.3 1.3 iota_compare_fusion.5
  18.6 1.0 and_or_fusion
  19.6 37.2 %all-gather.9.cloned.1.call-done = bf16[192,9216]{1,0:T(8,128)(2,1)} async-done(((bf16[24,9216]{1,0:T(8,128)(2,1)}), bf16[192,9216]{1,0:T(8,128)(2,1)}) %all-gather.9.cloned.1.call-update) | async-done | bytes 3538960 | tf_op jit(solution)/shard_map/all_gather | solution.py:113
  56.8 6.4 %gather_fusion = bf16[80,9216]{1,0:T(8,128)(2,1)} fusion(bf16[192,9216]{1,0:T(8,128)(2,1)} %all-gather.9.cloned.1.call-done, s32[1024]{0:T(1024)S(1)} %pad_clamp_fusion), kind=kCustom, calls=%fused_computation | custom fusion | bytes 2949440 | tf_op jit(solution)/shard_map/jit(_take)/gather | solution.py:136
  63.2 3.9 %reshape.200 = bf16[1280,576]{1,0:T(8,128)(2,1)} reshape(bf16[80,9216]{1,0:T(8,128)(2,1)} %gather_fusion) | data formatting | bytes 2949120 | tf_op jit(solution)/shard_map/reshape | solution.py:136
  67.0 2.6 %fusion.4 = f32[128,4,1280]{0,2,1:T(8,128)S(1)} fusion(bf16[128,4,576]{0,2,1:T(8,128)(2,1)S(1)} %bitcast.63, bf16[1280,576]{1,0:T(8,128)(2,1)} %reshape.200, pred[128,1280]{0,1:T(8,128)(4,1)S(1)} %and_or_fusion), kind=kOutput, calls=%fused_computation.9 | convolution fusion | flops 756285440 | bytes 4849664 | tf_op jit(solution)/shard_map/thd,kd->thk/dot_general | solution.py:141
  69.7 1.5 copy-done.2
  71.2 0.6 fusion.29
  71.8 0.4 copy-done.7
  72.2 4.2 %fusion.12 = bf16[4,128,128]{1,2,0:T(8,128)(2,1)S(1)} fusion(bf16[512,4,128]{0,2,1:T(8,128)(2,1)S(1)} %bitcast.64, bf16[1280,576]{1,0:T(8,128)(2,1)} %reshape.200, f32[128,4]{0,1:T(4,128)S(1)} %fusion.29, f32[128,4,1280]{0,2,1:T(8,128)} %copy-done.2), kind=kOutput, calls=%fused_computation.22 | convolution fusion | flops 740493056 | bytes 7211008 | tf_op jit(solution)/shard_map/thl,lhd->thd/dot_general | solution.py:157
  76.5 1.3 convolution_convert_fusion.2
  77.7 0.0 reduce-scatter.4.cloned.1.call-update
  77.8 0.0 all-gather.5.cloned.1.call-start
  77.8 6.9 %reduce-scatter.4.cloned.1.call-done = bf16[128,1024]{1,0:T(8,128)(2,1)} async-done(((bf16[128,2048]{1,0:T(8,128)(2,1)}), bf16[128,1024]{1,0:T(8,128)(2,1)}) %reduce-scatter.4.cloned.1.call-update) | async-done | bytes 262160 | tf_op jit(solution)/shard_map/reduce_scatter | solution.py:163
  84.7 1.1 fusion.15
  85.9 2.5 %psum.7 = f32[128,1]{0,1:T(1,128)S(1)} all-reduce(f32[128,1]{0,1:T(1,128)S(1)} %bitcast.68), channel_id=1, replica_groups=mesh['req'=4,'exp'=4,'ffn'=2] {'ffn'}, use_global_device_ids=true, to_apply=%region_6.7 | all-reduce | flops 128 | bytes 1024 | tf_op jit(solution)/shard_map/psum | solution.py:169
  88.3 0.8 fusion.17
  89.2 0.0 all-gather.5.cloned.1.call-update
  89.2 0.0 all-gather.7.cloned.1.call-start
  89.3 29.2 %all-gather.5.cloned.1.call-done = bf16[512,1024]{1,0:T(8,128)(2,1)} async-done(((bf16[128,1024]{1,0:T(8,128)(2,1)}), bf16[512,1024]{1,0:T(8,128)(2,1)}) %all-gather.5.cloned.1.call-update) | async-done | bytes 1048592 | tf_op jit(solution)/shard_map/all_gather | solution.py:175
  118.5 0.0 all-gather.7.cloned.1.call-update
  118.5 0.2 reduce-scatter.6.cloned.1.call-start
  118.7 0.1 add.120
  118.8 0.1 add.121
  118.9 1.1 slice.15
  120.1 0.2 reshape.208
  120.3 0.3 fusion.11
  120.6 0.1 copy.38
  120.7 0.2 convert_element_type.102
  120.9 0.1 add_select_fusion
  121.1 0.1 copy.37
  121.2 1.4 fusion.1
  122.6 7.5 %all-gather.7.cloned.1.call-done = bf16[512,2048]{1,0:T(8,128)(2,1)} async-done(((bf16[512,1024]{1,0:T(8,128)(2,1)}), bf16[512,2048]{1,0:T(8,128)(2,1)}) %all-gather.7.cloned.1.call-update) | async-done | bytes 2097168 | tf_op jit(solution)/shard_map/all_gather | solution.py:176
  130.0 2.5 %fusion.30 = f32[512,32]{0,1:T(8,128)S(1)} fusion(bf16[512,2048]{1,0:T(8,128)(2,1)} %all-gather.7.cloned.1.call-done, bf16[2048,32]{0,1:T(8,128)(2,1)S(1)} %copy-done.8), kind=kOutput, calls=%fused_computation.73 | convolution fusion | flops 67108864 | bytes 2293760 | tf_op jit(solution)/shard_map/dot_general | solution.py:198
  132.5 0.1 select_reduce_fusion.1
  132.6 1.7 select_reduce_fusion
  134.4 1.1 copy.39.scale_ref
  135.4 4.4 %convolution_convert_fusion.rows_ref = bf16[2048,1024]{1,0:T(8,128)(2,1)} fusion(bf16[512,2048]{1,0:T(8,128)(2,1)S(1)} %copy-done.3, pred[512,1024]{1,0:T(8,128)(4,1)S(1)} %fusion.1), kind=kOutput, calls=%fused_computation.5 | convolution fusion | flops 2149580800 | bytes 6815744 | tf_op jit(solution)/shard_map/td,ts->ds/dot_general | solution.py:207
  139.8 28.5 %shard_map.158 = bf16[8,128,2048]{2,1,0:T(8,128)(2,1)} custom-call(bf16[2048,1024]{1,0:T(8,128)(2,1)} %convolution_convert_fusion.rows_ref, bf16[8,704,2048]{2,1,0:T(8,128)(2,1)} %bitcast.60, bf16[8,704,2048]{2,1,0:T(8,128)(2,1)} %bitcast.61, bf16[8,704,2048]{2,1,0:T(8,128)(2,1)} %down_ref.1, f32[8,128,1]{2,1,0:T(8,128)} %copy.39.scale_ref), custom_call_target="tpu_custom_call" | custom-call | tf_op jit(solution)/shard_map/pallas_call | solution.py:45
  168.4 6.0 %convolution_convert_fusion.1 = bf16[512,2048]{1,0:T(8,128)(2,1)} fusion(pred[512,1024]{1,0:T(8,128)(4,1)S(1)} %fusion.1, bf16[1024,2048]{1,0:T(8,128)(2,1)} %bitcast.62), kind=kOutput, calls=%fused_computation.11 | convolution fusion | flops 2148532224 | bytes 6815744 | tf_op jit(solution)/shard_map/dot_general | solution.py:217
  174.4 0.0 reduce-scatter.6.cloned.1.call-update
  174.4 0.0 reduce-scatter.8.cloned.1.call-start
  174.4 10.9 %reduce-scatter.6.cloned.1.call-done = bf16[512,1024]{1,0:T(8,128)(2,1)} async-done(((bf16[512,2048]{1,0:T(8,128)(2,1)}), bf16[512,1024]{1,0:T(8,128)(2,1)}) %reduce-scatter.6.cloned.1.call-update) | async-done | bytes 1048592 | tf_op jit(solution)/shard_map/reduce_scatter | solution.py:218
  185.3 0.0 reduce-scatter.8.cloned.1.call-update
  185.4 31.1 %reduce-scatter.8.cloned.1.call-done = bf16[128,1024]{1,0:T(8,128)(2,1)} async-done(((bf16[512,1024]{1,0:T(8,128)(2,1)}), bf16[128,1024]{1,0:T(8,128)(2,1)}) %reduce-scatter.8.cloned.1.call-update) | async-done | bytes 262160 | tf_op jit(solution)/shard_map/reduce_scatter | solution.py:219
  (35 shorter events, 0.2 us)
Async XLA Ops:
  7.2 69.3 %copy-start = (bf16[512,2048]{1,0:T(8,128)(2,1)S(1)}, bf16[512,2048]{1,0:T(8,128)(2,1)}, u32[]{:S(2)}) copy-start(bf16[512,2048]{1,0:T(8,128)(2,1)} %param.24) | copy-start | bytes 6291460
  7.2 8.0 %copy-start.6 = (bf16[512,512]{1,0:T(8,128)(2,1)S(1)}, bf16[512,512]{1,0:T(8,128)(2,1)}, u32[]{:S(2)}) copy-start(bf16[512,512]{1,0:T(8,128)(2,1)} %param.23) | copy-start | bytes 1572868
  7.2 9.0 %copy-start.5 = (bf16[128,2304]{1,0:T(8,128)(2,1)S(1)}, bf16[128,2304]{1,0:T(8,128)(2,1)}, u32[]{:S(2)}) copy-start(bf16[128,2304]{1,0:T(8,128)(2,1)} %param.16) | copy-start | bytes 1769476
  7.2 49.6 %all-gather.9.cloned.1.call-start = ((), (), s32[]{:S(2)}) async-start(), calls=%async_computation.8 | async-start | bytes 3981312 | tf_op jit(solution)/shard_map/all_gather | solution.py:113
  12.4 72.3 %reduce-scatter.4.cloned.1.call-start = ((), (), s32[]{:S(2)}) async-start(), calls=%async_computation.3 | async-start | bytes 786432 | tf_op jit(solution)/shard_map/reduce_scatter | solution.py:163
  69.7 1.5 copy-start.2
  71.2 1.0 copy-start.7
  76.4 1.4 copy-start.10
  76.4 8.3 %copy-start.9 = (bf16[128,2048]{1,0:T(8,128)(2,1)S(1)}, bf16[128,2048]{1,0:T(8,128)(2,1)}, u32[]{:S(2)}) copy-start(bf16[128,2048]{1,0:T(8,128)(2,1)} %param.15) | copy-start | bytes 1572868
  77.8 40.7 %all-gather.5.cloned.1.call-start = ((), (), s32[]{:S(2)}) async-start(), calls=%async_computation.4 | async-start | bytes 1310720 | tf_op jit(solution)/shard_map/all_gather | solution.py:175
  85.9 36.7 %copy-start.4 = (bf16[128,1024]{1,0:T(8,128)(2,1)}, bf16[128,1024]{1,0:T(8,128)(2,1)S(1)}, u32[]{:S(2)}) copy-start(bf16[128,1024]{1,0:T(8,128)(2,1)S(1)} %get-tuple-element.3) | copy-start | bytes 786436
  89.2 40.8 %copy-start.8 = (bf16[2048,32]{0,1:T(8,128)(2,1)S(1)}, bf16[2048,32]{0,1:T(8,128)(2,1)}, u32[]{:S(2)}) copy-start(bf16[2048,32]{0,1:T(8,128)(2,1)} %param.26) | copy-start | bytes 393220
  89.2 40.8 %all-gather.7.cloned.1.call-start = ((), (), s32[]{:S(2)}) async-start(), calls=%async_computation.5 | async-start | bytes 3145728 | tf_op jit(solution)/shard_map/all_gather | solution.py:176
  118.5 66.9 %reduce-scatter.6.cloned.1.call-start = ((), (), s32[]{:S(2)}) async-start(), calls=%async_computation.6 | async-start | bytes 3145728 | tf_op jit(solution)/shard_map/reduce_scatter | solution.py:218
  130.0 5.4 %copy-start.3 = (bf16[512,2048]{1,0:T(8,128)(2,1)S(1)}, bf16[512,2048]{1,0:T(8,128)(2,1)}, u32[]{:S(2)}) copy-start(bf16[512,2048]{1,0:T(8,128)(2,1)} %all-gather.7.cloned.1.call-done) | copy-start | bytes 6291460
  168.4 48.0 %copy-start.1 = (bf16[512,2048]{1,0:T(8,128)(2,1)S(1)}, bf16[512,2048]{1,0:T(8,128)(2,1)}, u32[]{:S(2)}) copy-start(bf16[512,2048]{1,0:T(8,128)(2,1)} %param.24) | copy-start | bytes 6291460
  174.4 42.0 %reduce-scatter.8.cloned.1.call-start = ((), (), s32[]{:S(2)}) async-start(), calls=%async_computation.7 | async-start | bytes 1310720 | tf_op jit(solution)/shard_map/reduce_scatter | solution.py:219
Sparse Core Ops, SparseCore 0:
  12.6 44.2 all-gather.8
  77.9 6.8 reduce-scatter.3
  89.3 29.0 all-gather.4
  119.9 10.0 all-gather.6
  174.5 10.7 reduce-scatter.5
  188.0 28.3 reduce-scatter.7

commit v12 on v11

--- a/solution.py
+++ b/solution.py
@@ -59,6 +59,28 @@
             vmem_limit_bytes=56 * 1024 * 1024,
         ),
     )(grouped_t, gate_rows, up_rows, down_weight, scale)
+
+
+def pair_swap(x):
+    return lax.ppermute(x, "ffn", [(0, 1), (1, 0)])
+
+
+def ffn_sum_scatter(x, ffn_index, ffn_size, axis):
+    if ffn_size != 2:
+        return lax.psum_scatter(x, "ffn", scatter_dimension=axis, tiled=True).astype(jnp.float32)
+    width = x.shape[axis] // 2
+    mine = lax.dynamic_slice_in_dim(x, ffn_index * width, width, axis)
+    other = lax.dynamic_slice_in_dim(x, (1 - ffn_index) * width, width, axis)
+    return mine.astype(jnp.float32) + pair_swap(other).astype(jnp.float32)
+
+
+def ffn_gather_columns(x, ffn_index, ffn_size):
+    if ffn_size != 2:
+        return lax.all_gather(x, "ffn", axis=1, tiled=True)
+    other = pair_swap(x)
+    first = jnp.where(ffn_index == 0, x, other)
+    second = jnp.where(ffn_index == 0, other, x)
+    return jnp.concatenate([first, second], axis=1)
 
 
 def local(
@@ -160,9 +182,7 @@
     head_out = head_out.astype(jnp.bfloat16).reshape(token_rows, heads_here * HEAD_DIM)
     partial_value = jnp.dot(head_out, out_proj, preferred_element_type=jnp.float32)
     column_count = feature_count // ffn_size
-    attn_cols = lax.psum_scatter(
-        partial_value.astype(jnp.bfloat16), "ffn", scatter_dimension=1, tiled=True
-    ).astype(jnp.float32)
+    attn_cols = ffn_sum_scatter(partial_value.astype(jnp.bfloat16), ffn_index, ffn_size, 1)
     residual_cols = lax.dynamic_slice_in_dim(residual, ffn_index * column_count, column_count, 1)
     hidden_out = (residual_cols.astype(jnp.float32) + attn_cols).astype(jnp.bfloat16)
     hidden_wide = hidden_out.astype(jnp.float32)
@@ -173,7 +193,7 @@
         hidden_wide * lax.rsqrt(mean_square + EPSILON) * gain_cols.astype(jnp.float32)
     ).astype(jnp.bfloat16)
     normed_half = lax.all_gather(normed_cols, "exp", axis=0, tiled=True)
-    normed_all = lax.all_gather(normed_half, "ffn", axis=1, tiled=True)
+    normed_all = ffn_gather_columns(normed_half, ffn_index, ffn_size)
 
     expert_ids = lax.broadcasted_iota(jnp.int32, (1, 1, EXPERTS), 2)
     route_hot = routes_all[:, :, None] == expert_ids
@@ -215,7 +235,7 @@
         slot_weight.reshape(local_count, slot_count, 1),
     ).reshape(total_slots, feature_count)
     mixture = jnp.dot(combine, weighted, preferred_element_type=jnp.float32).astype(jnp.bfloat16)
-    moe_cols = lax.psum_scatter(mixture, "ffn", scatter_dimension=1, tiled=True)
+    moe_cols = ffn_sum_scatter(mixture, ffn_index, ffn_size, 1).astype(jnp.bfloat16)
     moe_out = lax.psum_scatter(moe_cols, "exp", scatter_dimension=0, tiled=True)
     return (hidden_out, moe_out)
 

time: 224 us -> 196 us (0.88)
  waiting for transfers between devices: 123 us -> 94.4 us
  matrix products: 21.2 us -> 18.7 us
    reduce_scatter x2 -> x0, waiting for transfers between devices: 17.8 us -> none  [the longest x1 10.9 us: local(): moe_cols = lax.psum_scatter(mixture, 'ffn', scatter_dimension=1, tiled=True)]
    all_gather x1 -> x0, waiting for transfers between devices: 7.45 us -> none  [local(): normed_all = lax.all_gather(normed_half, 'ffn', axis=1, tiled=True)]
    reduce_scatter x1, waiting for transfers between devices: 31.1 us -> 26.8 us  [local(): moe_out = lax.psum_scatter(moe_cols, 'exp', scatter_dimension=0, tiled=True)]
    ppermute x0 -> x3, waiting for transfers between devices: none -> 3.58 us  [pair_swap(): return lax.ppermute(x, 'ffn', [(0, 1), (1, 0)])]
    all_gather x1, waiting for transfers between devices: 29.2 us -> 26.7 us  [local(): normed_half = lax.all_gather(normed_cols, 'exp', axis=0, tiled=True)]
  transfers between devices with their start and end apart: 6 -> 6, of which waited for: 6 -> 5; matrix products, arithmetic and copies ran while one was open for 5% -> 6% of each run, Pallas kernels for 0% -> 0%
where the time goes in v12:
time: 196 us
  waiting for transfers between devices  94.4 us (48%)
  Pallas kernels  28.5 us (15%)
  local copies, waits for them, and re-layouts  22.6 us (12%)
  matrix products  18.7 us (10%)
  between operations  14.1 us (7%)
  other arithmetic  13.6 us (7%)
  blocking collectives  2.47 us (1%)
    all_gather x1, waiting for transfers between devices, local(): gathered = lax.all_gather(share, ('exp', 'ffn'), axis=0, tiled=False)  37.2 us
    pallas_call x1, Pallas kernels, expert_ffn(): pl.pallas_call(expert_kernel, grid=(local_count, tiles), in_specs=[pl.Blo...  28.5 us
    reduce_scatter x1, waiting for transfers between devices, local(): moe_out = lax.psum_scatter(moe_cols, 'exp', scatter_dimension=0, tiled=True)  26.8 us
    all_gather x1, waiting for transfers between devices, local(): normed_half = lax.all_gather(normed_cols, 'exp', axis=0, tiled=True)  26.7 us
    gather x1, local copies, waits for them, and re-layouts, local(): jnp.take(flat_pages, key_rows, axis=0, mode='clip')  6.36 us
    dot_general x1, matrix products, local(): jnp.einsum('td,ts->ds', normed_all, combine, preferred_element_type=jnp.f...  5.87 us
    dot_general x1, matrix products, local(): jnp.dot(combine, weighted, preferred_element_type=jnp.float32)  4.52 us
    unnamed x27, local copies, waits for them, and re-layouts  4.39 us
  transfers between devices with their start and end apart: 6, of which 5 were waited for; matrix products, arithmetic and copies ran while one was open for 6% of the time, Pallas kernels for 0%

profile of v12, /device:TPU:0, one launch (start us, length us, event | category | flops | bytes accessed | tf_op | source)
XLA Modules:
  0.0 195.5 jit_solution(17294807424695028551)
XLA Ops:
  7.2 0.0 all-gather.6.cloned.1.call-start
  7.3 0.8 convert_element_type.98
  8.1 0.1 copy.31
  8.2 0.2 convert_element_type.99
  8.4 0.6 reshape.199
  9.0 1.1 copy.30
  10.1 0.2 reshape.198
  10.3 0.1 pad_dynamic-slice_fusion.3
  10.4 2.0 %fusion.21 = bf16[24,9216]{1,0:T(8,128)(2,1)} fusion(s32[]{:T(128)S(6)} %select_n.69, bf16[32,9216]{1,0:T(8,128)(2,1)} %param.18, bf16[8,9216]{1,0:T(8,128)(2,1)S(1)} %reshape.198, bf16[1,9216]{1,0:T(2,128)(2,1)} %reshape.199, bf16[24]{0:T(256)(128)(2,1)S(1)} %pad_dynamic-slice_fusion.3), kind=kLoop, calls=%fused_computation.42 | loop fusion | flops 1769472 | bytes 1198132 | tf_op jit(solution)/shard_map/concatenate | solution.py:125
  12.4 0.0 all-gather.6.cloned.1.call-update
  12.4 0.0 all-gather.4.cloned.1.call-start
  12.5 1.2 dynamic_slice.31
  13.8 1.2 dynamic_slice.32
  15.0 0.1 iota_add_fusion.1
  15.1 0.1 add.126
  15.2 1.0 copy.43
  16.2 0.3 copy.32
  16.5 0.7 fusion.25
  17.2 0.1 pad_add_fusion
  17.3 1.3 iota_compare_fusion.5
  18.6 1.0 and_or_fusion
  19.6 37.2 %all-gather.6.cloned.1.call-done = bf16[192,9216]{1,0:T(8,128)(2,1)} async-done(((bf16[24,9216]{1,0:T(8,128)(2,1)}), bf16[192,9216]{1,0:T(8,128)(2,1)}) %all-gather.6.cloned.1.call-update) | async-done | bytes 3538960 | tf_op jit(solution)/shard_map/all_gather | solution.py:135
  56.8 6.4 %gather_fusion = bf16[80,9216]{1,0:T(8,128)(2,1)} fusion(bf16[192,9216]{1,0:T(8,128)(2,1)} %all-gather.6.cloned.1.call-done, s32[1024]{0:T(1024)S(1)} %pad_clamp_fusion), kind=kCustom, calls=%fused_computation | custom fusion | bytes 2949440 | tf_op jit(solution)/shard_map/jit(_take)/gather | solution.py:158
  63.2 3.9 %reshape.200 = bf16[1280,576]{1,0:T(8,128)(2,1)} reshape(bf16[80,9216]{1,0:T(8,128)(2,1)} %gather_fusion) | data formatting | bytes 2949120 | tf_op jit(solution)/shard_map/reshape | solution.py:158
  67.0 2.6 %fusion.4 = f32[128,4,1280]{0,2,1:T(8,128)S(1)} fusion(bf16[128,4,576]{0,2,1:T(8,128)(2,1)S(1)} %bitcast.61, bf16[1280,576]{1,0:T(8,128)(2,1)} %reshape.200, pred[128,1280]{0,1:T(8,128)(4,1)S(1)} %and_or_fusion), kind=kOutput, calls=%fused_computation.9 | convolution fusion | flops 756285440 | bytes 4849664 | tf_op jit(solution)/shard_map/thd,kd->thk/dot_general | solution.py:163
  69.7 1.5 copy-done.2
  71.2 0.6 fusion.32
  71.8 0.4 copy-done.9
  72.2 4.2 %fusion.13 = bf16[4,128,128]{1,2,0:T(8,128)(2,1)S(1)} fusion(bf16[512,4,128]{0,2,1:T(8,128)(2,1)S(1)} %bitcast.62, bf16[1280,576]{1,0:T(8,128)(2,1)} %reshape.200, f32[128,4]{0,1:T(4,128)S(1)} %fusion.32, f32[128,4,1280]{0,2,1:T(8,128)} %copy-done.2), kind=kOutput, calls=%fused_computation.25 | convolution fusion | flops 740493056 | bytes 7211008 | tf_op jit(solution)/shard_map/thl,lhd->thd/dot_general | solution.py:179
  76.5 0.5 convolution_convert_fusion.2
  77.0 0.3 collective-permute-start
  77.3 1.3 collective-permute-done
  78.6 1.2 fusion.16
  79.7 2.5 %psum.7 = f32[128,1]{0,1:T(1,128)S(1)} all-reduce(f32[128,1]{0,1:T(1,128)S(1)} %bitcast.66), channel_id=1, replica_groups=mesh['req'=4,'exp'=4,'ffn'=2] {'ffn'}, use_global_device_ids=true, to_apply=%region_5.6 | all-reduce | flops 128 | bytes 1024 | tf_op jit(solution)/shard_map/psum | solution.py:189
  82.2 0.8 fusion.18
  83.1 0.0 all-gather.4.cloned.1.call-update
  83.1 0.2 reduce-scatter.2.cloned.1.call-start
  83.3 26.7 %all-gather.4.cloned.1.call-done = bf16[512,1024]{1,0:T(8,128)(2,1)} async-done(((bf16[128,1024]{1,0:T(8,128)(2,1)}), bf16[512,1024]{1,0:T(8,128)(2,1)}) %all-gather.4.cloned.1.call-update) | async-done | bytes 1048592 | tf_op jit(solution)/shard_map/all_gather | solution.py:195
  110.0 0.1 add.130
  110.1 0.1 add.131
  110.2 1.2 slice.15
  111.5 0.2 reshape.208
  111.7 0.3 fusion.12
  112.0 0.1 copy.38
  112.1 0.2 convert_element_type.115
  112.4 0.1 add_select_fusion
  112.5 0.1 copy.37
  112.6 1.4 fusion.1
  114.0 0.1 broadcast_select_fusion.1
  114.2 1.0 copy-done.4
  115.2 0.7 fusion.7
  115.9 0.0 copy-done.5
  115.9 0.1 select_reduce_fusion.1
  116.1 1.7 select_reduce_fusion
  117.8 1.1 copy.39.scale_ref
  118.9 5.9 %convolution_convert_fusion.rows_ref = bf16[2048,1024]{1,0:T(8,128)(2,1)} fusion(pred[512,1024]{1,0:T(8,128)(4,1)S(1)} %fusion.1, bf16[512,1024]{1,0:T(8,128)(2,1)} %copy-done.5, bf16[512,1024]{1,0:T(8,128)(2,1)} %copy-done.4), kind=kOutput, calls=%fused_computation.5 | convolution fusion | flops 2153775104 | bytes 6815744 | tf_op jit(solution)/shard_map/td,ts->ds/dot_general | solution.py:227
  124.7 28.5 %shard_map.158 = bf16[8,128,2048]{2,1,0:T(8,128)(2,1)} custom-call(bf16[2048,1024]{1,0:T(8,128)(2,1)} %convolution_convert_fusion.rows_ref, bf16[8,704,2048]{2,1,0:T(8,128)(2,1)} %bitcast.58, bf16[8,704,2048]{2,1,0:T(8,128)(2,1)} %bitcast.59, bf16[8,704,2048]{2,1,0:T(8,128)(2,1)} %down_ref.1, f32[8,128,1]{2,1,0:T(8,128)} %copy.39.scale_ref), custom_call_target="tpu_custom_call" | custom-call | tf_op jit(solution)/shard_map/pallas_call | solution.py:45
  153.3 4.5 %convolution_convert_fusion.1 = bf16[512,2048]{1,0:T(8,128)(2,1)S(1)} fusion(pred[512,1024]{1,0:T(8,128)(4,1)S(1)} %fusion.1, bf16[1024,2048]{1,0:T(8,128)(2,1)} %bitcast.60), kind=kOutput, calls=%fused_computation.11 | convolution fusion | flops 2148532224 | bytes 6815744 | tf_op jit(solution)/shard_map/dot_general | solution.py:237
  157.8 0.1 constant_dynamic-slice_fusion
  157.9 0.5 collective-permute-start.2
  158.4 2.3 %collective-permute-done.2 = bf16[512,1024]{1,0:T(8,128)(2,1)S(1)} collective-permute-done((bf16[512,1024]{1,0:T(8,128)(2,1)S(1)}, bf16[512,1024]{1,0:T(8,128)(2,1)S(1)}, u32[]{:S(2)}, u32[]{:S(2)}) %collective-permute-start.2) | collective-permute-done | bytes 1048608 | tf_op jit(solution)/shard_map/ppermute | solution.py:65
  160.7 1.4 add_convert_fusion
  162.1 0.0 reduce-scatter.2.cloned.1.call-update
  162.1 26.8 %reduce-scatter.2.cloned.1.call-done = bf16[128,1024]{1,0:T(8,128)(2,1)} async-done(((bf16[512,1024]{1,0:T(8,128)(2,1)}), bf16[128,1024]{1,0:T(8,128)(2,1)}) %reduce-scatter.2.cloned.1.call-update) | async-done | bytes 262160 | tf_op jit(solution)/shard_map/reduce_scatter | solution.py:239
  (38 shorter events, 0.2 us)
Async XLA Ops:
  7.2 69.3 %copy-start = (bf16[512,2048]{1,0:T(8,128)(2,1)S(1)}, bf16[512,2048]{1,0:T(8,128)(2,1)}, u32[]{:S(2)}) copy-start(bf16[512,2048]{1,0:T(8,128)(2,1)} %param.24) | copy-start | bytes 6291460
  7.2 8.0 %copy-start.8 = (bf16[512,512]{1,0:T(8,128)(2,1)S(1)}, bf16[512,512]{1,0:T(8,128)(2,1)}, u32[]{:S(2)}) copy-start(bf16[512,512]{1,0:T(8,128)(2,1)} %param.23) | copy-start | bytes 1572868
  7.2 9.0 %copy-start.7 = (bf16[128,2304]{1,0:T(8,128)(2,1)S(1)}, bf16[128,2304]{1,0:T(8,128)(2,1)}, u32[]{:S(2)}) copy-start(bf16[128,2304]{1,0:T(8,128)(2,1)} %param.16) | copy-start | bytes 1769476
  7.2 49.6 %all-gather.6.cloned.1.call-start = ((), (), s32[]{:S(2)}) async-start(), calls=%async_computation.3 | async-start | bytes 3981312 | tf_op jit(solution)/shard_map/all_gather | solution.py:135
  12.4 97.6 %all-gather.4.cloned.1.call-start = ((), (), s32[]{:S(2)}) async-start(), calls=%async_computation.1 | async-start | bytes 1310720 | tf_op jit(solution)/shard_map/all_gather | solution.py:195
  69.7 1.5 copy-start.2
  71.2 1.0 copy-start.9
  76.4 0.8 copy-start.10
  77.0 1.6 collective-permute-start
  79.7 34.4 %copy-start.6 = (bf16[128,1024]{1,0:T(8,128)(2,1)}, bf16[128,1024]{1,0:T(8,128)(2,1)S(1)}, u32[]{:S(2)}) copy-start(bf16[128,1024]{1,0:T(8,128)(2,1)S(1)} %get-tuple-element.3) | copy-start | bytes 786436
  83.1 105.9 %reduce-scatter.2.cloned.1.call-start = ((), (), s32[]{:S(2)}) async-start(), calls=%async_computation.2 | async-start | bytes 1310720 | tf_op jit(solution)/shard_map/reduce_scatter | solution.py:239
  110.0 4.0 %copy-start.3 = (bf16[512,1024]{1,0:T(8,128)(2,1)S(1)}, bf16[512,1024]{1,0:T(8,128)(2,1)}, u32[]{:S(2)}) copy-start(bf16[512,1024]{1,0:T(8,128)(2,1)} %all-gather.4.cloned.1.call-done) | copy-start | bytes 3145732
  110.0 4.0 %collective-permute-start.1 = (bf16[512,1024]{1,0:T(8,128)(2,1)}, bf16[512,1024]{1,0:T(8,128)(2,1)S(1)}, u32[]{:S(2)}, u32[]{:S(2)}) collective-permute-start(bf16[512,1024]{1,0:T(8,128)(2,1)} %all-gather.4.cloned.1.call-done), channel_id=1, source_target_pairs={{0,1},{1,0},{2,3},{3,2},{4,5},{5,4},{6,7},{7,6},{8,9},{9,8},{10,11... | collective-permute-start | bytes 3145736 | tf_op jit(solution)/shard_map/ppermute | solution.py:65
  112.5 2.7 %copy-start.11 = (bf16[2048,32]{0,1:T(8,128)(2,1)S(1)}, bf16[2048,32]{0,1:T(8,128)(2,1)}, u32[]{:S(2)}) copy-start(bf16[2048,32]{0,1:T(8,128)(2,1)} %param.26) | copy-start | bytes 393220
  114.2 1.0 copy-start.4
  114.2 1.7 copy-start.5
  157.8 31.2 %copy-start.1 = (bf16[512,2048]{1,0:T(8,128)(2,1)S(1)}, bf16[512,2048]{1,0:T(8,128)(2,1)}, u32[]{:S(2)}) copy-start(bf16[512,2048]{1,0:T(8,128)(2,1)} %param.24) | copy-start | bytes 6291460
  157.9 2.8 %collective-permute-start.2 = (bf16[512,1024]{1,0:T(8,128)(2,1)S(1)}, bf16[512,1024]{1,0:T(8,128)(2,1)S(1)}, u32[]{:S(2)}, u32[]{:S(2)}) collective-permute-start(bf16[512,1024]{1,0:T(8,128)(2,1)S(1)} %constant_dynamic-slice_fusion), channel_id=1, source_target_pairs={{0,1},{1,0},{2,3},{3,2},{4,5},{5,4},{6,7},{7,6},{8,9},{9,8},{10,11... | collective-permute-start | bytes 3145736 | tf_op jit(solution)/shard_map/ppermute | solution.py:65
Sparse Core Ops, SparseCore 0:
  12.6 44.2 all-gather.5
  83.2 26.7 all-gather.3
  162.3 26.6 reduce-scatter.1

commit v13 on v12

--- a/solution.py
+++ b/solution.py
@@ -132,8 +132,16 @@
         axis=0,
     )
     share = lax.dynamic_slice_in_dim(packed, ffn_index * share_rows, share_rows, 0)
-    gathered = lax.all_gather(share, ("exp", "ffn"), axis=0, tiled=False)
-    gathered = gathered.reshape(exp_size, ffn_size * share_rows, page_width)
+    if ffn_size == 2:
+        mine = lax.all_gather(share, "exp", axis=0, tiled=False)
+        other = pair_swap(mine)
+        gathered = jnp.concatenate(
+            [jnp.where(ffn_index == 0, mine, other), jnp.where(ffn_index == 0, other, mine)],
+            axis=1,
+        )
+    else:
+        gathered = lax.all_gather(share, ("exp", "ffn"), axis=0, tiled=False)
+        gathered = gathered.reshape(exp_size, ffn_size * share_rows, page_width)
     stride = ffn_size * share_rows
     group_rows = exp_size * token_rows
     routes_all = (

time: 196 us -> 213 us (1.087)
  other arithmetic: 13.6 us -> 19.5 us
  waiting for transfers between devices: 94.4 us -> 100 us
  local copies, waits for them, and re-layouts: 22.6 us -> 27.4 us
    all_gather x1, waiting for transfers between devices: 37.2 us -> 43.1 us  [local(): mine = lax.all_gather(share, 'exp', axis=0, tiled=False)]
    all_gather x0 -> x1, local copies, waits for them, and re-layouts: none -> 4.07 us  [local(): mine = lax.all_gather(share, 'exp', axis=0, tiled=False)]
    select_n x0 -> x1, other arithmetic: none -> 3.6 us  [local(): jnp.where(ffn_index == 0, mine, other)]
    concatenate x0 -> x1, local copies, waits for them, and re-layouts: none -> 2.82 us  [local(): jnp.concatenate([jnp.where(ffn_index == 0, mine, other), jnp.where(ffn_in...]
    concatenate x0 -> x1, other arithmetic: none -> 2.28 us  [local(): jnp.concatenate([jnp.where(ffn_index == 0, mine, other), jnp.where(ffn_in...]
    unnamed x27 -> x32, local copies, waits for them, and re-layouts: 4.39 us -> 4.37 us
  transfers between devices with their start and end apart: 6 -> 7, of which waited for: 5 -> 5; matrix products, arithmetic and copies ran while one was open for 6% -> 4% of each run, Pallas kernels for 0% -> 0%
where the time goes in v13:
time: 213 us; the launch traced here: 212 us
  waiting for transfers between devices  100 us (47%)
  Pallas kernels  28.6 us (13%)
  local copies, waits for them, and re-layouts  27.4 us (13%)
  other arithmetic  19.5 us (9%)
  matrix products  18.7 us (9%)
  between operations  14.1 us (7%)
  blocking collectives  2.51 us (1%)
    all_gather x1, waiting for transfers between devices, local(): mine = lax.all_gather(share, 'exp', axis=0, tiled=False)  43.1 us
    pallas_call x1, Pallas kernels, expert_ffn(): pl.pallas_call(expert_kernel, grid=(local_count, tiles), in_specs=[pl.Blo...  28.6 us
    reduce_scatter x1, waiting for transfers between devices, local(): moe_out = lax.psum_scatter(moe_cols, 'exp', scatter_dimension=0, tiled=True)  26.8 us
    all_gather x1, waiting for transfers between devices, local(): normed_half = lax.all_gather(normed_cols, 'exp', axis=0, tiled=True)  26.8 us
    gather x1, local copies, waits for them, and re-layouts, local(): jnp.take(flat_pages, key_rows, axis=0, mode='clip')  6.37 us
    dot_general x1, matrix products, local(): jnp.einsum('td,ts->ds', normed_all, combine, preferred_element_type=jnp.f...  5.86 us
    dot_general x1, matrix products, local(): jnp.dot(combine, weighted, preferred_element_type=jnp.float32)  4.52 us
    unnamed x32, local copies, waits for them, and re-layouts  4.37 us
  transfers between devices with their start and end apart: 7, of which 5 were waited for; matrix products, arithmetic and copies ran while one was open for 4% of the time, Pallas kernels for 0%

profile of v13, /device:TPU:0, one launch (start us, length us, event | category | flops | bytes accessed | tf_op | source)
XLA Modules:
  0.0 212.2 jit_solution(4657901455156829884)
XLA Ops:
  7.2 0.0 all-gather.6.cloned.1.call-start
  7.2 0.8 convert_element_type.98
  8.1 0.1 copy.34
  8.2 0.2 convert_element_type.99
  8.4 1.1 copy.33
  9.5 0.2 reshape.198
  9.6 0.1 pad_dynamic-slice_fusion.3
  9.7 2.1 fusion.21
  11.8 0.0 all-gather.6.cloned.1.call-update
  11.9 0.0 all-gather.4.cloned.1.call-start
  11.9 43.1 %all-gather.6.cloned.1.call-done = bf16[96,9216]{1,0:T(8,128)(2,1)} async-done(((bf16[24,9216]{1,0:T(8,128)(2,1)}), bf16[96,9216]{1,0:T(8,128)(2,1)}) %all-gather.6.cloned.1.call-update) | async-done | bytes 1769488 | tf_op jit(solution)/shard_map/all_gather | solution.py:136
  55.0 4.1 %copy.36 = bf16[4,24,9216]{2,0,1:T(4,128)(2,1)} copy(bf16[4,24,9216]{2,1,0:T(8,128)(2,1)} %bitcast.60) | data formatting | bytes 3538944 | tf_op jit(solution)/shard_map/all_gather | solution.py:136
  59.1 0.6 dynamic_slice.31
  59.7 0.6 dynamic_slice.32
  60.3 0.1 iota_add_fusion.1
  60.4 0.1 add.126
  60.5 1.1 copy.49
  61.5 0.3 copy.39
  61.8 0.7 fusion.25
  62.5 0.1 pad_add_fusion
  62.6 1.3 iota_compare_fusion.5
  64.0 1.0 and_or_fusion
  65.0 3.6 %broadcast_select_fusion.1 = (bf16[4,24,9216]{2,0,1:T(4,128)(2,1)S(1)}, bf16[4,24,9216]{2,0,1:T(4,128)(2,1)S(1)}) fusion(bf16[4,24,9216]{2,0,1:T(4,128)(2,1)} %collective-permute-done, pred[]{:T(512)S(6)} %eq.41, bf16[4,24,9216]{2,1,0:T(8,128)(2,1)} %bitcast.61), kind=kLoop, calls=%fused_computation.18 | loop fusion | flops 1769472 | bytes 7077889 | tf_op jit(solution)/shard_map/jit(_where)/select_n | solution.py:139
  68.6 2.3 %pad_maximum_fusion = bf16[4,48,9216]{2,0,1:T(4,128)(2,1)S(1)} fusion(bf16[4,24,9216]{2,0,1:T(4,128)(2,1)S(1)} %get-tuple-element.5, bf16[4,24,9216]{2,0,1:T(4,128)(2,1)S(1)} %get-tuple-element.4), kind=kLoop, calls=%fused_computation.7 | loop fusion | flops 1769472 | bytes 7077888 | tf_op jit(solution)/shard_map/concatenate | solution.py:138
  70.9 2.8 %copy.38 = bf16[4,48,9216]{2,1,0:T(8,128)(2,1)} copy(bf16[4,48,9216]{2,0,1:T(4,128)(2,1)S(1)} %pad_maximum_fusion) | data formatting | bytes 7077888 | tf_op jit(solution)/shard_map/concatenate | solution.py:138
  73.7 6.4 %gather_fusion = bf16[80,9216]{1,0:T(8,128)(2,1)} fusion(bf16[192,9216]{1,0:T(8,128)(2,1)} %bitcast.57, s32[1024]{0:T(1024)S(1)} %pad_clamp_fusion), kind=kCustom, calls=%fused_computation | custom fusion | bytes 2949440 | tf_op jit(solution)/shard_map/jit(_take)/gather | solution.py:166
  80.1 3.9 %reshape.201 = bf16[1280,576]{1,0:T(8,128)(2,1)} reshape(bf16[80,9216]{1,0:T(8,128)(2,1)} %gather_fusion) | data formatting | bytes 2949120 | tf_op jit(solution)/shard_map/reshape | solution.py:166
  84.0 2.6 %fusion.4 = f32[128,4,1280]{0,2,1:T(8,128)S(1)} fusion(bf16[128,4,576]{0,2,1:T(8,128)(2,1)S(1)} %bitcast.63, bf16[1280,576]{1,0:T(8,128)(2,1)} %reshape.201, pred[128,1280]{0,1:T(8,128)(4,1)S(1)} %and_or_fusion), kind=kOutput, calls=%fused_computation.10 | convolution fusion | flops 756285440 | bytes 4849664 | tf_op jit(solution)/shard_map/thd,kd->thk/dot_general | solution.py:171
  86.7 1.5 copy-done.3
  88.2 0.6 fusion.32
  88.8 0.4 copy-done.10
  89.2 4.2 %fusion.13 = bf16[4,128,128]{1,2,0:T(8,128)(2,1)S(1)} fusion(bf16[512,4,128]{0,2,1:T(8,128)(2,1)S(1)} %bitcast.64, bf16[1280,576]{1,0:T(8,128)(2,1)} %reshape.201, f32[128,4]{0,1:T(4,128)S(1)} %fusion.32, f32[128,4,1280]{0,2,1:T(8,128)} %copy-done.3), kind=kOutput, calls=%fused_computation.28 | convolution fusion | flops 740493056 | bytes 7211008 | tf_op jit(solution)/shard_map/thl,lhd->thd/dot_general | solution.py:187
  93.4 0.5 convolution_convert_fusion.2
  93.9 0.6 collective-permute-start.1
  94.5 1.2 collective-permute-done.1
  95.6 1.2 fusion.16
  96.8 2.5 %psum.7 = f32[128,1]{0,1:T(1,128)S(1)} all-reduce(f32[128,1]{0,1:T(1,128)S(1)} %bitcast.67), channel_id=1, replica_groups=mesh['req'=4,'exp'=4,'ffn'=2] {'ffn'}, use_global_device_ids=true, to_apply=%region_5.6 | all-reduce | flops 128 | bytes 1024 | tf_op jit(solution)/shard_map/psum | solution.py:197
  99.3 0.8 fusion.18
  100.2 0.0 reduce-scatter.2.cloned.1.call-start
  100.3 0.1 add.130
  100.3 0.1 add.131
  100.4 26.8 %all-gather.4.cloned.1.call-done = bf16[512,1024]{1,0:T(8,128)(2,1)} async-done(((bf16[128,1024]{1,0:T(8,128)(2,1)}), bf16[512,1024]{1,0:T(8,128)(2,1)}) %all-gather.4.cloned.1.call-update) | async-done | bytes 1048592 | tf_op jit(solution)/shard_map/all_gather | solution.py:203
  127.2 1.0 slice_bitcast_fusion.8
  128.2 0.2 reshape.208
  128.4 0.3 fusion.12
  128.7 0.1 copy.44
  128.8 0.2 convert_element_type.115
  129.1 0.1 add_select_fusion
  129.2 0.1 copy.43
  129.3 1.4 fusion.1
  130.7 0.1 broadcast_select_fusion.3
  130.9 1.0 copy-done.5
  131.9 0.7 fusion.7
  132.7 0.1 select_reduce_fusion.1
  132.8 1.7 select_reduce_fusion
  134.5 1.1 copy.45.scale_ref
  135.6 5.9 %convolution_convert_fusion.rows_ref = bf16[2048,1024]{1,0:T(8,128)(2,1)} fusion(pred[512,1024]{1,0:T(8,128)(4,1)S(1)} %fusion.1, bf16[512,1024]{1,0:T(8,128)(2,1)} %copy-done.6, bf16[512,1024]{1,0:T(8,128)(2,1)} %copy-done.5), kind=kOutput, calls=%fused_computation.5 | convolution fusion | flops 2153775104 | bytes 6815744 | tf_op jit(solution)/shard_map/td,ts->ds/dot_general | solution.py:235
  141.5 28.6 %shard_map.158 = bf16[8,128,2048]{2,1,0:T(8,128)(2,1)} custom-call(bf16[2048,1024]{1,0:T(8,128)(2,1)} %convolution_convert_fusion.rows_ref, bf16[8,704,2048]{2,1,0:T(8,128)(2,1)} %bitcast.58, bf16[8,704,2048]{2,1,0:T(8,128)(2,1)} %bitcast.59, bf16[8,704,2048]{2,1,0:T(8,128)(2,1)} %down_ref.1, f32[8,128,1]{2,1,0:T(8,128)} %copy.45.scale_ref), custom_call_target="tpu_custom_call" | custom-call | tf_op jit(solution)/shard_map/pallas_call | solution.py:45
  170.0 4.5 %convolution_convert_fusion.1 = bf16[512,2048]{1,0:T(8,128)(2,1)S(1)} fusion(pred[512,1024]{1,0:T(8,128)(4,1)S(1)} %fusion.1, bf16[1024,2048]{1,0:T(8,128)(2,1)} %bitcast.62), kind=kOutput, calls=%fused_computation.12 | convolution fusion | flops 2148532224 | bytes 6815744 | tf_op jit(solution)/shard_map/dot_general | solution.py:245
  174.6 0.1 constant_dynamic-slice_fusion
  174.7 0.5 collective-permute-start.3
  175.1 2.3 %collective-permute-done.3 = bf16[512,1024]{1,0:T(8,128)(2,1)S(1)} collective-permute-done((bf16[512,1024]{1,0:T(8,128)(2,1)S(1)}, bf16[512,1024]{1,0:T(8,128)(2,1)S(1)}, u32[]{:S(2)}, u32[]{:S(2)}) %collective-permute-start.3) | collective-permute-done | bytes 1048608 | tf_op jit(solution)/shard_map/ppermute | solution.py:65
  177.4 1.4 add_convert_fusion
  178.8 26.8 %reduce-scatter.2.cloned.1.call-done = bf16[128,1024]{1,0:T(8,128)(2,1)} async-done(((bf16[512,1024]{1,0:T(8,128)(2,1)}), bf16[128,1024]{1,0:T(8,128)(2,1)}) %reduce-scatter.2.cloned.1.call-update) | async-done | bytes 262160 | tf_op jit(solution)/shard_map/reduce_scatter | solution.py:247
  (49 shorter events, 0.3 us)
Async XLA Ops:
  7.2 86.2 %copy-start = (bf16[512,2048]{1,0:T(8,128)(2,1)S(1)}, bf16[512,2048]{1,0:T(8,128)(2,1)}, u32[]{:S(2)}) copy-start(bf16[512,2048]{1,0:T(8,128)(2,1)} %param.24) | copy-start | bytes 6291460
  7.2 47.9 %all-gather.6.cloned.1.call-start = ((), (), s32[]{:S(2)}) async-start(), calls=%async_computation.3 | async-start | bytes 2211840 | tf_op jit(solution)/shard_map/all_gather | solution.py:136
  9.7 49.4 %copy-start.13 = (s32[8]{0:T(128)S(1)}, s32[8]{0:T(128)}, u32[]{:S(2)}) copy-start(s32[8]{0:T(128)} %param.21) | copy-start | bytes 100
  9.7 50.0 %copy-start.14 = (s32[8]{0:T(128)S(1)}, s32[8]{0:T(128)}, u32[]{:S(2)}) copy-start(s32[8]{0:T(128)} %param.20) | copy-start | bytes 100
  9.7 50.7 %copy-start.9 = (bf16[512,512]{1,0:T(8,128)(2,1)S(1)}, bf16[512,512]{1,0:T(8,128)(2,1)}, u32[]{:S(2)}) copy-start(bf16[512,512]{1,0:T(8,128)(2,1)} %param.23) | copy-start | bytes 1572868
  11.8 49.7 %copy-start.8 = (bf16[128,2304]{1,0:T(8,128)(2,1)S(1)}, bf16[128,2304]{1,0:T(8,128)(2,1)}, u32[]{:S(2)}) copy-start(bf16[128,2304]{1,0:T(8,128)(2,1)} %param.16) | copy-start | bytes 1769476
  11.9 115.3 %all-gather.4.cloned.1.call-start = ((), (), s32[]{:S(2)}) async-start(), calls=%async_computation.1 | async-start | bytes 1310720 | tf_op jit(solution)/shard_map/all_gather | solution.py:203
  59.1 5.9 %collective-permute-start = (bf16[4,24,9216]{2,0,1:T(4,128)(2,1)}, bf16[4,24,9216]{2,0,1:T(4,128)(2,1)}, u32[]{:S(2)}, u32[]{:S(2)}) collective-permute-start(bf16[4,24,9216]{2,0,1:T(4,128)(2,1)} %copy.36), channel_id=1, source_target_pairs={{0,1},{1,0},{2,3},{3,2},{4,5},{5,4},{6,7},{7,6},{8,9},{9,8},{10,11... | collective-permute-start | bytes 5308424 | tf_op jit(solution)/shard_map/ppermute | solution.py:65
  68.6 2.3 %copy-start.2 = (bf16[4,24,9216]{2,0,1:T(4,128)(2,1)}, bf16[4,24,9216]{2,0,1:T(4,128)(2,1)S(1)}, u32[]{:S(2)}) copy-start(bf16[4,24,9216]{2,0,1:T(4,128)(2,1)S(1)} %get-tuple-element.5) | copy-start | bytes 5308420
  86.7 1.5 copy-start.3
  88.2 1.0 copy-start.10
  93.4 1.1 copy-start.11
  93.9 1.7 collective-permute-start.1
  96.8 34.1 %copy-start.7 = (bf16[128,1024]{1,0:T(8,128)(2,1)}, bf16[128,1024]{1,0:T(8,128)(2,1)S(1)}, u32[]{:S(2)}) copy-start(bf16[128,1024]{1,0:T(8,128)(2,1)S(1)} %get-tuple-element.3) | copy-start | bytes 786436
  100.2 105.5 %reduce-scatter.2.cloned.1.call-start = ((), (), s32[]{:S(2)}) async-start(), calls=%async_computation.2 | async-start | bytes 1310720 | tf_op jit(solution)/shard_map/reduce_scatter | solution.py:247
  127.2 3.5 %copy-start.4 = (bf16[512,1024]{1,0:T(8,128)(2,1)S(1)}, bf16[512,1024]{1,0:T(8,128)(2,1)}, u32[]{:S(2)}) copy-start(bf16[512,1024]{1,0:T(8,128)(2,1)} %all-gather.4.cloned.1.call-done) | copy-start | bytes 3145732
  127.2 3.5 %collective-permute-start.2 = (bf16[512,1024]{1,0:T(8,128)(2,1)}, bf16[512,1024]{1,0:T(8,128)(2,1)S(1)}, u32[]{:S(2)}, u32[]{:S(2)}) collective-permute-start(bf16[512,1024]{1,0:T(8,128)(2,1)} %all-gather.4.cloned.1.call-done), channel_id=1, source_target_pairs={{0,1},{1,0},{2,3},{3,2},{4,5},{5,4},{6,7},{7,6},{8,9},{9,8},{10,11... | collective-permute-start | bytes 3145736 | tf_op jit(solution)/shard_map/ppermute | solution.py:65
  129.2 2.7 %copy-start.12 = (bf16[2048,32]{0,1:T(8,128)(2,1)S(1)}, bf16[2048,32]{0,1:T(8,128)(2,1)}, u32[]{:S(2)}) copy-start(bf16[2048,32]{0,1:T(8,128)(2,1)} %param.26) | copy-start | bytes 393220
  130.9 1.0 copy-start.5
  130.9 1.7 copy-start.6
  174.5 31.1 %copy-start.1 = (bf16[512,2048]{1,0:T(8,128)(2,1)S(1)}, bf16[512,2048]{1,0:T(8,128)(2,1)}, u32[]{:S(2)}) copy-start(bf16[512,2048]{1,0:T(8,128)(2,1)} %param.24) | copy-start | bytes 6291460
  174.7 2.8 %collective-permute-start.3 = (bf16[512,1024]{1,0:T(8,128)(2,1)S(1)}, bf16[512,1024]{1,0:T(8,128)(2,1)S(1)}, u32[]{:S(2)}, u32[]{:S(2)}) collective-permute-start(bf16[512,1024]{1,0:T(8,128)(2,1)S(1)} %constant_dynamic-slice_fusion), channel_id=1, source_target_pairs={{0,1},{1,0},{2,3},{3,2},{4,5},{5,4},{6,7},{7,6},{8,9},{9,8},{10,11... | collective-permute-start | bytes 3145736 | tf_op jit(solution)/shard_map/ppermute | solution.py:65
Sparse Core Ops, SparseCore 0:
  12.0 43.0 all-gather.5
  100.3 26.8 all-gather.3
  179.0 26.6 reduce-scatter.1

commit v14 on v12

--- a/solution.py
+++ b/solution.py
@@ -192,8 +192,12 @@
     normed_cols = (
         hidden_wide * lax.rsqrt(mean_square + EPSILON) * gain_cols.astype(jnp.float32)
     ).astype(jnp.bfloat16)
-    normed_half = lax.all_gather(normed_cols, "exp", axis=0, tiled=True)
-    normed_all = ffn_gather_columns(normed_half, ffn_index, ffn_size)
+    normed_grid = lax.all_gather(normed_cols, ("exp", "ffn"), axis=0, tiled=False)
+    normed_all = (
+        normed_grid.reshape(exp_size, ffn_size, token_rows, column_count)
+        .transpose(0, 2, 1, 3)
+        .reshape(group_rows, feature_count)
+    )
 
     expert_ids = lax.broadcasted_iota(jnp.int32, (1, 1, EXPERTS), 2)
     route_hot = routes_all[:, :, None] == expert_ids

time: 196 us -> 194 us (0.990)
  local copies, waits for them, and re-layouts: 22.6 us -> 26.2 us
  waiting for transfers between devices: 94.4 us -> 91.8 us
    reshape x0 -> x1, local copies, waits for them, and re-layouts: none -> 3.75 us  [local(): normed_grid.reshape(exp_size, ffn_size, token_rows, column_count)]
    all_gather x1, waiting for transfers between devices: 26.7 us -> 24 us  [local(): lax.all_gather(normed_cols, ('exp', 'ffn'), axis=0, tiled=False)]
    unnamed x27 -> x24, local copies, waits for them, and re-layouts: 4.39 us -> 4.27 us
  transfers between devices with their start and end apart: 6 -> 5, of which waited for: 5 -> 5; matrix products, arithmetic and copies ran while one was open for 6% -> 6% of each run, Pallas kernels for 0% -> 0%
where the time goes in v14:
time: 194 us
  waiting for transfers between devices  91.8 us (47%)
  Pallas kernels  28.6 us (15%)
  local copies, waits for them, and re-layouts  26.2 us (14%)
  matrix products  17.2 us (9%)
  between operations  14.1 us (7%)
  other arithmetic  12.7 us (7%)
  blocking collectives  2.47 us (1%)
    all_gather x1, waiting for transfers between devices, local(): gathered = lax.all_gather(share, ('exp', 'ffn'), axis=0, tiled=False)  37.2 us
    pallas_call x1, Pallas kernels, expert_ffn(): pl.pallas_call(expert_kernel, grid=(local_count, tiles), in_specs=[pl.Blo...  28.6 us
    reduce_scatter x1, waiting for transfers between devices, local(): moe_out = lax.psum_scatter(moe_cols, 'exp', scatter_dimension=0, tiled=True)  26.8 us
    all_gather x1, waiting for transfers between devices, local(): lax.all_gather(normed_cols, ('exp', 'ffn'), axis=0, tiled=False)  24 us
    gather x1, local copies, waits for them, and re-layouts, local(): jnp.take(flat_pages, key_rows, axis=0, mode='clip')  6.36 us
    dot_general x1, matrix products, local(): jnp.dot(combine, weighted, preferred_element_type=jnp.float32)  4.52 us
    dot_general x1, matrix products, local(): jnp.einsum('td,ts->ds', normed_all, combine, preferred_element_type=jnp.f...  4.32 us
    unnamed x24, local copies, waits for them, and re-layouts  4.27 us
  transfers between devices with their start and end apart: 5, of which 5 were waited for; matrix products, arithmetic and copies ran while one was open for 6% of the time, Pallas kernels for 0%

profile of v14, /device:TPU:0, one launch (start us, length us, event | category | flops | bytes accessed | tf_op | source)
XLA Modules:
  0.0 193.6 jit_solution(18433856126832439776)
XLA Ops:
  7.2 0.0 all-gather.5.cloned.1.call-start
  7.3 0.8 convert_element_type.98
  8.1 0.1 copy.32
  8.2 0.2 convert_element_type.99
  8.4 0.6 reshape.205
  9.0 1.1 copy.31
  10.1 0.2 reshape.204
  10.3 0.1 pad_dynamic-slice_fusion.3
  10.4 2.0 %fusion.20 = bf16[24,9216]{1,0:T(8,128)(2,1)} fusion(s32[]{:T(128)S(6)} %select_n.57, bf16[32,9216]{1,0:T(8,128)(2,1)} %param.18, bf16[8,9216]{1,0:T(8,128)(2,1)S(1)} %reshape.204, bf16[1,9216]{1,0:T(2,128)(2,1)} %reshape.205, bf16[24]{0:T(256)(128)(2,1)S(1)} %pad_dynamic-slice_fusion.3), kind=kLoop, calls=%fused_computation.38 | loop fusion | flops 1769472 | bytes 1198132 | tf_op jit(solution)/shard_map/concatenate | solution.py:125
  12.4 0.0 all-gather.5.cloned.1.call-update
  12.4 0.0 all-gather.7.cloned.1.call-start
  12.5 1.2 dynamic_slice.31
  13.8 1.2 dynamic_slice.32
  15.0 0.1 iota_add_fusion.1
  15.1 0.1 add.126
  15.2 1.0 copy.45
  16.2 0.3 copy.33
  16.5 0.7 fusion.24
  17.2 0.1 pad_add_fusion
  17.3 1.3 iota_compare_fusion.5
  18.6 1.0 and_or_fusion
  19.6 37.2 %all-gather.5.cloned.1.call-done = bf16[192,9216]{1,0:T(8,128)(2,1)} async-done(((bf16[24,9216]{1,0:T(8,128)(2,1)}), bf16[192,9216]{1,0:T(8,128)(2,1)}) %all-gather.5.cloned.1.call-update) | async-done | bytes 3538960 | tf_op jit(solution)/shard_map/all_gather | solution.py:135
  56.8 6.4 %gather_fusion = bf16[80,9216]{1,0:T(8,128)(2,1)} fusion(bf16[192,9216]{1,0:T(8,128)(2,1)} %all-gather.5.cloned.1.call-done, s32[1024]{0:T(1024)S(1)} %pad_clamp_fusion), kind=kCustom, calls=%fused_computation | custom fusion | bytes 2949440 | tf_op jit(solution)/shard_map/jit(_take)/gather | solution.py:158
  63.2 3.9 %reshape.206 = bf16[1280,576]{1,0:T(8,128)(2,1)} reshape(bf16[80,9216]{1,0:T(8,128)(2,1)} %gather_fusion) | data formatting | bytes 2949120 | tf_op jit(solution)/shard_map/reshape | solution.py:158
  67.0 2.6 %fusion.4 = f32[128,4,1280]{0,2,1:T(8,128)S(1)} fusion(bf16[128,4,576]{0,2,1:T(8,128)(2,1)S(1)} %bitcast.72, bf16[1280,576]{1,0:T(8,128)(2,1)} %reshape.206, pred[128,1280]{0,1:T(8,128)(4,1)S(1)} %and_or_fusion), kind=kOutput, calls=%fused_computation.9 | convolution fusion | flops 756285440 | bytes 4849664 | tf_op jit(solution)/shard_map/thd,kd->thk/dot_general | solution.py:163
  69.7 1.5 copy-done.2
  71.2 0.6 fusion.29
  71.8 0.4 copy-done.6
  72.2 4.2 %fusion.12 = bf16[4,128,128]{1,2,0:T(8,128)(2,1)S(1)} fusion(bf16[512,4,128]{0,2,1:T(8,128)(2,1)S(1)} %bitcast.73, bf16[1280,576]{1,0:T(8,128)(2,1)} %reshape.206, f32[128,4]{0,1:T(4,128)S(1)} %fusion.29, f32[128,4,1280]{0,2,1:T(8,128)} %copy-done.2), kind=kOutput, calls=%fused_computation.23 | convolution fusion | flops 740493056 | bytes 7211008 | tf_op jit(solution)/shard_map/thl,lhd->thd/dot_general | solution.py:179
  76.5 0.5 convolution_convert_fusion.2
  77.0 0.3 collective-permute-start
  77.3 1.3 collective-permute-done
  78.6 0.2 fusion.15
  78.8 2.5 %psum.7 = f32[128,1]{0,1:T(1,128)S(1)} all-reduce(f32[128,1]{0,1:T(1,128)S(1)} %bitcast.77), channel_id=1, replica_groups=mesh['req'=4,'exp'=4,'ffn'=2] {'ffn'}, use_global_device_ids=true, to_apply=%region_5.6 | all-reduce | flops 128 | bytes 1024 | tf_op jit(solution)/shard_map/psum | solution.py:189
  81.3 0.8 fusion.17
  82.1 0.0 all-gather.7.cloned.1.call-update
  82.2 0.0 reduce-scatter.2.cloned.1.call-start
  82.2 0.1 add.130
  82.3 0.1 add.131
  82.4 1.1 slice.15
  83.6 0.2 reshape.216
  83.8 0.3 fusion.11
  84.1 0.1 copy.40
  84.2 0.2 convert_element_type.115
  84.4 0.1 add_select_fusion
  84.6 0.1 copy.38
  84.7 1.5 fusion.1
  86.3 24.0 %all-gather.7.cloned.1.call-done = bf16[1024,1024]{1,0:T(8,128)(2,1)} async-done(((bf16[128,1024]{1,0:T(8,128)(2,1)}), bf16[1024,1024]{1,0:T(8,128)(2,1)}) %all-gather.7.cloned.1.call-update) | async-done | bytes 2097168 | tf_op jit(solution)/shard_map/all_gather | solution.py:195
  110.3 3.7 %copy.39 = bf16[4,2,128,1024]{3,1,2,0:T(2,128)(2,1)S(1)} copy(bf16[4,2,128,1024]{3,2,1,0:T(8,128)(2,1)} %bitcast.71) | data formatting | bytes 4194304 | tf_op jit(solution)/shard_map/reshape | solution.py:197
  114.0 0.6 copy.47
  114.7 0.3 copy-done.8
  114.9 0.7 fusion.30
  115.7 0.1 select_reduce_fusion.1
  115.8 1.7 select_reduce_fusion
  117.5 1.1 copy.41.scale_ref
  118.6 4.3 %convolution_convert_fusion.rows_ref = bf16[2048,1024]{1,0:T(8,128)(2,1)} fusion(bf16[512,2048]{1,0:T(8,128)(2,1)S(1)} %bitcast.68, pred[512,1024]{1,0:T(8,128)(4,1)S(1)} %fusion.1), kind=kOutput, calls=%fused_computation.5 | convolution fusion | flops 2149580800 | bytes 6815744 | tf_op jit(solution)/shard_map/td,ts->ds/dot_general | solution.py:231
  122.9 28.6 %shard_map.158 = bf16[8,128,2048]{2,1,0:T(8,128)(2,1)} custom-call(bf16[2048,1024]{1,0:T(8,128)(2,1)} %convolution_convert_fusion.rows_ref, bf16[8,704,2048]{2,1,0:T(8,128)(2,1)} %bitcast.65, bf16[8,704,2048]{2,1,0:T(8,128)(2,1)} %bitcast.66, bf16[8,704,2048]{2,1,0:T(8,128)(2,1)} %down_ref.1, f32[8,128,1]{2,1,0:T(8,128)} %copy.41.scale_ref), custom_call_target="tpu_custom_call" | custom-call | tf_op jit(solution)/shard_map/pallas_call | solution.py:45
  151.5 4.5 %convolution_convert_fusion.1 = bf16[512,2048]{1,0:T(8,128)(2,1)S(1)} fusion(pred[512,1024]{1,0:T(8,128)(4,1)S(1)} %fusion.1, bf16[1024,2048]{1,0:T(8,128)(2,1)} %bitcast.70), kind=kOutput, calls=%fused_computation.11 | convolution fusion | flops 2148532224 | bytes 6815744 | tf_op jit(solution)/shard_map/dot_general | solution.py:241
  156.0 0.1 constant_dynamic-slice_fusion
  156.1 0.3 collective-permute-start.1
  156.4 2.4 %collective-permute-done.1 = bf16[512,1024]{1,0:T(8,128)(2,1)S(1)} collective-permute-done((bf16[512,1024]{1,0:T(8,128)(2,1)S(1)}, bf16[512,1024]{1,0:T(8,128)(2,1)S(1)}, u32[]{:S(2)}, u32[]{:S(2)}) %collective-permute-start.1) | collective-permute-done | bytes 1048608 | tf_op jit(solution)/shard_map/ppermute | solution.py:65
  158.9 1.4 add_convert_fusion
  160.3 0.0 reduce-scatter.2.cloned.1.call-update
  160.3 26.8 %reduce-scatter.2.cloned.1.call-done = bf16[128,1024]{1,0:T(8,128)(2,1)} async-done(((bf16[512,1024]{1,0:T(8,128)(2,1)}), bf16[128,1024]{1,0:T(8,128)(2,1)}) %reduce-scatter.2.cloned.1.call-update) | async-done | bytes 262160 | tf_op jit(solution)/shard_map/reduce_scatter | solution.py:243
  (33 shorter events, 0.2 us)
Async XLA Ops:
  7.2 69.3 %copy-start = (bf16[512,2048]{1,0:T(8,128)(2,1)S(1)}, bf16[512,2048]{1,0:T(8,128)(2,1)}, u32[]{:S(2)}) copy-start(bf16[512,2048]{1,0:T(8,128)(2,1)} %param.24) | copy-start | bytes 6291460
  7.2 8.0 %copy-start.5 = (bf16[512,512]{1,0:T(8,128)(2,1)S(1)}, bf16[512,512]{1,0:T(8,128)(2,1)}, u32[]{:S(2)}) copy-start(bf16[512,512]{1,0:T(8,128)(2,1)} %param.23) | copy-start | bytes 1572868
  7.2 9.0 %copy-start.4 = (bf16[128,2304]{1,0:T(8,128)(2,1)S(1)}, bf16[128,2304]{1,0:T(8,128)(2,1)}, u32[]{:S(2)}) copy-start(bf16[128,2304]{1,0:T(8,128)(2,1)} %param.16) | copy-start | bytes 1769476
  7.2 49.6 %all-gather.5.cloned.1.call-start = ((), (), s32[]{:S(2)}) async-start(), calls=%async_computation.2 | async-start | bytes 3981312 | tf_op jit(solution)/shard_map/all_gather | solution.py:135
  12.4 97.8 %all-gather.7.cloned.1.call-start = ((), (), s32[]{:S(2)}) async-start(), calls=%async_computation.3 | async-start | bytes 2359296 | tf_op jit(solution)/shard_map/all_gather | solution.py:195
  69.7 1.5 copy-start.2
  71.2 1.0 copy-start.6
  76.4 0.9 copy-start.9
  76.4 2.1 %copy-start.7 = (bf16[128,2048]{1,0:T(8,128)(2,1)S(1)}, bf16[128,2048]{1,0:T(8,128)(2,1)}, u32[]{:S(2)}) copy-start(bf16[128,2048]{1,0:T(8,128)(2,1)} %param.15) | copy-start | bytes 1572868
  77.0 1.6 collective-permute-start
  78.8 35.2 %copy-start.3 = (bf16[128,1024]{1,0:T(8,128)(2,1)}, bf16[128,1024]{1,0:T(8,128)(2,1)S(1)}, u32[]{:S(2)}) copy-start(bf16[128,1024]{1,0:T(8,128)(2,1)S(1)} %get-tuple-element.3) | copy-start | bytes 786436
  82.2 104.9 %reduce-scatter.2.cloned.1.call-start = ((), (), s32[]{:S(2)}) async-start(), calls=%async_computation.1 | async-start | bytes 1310720 | tf_op jit(solution)/shard_map/reduce_scatter | solution.py:243
  114.0 0.9 copy-start.8
  156.0 31.1 %copy-start.1 = (bf16[512,2048]{1,0:T(8,128)(2,1)S(1)}, bf16[512,2048]{1,0:T(8,128)(2,1)}, u32[]{:S(2)}) copy-start(bf16[512,2048]{1,0:T(8,128)(2,1)} %param.24) | copy-start | bytes 6291460
  156.1 2.7 %collective-permute-start.1 = (bf16[512,1024]{1,0:T(8,128)(2,1)S(1)}, bf16[512,1024]{1,0:T(8,128)(2,1)S(1)}, u32[]{:S(2)}, u32[]{:S(2)}) collective-permute-start(bf16[512,1024]{1,0:T(8,128)(2,1)S(1)} %constant_dynamic-slice_fusion), channel_id=1, source_target_pairs={{0,1},{1,0},{2,3},{3,2},{4,5},{5,4},{6,7},{7,6},{8,9},{9,8},{10,11... | collective-permute-start | bytes 3145736 | tf_op jit(solution)/shard_map/ppermute | solution.py:65
Sparse Core Ops, SparseCore 0:
  12.6 44.2 all-gather.4
  82.3 27.9 all-gather.6
  160.4 26.6 reduce-scatter.1

commit v15 on v14

--- a/solution.py
+++ b/solution.py
@@ -115,47 +115,52 @@
     page_width = cache_pool.shape[1]
     latent_pages = token_rows * QKD // page_width
     route_count = token_rows * TOP
-    route_pages = -(-route_count // page_width)
+    route_width = 128
+    route_lines = -(-route_count // (route_width * 8)) * 8
     route_rows = jnp.pad(
         routes.reshape(route_count).astype(jnp.bfloat16),
-        (0, route_pages * page_width - route_count),
-    ).reshape(route_pages, page_width)
-    packed_rows = pool_pages + latent_pages + route_pages
-    share_rows = -(-packed_rows // (ffn_size * 8)) * 8
-    packed = jnp.concatenate(
+        (0, route_lines * route_width - route_count),
+    ).reshape(route_lines, route_width)
+    group_rows = exp_size * token_rows
+    routes_all = (
+        lax.all_gather(route_rows, "exp", axis=0, tiled=False)
+        .reshape(exp_size, route_lines * route_width)[:, :route_count]
+        .reshape(group_rows, TOP)
+        .astype(jnp.int32)
+    )
+    pool_share = pool_pages // ffn_size
+    latent_share = latent_pages // ffn_size
+    share = jnp.concatenate(
         [
-            cache_pool,
-            new_latent.reshape(latent_pages, page_width),
-            route_rows,
-            jnp.zeros((share_rows * ffn_size - packed_rows, page_width), jnp.bfloat16),
+            lax.dynamic_slice_in_dim(cache_pool, ffn_index * pool_share, pool_share, 0),
+            lax.dynamic_slice_in_dim(
+                new_latent.reshape(latent_pages, page_width),
+                ffn_index * latent_share,
+                latent_share,
+                0,
+            ),
         ],
         axis=0,
     )
-    share = lax.dynamic_slice_in_dim(packed, ffn_index * share_rows, share_rows, 0)
     gathered = lax.all_gather(share, ("exp", "ffn"), axis=0, tiled=False)
-    gathered = gathered.reshape(exp_size, ffn_size * share_rows, page_width)
-    stride = ffn_size * share_rows
-    group_rows = exp_size * token_rows
-    routes_all = (
-        gathered[:, pool_pages + latent_pages : packed_rows]
-        .reshape(exp_size, route_pages * page_width)[:, :route_count]
-        .reshape(group_rows, TOP)
-        .astype(jnp.int32)
-    )
-    flat_pages = gathered.reshape(exp_size * stride, page_width)
     pool_base = req_index * exp_size * pool_pages
     page_rows = page_table[request] - pool_base
-    cached_rows = (page_rows // pool_pages) * stride + page_rows % pool_pages
+    page_within = page_rows % pool_pages
+    cached_share = (page_rows // pool_pages) * ffn_size + page_within // pool_share
+    cached_row = page_within % pool_share
     local_request = request - req_index * REQ_GRP
     fresh_devices = fresh_len // token_rows
-    fresh_index = lax.broadcasted_iota(jnp.int32, (fresh_devices, latent_pages), 0)
-    fresh_rows = (
-        (local_request * fresh_devices + fresh_index) * stride
-        + pool_pages
-        + lax.broadcasted_iota(jnp.int32, (fresh_devices, latent_pages), 1)
-    ).reshape(fresh_devices * latent_pages)
-    key_rows = jnp.concatenate([cached_rows, fresh_rows], axis=0)
-    all_keys = jnp.take(flat_pages, key_rows, axis=0, mode="clip").reshape(CMAX + fresh_len, QKD)
+    fresh_device = local_request * fresh_devices + lax.broadcasted_iota(
+        jnp.int32, (fresh_devices, latent_pages), 0
+    )
+    fresh_page = lax.broadcasted_iota(jnp.int32, (fresh_devices, latent_pages), 1)
+    fresh_share = (fresh_device * ffn_size + fresh_page // latent_share).reshape(-1)
+    fresh_row = (pool_share + fresh_page % latent_share).reshape(-1)
+    key_share = jnp.concatenate([cached_share, fresh_share], axis=0)
+    key_row = jnp.concatenate([cached_row, fresh_row], axis=0)
+    all_keys = (
+        gathered.at[key_share, key_row].get(mode="clip").reshape(CMAX + fresh_len, QKD)
+    )
     heads_here = queries.shape[1] // QKD
     query_heads = queries.reshape(token_rows, heads_here, QKD)
     scale_factor = (HEAD_DIM + ROPE_DIM) ** (-0.5)

time: 194 us -> 202 us (1.041)
  blocking collectives: 2.47 us -> 14.7 us
  waiting for transfers between devices: 91.8 us -> 81.9 us
  local copies, waits for them, and re-layouts: 26.2 us -> 33.5 us
  other arithmetic: 12.7 us -> 10.5 us
    all_gather x0 -> x1, blocking collectives: none -> 12 us  [local(): lax.all_gather(route_rows, 'exp', axis=0, tiled=False)]
    all_gather x1, waiting for transfers between devices: 24 us -> 13.1 us  [local(): lax.all_gather(normed_cols, ('exp', 'ffn'), axis=0, tiled=False)]
    all_gather x0 -> x1, local copies, waits for them, and re-layouts: none -> 5.23 us  [local(): gathered = lax.all_gather(share, ('exp', 'ffn'), axis=0, tiled=False)]
    gather x1, local copies, waits for them, and re-layouts: 6.36 us -> 10.3 us  [local(): gathered.at[key_share, key_row].get(mode='clip')]
    reshape x2 -> x1, local copies, waits for them, and re-layouts: 4.5 us -> 3.88 us  [local(): gathered.at[key_share, key_row].get(mode='clip')]
    unnamed x24 -> x30, local copies, waits for them, and re-layouts: 4.27 us -> 4.4 us
  transfers between devices with their start and end apart: 5 -> 5, of which waited for: 5 -> 5; matrix products, arithmetic and copies ran while one was open for 6% -> 4% of each run, Pallas kernels for 0% -> 0%
where the time goes in v15:
time: 202 us; the launch traced here: 201 us
  waiting for transfers between devices  81.9 us (41%)
  local copies, waits for them, and re-layouts  33.5 us (17%)
  Pallas kernels  28.5 us (14%)
  matrix products  17.1 us (8%)
  blocking collectives  14.7 us (7%)
  between operations  14.1 us (7%)
  other arithmetic  10.5 us (5%)
    all_gather x1, waiting for transfers between devices, local(): gathered = lax.all_gather(share, ('exp', 'ffn'), axis=0, tiled=False)  38.3 us
    pallas_call x1, Pallas kernels, expert_ffn(): pl.pallas_call(expert_kernel, grid=(local_count, tiles), in_specs=[pl.Blo...  28.5 us
    reduce_scatter x1, waiting for transfers between devices, local(): moe_out = lax.psum_scatter(moe_cols, 'exp', scatter_dimension=0, tiled=True)  26.8 us
    all_gather x1, waiting for transfers between devices, local(): lax.all_gather(normed_cols, ('exp', 'ffn'), axis=0, tiled=False)  13.1 us
    all_gather x1, blocking collectives, local(): lax.all_gather(route_rows, 'exp', axis=0, tiled=False)  12 us
    gather x1, local copies, waits for them, and re-layouts, local(): gathered.at[key_share, key_row].get(mode='clip')  10.3 us
    all_gather x1, local copies, waits for them, and re-layouts, local(): gathered = lax.all_gather(share, ('exp', 'ffn'), axis=0, tiled=False)  5.23 us
    dot_general x1, matrix products, local(): jnp.dot(combine, weighted, preferred_element_type=jnp.float32)  4.52 us
  transfers between devices with their start and end apart: 5, of which 5 were waited for; matrix products, arithmetic and copies ran while one was open for 4% of the time, Pallas kernels for 0%

profile of v15, /device:TPU:0, one launch (start us, length us, event | category | flops | bytes accessed | tf_op | source)
XLA Modules:
  0.0 201.1 jit_solution(3648999694646165501)
XLA Ops:
  7.2 0.0 all-gather.8.cloned.1.call-start
  7.3 1.2 copy.41
  8.5 0.2 reshape.440
  8.7 1.0 constant_dynamic-slice_fusion.4
  9.7 0.8 maximum_bitcast_fusion
  10.5 0.0 all-gather.8.cloned.1.call-update
  10.5 0.0 all-gather.6.cloned.1.call-start
  10.6 0.6 dynamic_slice.34
  11.2 0.6 dynamic_slice.35
  11.8 0.1 select_add_fusion.1
  11.9 0.1 concatenate.60
  12.0 0.1 concatenate.63
  12.1 1.0 copy.55
  13.1 0.3 copy.43
  13.4 0.7 add_bitcast_fusion
  14.1 0.1 fusion.31
  14.2 1.3 iota_compare_fusion.5
  15.5 1.0 and_or_fusion
  16.6 38.3 %all-gather.8.cloned.1.call-done = bf16[8,20,9216]{2,1,0:T(8,128)(2,1)} async-done(((bf16[1,20,9216]{2,1,0:T(8,128)(2,1)}), bf16[8,20,9216]{2,1,0:T(8,128)(2,1)}) %all-gather.8.cloned.1.call-update) | async-done | bytes 2949136 | tf_op jit(solution)/shard_map/all_gather | solution.py:145
  54.9 5.2 %copy.42 = bf16[8,20,9216]{2,0,1:T(8,128)(2,1)} copy(bf16[8,20,9216]{2,1,0:T(8,128)(2,1)} %all-gather.8.cloned.1.call-done) | data formatting | bytes 5898240 | tf_op jit(solution)/shard_map/all_gather | solution.py:145
  60.2 10.3 %gather_fusion = bf16[80,9216]{1,0:T(8,128)(2,1)} fusion(bf16[8,20,9216]{2,0,1:T(8,128)(2,1)} %copy.42, s32[80]{0:T(128)S(1)} %fusion.31), kind=kCustom, calls=%fused_computation | custom fusion | bytes 2949760 | tf_op jit(solution)/shard_map/gather | solution.py:162
  70.5 3.9 %reshape.441 = bf16[1280,576]{1,0:T(8,128)(2,1)} reshape(bf16[80,9216]{1,0:T(8,128)(2,1)} %gather_fusion) | data formatting | bytes 2949120 | tf_op jit(solution)/shard_map/reshape | solution.py:162
  74.4 2.6 %fusion.4 = f32[128,4,1280]{0,2,1:T(8,128)S(1)} fusion(bf16[128,4,576]{0,2,1:T(8,128)(2,1)S(1)} %bitcast.85, bf16[1280,576]{1,0:T(8,128)(2,1)} %reshape.441, pred[128,1280]{0,1:T(8,128)(4,1)S(1)} %and_or_fusion), kind=kOutput, calls=%fused_computation.9 | convolution fusion | flops 756285440 | bytes 4849664 | tf_op jit(solution)/shard_map/thd,kd->thk/dot_general | solution.py:168
  77.0 1.5 copy-done.2
  78.5 0.6 fusion.32
  79.1 0.4 copy-done.6
  79.6 4.2 %fusion.12 = bf16[4,128,128]{1,2,0:T(8,128)(2,1)S(1)} fusion(bf16[512,4,128]{0,2,1:T(8,128)(2,1)S(1)} %bitcast.86, bf16[1280,576]{1,0:T(8,128)(2,1)} %reshape.441, f32[128,4]{0,1:T(4,128)S(1)} %fusion.32, f32[128,4,1280]{0,2,1:T(8,128)} %copy-done.2), kind=kOutput, calls=%fused_computation.23 | convolution fusion | flops 740493056 | bytes 7211008 | tf_op jit(solution)/shard_map/thl,lhd->thd/dot_general | solution.py:184
  83.8 0.5 convolution_convert_fusion.2
  84.3 0.3 collective-permute-start
  84.6 1.3 collective-permute-done
  85.9 0.2 fusion.15
  86.1 2.7 %psum.7 = f32[128,1]{0,1:T(1,128)S(1)} all-reduce(f32[128,1]{0,1:T(1,128)S(1)} %bitcast.91), channel_id=1, replica_groups=mesh['req'=4,'exp'=4,'ffn'=2] {'ffn'}, use_global_device_ids=true, to_apply=%region_5.6 | all-reduce | flops 128 | bytes 1024 | tf_op jit(solution)/shard_map/psum | solution.py:194
  88.8 0.8 fusion.17
  89.6 0.0 all-gather.6.cloned.1.call-update
  89.7 0.0 reduce-scatter.2.cloned.1.call-start
  89.7 0.1 copy.47
  89.9 0.2 convert_element_type.107
  90.0 12.0 %all_gather.17 = bf16[4,8,128]{2,1,0:T(8,128)(2,1)S(1)} all-gather(bf16[1,8,128]{2,1,0:T(8,128)(2,1)S(1)} %pad_bitcast_fusion), channel_id=1, replica_groups=mesh['req'=4,'exp'=4,'ffn'=2] {'exp'}, dimensions={0}, use_global_device_ids=true | all-gather | bytes 10240 | tf_op jit(solution)/shard_map/all_gather | solution.py:126
  102.1 0.2 reshape.450
  102.3 0.1 add.272
  102.4 0.1 add.273
  102.5 0.3 fusion.11
  102.7 0.1 copy.50
  102.9 0.2 convert_element_type.115
  103.1 0.1 add_select_fusion
  103.2 0.1 copy.48
  103.3 1.4 fusion.1
  104.7 13.1 %all-gather.6.cloned.1.call-done = bf16[1024,1024]{1,0:T(8,128)(2,1)} async-done(((bf16[128,1024]{1,0:T(8,128)(2,1)}), bf16[1024,1024]{1,0:T(8,128)(2,1)}) %all-gather.6.cloned.1.call-update) | async-done | bytes 2097168 | tf_op jit(solution)/shard_map/all_gather | solution.py:200
  117.8 3.7 %copy.49 = bf16[4,2,128,1024]{3,1,2,0:T(2,128)(2,1)S(1)} copy(bf16[4,2,128,1024]{3,2,1,0:T(8,128)(2,1)} %bitcast.84) | data formatting | bytes 4194304 | tf_op jit(solution)/shard_map/reshape | solution.py:202
  121.5 0.6 copy.57
  122.1 0.3 copy-done.8
  122.4 0.7 fusion.33
  123.2 0.1 select_reduce_fusion.1
  123.3 1.7 select_reduce_fusion
  125.0 1.1 copy.51.scale_ref
  126.1 4.3 %convolution_convert_fusion.rows_ref = bf16[2048,1024]{1,0:T(8,128)(2,1)} fusion(bf16[512,2048]{1,0:T(8,128)(2,1)S(1)} %bitcast.81, pred[512,1024]{1,0:T(8,128)(4,1)S(1)} %fusion.1), kind=kOutput, calls=%fused_computation.5 | convolution fusion | flops 2149580800 | bytes 6815744 | tf_op jit(solution)/shard_map/td,ts->ds/dot_general | solution.py:236
  130.4 28.5 %shard_map.158 = bf16[8,128,2048]{2,1,0:T(8,128)(2,1)} custom-call(bf16[2048,1024]{1,0:T(8,128)(2,1)} %convolution_convert_fusion.rows_ref, bf16[8,704,2048]{2,1,0:T(8,128)(2,1)} %bitcast.78, bf16[8,704,2048]{2,1,0:T(8,128)(2,1)} %bitcast.79, bf16[8,704,2048]{2,1,0:T(8,128)(2,1)} %down_ref.1, f32[8,128,1]{2,1,0:T(8,128)} %copy.51.scale_ref), custom_call_target="tpu_custom_call" | custom-call | tf_op jit(solution)/shard_map/pallas_call | solution.py:45
  159.0 4.5 %convolution_convert_fusion.1 = bf16[512,2048]{1,0:T(8,128)(2,1)S(1)} fusion(pred[512,1024]{1,0:T(8,128)(4,1)S(1)} %fusion.1, bf16[1024,2048]{1,0:T(8,128)(2,1)} %bitcast.83), kind=kOutput, calls=%fused_computation.11 | convolution fusion | flops 2148532224 | bytes 6815744 | tf_op jit(solution)/shard_map/dot_general | solution.py:246
  163.5 0.1 constant_dynamic-slice_fusion
  163.6 0.3 collective-permute-start.1
  163.9 2.4 %collective-permute-done.1 = bf16[512,1024]{1,0:T(8,128)(2,1)S(1)} collective-permute-done((bf16[512,1024]{1,0:T(8,128)(2,1)S(1)}, bf16[512,1024]{1,0:T(8,128)(2,1)S(1)}, u32[]{:S(2)}, u32[]{:S(2)}) %collective-permute-start.1) | collective-permute-done | bytes 1048608 | tf_op jit(solution)/shard_map/ppermute | solution.py:65
  166.3 1.4 add_convert_fusion
  167.7 0.0 reduce-scatter.2.cloned.1.call-update
  167.8 26.8 %reduce-scatter.2.cloned.1.call-done = bf16[128,1024]{1,0:T(8,128)(2,1)} async-done(((bf16[512,1024]{1,0:T(8,128)(2,1)}), bf16[128,1024]{1,0:T(8,128)(2,1)}) %reduce-scatter.2.cloned.1.call-update) | async-done | bytes 262160 | tf_op jit(solution)/shard_map/reduce_scatter | solution.py:248
  (44 shorter events, 0.3 us)
Async XLA Ops:
  7.2 76.6 %copy-start = (bf16[512,2048]{1,0:T(8,128)(2,1)S(1)}, bf16[512,2048]{1,0:T(8,128)(2,1)}, u32[]{:S(2)}) copy-start(bf16[512,2048]{1,0:T(8,128)(2,1)} %param.24) | copy-start | bytes 6291460
  7.2 3.4 %copy-start.11 = (s32[8]{0:T(128)S(1)}, s32[8]{0:T(128)}, u32[]{:S(2)}) copy-start(s32[8]{0:T(128)} %param.21) | copy-start | bytes 100
  7.2 4.0 %copy-start.12 = (s32[8]{0:T(128)S(1)}, s32[8]{0:T(128)}, u32[]{:S(2)}) copy-start(s32[8]{0:T(128)} %param.20) | copy-start | bytes 100
  7.2 4.9 %copy-start.5 = (bf16[512,512]{1,0:T(8,128)(2,1)S(1)}, bf16[512,512]{1,0:T(8,128)(2,1)}, u32[]{:S(2)}) copy-start(bf16[512,512]{1,0:T(8,128)(2,1)} %param.23) | copy-start | bytes 1572868
  7.2 5.9 %copy-start.4 = (bf16[128,2304]{1,0:T(8,128)(2,1)S(1)}, bf16[128,2304]{1,0:T(8,128)(2,1)}, u32[]{:S(2)}) copy-start(bf16[128,2304]{1,0:T(8,128)(2,1)} %param.16) | copy-start | bytes 1769476
  7.2 47.7 %all-gather.8.cloned.1.call-start = ((), (), s32[]{:S(2)}) async-start(), calls=%async_computation.3 | async-start | bytes 3981312 | tf_op jit(solution)/shard_map/all_gather | solution.py:145
  10.5 107.2 %all-gather.6.cloned.1.call-start = ((), (), s32[]{:S(2)}) async-start(), calls=%async_computation.2 | async-start | bytes 2359296 | tf_op jit(solution)/shard_map/all_gather | solution.py:200
  77.0 1.5 copy-start.2
  78.5 1.0 copy-start.6
  83.8 0.9 copy-start.10
  83.8 2.1 %copy-start.7 = (bf16[128,2048]{1,0:T(8,128)(2,1)S(1)}, bf16[128,2048]{1,0:T(8,128)(2,1)}, u32[]{:S(2)}) copy-start(bf16[128,2048]{1,0:T(8,128)(2,1)} %param.15) | copy-start | bytes 1572868
  83.8 5.9 %copy-start.9 = (s32[128,6]{0,1:T(8,128)S(1)}, s32[128,6]{0,1:T(8,128)}, u32[]{:S(2)}) copy-start(s32[128,6]{0,1:T(8,128)} %param.22) | copy-start | bytes 9220
  84.3 1.6 collective-permute-start
  86.1 35.4 %copy-start.3 = (bf16[128,1024]{1,0:T(8,128)(2,1)}, bf16[128,1024]{1,0:T(8,128)(2,1)S(1)}, u32[]{:S(2)}) copy-start(bf16[128,1024]{1,0:T(8,128)(2,1)S(1)} %get-tuple-element.3) | copy-start | bytes 786436
  89.7 104.9 %reduce-scatter.2.cloned.1.call-start = ((), (), s32[]{:S(2)}) async-start(), calls=%async_computation.1 | async-start | bytes 1310720 | tf_op jit(solution)/shard_map/reduce_scatter | solution.py:248
  121.5 0.9 copy-start.8
  163.5 31.1 %copy-start.1 = (bf16[512,2048]{1,0:T(8,128)(2,1)S(1)}, bf16[512,2048]{1,0:T(8,128)(2,1)}, u32[]{:S(2)}) copy-start(bf16[512,2048]{1,0:T(8,128)(2,1)} %param.24) | copy-start | bytes 6291460
  163.6 2.7 %collective-permute-start.1 = (bf16[512,1024]{1,0:T(8,128)(2,1)S(1)}, bf16[512,1024]{1,0:T(8,128)(2,1)S(1)}, u32[]{:S(2)}, u32[]{:S(2)}) collective-permute-start(bf16[512,1024]{1,0:T(8,128)(2,1)S(1)} %constant_dynamic-slice_fusion), channel_id=1, source_target_pairs={{0,1},{1,0},{2,3},{3,2},{4,5},{5,4},{6,7},{7,6},{8,9},{9,8},{10,11... | collective-permute-start | bytes 3145736 | tf_op jit(solution)/shard_map/ppermute | solution.py:65
Sparse Core Ops, SparseCore 0:
  10.7 44.2 all-gather.7
  89.8 27.9 all-gather.5
  167.9 26.6 reduce-scatter.1

commit v16 on v14

--- a/solution.py
+++ b/solution.py
@@ -186,7 +186,11 @@
     residual_cols = lax.dynamic_slice_in_dim(residual, ffn_index * column_count, column_count, 1)
     hidden_out = (residual_cols.astype(jnp.float32) + attn_cols).astype(jnp.bfloat16)
     hidden_wide = hidden_out.astype(jnp.float32)
-    square_sum = lax.psum(jnp.sum(hidden_wide * hidden_wide, axis=1, keepdims=True), "ffn")
+    square_part = jnp.sum(hidden_wide * hidden_wide, axis=1, keepdims=True)
+    if ffn_size == 2:
+        square_sum = square_part + pair_swap(square_part)
+    else:
+        square_sum = lax.psum(square_part, "ffn")
     mean_square = square_sum / feature_count
     gain_cols = lax.dynamic_slice_in_dim(norm_gain, ffn_index * column_count, column_count, 0)
     normed_cols = (

time: 194 us -> 193 us (level)
  blocking collectives: 2.47 us -> 0 us
    psum x1 -> x0, blocking collectives: 2.47 us -> none  [local(): lax.psum(jnp.sum(hidden_wide * hidden_wide, axis=1, keepdims=True), 'ffn')]
    ppermute x2 -> x3, waiting for transfers between devices: 3.73 us -> 4.6 us  [pair_swap(): return lax.ppermute(x, 'ffn', [(0, 1), (1, 0)])]
  transfers between devices with their start and end apart: 5 -> 6, of which waited for: 5 -> 6; matrix products, arithmetic and copies ran while one was open for 6% -> 6% of each run, Pallas kernels for 0% -> 0%
where the time goes in v16:
time: 193 us; the launch traced here: 192 us
  waiting for transfers between devices  92.6 us (48%)
  Pallas kernels  28.6 us (15%)
  local copies, waits for them, and re-layouts  26.2 us (14%)
  matrix products  17.2 us (9%)
  between operations  14.1 us (7%)
  other arithmetic  12.7 us (7%)
    all_gather x1, waiting for transfers between devices, local(): gathered = lax.all_gather(share, ('exp', 'ffn'), axis=0, tiled=False)  37.2 us
    pallas_call x1, Pallas kernels, expert_ffn(): pl.pallas_call(expert_kernel, grid=(local_count, tiles), in_specs=[pl.Blo...  28.6 us
    reduce_scatter x1, waiting for transfers between devices, local(): moe_out = lax.psum_scatter(moe_cols, 'exp', scatter_dimension=0, tiled=True)  26.8 us
    all_gather x1, waiting for transfers between devices, local(): lax.all_gather(normed_cols, ('exp', 'ffn'), axis=0, tiled=False)  24 us
    gather x1, local copies, waits for them, and re-layouts, local(): jnp.take(flat_pages, key_rows, axis=0, mode='clip')  6.36 us
    ppermute x3, waiting for transfers between devices, pair_swap(): return lax.ppermute(x, 'ffn', [(0, 1), (1, 0)])  4.6 us
    dot_general x1, matrix products, local(): jnp.dot(combine, weighted, preferred_element_type=jnp.float32)  4.52 us
    dot_general x1, matrix products, local(): jnp.einsum('td,ts->ds', normed_all, combine, preferred_element_type=jnp.f...  4.32 us
  transfers between devices with their start and end apart: 6, of which 6 were waited for; matrix products, arithmetic and copies ran while one was open for 6% of the time, Pallas kernels for 0%

profile of v16, /device:TPU:0, one launch (start us, length us, event | category | flops | bytes accessed | tf_op | source)
XLA Modules:
  0.0 192.3 jit_solution(6164431424483624409)
XLA Ops:
  7.2 0.0 all-gather.5.cloned.1.call-start
  7.3 0.8 convert_element_type.98
  8.1 0.1 copy.32
  8.2 0.2 convert_element_type.99
  8.4 0.6 reshape.205
  9.0 1.1 copy.31
  10.1 0.2 reshape.204
  10.3 0.1 pad_dynamic-slice_fusion.3
  10.4 2.0 %fusion.20 = bf16[24,9216]{1,0:T(8,128)(2,1)} fusion(s32[]{:T(128)S(6)} %select_n.57, bf16[32,9216]{1,0:T(8,128)(2,1)} %param.18, bf16[8,9216]{1,0:T(8,128)(2,1)S(1)} %reshape.204, bf16[1,9216]{1,0:T(2,128)(2,1)} %reshape.205, bf16[24]{0:T(256)(128)(2,1)S(1)} %pad_dynamic-slice_fusion.3), kind=kLoop, calls=%fused_computation.38 | loop fusion | flops 1769472 | bytes 1198132 | tf_op jit(solution)/shard_map/concatenate | solution.py:125
  12.4 0.0 all-gather.5.cloned.1.call-update
  12.4 0.0 all-gather.7.cloned.1.call-start
  12.5 1.2 dynamic_slice.31
  13.8 1.2 dynamic_slice.32
  15.0 0.1 iota_add_fusion.1
  15.1 0.1 add.127
  15.2 1.0 copy.45
  16.2 0.3 copy.33
  16.5 0.7 fusion.24
  17.2 0.1 pad_add_fusion
  17.3 1.3 iota_compare_fusion.5
  18.6 1.0 and_or_fusion
  19.6 37.2 %all-gather.5.cloned.1.call-done = bf16[192,9216]{1,0:T(8,128)(2,1)} async-done(((bf16[24,9216]{1,0:T(8,128)(2,1)}), bf16[192,9216]{1,0:T(8,128)(2,1)}) %all-gather.5.cloned.1.call-update) | async-done | bytes 3538960 | tf_op jit(solution)/shard_map/all_gather | solution.py:135
  56.8 6.4 %gather_fusion = bf16[80,9216]{1,0:T(8,128)(2,1)} fusion(bf16[192,9216]{1,0:T(8,128)(2,1)} %all-gather.5.cloned.1.call-done, s32[1024]{0:T(1024)S(1)} %pad_clamp_fusion), kind=kCustom, calls=%fused_computation | custom fusion | bytes 2949440 | tf_op jit(solution)/shard_map/jit(_take)/gather | solution.py:158
  63.2 3.9 %reshape.206 = bf16[1280,576]{1,0:T(8,128)(2,1)} reshape(bf16[80,9216]{1,0:T(8,128)(2,1)} %gather_fusion) | data formatting | bytes 2949120 | tf_op jit(solution)/shard_map/reshape | solution.py:158
  67.0 2.6 %fusion.4 = f32[128,4,1280]{0,2,1:T(8,128)S(1)} fusion(bf16[128,4,576]{0,2,1:T(8,128)(2,1)S(1)} %bitcast.73, bf16[1280,576]{1,0:T(8,128)(2,1)} %reshape.206, pred[128,1280]{0,1:T(8,128)(4,1)S(1)} %and_or_fusion), kind=kOutput, calls=%fused_computation.9 | convolution fusion | flops 756285440 | bytes 4849664 | tf_op jit(solution)/shard_map/thd,kd->thk/dot_general | solution.py:163
  69.7 1.5 copy-done.2
  71.2 0.6 fusion.29
  71.8 0.4 copy-done.6
  72.2 4.2 %fusion.12 = bf16[4,128,128]{1,2,0:T(8,128)(2,1)S(1)} fusion(bf16[512,4,128]{0,2,1:T(8,128)(2,1)S(1)} %bitcast.74, bf16[1280,576]{1,0:T(8,128)(2,1)} %reshape.206, f32[128,4]{0,1:T(4,128)S(1)} %fusion.29, f32[128,4,1280]{0,2,1:T(8,128)} %copy-done.2), kind=kOutput, calls=%fused_computation.23 | convolution fusion | flops 740493056 | bytes 7211008 | tf_op jit(solution)/shard_map/thl,lhd->thd/dot_general | solution.py:179
  76.5 0.5 convolution_convert_fusion.2
  77.0 0.3 collective-permute-start
  77.3 1.3 collective-permute-done
  78.6 0.2 fusion.15
  78.8 0.3 collective-permute-start.1
  79.1 0.9 collective-permute-done.1
  80.0 0.8 fusion.17
  80.8 0.0 all-gather.7.cloned.1.call-update
  80.9 0.0 reduce-scatter.2.cloned.1.call-start
  80.9 0.1 add.131
  81.0 0.1 add.132
  81.1 1.1 slice.15
  82.3 0.2 reshape.216
  82.5 0.3 fusion.11
  82.8 0.1 copy.40
  82.9 0.2 convert_element_type.115
  83.2 0.1 add_select_fusion
  83.3 0.1 copy.38
  83.4 1.5 fusion.1
  85.0 24.0 %all-gather.7.cloned.1.call-done = bf16[1024,1024]{1,0:T(8,128)(2,1)} async-done(((bf16[128,1024]{1,0:T(8,128)(2,1)}), bf16[1024,1024]{1,0:T(8,128)(2,1)}) %all-gather.7.cloned.1.call-update) | async-done | bytes 2097168 | tf_op jit(solution)/shard_map/all_gather | solution.py:199
  109.0 3.7 %copy.39 = bf16[4,2,128,1024]{3,1,2,0:T(2,128)(2,1)S(1)} copy(bf16[4,2,128,1024]{3,2,1,0:T(8,128)(2,1)} %bitcast.72) | data formatting | bytes 4194304 | tf_op jit(solution)/shard_map/reshape | solution.py:201
  112.8 0.6 copy.47
  113.4 0.3 copy-done.8
  113.7 0.7 fusion.30
  114.4 0.1 select_reduce_fusion.1
  114.5 1.7 select_reduce_fusion
  116.2 1.1 copy.41.scale_ref
  117.3 4.3 %convolution_convert_fusion.rows_ref = bf16[2048,1024]{1,0:T(8,128)(2,1)} fusion(bf16[512,2048]{1,0:T(8,128)(2,1)S(1)} %bitcast.69, pred[512,1024]{1,0:T(8,128)(4,1)S(1)} %fusion.1), kind=kOutput, calls=%fused_computation.5 | convolution fusion | flops 2149580800 | bytes 6815744 | tf_op jit(solution)/shard_map/td,ts->ds/dot_general | solution.py:235
  121.7 28.6 %shard_map.158 = bf16[8,128,2048]{2,1,0:T(8,128)(2,1)} custom-call(bf16[2048,1024]{1,0:T(8,128)(2,1)} %convolution_convert_fusion.rows_ref, bf16[8,704,2048]{2,1,0:T(8,128)(2,1)} %bitcast.66, bf16[8,704,2048]{2,1,0:T(8,128)(2,1)} %bitcast.67, bf16[8,704,2048]{2,1,0:T(8,128)(2,1)} %down_ref.1, f32[8,128,1]{2,1,0:T(8,128)} %copy.41.scale_ref), custom_call_target="tpu_custom_call" | custom-call | tf_op jit(solution)/shard_map/pallas_call | solution.py:45
  150.2 4.5 %convolution_convert_fusion.1 = bf16[512,2048]{1,0:T(8,128)(2,1)S(1)} fusion(pred[512,1024]{1,0:T(8,128)(4,1)S(1)} %fusion.1, bf16[1024,2048]{1,0:T(8,128)(2,1)} %bitcast.71), kind=kOutput, calls=%fused_computation.11 | convolution fusion | flops 2148532224 | bytes 6815744 | tf_op jit(solution)/shard_map/dot_general | solution.py:245
  154.7 0.1 constant_dynamic-slice_fusion
  154.8 0.3 collective-permute-start.2
  155.2 2.4 %collective-permute-done.2 = bf16[512,1024]{1,0:T(8,128)(2,1)S(1)} collective-permute-done((bf16[512,1024]{1,0:T(8,128)(2,1)S(1)}, bf16[512,1024]{1,0:T(8,128)(2,1)S(1)}, u32[]{:S(2)}, u32[]{:S(2)}) %collective-permute-start.2) | collective-permute-done | bytes 1048608 | tf_op jit(solution)/shard_map/ppermute | solution.py:65
  157.6 1.4 add_convert_fusion
  159.0 26.8 %reduce-scatter.2.cloned.1.call-done = bf16[128,1024]{1,0:T(8,128)(2,1)} async-done(((bf16[512,1024]{1,0:T(8,128)(2,1)}), bf16[128,1024]{1,0:T(8,128)(2,1)}) %reduce-scatter.2.cloned.1.call-update) | async-done | bytes 262160 | tf_op jit(solution)/shard_map/reduce_scatter | solution.py:247
  (34 shorter events, 0.2 us)
Async XLA Ops:
  7.2 69.3 %copy-start = (bf16[512,2048]{1,0:T(8,128)(2,1)S(1)}, bf16[512,2048]{1,0:T(8,128)(2,1)}, u32[]{:S(2)}) copy-start(bf16[512,2048]{1,0:T(8,128)(2,1)} %param.24) | copy-start | bytes 6291460
  7.2 8.0 %copy-start.5 = (bf16[512,512]{1,0:T(8,128)(2,1)S(1)}, bf16[512,512]{1,0:T(8,128)(2,1)}, u32[]{:S(2)}) copy-start(bf16[512,512]{1,0:T(8,128)(2,1)} %param.23) | copy-start | bytes 1572868
  7.2 9.0 %copy-start.4 = (bf16[128,2304]{1,0:T(8,128)(2,1)S(1)}, bf16[128,2304]{1,0:T(8,128)(2,1)}, u32[]{:S(2)}) copy-start(bf16[128,2304]{1,0:T(8,128)(2,1)} %param.16) | copy-start | bytes 1769476
  7.2 49.6 %all-gather.5.cloned.1.call-start = ((), (), s32[]{:S(2)}) async-start(), calls=%async_computation.2 | async-start | bytes 3981312 | tf_op jit(solution)/shard_map/all_gather | solution.py:135
  12.4 96.6 %all-gather.7.cloned.1.call-start = ((), (), s32[]{:S(2)}) async-start(), calls=%async_computation.3 | async-start | bytes 2359296 | tf_op jit(solution)/shard_map/all_gather | solution.py:199
  69.7 1.5 copy-start.2
  71.2 1.0 copy-start.6
  76.4 2.2 %copy-start.7 = (bf16[128,2048]{1,0:T(8,128)(2,1)S(1)}, bf16[128,2048]{1,0:T(8,128)(2,1)}, u32[]{:S(2)}) copy-start(bf16[128,2048]{1,0:T(8,128)(2,1)} %param.15) | copy-start | bytes 1572868
  76.4 2.7 %copy-start.9 = (bf16[2048]{0:T(1024)(128)(2,1)S(1)}, bf16[2048]{0:T(1024)(128)(2,1)}, u32[]{:S(2)}) copy-start(bf16[2048]{0:T(1024)(128)(2,1)} %param.25) | copy-start | bytes 12292
  77.0 1.6 collective-permute-start
  78.8 33.9 %copy-start.3 = (bf16[128,1024]{1,0:T(8,128)(2,1)}, bf16[128,1024]{1,0:T(8,128)(2,1)S(1)}, u32[]{:S(2)}) copy-start(bf16[128,1024]{1,0:T(8,128)(2,1)S(1)} %get-tuple-element.3) | copy-start | bytes 786436
  78.8 1.2 collective-permute-start.1
  80.9 104.9 %reduce-scatter.2.cloned.1.call-start = ((), (), s32[]{:S(2)}) async-start(), calls=%async_computation.1 | async-start | bytes 1310720 | tf_op jit(solution)/shard_map/reduce_scatter | solution.py:247
  112.8 0.9 copy-start.8
  154.7 31.1 %copy-start.1 = (bf16[512,2048]{1,0:T(8,128)(2,1)S(1)}, bf16[512,2048]{1,0:T(8,128)(2,1)}, u32[]{:S(2)}) copy-start(bf16[512,2048]{1,0:T(8,128)(2,1)} %param.24) | copy-start | bytes 6291460
  154.8 2.7 %collective-permute-start.2 = (bf16[512,1024]{1,0:T(8,128)(2,1)S(1)}, bf16[512,1024]{1,0:T(8,128)(2,1)S(1)}, u32[]{:S(2)}, u32[]{:S(2)}) collective-permute-start(bf16[512,1024]{1,0:T(8,128)(2,1)S(1)} %constant_dynamic-slice_fusion), channel_id=1, source_target_pairs={{0,1},{1,0},{2,3},{3,2},{4,5},{5,4},{6,7},{7,6},{8,9},{9,8},{10,11... | collective-permute-start | bytes 3145736 | tf_op jit(solution)/shard_map/ppermute | solution.py:65
Sparse Core Ops, SparseCore 0:
  12.6 44.2 all-gather.4
  81.0 27.9 all-gather.6
  159.1 26.6 reduce-scatter.1

commit v17 on v16

--- a/solution.py
+++ b/solution.py
@@ -196,12 +196,8 @@
     normed_cols = (
         hidden_wide * lax.rsqrt(mean_square + EPSILON) * gain_cols.astype(jnp.float32)
     ).astype(jnp.bfloat16)
-    normed_grid = lax.all_gather(normed_cols, ("exp", "ffn"), axis=0, tiled=False)
-    normed_all = (
-        normed_grid.reshape(exp_size, ffn_size, token_rows, column_count)
-        .transpose(0, 2, 1, 3)
-        .reshape(group_rows, feature_count)
-    )
+    normed_grid = lax.all_gather(normed_cols, ("ffn", "exp"), axis=0, tiled=False)
+    normed_grid = normed_grid.reshape(ffn_size, group_rows, column_count)
 
     expert_ids = lax.broadcasted_iota(jnp.int32, (1, 1, EXPERTS), 2)
     route_hot = routes_all[:, :, None] == expert_ids
@@ -223,7 +219,11 @@
     is_local = (local_expert >= 0) & (local_expert < local_count)
     target = jnp.where(is_local, local_expert * slot_count + slot_index, -1)
 
-    logits = jnp.dot(normed_all, router, preferred_element_type=jnp.float32)
+    router_parts = router.reshape(ffn_size, column_count, EXPERTS)
+    logits = sum(
+        jnp.dot(normed_grid[part], router_parts[part], preferred_element_type=jnp.float32)
+        for part in range(ffn_size)
+    )
     chosen = jnp.sum(jnp.where(route_hot, logits[:, None, :], 0.0), axis=2)
     raised = jnp.exp(chosen)
     gate_weights = raised / jnp.sum(raised, axis=1, keepdims=True)
@@ -233,8 +233,8 @@
     combine = jnp.any(slot_hit, axis=1).astype(jnp.bfloat16)
     slot_weight = jnp.sum(jnp.where(slot_hit, gate_weights[:, :, None], 0.0), axis=(0, 1))
     grouped_t = jnp.einsum(
-        "td,ts->ds", normed_all, combine, preferred_element_type=jnp.float32
-    ).astype(jnp.bfloat16)
+        "ftc,ts->fcs", normed_grid, combine, preferred_element_type=jnp.float32
+    ).astype(jnp.bfloat16).reshape(feature_count, total_slots)
     weighted = expert_ffn(
         grouped_t,
         gate_weight,

time: 193 us -> 192 us (level)
  local copies, waits for them, and re-layouts: 26.2 us -> 21.5 us
  matrix products: 17.2 us -> 21.3 us
    dot_general x2 -> x3, matrix products: 5.04 us -> 9.18 us  [the longest x1 5.91 us: local(): jnp.einsum('ftc,ts->fcs', normed_grid, combine, preferred_element_type=jn...]
    reshape x1 -> x0, local copies, waits for them, and re-layouts: 3.75 us -> none  [local(): normed_grid.reshape(exp_size, ffn_size, token_rows, column_count)]
    unnamed x24 -> x23, local copies, waits for them, and re-layouts: 4.27 us -> 3.39 us
where the time goes in v17:
time: 192 us
  waiting for transfers between devices  92.7 us (48%)
  Pallas kernels  28.6 us (15%)
  local copies, waits for them, and re-layouts  21.5 us (11%)
  matrix products  21.3 us (11%)
  between operations  14.1 us (7%)
  other arithmetic  12.5 us (7%)
    all_gather x1, waiting for transfers between devices, local(): gathered = lax.all_gather(share, ('exp', 'ffn'), axis=0, tiled=False)  37.2 us
    pallas_call x1, Pallas kernels, expert_ffn(): pl.pallas_call(expert_kernel, grid=(local_count, tiles), in_specs=[pl.Blo...  28.6 us
    reduce_scatter x1, waiting for transfers between devices, local(): moe_out = lax.psum_scatter(moe_cols, 'exp', scatter_dimension=0, tiled=True)  26.8 us
    all_gather x1, waiting for transfers between devices, local(): lax.all_gather(normed_cols, ('ffn', 'exp'), axis=0, tiled=False)  24 us
    gather x1, local copies, waits for them, and re-layouts, local(): jnp.take(flat_pages, key_rows, axis=0, mode='clip')  6.36 us
    dot_general x1, matrix products, local(): jnp.einsum('ftc,ts->fcs', normed_grid, combine, preferred_element_type=jn...  5.91 us
    ppermute x3, waiting for transfers between devices, pair_swap(): return lax.ppermute(x, 'ffn', [(0, 1), (1, 0)])  4.62 us
    dot_general x1, matrix products, local(): jnp.dot(combine, weighted, preferred_element_type=jnp.float32)  4.52 us
  transfers between devices with their start and end apart: 6, of which 6 were waited for; matrix products, arithmetic and copies ran while one was open for 6% of the time, Pallas kernels for 0%

profile of v17, /device:TPU:0, one launch (start us, length us, event | category | flops | bytes accessed | tf_op | source)
XLA Modules:
  0.0 191.8 jit_solution(12529258322684605991)
XLA Ops:
  7.2 0.0 all-gather.5.cloned.1.call-start
  7.3 0.8 convert_element_type.98
  8.1 0.1 copy.33
  8.2 0.2 convert_element_type.99
  8.4 0.6 reshape.214
  9.0 1.1 copy.32
  10.1 0.2 reshape.213
  10.3 0.1 pad_dynamic-slice_fusion.3
  10.4 2.0 %fusion.24 = bf16[24,9216]{1,0:T(8,128)(2,1)} fusion(s32[]{:T(128)S(6)} %select_n.57, bf16[32,9216]{1,0:T(8,128)(2,1)} %param.18, bf16[8,9216]{1,0:T(8,128)(2,1)S(1)} %reshape.213, bf16[1,9216]{1,0:T(2,128)(2,1)} %reshape.214, bf16[24]{0:T(256)(128)(2,1)S(1)} %pad_dynamic-slice_fusion.3), kind=kLoop, calls=%fused_computation.43 | loop fusion | flops 1769472 | bytes 1198132 | tf_op jit(solution)/shard_map/concatenate | solution.py:125
  12.4 0.0 all-gather.5.cloned.1.call-update
  12.4 0.0 all-gather.7.cloned.1.call-start
  12.5 1.2 dynamic_slice.31
  13.8 1.2 dynamic_slice.32
  15.0 0.1 iota_add_fusion.1
  15.1 0.1 add.130
  15.2 1.0 copy.47
  16.2 0.3 copy.34
  16.5 0.7 fusion.30
  17.2 0.1 pad_add_fusion
  17.3 1.3 iota_compare_fusion.5
  18.6 1.0 and_or_fusion
  19.6 37.2 %all-gather.5.cloned.1.call-done = bf16[192,9216]{1,0:T(8,128)(2,1)} async-done(((bf16[24,9216]{1,0:T(8,128)(2,1)}), bf16[192,9216]{1,0:T(8,128)(2,1)}) %all-gather.5.cloned.1.call-update) | async-done | bytes 3538960 | tf_op jit(solution)/shard_map/all_gather | solution.py:135
  56.8 6.4 %gather_fusion = bf16[80,9216]{1,0:T(8,128)(2,1)} fusion(bf16[192,9216]{1,0:T(8,128)(2,1)} %all-gather.5.cloned.1.call-done, s32[1024]{0:T(1024)S(1)} %pad_clamp_fusion), kind=kCustom, calls=%fused_computation | custom fusion | bytes 2949440 | tf_op jit(solution)/shard_map/jit(_take)/gather | solution.py:158
  63.2 3.9 %reshape.215 = bf16[1280,576]{1,0:T(8,128)(2,1)} reshape(bf16[80,9216]{1,0:T(8,128)(2,1)} %gather_fusion) | data formatting | bytes 2949120 | tf_op jit(solution)/shard_map/reshape | solution.py:158
  67.0 2.6 %fusion.4 = f32[128,4,1280]{0,2,1:T(8,128)S(1)} fusion(bf16[128,4,576]{0,2,1:T(8,128)(2,1)S(1)} %bitcast.67, bf16[1280,576]{1,0:T(8,128)(2,1)} %reshape.215, pred[128,1280]{0,1:T(8,128)(4,1)S(1)} %and_or_fusion), kind=kOutput, calls=%fused_computation.8 | convolution fusion | flops 756285440 | bytes 4849664 | tf_op jit(solution)/shard_map/thd,kd->thk/dot_general | solution.py:163
  69.7 1.5 copy-done.2
  71.2 0.6 fusion.35
  71.8 0.4 copy-done.6
  72.2 4.2 %fusion.13 = bf16[4,128,128]{1,2,0:T(8,128)(2,1)S(1)} fusion(bf16[512,4,128]{0,2,1:T(8,128)(2,1)S(1)} %bitcast.68, bf16[1280,576]{1,0:T(8,128)(2,1)} %reshape.215, f32[128,4]{0,1:T(4,128)S(1)} %fusion.35, f32[128,4,1280]{0,2,1:T(8,128)} %copy-done.2), kind=kOutput, calls=%fused_computation.24 | convolution fusion | flops 740493056 | bytes 7211008 | tf_op jit(solution)/shard_map/thl,lhd->thd/dot_general | solution.py:179
  76.5 0.5 convolution_convert_fusion.2
  77.0 0.3 collective-permute-start
  77.3 1.3 collective-permute-done
  78.6 0.2 fusion.19
  78.8 0.3 collective-permute-start.1
  79.1 0.9 collective-permute-done.1
  80.0 0.8 fusion.21
  80.8 0.0 all-gather.7.cloned.1.call-update
  80.9 0.2 reduce-scatter.2.cloned.1.call-start
  81.1 0.1 add.134
  81.2 0.1 add.135
  81.3 1.1 slice.37
  82.5 0.2 reshape.225
  82.7 0.3 fusion.12
  83.0 0.1 copy.41
  83.1 0.2 convert_element_type.115
  83.3 0.1 add_select_fusion
  83.5 0.1 copy.39
  83.6 1.4 fusion.1
  85.0 24.0 %all-gather.7.cloned.1.call-done = bf16[1024,1024]{1,0:T(8,128)(2,1)} async-done(((bf16[128,1024]{1,0:T(8,128)(2,1)}), bf16[1024,1024]{1,0:T(8,128)(2,1)}) %all-gather.7.cloned.1.call-update) | async-done | bytes 2097168 | tf_op jit(solution)/shard_map/all_gather | solution.py:199
  109.0 1.6 fusion.15
  110.6 0.0 copy-done.3
  110.6 1.6 convolution_add_fusion
  112.3 0.1 select_reduce_fusion.1
  112.4 1.7 select_reduce_fusion
  114.2 1.1 copy.42.scale_ref
  115.2 5.9 %convolution_convert_fusion.1 = bf16[2,1024,1024]{2,1,0:T(8,128)(2,1)} fusion(bf16[2,512,1024]{2,1,0:T(8,128)(2,1)} %bitcast.73, pred[512,1024]{1,0:T(8,128)(4,1)S(1)} %fusion.1), kind=kOutput, calls=%fused_computation.11 | convolution fusion | flops 2149580800 | bytes 6815744 | tf_op jit(solution)/shard_map/ftc,ts->fcs/dot_general | solution.py:235
  121.1 28.6 %shard_map.158 = bf16[8,128,2048]{2,1,0:T(8,128)(2,1)} custom-call(bf16[2048,1024]{1,0:T(8,128)(2,1)} %bitcast.66, bf16[8,704,2048]{2,1,0:T(8,128)(2,1)} %bitcast.63, bf16[8,704,2048]{2,1,0:T(8,128)(2,1)} %bitcast.64, bf16[8,704,2048]{2,1,0:T(8,128)(2,1)} %down_ref.1, f32[8,128,1]{2,1,0:T(8,128)} %copy.42.scale_ref), custom_call_target="tpu_custom_call" | custom-call | tf_op jit(solution)/shard_map/pallas_call | solution.py:45
  149.7 4.5 %convolution_convert_fusion = bf16[512,2048]{1,0:T(8,128)(2,1)S(1)} fusion(pred[512,1024]{1,0:T(8,128)(4,1)S(1)} %fusion.1, bf16[1024,2048]{1,0:T(8,128)(2,1)} %bitcast.65), kind=kOutput, calls=%fused_computation.10 | convolution fusion | flops 2148532224 | bytes 6815744 | tf_op jit(solution)/shard_map/dot_general | solution.py:245
  154.2 0.1 constant_dynamic-slice_fusion
  154.3 0.3 collective-permute-start.2
  154.6 2.4 %collective-permute-done.2 = bf16[512,1024]{1,0:T(8,128)(2,1)S(1)} collective-permute-done((bf16[512,1024]{1,0:T(8,128)(2,1)S(1)}, bf16[512,1024]{1,0:T(8,128)(2,1)S(1)}, u32[]{:S(2)}, u32[]{:S(2)}) %collective-permute-start.2) | collective-permute-done | bytes 1048608 | tf_op jit(solution)/shard_map/ppermute | solution.py:65
  157.1 1.4 add_convert_fusion
  158.5 0.0 reduce-scatter.2.cloned.1.call-update
  158.5 26.8 %reduce-scatter.2.cloned.1.call-done = bf16[128,1024]{1,0:T(8,128)(2,1)} async-done(((bf16[512,1024]{1,0:T(8,128)(2,1)}), bf16[128,1024]{1,0:T(8,128)(2,1)}) %reduce-scatter.2.cloned.1.call-update) | async-done | bytes 262160 | tf_op jit(solution)/shard_map/reduce_scatter | solution.py:247
  (33 shorter events, 0.2 us)
Async XLA Ops:
  7.2 69.3 %copy-start = (bf16[512,2048]{1,0:T(8,128)(2,1)S(1)}, bf16[512,2048]{1,0:T(8,128)(2,1)}, u32[]{:S(2)}) copy-start(bf16[512,2048]{1,0:T(8,128)(2,1)} %param.24) | copy-start | bytes 6291460
  7.2 8.0 %copy-start.5 = (bf16[512,512]{1,0:T(8,128)(2,1)S(1)}, bf16[512,512]{1,0:T(8,128)(2,1)}, u32[]{:S(2)}) copy-start(bf16[512,512]{1,0:T(8,128)(2,1)} %param.23) | copy-start | bytes 1572868
  7.2 9.0 %copy-start.4 = (bf16[128,2304]{1,0:T(8,128)(2,1)S(1)}, bf16[128,2304]{1,0:T(8,128)(2,1)}, u32[]{:S(2)}) copy-start(bf16[128,2304]{1,0:T(8,128)(2,1)} %param.16) | copy-start | bytes 1769476
  7.2 49.6 %all-gather.5.cloned.1.call-start = ((), (), s32[]{:S(2)}) async-start(), calls=%async_computation.2 | async-start | bytes 3981312 | tf_op jit(solution)/shard_map/all_gather | solution.py:135
  12.4 96.6 %all-gather.7.cloned.1.call-start = ((), (), s32[]{:S(2)}) async-start(), calls=%async_computation.3 | async-start | bytes 2359296 | tf_op jit(solution)/shard_map/all_gather | solution.py:199
  69.7 1.5 copy-start.2
  71.2 1.0 copy-start.6
  76.4 2.2 %copy-start.7 = (bf16[128,2048]{1,0:T(8,128)(2,1)S(1)}, bf16[128,2048]{1,0:T(8,128)(2,1)}, u32[]{:S(2)}) copy-start(bf16[128,2048]{1,0:T(8,128)(2,1)} %param.15) | copy-start | bytes 1572868
  76.4 2.7 %copy-start.8 = (bf16[2048]{0:T(1024)(128)(2,1)S(1)}, bf16[2048]{0:T(1024)(128)(2,1)}, u32[]{:S(2)}) copy-start(bf16[2048]{0:T(1024)(128)(2,1)} %param.25) | copy-start | bytes 12292
  77.0 1.6 collective-permute-start
  77.3 31.7 %copy-start.9 = (bf16[2048,32]{0,1:T(8,128)(2,1)S(1)}, bf16[2048,32]{0,1:T(8,128)(2,1)}, u32[]{:S(2)}) copy-start(bf16[2048,32]{0,1:T(8,128)(2,1)} %param.26) | copy-start | bytes 393220
  78.8 31.8 %copy-start.3 = (bf16[128,1024]{1,0:T(8,128)(2,1)}, bf16[128,1024]{1,0:T(8,128)(2,1)S(1)}, u32[]{:S(2)}) copy-start(bf16[128,1024]{1,0:T(8,128)(2,1)S(1)} %get-tuple-element.3) | copy-start | bytes 786436
  78.8 1.2 collective-permute-start.1
  80.9 104.4 %reduce-scatter.2.cloned.1.call-start = ((), (), s32[]{:S(2)}) async-start(), calls=%async_computation.1 | async-start | bytes 1310720 | tf_op jit(solution)/shard_map/reduce_scatter | solution.py:247
  154.2 31.1 %copy-start.1 = (bf16[512,2048]{1,0:T(8,128)(2,1)S(1)}, bf16[512,2048]{1,0:T(8,128)(2,1)}, u32[]{:S(2)}) copy-start(bf16[512,2048]{1,0:T(8,128)(2,1)} %param.24) | copy-start | bytes 6291460
  154.3 2.7 %collective-permute-start.2 = (bf16[512,1024]{1,0:T(8,128)(2,1)S(1)}, bf16[512,1024]{1,0:T(8,128)(2,1)S(1)}, u32[]{:S(2)}, u32[]{:S(2)}) collective-permute-start(bf16[512,1024]{1,0:T(8,128)(2,1)S(1)} %constant_dynamic-slice_fusion), channel_id=1, source_target_pairs={{0,1},{1,0},{2,3},{3,2},{4,5},{5,4},{6,7},{7,6},{8,9},{9,8},{10,11... | collective-permute-start | bytes 3145736 | tf_op jit(solution)/shard_map/ppermute | solution.py:65
Sparse Core Ops, SparseCore 0:
  12.6 44.2 all-gather.4
  81.0 27.9 all-gather.6
  158.6 26.6 reduce-scatter.1

commit v18 on v17

--- a/solution.py
+++ b/solution.py
@@ -28,15 +28,16 @@
     columns = rows_ref[...]
     gate_part = jnp.dot(gate_ref[0], columns, preferred_element_type=jnp.float32)
     up_part = jnp.dot(up_ref[0], columns, preferred_element_type=jnp.float32)
-    active = (gate_part / (1.0 + jnp.exp(-gate_part)) * up_part).astype(jnp.bfloat16)
+    active = gate_part / (1.0 + jnp.exp(-gate_part)) * up_part
+    active = (active * scale_ref[0]).astype(jnp.bfloat16)
     contract = (((0,), (0,)), ((), ()))
     result = lax.dot_general(active, down_ref[0], contract, preferred_element_type=jnp.float32)
-    out_ref[0] = (result * scale_ref[0]).astype(out_ref.dtype)
+    out_ref[0] = result.astype(out_ref.dtype)
 
 
 def expert_ffn(grouped_t, gate_weight, up_weight, down_weight, scale):
     feature_count = grouped_t.shape[0]
-    local_count, slot_count, _ = scale.shape
+    local_count, _, slot_count = scale.shape
     hidden = gate_weight.shape[2]
     gate_rows = jnp.transpose(gate_weight, (0, 2, 1))
     up_rows = jnp.transpose(up_weight, (0, 2, 1))
@@ -50,7 +51,7 @@
             pl.BlockSpec((1, hidden, feature_count), lambda j, m: (j, 0, 0)),
             pl.BlockSpec((1, hidden, feature_count), lambda j, m: (j, 0, 0)),
             pl.BlockSpec((1, hidden, feature_count), lambda j, m: (j, 0, 0)),
-            pl.BlockSpec((1, tile, 1), lambda j, m: (j, m, 0)),
+            pl.BlockSpec((1, 1, tile), lambda j, m: (j, 0, m)),
         ],
         out_specs=pl.BlockSpec((1, tile, feature_count), lambda j, m: (j, m, 0)),
         out_shape=jax.ShapeDtypeStruct((local_count, slot_count, feature_count), jnp.bfloat16),
@@ -240,7 +241,7 @@
         gate_weight,
         up_weight,
         down_weight,
-        slot_weight.reshape(local_count, slot_count, 1),
+        slot_weight.reshape(local_count, 1, slot_count),
     ).reshape(total_slots, feature_count)
     mixture = jnp.dot(combine, weighted, preferred_element_type=jnp.float32).astype(jnp.bfloat16)
     moe_cols = ffn_sum_scatter(mixture, ffn_index, ffn_size, 1).astype(jnp.bfloat16)

time: 192 us -> 190 us (0.990)
  no operation moved by 1% of the time
where the time goes in v18:
time: 190 us
  waiting for transfers between devices  92.7 us (49%)
  Pallas kernels  28.5 us (15%)
  local copies, waits for them, and re-layouts  20.5 us (11%)
  matrix products  19.9 us (10%)
  between operations  14.1 us (7%)
  other arithmetic  13.1 us (7%)
    all_gather x1, waiting for transfers between devices, local(): gathered = lax.all_gather(share, ('exp', 'ffn'), axis=0, tiled=False)  37.2 us
    pallas_call x1, Pallas kernels, expert_ffn(): pl.pallas_call(expert_kernel, grid=(local_count, tiles), in_specs=[pl.Blo...  28.5 us
    reduce_scatter x1, waiting for transfers between devices, local(): moe_out = lax.psum_scatter(moe_cols, 'exp', scatter_dimension=0, tiled=True)  26.8 us
    all_gather x1, waiting for transfers between devices, local(): lax.all_gather(normed_cols, ('ffn', 'exp'), axis=0, tiled=False)  24 us
    gather x1, local copies, waits for them, and re-layouts, local(): jnp.take(flat_pages, key_rows, axis=0, mode='clip')  6.36 us
    ppermute x3, waiting for transfers between devices, pair_swap(): return lax.ppermute(x, 'ffn', [(0, 1), (1, 0)])  4.62 us
    dot_general x1, matrix products, local(): jnp.dot(combine, weighted, preferred_element_type=jnp.float32)  4.52 us
    dot_general x1, matrix products, local(): jnp.einsum('ftc,ts->fcs', normed_grid, combine, preferred_element_type=jn...  4.33 us
  transfers between devices with their start and end apart: 6, of which 6 were waited for; matrix products, arithmetic and copies ran while one was open for 6% of the time, Pallas kernels for 0%

profile of v18, /device:TPU:0, one launch (start us, length us, event | category | flops | bytes accessed | tf_op | source)
XLA Modules:
  0.0 189.9 jit_solution(11353533512985446817)
XLA Ops:
  7.2 0.0 copy-start
  7.2 0.0 all-gather.5.cloned.1.call-start
  7.3 0.8 convert_element_type.98
  8.1 0.1 copy.32
  8.2 0.2 convert_element_type.99
  8.4 0.6 reshape.214
  9.0 1.1 copy.31
  10.1 0.2 reshape.213
  10.3 0.1 pad_dynamic-slice_fusion.3
  10.4 2.0 %fusion.24 = bf16[24,9216]{1,0:T(8,128)(2,1)} fusion(s32[]{:T(128)S(6)} %select_n.57, bf16[32,9216]{1,0:T(8,128)(2,1)} %param.18, bf16[8,9216]{1,0:T(8,128)(2,1)S(1)} %reshape.213, bf16[1,9216]{1,0:T(2,128)(2,1)} %reshape.214, bf16[24]{0:T(256)(128)(2,1)S(1)} %pad_dynamic-slice_fusion.3), kind=kLoop, calls=%fused_computation.43 | loop fusion | flops 1769472 | bytes 1198132 | tf_op jit(solution)/shard_map/concatenate | solution.py:126
  12.4 0.0 all-gather.5.cloned.1.call-update
  12.4 0.0 all-gather.7.cloned.1.call-start
  12.5 1.2 dynamic_slice.31
  13.8 1.2 dynamic_slice.32
  15.0 0.1 iota_add_fusion.1
  15.1 0.1 add.130
  15.2 1.0 copy.45
  16.2 0.3 copy.33
  16.5 0.7 fusion.30
  17.2 0.1 pad_add_fusion
  17.3 1.3 iota_compare_fusion.5
  18.6 1.0 and_or_fusion
  19.6 37.2 %all-gather.5.cloned.1.call-done = bf16[192,9216]{1,0:T(8,128)(2,1)} async-done(((bf16[24,9216]{1,0:T(8,128)(2,1)}), bf16[192,9216]{1,0:T(8,128)(2,1)}) %all-gather.5.cloned.1.call-update) | async-done | bytes 3538960 | tf_op jit(solution)/shard_map/all_gather | solution.py:136
  56.8 6.4 %gather_fusion = bf16[80,9216]{1,0:T(8,128)(2,1)} fusion(bf16[192,9216]{1,0:T(8,128)(2,1)} %all-gather.5.cloned.1.call-done, s32[1024]{0:T(1024)S(1)} %pad_clamp_fusion), kind=kCustom, calls=%fused_computation | custom fusion | bytes 2949440 | tf_op jit(solution)/shard_map/jit(_take)/gather | solution.py:159
  63.2 3.9 %reshape.215 = bf16[1280,576]{1,0:T(8,128)(2,1)} reshape(bf16[80,9216]{1,0:T(8,128)(2,1)} %gather_fusion) | data formatting | bytes 2949120 | tf_op jit(solution)/shard_map/reshape | solution.py:159
  67.0 2.6 %fusion.4 = f32[128,4,1280]{0,2,1:T(8,128)S(1)} fusion(bf16[128,4,576]{0,2,1:T(8,128)(2,1)S(1)} %bitcast.67, bf16[1280,576]{1,0:T(8,128)(2,1)} %reshape.215, pred[128,1280]{0,1:T(8,128)(4,1)S(1)} %and_or_fusion), kind=kOutput, calls=%fused_computation.8 | convolution fusion | flops 756285440 | bytes 4849664 | tf_op jit(solution)/shard_map/thd,kd->thk/dot_general | solution.py:164
  69.7 1.5 copy-done.2
  71.2 0.6 fusion.35
  71.8 0.4 copy-done.6
  72.2 4.2 %fusion.13 = bf16[4,128,128]{1,2,0:T(8,128)(2,1)S(1)} fusion(bf16[512,4,128]{0,2,1:T(8,128)(2,1)S(1)} %bitcast.68, bf16[1280,576]{1,0:T(8,128)(2,1)} %reshape.215, f32[128,4]{0,1:T(4,128)S(1)} %fusion.35, f32[128,4,1280]{0,2,1:T(8,128)} %copy-done.2), kind=kOutput, calls=%fused_computation.24 | convolution fusion | flops 740493056 | bytes 7211008 | tf_op jit(solution)/shard_map/thl,lhd->thd/dot_general | solution.py:180
  76.5 0.5 convolution_convert_fusion.2
  77.0 0.3 collective-permute-start
  77.3 1.3 collective-permute-done
  78.6 0.2 fusion.19
  78.8 0.3 collective-permute-start.1
  79.1 0.9 collective-permute-done.1
  80.0 0.8 fusion.21
  80.8 0.0 all-gather.7.cloned.1.call-update
  80.9 0.2 reduce-scatter.2.cloned.1.call-start
  81.1 0.1 add.134
  81.2 0.1 add.135
  81.3 1.1 slice.37
  82.5 0.2 reshape.225
  82.7 0.3 fusion.12
  83.0 0.1 copy.40
  83.1 0.2 convert_element_type.115
  83.3 0.1 add_select_fusion
  83.5 0.1 copy.38
  83.6 1.4 fusion.1
  85.0 24.0 %all-gather.7.cloned.1.call-done = bf16[1024,1024]{1,0:T(8,128)(2,1)} async-done(((bf16[128,1024]{1,0:T(8,128)(2,1)}), bf16[1024,1024]{1,0:T(8,128)(2,1)}) %all-gather.7.cloned.1.call-update) | async-done | bytes 2097168 | tf_op jit(solution)/shard_map/all_gather | solution.py:200
  109.0 1.8 fusion.15
  110.8 0.0 copy-done.3
  110.8 1.6 convolution_add_fusion
  112.4 0.1 select_reduce_fusion.1
  112.6 2.3 %select_reduce_fusion = f32[1024]{0:T(1024)} fusion(f32[512,6]{0,1:T(8,128)S(1)} %exponential_divide_fusion, s32[512,6]{0,1:T(8,128)S(1)} %copy.38), kind=kLoop, calls=%fused_computation.2 | loop fusion | flops 9436160 | bytes 28672 | tf_op jit(solution)/shard_map/reduce_sum | solution.py:235
  114.9 4.3 %convolution_convert_fusion.1 = bf16[2,1024,1024]{2,1,0:T(8,128)(2,1)} fusion(bf16[2,512,1024]{2,1,0:T(8,128)(2,1)S(1)} %bitcast.73, pred[512,1024]{1,0:T(8,128)(4,1)S(1)} %fusion.1), kind=kOutput, calls=%fused_computation.11 | convolution fusion | flops 2149580800 | bytes 6815744 | tf_op jit(solution)/shard_map/ftc,ts->fcs/dot_general | solution.py:236
  119.2 28.5 %shard_map.158 = bf16[8,128,2048]{2,1,0:T(8,128)(2,1)} custom-call(bf16[2048,1024]{1,0:T(8,128)(2,1)} %bitcast.66, bf16[8,704,2048]{2,1,0:T(8,128)(2,1)} %bitcast.63, bf16[8,704,2048]{2,1,0:T(8,128)(2,1)} %bitcast.64, bf16[8,704,2048]{2,1,0:T(8,128)(2,1)} %down_ref.1, f32[8,1,128]{2,1,0:T(1,128)} %bitcast.71), custom_call_target="tpu_custom_call" | custom-call | tf_op jit(solution)/shard_map/pallas_call | solution.py:46
  147.8 4.5 %convolution_convert_fusion = bf16[512,2048]{1,0:T(8,128)(2,1)S(1)} fusion(pred[512,1024]{1,0:T(8,128)(4,1)S(1)} %fusion.1, bf16[1024,2048]{1,0:T(8,128)(2,1)} %bitcast.65), kind=kOutput, calls=%fused_computation.10 | convolution fusion | flops 2148532224 | bytes 6815744 | tf_op jit(solution)/shard_map/dot_general | solution.py:246
  152.3 0.1 constant_dynamic-slice_fusion
  152.4 0.3 collective-permute-start.2
  152.7 2.4 %collective-permute-done.2 = bf16[512,1024]{1,0:T(8,128)(2,1)S(1)} collective-permute-done((bf16[512,1024]{1,0:T(8,128)(2,1)S(1)}, bf16[512,1024]{1,0:T(8,128)(2,1)S(1)}, u32[]{:S(2)}, u32[]{:S(2)}) %collective-permute-start.2) | collective-permute-done | bytes 1048608 | tf_op jit(solution)/shard_map/ppermute | solution.py:66
  155.1 1.4 add_convert_fusion
  156.5 0.0 reduce-scatter.2.cloned.1.call-update
  156.6 26.8 %reduce-scatter.2.cloned.1.call-done = bf16[128,1024]{1,0:T(8,128)(2,1)} async-done(((bf16[512,1024]{1,0:T(8,128)(2,1)}), bf16[128,1024]{1,0:T(8,128)(2,1)}) %reduce-scatter.2.cloned.1.call-update) | async-done | bytes 262160 | tf_op jit(solution)/shard_map/reduce_scatter | solution.py:248
  (34 shorter events, 0.2 us)
Async XLA Ops:
  7.2 69.3 %copy-start = (bf16[512,2048]{1,0:T(8,128)(2,1)S(1)}, bf16[512,2048]{1,0:T(8,128)(2,1)}, u32[]{:S(2)}) copy-start(bf16[512,2048]{1,0:T(8,128)(2,1)} %param.24) | copy-start | bytes 6291460
  7.2 8.0 %copy-start.5 = (bf16[512,512]{1,0:T(8,128)(2,1)S(1)}, bf16[512,512]{1,0:T(8,128)(2,1)}, u32[]{:S(2)}) copy-start(bf16[512,512]{1,0:T(8,128)(2,1)} %param.23) | copy-start | bytes 1572868
  7.2 9.0 %copy-start.4 = (bf16[128,2304]{1,0:T(8,128)(2,1)S(1)}, bf16[128,2304]{1,0:T(8,128)(2,1)}, u32[]{:S(2)}) copy-start(bf16[128,2304]{1,0:T(8,128)(2,1)} %param.16) | copy-start | bytes 1769476
  7.2 49.6 %all-gather.5.cloned.1.call-start = ((), (), s32[]{:S(2)}) async-start(), calls=%async_computation.2 | async-start | bytes 3981312 | tf_op jit(solution)/shard_map/all_gather | solution.py:136
  12.4 96.6 %all-gather.7.cloned.1.call-start = ((), (), s32[]{:S(2)}) async-start(), calls=%async_computation.3 | async-start | bytes 2359296 | tf_op jit(solution)/shard_map/all_gather | solution.py:200
  69.7 1.5 copy-start.2
  71.2 1.0 copy-start.6
  76.4 2.2 %copy-start.7 = (bf16[128,2048]{1,0:T(8,128)(2,1)S(1)}, bf16[128,2048]{1,0:T(8,128)(2,1)}, u32[]{:S(2)}) copy-start(bf16[128,2048]{1,0:T(8,128)(2,1)} %param.15) | copy-start | bytes 1572868
  76.4 2.7 %copy-start.8 = (bf16[2048]{0:T(1024)(128)(2,1)S(1)}, bf16[2048]{0:T(1024)(128)(2,1)}, u32[]{:S(2)}) copy-start(bf16[2048]{0:T(1024)(128)(2,1)} %param.25) | copy-start | bytes 12292
  77.0 1.6 collective-permute-start
  77.3 31.7 %copy-start.10 = (bf16[2048,32]{0,1:T(8,128)(2,1)S(1)}, bf16[2048,32]{0,1:T(8,128)(2,1)}, u32[]{:S(2)}) copy-start(bf16[2048,32]{0,1:T(8,128)(2,1)} %param.26) | copy-start | bytes 393220
  78.8 32.0 %copy-start.3 = (bf16[128,1024]{1,0:T(8,128)(2,1)}, bf16[128,1024]{1,0:T(8,128)(2,1)S(1)}, u32[]{:S(2)}) copy-start(bf16[128,1024]{1,0:T(8,128)(2,1)S(1)} %get-tuple-element.3) | copy-start | bytes 786436
  78.8 1.2 collective-permute-start.1
  80.9 102.5 %reduce-scatter.2.cloned.1.call-start = ((), (), s32[]{:S(2)}) async-start(), calls=%async_computation.1 | async-start | bytes 1310720 | tf_op jit(solution)/shard_map/reduce_scatter | solution.py:248
  109.0 5.9 %copy-start.9 = (bf16[1024,1024]{1,0:T(8,128)(2,1)S(1)}, bf16[1024,1024]{1,0:T(8,128)(2,1)}, u32[]{:S(2)}) copy-start(bf16[1024,1024]{1,0:T(8,128)(2,1)} %all-gather.7.cloned.1.call-done) | copy-start | bytes 6291460
  152.3 31.1 %copy-start.1 = (bf16[512,2048]{1,0:T(8,128)(2,1)S(1)}, bf16[512,2048]{1,0:T(8,128)(2,1)}, u32[]{:S(2)}) copy-start(bf16[512,2048]{1,0:T(8,128)(2,1)} %param.24) | copy-start | bytes 6291460
  152.4 2.7 %collective-permute-start.2 = (bf16[512,1024]{1,0:T(8,128)(2,1)S(1)}, bf16[512,1024]{1,0:T(8,128)(2,1)S(1)}, u32[]{:S(2)}, u32[]{:S(2)}) collective-permute-start(bf16[512,1024]{1,0:T(8,128)(2,1)S(1)} %constant_dynamic-slice_fusion), channel_id=1, source_target_pairs={{0,1},{1,0},{2,3},{3,2},{4,5},{5,4},{6,7},{7,6},{8,9},{9,8},{10,11... | collective-permute-start | bytes 3145736 | tf_op jit(solution)/shard_map/ppermute | solution.py:66
Sparse Core Ops, SparseCore 0:
  12.6 44.2 all-gather.4
  81.0 27.9 all-gather.6
  156.7 26.6 reduce-scatter.1

commit v19 on v18

--- a/solution.py
+++ b/solution.py
@@ -132,7 +132,10 @@
         ],
         axis=0,
     )
-    share = lax.dynamic_slice_in_dim(packed, ffn_index * share_rows, share_rows, 0)
+    share = lax.select_n(
+        ffn_index,
+        *[packed[part * share_rows : (part + 1) * share_rows] for part in range(ffn_size)],
+    )
     gathered = lax.all_gather(share, ("exp", "ffn"), axis=0, tiled=False)
     gathered = gathered.reshape(exp_size, ffn_size * share_rows, page_width)
     stride = ffn_size * share_rows

time: 190 us -> 190 us (level)
    concatenate x1 -> x0, other arithmetic: 2.04 us -> none  [local(): jnp.concatenate([cache_pool, new_latent.reshape(latent_pages, page_width)...]
    select_n x0 -> x1, other arithmetic: none -> 2.02 us  [local(): lax.select_n(ffn_index, *[packed[part * share_rows:(part + 1) * share_row...]
  transfers between devices with their start and end apart: 6 -> 6, of which waited for: 6 -> 6; matrix products, arithmetic and copies ran while one was open for 6% -> 5% of each run, Pallas kernels for 0% -> 0%
where the time goes in v19:
time: 190 us
  waiting for transfers between devices  93.9 us (49%)
  Pallas kernels  28.5 us (15%)
  matrix products  19.8 us (10%)
  local copies, waits for them, and re-layouts  19.2 us (10%)
  between operations  14.1 us (7%)
  other arithmetic  13.1 us (7%)
    all_gather x1, waiting for transfers between devices, local(): gathered = lax.all_gather(share, ('exp', 'ffn'), axis=0, tiled=False)  38.5 us
    pallas_call x1, Pallas kernels, expert_ffn(): pl.pallas_call(expert_kernel, grid=(local_count, tiles), in_specs=[pl.Blo...  28.5 us
    reduce_scatter x1, waiting for transfers between devices, local(): moe_out = lax.psum_scatter(moe_cols, 'exp', scatter_dimension=0, tiled=True)  26.8 us
    all_gather x1, waiting for transfers between devices, local(): lax.all_gather(normed_cols, ('ffn', 'exp'), axis=0, tiled=False)  24 us
    gather x1, local copies, waits for them, and re-layouts, local(): jnp.take(flat_pages, key_rows, axis=0, mode='clip')  6.36 us
    ppermute x3, waiting for transfers between devices, pair_swap(): return lax.ppermute(x, 'ffn', [(0, 1), (1, 0)])  4.58 us
    dot_general x1, matrix products, local(): jnp.dot(combine, weighted, preferred_element_type=jnp.float32)  4.52 us
    dot_general x1, matrix products, local(): jnp.einsum('ftc,ts->fcs', normed_grid, combine, preferred_element_type=jn...  4.32 us
  transfers between devices with their start and end apart: 6, of which 6 were waited for; matrix products, arithmetic and copies ran while one was open for 5% of the time, Pallas kernels for 0%

profile of v19, /device:TPU:0, one launch (start us, length us, event | category | flops | bytes accessed | tf_op | source)
XLA Modules:
  0.0 189.9 jit_solution(5672767825719355584)
XLA Ops:
  7.2 0.0 copy-start
  7.2 0.0 all-gather.5.cloned.1.call-start
  7.3 0.1 pad_slice_fusion
  7.4 0.8 convert_element_type.98
  8.2 0.1 copy.32
  8.3 0.2 convert_element_type.99
  8.5 0.6 reshape.214
  9.1 1.1 copy.31
  10.2 0.2 reshape.213
  10.4 2.0 %fusion.23 = bf16[24,9216]{1,0:T(8,128)(2,1)} fusion(bf16[1,9216]{1,0:T(2,128)(2,1)} %reshape.214, bf16[8,9216]{1,0:T(8,128)(2,1)S(1)} %reshape.213, bf16[32,9216]{1,0:T(8,128)(2,1)} %param.18, pred[]{:T(512)S(6)} %select_n.63, bf16[24]{0:T(256)(128)(2,1)S(1)} %pad_slice_fusion), kind=kLoop, calls=%fused_computation.40 | loop fusion | flops 1990656 | bytes 1658929 | tf_op jit(solution)/shard_map/select_n | solution.py:135
  12.4 0.0 all-gather.5.cloned.1.call-update
  12.4 0.0 all-gather.7.cloned.1.call-start
  12.5 0.6 dynamic_slice.28
  13.1 0.6 dynamic_slice.29
  13.7 0.1 iota_add_fusion.1
  13.8 0.1 add.126
  13.9 1.0 copy.45
  14.9 0.3 copy.33
  15.2 0.7 fusion.29
  15.9 0.1 pad_add_fusion
  16.0 1.3 iota_compare_fusion.5
  17.3 1.0 and_or_fusion
  18.3 38.5 %all-gather.5.cloned.1.call-done = bf16[192,9216]{1,0:T(8,128)(2,1)} async-done(((bf16[24,9216]{1,0:T(8,128)(2,1)}), bf16[192,9216]{1,0:T(8,128)(2,1)}) %all-gather.5.cloned.1.call-update) | async-done | bytes 3538960 | tf_op jit(solution)/shard_map/all_gather | solution.py:139
  56.8 6.4 %gather_fusion = bf16[80,9216]{1,0:T(8,128)(2,1)} fusion(bf16[192,9216]{1,0:T(8,128)(2,1)} %all-gather.5.cloned.1.call-done, s32[1024]{0:T(1024)S(1)} %pad_clamp_fusion), kind=kCustom, calls=%fused_computation | custom fusion | bytes 2949440 | tf_op jit(solution)/shard_map/jit(_take)/gather | solution.py:162
  63.2 3.9 %reshape.215 = bf16[1280,576]{1,0:T(8,128)(2,1)} reshape(bf16[80,9216]{1,0:T(8,128)(2,1)} %gather_fusion) | data formatting | bytes 2949120 | tf_op jit(solution)/shard_map/reshape | solution.py:162
  67.0 2.6 %fusion.4 = f32[128,4,1280]{0,2,1:T(8,128)S(1)} fusion(bf16[128,4,576]{0,2,1:T(8,128)(2,1)S(1)} %bitcast.67, bf16[1280,576]{1,0:T(8,128)(2,1)} %reshape.215, pred[128,1280]{0,1:T(8,128)(4,1)S(1)} %and_or_fusion), kind=kOutput, calls=%fused_computation.8 | convolution fusion | flops 756285440 | bytes 4849664 | tf_op jit(solution)/shard_map/thd,kd->thk/dot_general | solution.py:167
  69.7 1.5 copy-done.2
  71.2 0.6 fusion.34
  71.8 0.4 copy-done.6
  72.2 4.2 %fusion.13 = bf16[4,128,128]{1,2,0:T(8,128)(2,1)S(1)} fusion(bf16[512,4,128]{0,2,1:T(8,128)(2,1)S(1)} %bitcast.68, bf16[1280,576]{1,0:T(8,128)(2,1)} %reshape.215, f32[128,4]{0,1:T(4,128)S(1)} %fusion.34, f32[128,4,1280]{0,2,1:T(8,128)} %copy-done.2), kind=kOutput, calls=%fused_computation.24 | convolution fusion | flops 740493056 | bytes 7211008 | tf_op jit(solution)/shard_map/thl,lhd->thd/dot_general | solution.py:183
  76.5 0.5 convolution_convert_fusion.2
  77.0 0.3 collective-permute-start
  77.3 1.3 collective-permute-done
  78.6 0.2 fusion.19
  78.8 0.3 collective-permute-start.1
  79.1 0.9 collective-permute-done.1
  80.0 0.8 fusion.21
  80.9 0.0 all-gather.7.cloned.1.call-update
  80.9 0.2 reduce-scatter.2.cloned.1.call-start
  81.1 0.1 add.130
  81.2 0.1 add.131
  81.3 1.1 slice.46
  82.5 0.2 reshape.225
  82.7 0.3 fusion.12
  83.0 0.1 copy.40
  83.1 0.2 convert_element_type.115
  83.3 0.1 add_select_fusion
  83.5 0.1 copy.38
  83.6 1.4 fusion.1
  85.0 24.0 %all-gather.7.cloned.1.call-done = bf16[1024,1024]{1,0:T(8,128)(2,1)} async-done(((bf16[128,1024]{1,0:T(8,128)(2,1)}), bf16[1024,1024]{1,0:T(8,128)(2,1)}) %all-gather.7.cloned.1.call-update) | async-done | bytes 2097168 | tf_op jit(solution)/shard_map/all_gather | solution.py:203
  109.0 1.8 fusion.15
  110.8 0.0 copy-done.3
  110.8 1.6 convolution_add_fusion
  112.5 0.1 select_reduce_fusion.1
  112.6 2.3 %select_reduce_fusion = f32[1024]{0:T(1024)} fusion(f32[512,6]{0,1:T(8,128)S(1)} %exponential_divide_fusion, s32[512,6]{0,1:T(8,128)S(1)} %copy.38), kind=kLoop, calls=%fused_computation.2 | loop fusion | flops 9436160 | bytes 28672 | tf_op jit(solution)/shard_map/reduce_sum | solution.py:238
  114.9 4.3 %convolution_convert_fusion.1 = bf16[2,1024,1024]{2,1,0:T(8,128)(2,1)} fusion(bf16[2,512,1024]{2,1,0:T(8,128)(2,1)S(1)} %bitcast.73, pred[512,1024]{1,0:T(8,128)(4,1)S(1)} %fusion.1), kind=kOutput, calls=%fused_computation.11 | convolution fusion | flops 2149580800 | bytes 6815744 | tf_op jit(solution)/shard_map/ftc,ts->fcs/dot_general | solution.py:239
  119.2 28.5 %shard_map.158 = bf16[8,128,2048]{2,1,0:T(8,128)(2,1)} custom-call(bf16[2048,1024]{1,0:T(8,128)(2,1)} %bitcast.66, bf16[8,704,2048]{2,1,0:T(8,128)(2,1)} %bitcast.63, bf16[8,704,2048]{2,1,0:T(8,128)(2,1)} %bitcast.64, bf16[8,704,2048]{2,1,0:T(8,128)(2,1)} %down_ref.1, f32[8,1,128]{2,1,0:T(1,128)} %bitcast.71), custom_call_target="tpu_custom_call" | custom-call | tf_op jit(solution)/shard_map/pallas_call | solution.py:46
  147.8 4.5 %convolution_convert_fusion = bf16[512,2048]{1,0:T(8,128)(2,1)S(1)} fusion(pred[512,1024]{1,0:T(8,128)(4,1)S(1)} %fusion.1, bf16[1024,2048]{1,0:T(8,128)(2,1)} %bitcast.65), kind=kOutput, calls=%fused_computation.10 | convolution fusion | flops 2148532224 | bytes 6815744 | tf_op jit(solution)/shard_map/dot_general | solution.py:249
  152.3 0.1 constant_dynamic-slice_fusion
  152.4 0.3 collective-permute-start.2
  152.7 2.4 %collective-permute-done.2 = bf16[512,1024]{1,0:T(8,128)(2,1)S(1)} collective-permute-done((bf16[512,1024]{1,0:T(8,128)(2,1)S(1)}, bf16[512,1024]{1,0:T(8,128)(2,1)S(1)}, u32[]{:S(2)}, u32[]{:S(2)}) %collective-permute-start.2) | collective-permute-done | bytes 1048608 | tf_op jit(solution)/shard_map/ppermute | solution.py:66
  155.1 1.4 add_convert_fusion
  156.5 0.0 reduce-scatter.2.cloned.1.call-update
  156.6 26.8 %reduce-scatter.2.cloned.1.call-done = bf16[128,1024]{1,0:T(8,128)(2,1)} async-done(((bf16[512,1024]{1,0:T(8,128)(2,1)}), bf16[128,1024]{1,0:T(8,128)(2,1)}) %reduce-scatter.2.cloned.1.call-update) | async-done | bytes 262160 | tf_op jit(solution)/shard_map/reduce_scatter | solution.py:251
  (38 shorter events, 0.2 us)
Async XLA Ops:
  7.2 69.3 %copy-start = (bf16[512,2048]{1,0:T(8,128)(2,1)S(1)}, bf16[512,2048]{1,0:T(8,128)(2,1)}, u32[]{:S(2)}) copy-start(bf16[512,2048]{1,0:T(8,128)(2,1)} %param.24) | copy-start | bytes 6291460
  7.2 5.3 %copy-start.11 = (s32[8]{0:T(128)S(1)}, s32[8]{0:T(128)}, u32[]{:S(2)}) copy-start(s32[8]{0:T(128)} %param.21) | copy-start | bytes 100
  7.2 5.9 %copy-start.12 = (s32[8]{0:T(128)S(1)}, s32[8]{0:T(128)}, u32[]{:S(2)}) copy-start(s32[8]{0:T(128)} %param.20) | copy-start | bytes 100
  7.2 6.7 %copy-start.5 = (bf16[512,512]{1,0:T(8,128)(2,1)S(1)}, bf16[512,512]{1,0:T(8,128)(2,1)}, u32[]{:S(2)}) copy-start(bf16[512,512]{1,0:T(8,128)(2,1)} %param.23) | copy-start | bytes 1572868
  7.2 7.7 %copy-start.4 = (bf16[128,2304]{1,0:T(8,128)(2,1)S(1)}, bf16[128,2304]{1,0:T(8,128)(2,1)}, u32[]{:S(2)}) copy-start(bf16[128,2304]{1,0:T(8,128)(2,1)} %param.16) | copy-start | bytes 1769476
  7.2 49.6 %all-gather.5.cloned.1.call-start = ((), (), s32[]{:S(2)}) async-start(), calls=%async_computation.2 | async-start | bytes 3981312 | tf_op jit(solution)/shard_map/all_gather | solution.py:139
  12.4 96.6 %all-gather.7.cloned.1.call-start = ((), (), s32[]{:S(2)}) async-start(), calls=%async_computation.3 | async-start | bytes 2359296 | tf_op jit(solution)/shard_map/all_gather | solution.py:203
  69.7 1.5 copy-start.2
  71.2 1.0 copy-start.6
  76.5 2.1 %copy-start.7 = (bf16[128,2048]{1,0:T(8,128)(2,1)S(1)}, bf16[128,2048]{1,0:T(8,128)(2,1)}, u32[]{:S(2)}) copy-start(bf16[128,2048]{1,0:T(8,128)(2,1)} %param.15) | copy-start | bytes 1572868
  76.5 2.7 %copy-start.8 = (bf16[2048]{0:T(1024)(128)(2,1)S(1)}, bf16[2048]{0:T(1024)(128)(2,1)}, u32[]{:S(2)}) copy-start(bf16[2048]{0:T(1024)(128)(2,1)} %param.25) | copy-start | bytes 12292
  77.0 1.6 collective-permute-start
  77.3 31.7 %copy-start.10 = (bf16[2048,32]{0,1:T(8,128)(2,1)S(1)}, bf16[2048,32]{0,1:T(8,128)(2,1)}, u32[]{:S(2)}) copy-start(bf16[2048,32]{0,1:T(8,128)(2,1)} %param.26) | copy-start | bytes 393220
  78.8 32.0 %copy-start.3 = (bf16[128,1024]{1,0:T(8,128)(2,1)}, bf16[128,1024]{1,0:T(8,128)(2,1)S(1)}, u32[]{:S(2)}) copy-start(bf16[128,1024]{1,0:T(8,128)(2,1)S(1)} %get-tuple-element.3) | copy-start | bytes 786436
  78.8 1.2 collective-permute-start.1
  80.9 102.5 %reduce-scatter.2.cloned.1.call-start = ((), (), s32[]{:S(2)}) async-start(), calls=%async_computation.1 | async-start | bytes 1310720 | tf_op jit(solution)/shard_map/reduce_scatter | solution.py:251
  109.0 5.9 %copy-start.9 = (bf16[1024,1024]{1,0:T(8,128)(2,1)S(1)}, bf16[1024,1024]{1,0:T(8,128)(2,1)}, u32[]{:S(2)}) copy-start(bf16[1024,1024]{1,0:T(8,128)(2,1)} %all-gather.7.cloned.1.call-done) | copy-start | bytes 6291460
  152.3 31.1 %copy-start.1 = (bf16[512,2048]{1,0:T(8,128)(2,1)S(1)}, bf16[512,2048]{1,0:T(8,128)(2,1)}, u32[]{:S(2)}) copy-start(bf16[512,2048]{1,0:T(8,128)(2,1)} %param.24) | copy-start | bytes 6291460
  152.4 2.7 %collective-permute-start.2 = (bf16[512,1024]{1,0:T(8,128)(2,1)S(1)}, bf16[512,1024]{1,0:T(8,128)(2,1)S(1)}, u32[]{:S(2)}, u32[]{:S(2)}) collective-permute-start(bf16[512,1024]{1,0:T(8,128)(2,1)S(1)} %constant_dynamic-slice_fusion), channel_id=1, source_target_pairs={{0,1},{1,0},{2,3},{3,2},{4,5},{5,4},{6,7},{7,6},{8,9},{9,8},{10,11... | collective-permute-start | bytes 3145736 | tf_op jit(solution)/shard_map/ppermute | solution.py:66
Sparse Core Ops, SparseCore 0:
  12.5 44.2 all-gather.4
  81.0 27.9 all-gather.6
  156.7 26.6 reduce-scatter.1
